TPU v7x, 128 devices: a whole 4x4x4 slice. The times are simulated.
128 devices in a mesh: dp: 32 (over z, x_lo, y), seq: 4 (over x_hi, core).
Axes of the slice: x: 4 (x_hi: 2, x_lo: 2; x = x_hi * 2 + x_lo), y: 4, z: 4, core: 2. Of those that a mesh axis runs over, the one named last changes fastest.
Arguments:
- queries: bfloat16 [32, 1024, 2560], P('dp', 'seq'), may hold values from -6 to 6
- keys_in: bfloat16 [32, 1024, 2560], P('dp', 'seq'), may hold values from -6 to 6
- values_in: bfloat16 [32, 1024, 2560], P('dp', 'seq'), may hold values from -6 to 6
- head_gain: float32 [20, 128], replicated, may hold values from 0.1 to 1.9
- master_weight: float32 [2560, 5120], P('dp', 'seq'), may hold values from -0.125 to 0.125
- gradient: float32 [2560, 5120], P('dp', 'seq'), may hold values from -6 to 6
- first_moment: float32 [2560, 5120], P('dp', 'seq'), may hold values from -4 to 4
- second_moment: float32 [2560, 5120], P('dp', 'seq'), may hold values from 0.01 to 4
Outputs:
- layer_out: bfloat16 [32, 1024, 5120], P('dp', 'seq')
- new_master: float32 [2560, 5120], P('dp', 'seq')
- new_first: float32 [2560, 5120], P('dp', 'seq')
- new_second: float32 [2560, 5120], P('dp', 'seq')
All inputs are finite; a program needn't handle non-finite values.
Results may differ from a plain program's by a relative error of at most 0.0061.
Values may be sent and summed in bfloat16 or wider, within the bound.
No kernel may reach another device: no remote copies, remote signals or barrier semaphores. Data moves between devices by JAX's collectives and lax.ppermute only.
A program may use at most 192 MiB of HBM per device.

v0:
```python
import math

import jax
import jax.numpy as jnp
from jax import lax
from jax.sharding import PartitionSpec as P

HEAD = 128
H = 20
CH = 128


beta_one = 0.9
beta_two = 0.95
learn_rate = 0.0003
decay_rate = 0.1
adam_eps = 1e-08
step_count = 100
norm_eps = 1e-06


def featurize(block, seq_length):
    positions = jnp.arange(block.shape[0], dtype=jnp.int32).astype(jnp.float32)
    angles = positions * (math.pi / (2.0 * seq_length))
    rectified = jnp.maximum(block.astype(jnp.float32), 0.0)
    cosine = rectified * jnp.cos(angles)[:, None, None]
    sine = rectified * jnp.sin(angles)[:, None, None]
    return jnp.concatenate([cosine, sine], axis=2).astype(jnp.bfloat16)


def block_states(key_feat, value_heads):
    blocks = key_feat.shape[0] // CH
    key_blocks = key_feat.reshape(blocks, CH, key_feat.shape[1], key_feat.shape[2])
    value_blocks = value_heads.reshape(blocks, CH, value_heads.shape[1], value_heads.shape[2])
    return jnp.einsum(
        "cjhf,cjhe->chfe", key_blocks, value_blocks, preferred_element_type=jnp.float32
    )


def attend(query_feat, key_feat, value_heads, states):
    count = query_feat.shape[0]
    heads_here = query_feat.shape[1]
    blocks = count // CH
    query_blocks = query_feat.reshape(blocks, CH, heads_here, 2 * HEAD)
    key_blocks = key_feat.reshape(blocks, CH, heads_here, 2 * HEAD)
    value_blocks = value_heads.reshape(blocks, CH, heads_here, HEAD)
    scores = jnp.einsum(
        "cihf,cjhf->chij", query_blocks, key_blocks, preferred_element_type=jnp.float32
    )
    causal_mask = jnp.arange(CH)[:, None] >= jnp.arange(CH)[None, :]
    scores = jnp.where(causal_mask[None, None], scores, 0.0).astype(jnp.bfloat16)
    inside_block = jnp.einsum(
        "chij,cjhe->cihe", scores, value_blocks, preferred_element_type=jnp.float32
    )
    running = jnp.cumsum(states, axis=0)
    before = jnp.concatenate([jnp.zeros_like(states[:1]), running[:-1]], axis=0)
    before = before.astype(jnp.bfloat16)
    from_before = jnp.einsum(
        "cihf,chfe->cihe", query_blocks, before, preferred_element_type=jnp.float32
    )
    return (inside_block + from_before).reshape(count, heads_here, HEAD)


def normalize(attended, gain_rows):
    mean_square = jnp.mean(attended * attended, axis=2, keepdims=True)
    return (attended * lax.rsqrt(mean_square + norm_eps) * gain_rows[None]).astype(jnp.bfloat16)


def on_device(
    queries, keys_in, values_in, head_gain, master_weight, gradient, first_moment, second_moment
):
    moment_one = beta_one * first_moment + (1.0 - beta_one) * gradient
    moment_two = beta_two * second_moment + (1.0 - beta_two) * gradient * gradient
    corrected = (
        moment_one
        / (1.0 - beta_one**step_count)
        / (jnp.sqrt(moment_two / (1.0 - beta_two**step_count)) + adam_eps)
    )
    updated = master_weight - learn_rate * (corrected + decay_rate * master_weight)
    weights = updated.astype(jnp.bfloat16)
    tokens_here = queries.shape[1]
    seq_length = tokens_here * lax.axis_size("seq")
    query_heads = queries[0].reshape(tokens_here, H, HEAD)
    key_heads = keys_in[0].reshape(tokens_here, H, HEAD)
    value_heads = values_in[0].reshape(tokens_here, H, HEAD)
    query_group, key_group, value_group = (
        lax.all_to_all(query_heads, "seq", split_axis=1, concat_axis=0, tiled=True),
        lax.all_to_all(key_heads, "seq", split_axis=1, concat_axis=0, tiled=True),
        lax.all_to_all(value_heads, "seq", split_axis=1, concat_axis=0, tiled=True),
    )
    heads_here = query_group.shape[1]
    query_feat = featurize(query_group, seq_length)
    key_feat = featurize(key_group, seq_length)
    states = block_states(key_feat, value_group)
    attended = attend(query_feat, key_feat, value_group, states)
    gain_rows = lax.dynamic_slice_in_dim(
        head_gain, lax.axis_index("seq") * heads_here, heads_here, 0
    )
    normed_group = normalize(attended, gain_rows)
    normed_heads = lax.all_to_all(normed_group, "seq", split_axis=0, concat_axis=1, tiled=True)
    normed = normed_heads.reshape(tokens_here, H * HEAD)
    rows_wide = lax.all_gather(weights, "seq", axis=1, tiled=True)
    projected = jnp.dot(
        normed,
        lax.all_gather(rows_wide, "dp", axis=0, tiled=True),
        preferred_element_type=jnp.float32,
    )
    layer_out = projected.astype(jnp.bfloat16)[None]
    return (layer_out, updated, moment_one, moment_two)


def solution(mesh):
    in_specs = (
        P("dp", "seq", None),
        P("dp", "seq", None),
        P("dp", "seq", None),
        P(),
        P("dp", "seq"),
        P("dp", "seq"),
        P("dp", "seq"),
        P("dp", "seq"),
    )
    out_specs = (P("dp", "seq", None), P("dp", "seq"), P("dp", "seq"), P("dp", "seq"))
    return jax.shard_map(
        on_device, mesh=mesh, in_specs=in_specs, out_specs=out_specs, check_vma=False
    )
```

profile of v0, /device:TPU:1, one launch (start us, length us, event | category | flops | bytes accessed | tf_op | source)
XLA Modules:
  0.0 394.4 jit_solution(15426574116846061691)
XLA Ops:
  7.2 2.7 fusion.22
  9.9 12.1 %all_gather.6 = bf16[80,5120]{1,0:T(8,128)(2,1)} all-gather(bf16[80,1280]{1,0:T(8,128)(2,1)S(1)} %get-tuple-element.4), channel_id=1, replica_groups=mesh['dp'=32,'seq'=4] {'seq'}, dimensions={1}, use_global_device_ids=true | all-gather | bytes 1024000 | tf_op jit(solution)/shard_map/all_gather | solution.py:102
  22.1 1.5 copy.46
  23.5 4.0 %all-to-all-start = ((bf16[256,20,128]{0,2,1:T(8,128)(2,1)}), bf16[256,20,128]{0,2,1:T(8,128)(2,1)S(1)}, u32[]{:S(2)}, u32[]{:S(2)}) async-start(bf16[256,20,128]{0,2,1:T(8,128)(2,1)} %bitcast), calls=%async_computation | async-start | bytes 2621440 | tf_op jit(solution)/shard_map/all_to_all | solution.py:87
  27.6 1.4 copy.51
  29.0 26.0 %all-to-all-done = bf16[256,20,128]{0,2,1:T(8,128)(2,1)S(1)} async-done(((bf16[256,20,128]{0,2,1:T(8,128)(2,1)}), bf16[256,20,128]{0,2,1:T(8,128)(2,1)S(1)}, u32[]{:S(2)}, u32[]{:S(2)}) %all-to-all-start) | async-done | bytes 1310752 | tf_op jit(solution)/shard_map/all_to_all | solution.py:87
  55.0 5.2 %all-to-all-start.1 = ((bf16[256,20,128]{0,2,1:T(8,128)(2,1)}), bf16[256,20,128]{0,2,1:T(8,128)(2,1)S(1)}, u32[]{:S(2)}, u32[]{:S(2)}) async-start(bf16[256,20,128]{0,2,1:T(8,128)(2,1)} %bitcast.5), calls=%async_computation.1 | async-start | bytes 2621440 | tf_op jit(solution)/shard_map/all_to_all | solution.py:88
  60.2 2.5 copy.56
  62.7 28.8 %all-to-all-done.1 = bf16[256,20,128]{0,2,1:T(8,128)(2,1)S(1)} async-done(((bf16[256,20,128]{0,2,1:T(8,128)(2,1)}), bf16[256,20,128]{0,2,1:T(8,128)(2,1)S(1)}, u32[]{:S(2)}, u32[]{:S(2)}) %all-to-all-start.1) | async-done | bytes 1310752 | tf_op jit(solution)/shard_map/all_to_all | solution.py:88
  91.5 5.7 %all-to-all-start.2 = ((bf16[256,20,128]{0,2,1:T(8,128)(2,1)}), bf16[256,20,128]{0,2,1:T(8,128)(2,1)}, u32[]{:S(2)}, u32[]{:S(2)}) async-start(bf16[256,20,128]{0,2,1:T(8,128)(2,1)} %bitcast.10), calls=%async_computation.2 | async-start | bytes 2621440 | tf_op jit(solution)/shard_map/all_to_all | solution.py:89
  97.3 1.6 convert_maximum_fusion.1
  98.9 2.1 copy.48
  101.0 1.6 convert_maximum_fusion
  102.6 2.1 copy.53
  104.7 24.8 %all-to-all-done.2 = bf16[256,20,128]{0,2,1:T(8,128)(2,1)} async-done(((bf16[256,20,128]{0,2,1:T(8,128)(2,1)}), bf16[256,20,128]{0,2,1:T(8,128)(2,1)}, u32[]{:S(2)}, u32[]{:S(2)}) %all-to-all-start.2) | async-done | bytes 1310752 | tf_op jit(solution)/shard_map/all_to_all | solution.py:89
  129.5 2.5 copy.58
  131.9 3.7 multiply_convert_fusion.1
  135.6 1.1 copy-done.3
  138.8 5.7 %fusion.8 = f32[8,5,128,128]{3,2,1,0:T(8,128)} fusion(bf16[8,128,5,128]{3,1,2,0:T(8,128)(2,1)} %copy-done.4, bf16[8,128,5,128]{3,1,2,0:T(8,128)(2,1)} %copy-done.3, bf16[8,128,5,128]{3,1,2,0:T(8,128)(2,1)} %get-tuple-element.12, bf16[8,128,5,128]{3,1,2,0:T(8,128)(2,1)} %get-tuple-element.13, pred[128,128]{1,0:T(8,128)(4,1)S(1)} %iota_compare_fusion, ...), kind=kOutput, calls=%fused_computation.20 | convolution fusion | flops 515112960 | bytes 9191424 | tf_op jit(solution)/shard_map/chij,cjhe->cihe/dot_general | solution.py:52
  144.4 3.6 multiply_reduce_fusion
  150.3 52.4 %all_to_all.48 = bf16[1024,5,128]{2,1,0:T(8,128)(2,1)S(1)} all-to-all(bf16[1024,5,128]{2,1,0:T(8,128)(2,1)S(1)} %copy.63), channel_id=1, replica_groups=mesh['dp'=32,'seq'=4] {'seq'}, dimensions={0} | all-to-all | bytes 2621440 | tf_op jit(solution)/shard_map/all_to_all | solution.py:100
  202.7 1.1 copy.65
  203.9 169.8 %all-gather.2.cloned.1.call-done = bf16[2560,5120]{1,0:T(8,128)(2,1)} async-done(((bf16[80,5120]{1,0:T(8,128)(2,1)}), bf16[2560,5120]{1,0:T(8,128)(2,1)}) %all-gather.2.cloned.1.call-update) | async-done | bytes 26214416 | tf_op jit(solution)/shard_map/all_gather | solution.py:105
  373.6 13.9 %fusion = bf16[1,256,5120]{2,1,0:T(8,128)(2,1)} fusion(bf16[256,2560]{0,1:T(8,128)(2,1)S(1)} %bitcast.41, bf16[2560,5120]{1,0:T(8,128)(2,1)} %all-gather.2.cloned.1.call-done), kind=kOutput, calls=%fused_computation.1 | convolution fusion | flops 6712197120 | bytes 30146560 | tf_op jit(solution)/shard_map/dot_general | solution.py:103
  (31 shorter events, 4.5 us)
Async XLA Ops:
  7.2 90.1 %copy-start = (f32[20,128]{1,0:T(8,128)S(1)}, f32[20,128]{1,0:T(8,128)}, u32[]{:S(2)}) copy-start(f32[20,128]{1,0:T(8,128)} %param.11) | copy-start | bytes 30724
  7.2 14.9 %copy-start.8 = (bf16[1,256,2560]{2,1,0:T(8,128)(2,1)S(1)}, bf16[1,256,2560]{2,1,0:T(8,128)(2,1)}, u32[]{:S(2)}) copy-start(bf16[1,256,2560]{2,1,0:T(8,128)(2,1)} %param.8) | copy-start | bytes 3932164
  7.2 366.4 %all-gather.2.cloned.1.call-start = ((), (), s32[]{:S(2)}) async-start(), calls=%async_computation.4 | async-start | bytes 27033600 | tf_op jit(solution)/shard_map/all_gather | solution.py:105
  22.0 5.5 %copy-start.9 = (bf16[1,256,2560]{2,1,0:T(8,128)(2,1)S(1)}, bf16[1,256,2560]{2,1,0:T(8,128)(2,1)}, u32[]{:S(2)}) copy-start(bf16[1,256,2560]{2,1,0:T(8,128)(2,1)} %param.9) | copy-start | bytes 3932164
  23.5 31.5 %all-to-all-start = ((bf16[256,20,128]{0,2,1:T(8,128)(2,1)}), bf16[256,20,128]{0,2,1:T(8,128)(2,1)S(1)}, u32[]{:S(2)}, u32[]{:S(2)}) async-start(bf16[256,20,128]{0,2,1:T(8,128)(2,1)} %bitcast), calls=%async_computation | async-start | bytes 2621440 | tf_op jit(solution)/shard_map/all_to_all | solution.py:87
  55.0 7.7 %copy-start.6 = (bf16[256,20,128]{0,2,1:T(8,128)(2,1)}, bf16[256,20,128]{0,2,1:T(8,128)(2,1)S(1)}, u32[]{:S(2)}) copy-start(bf16[256,20,128]{0,2,1:T(8,128)(2,1)S(1)} %all-to-all-done) | copy-start | bytes 3932164
  55.0 36.5 %all-to-all-start.1 = ((bf16[256,20,128]{0,2,1:T(8,128)(2,1)}), bf16[256,20,128]{0,2,1:T(8,128)(2,1)S(1)}, u32[]{:S(2)}, u32[]{:S(2)}) async-start(bf16[256,20,128]{0,2,1:T(8,128)(2,1)} %bitcast.5), calls=%async_computation.1 | async-start | bytes 2621440 | tf_op jit(solution)/shard_map/all_to_all | solution.py:88
  91.5 5.8 %copy-start.7 = (bf16[256,20,128]{0,2,1:T(8,128)(2,1)}, bf16[256,20,128]{0,2,1:T(8,128)(2,1)S(1)}, u32[]{:S(2)}) copy-start(bf16[256,20,128]{0,2,1:T(8,128)(2,1)S(1)} %all-to-all-done.1) | copy-start | bytes 3932164
  91.5 37.9 %all-to-all-start.2 = ((bf16[256,20,128]{0,2,1:T(8,128)(2,1)}), bf16[256,20,128]{0,2,1:T(8,128)(2,1)}, u32[]{:S(2)}, u32[]{:S(2)}) async-start(bf16[256,20,128]{0,2,1:T(8,128)(2,1)} %bitcast.10), calls=%async_computation.2 | async-start | bytes 2621440 | tf_op jit(solution)/shard_map/all_to_all | solution.py:89
  104.7 27.2 %copy-start.2 = (f32[4,256,5,128]{3,1,0,2:T(8,128)S(1)}, f32[4,256,5,128]{3,1,0,2:T(8,128)}, u32[]{:S(2)}) copy-start(f32[4,256,5,128]{3,1,0,2:T(8,128)} %copy.48) | copy-start | bytes 7864324
  131.9 5.2 %copy-start.5 = (bf16[4,256,5,128]{3,1,0,2:T(8,128)(2,1)S(1)}, bf16[4,256,5,128]{3,1,0,2:T(8,128)(2,1)}, u32[]{:S(2)}) copy-start(bf16[4,256,5,128]{3,1,0,2:T(8,128)(2,1)} %copy.58) | copy-start | bytes 3932164
  135.6 1.1 copy-start.3
  135.6 1.5 copy-start.4
  373.6 13.9 %copy-start.1 = (f32[20,128]{1,0:T(8,128)S(1)}, f32[20,128]{1,0:T(8,128)}, u32[]{:S(2)}) copy-start(f32[20,128]{1,0:T(8,128)} %param.11) | copy-start | bytes 30724
Sparse Core Ops, SparseCore 0:
  22.2 351.4 all-gather.1
where the time goes:
time: 395 us; the launch traced here: 394 us
  waiting for transfers between devices  249 us (63%)
  blocking collectives  64.5 us (16%)
  matrix products  24 us (6%)
  local copies, waits for them, and re-layouts  16 us (4%)
  starting transfers between devices  15 us (4%)
  between operations  14.2 us (4%)
  other arithmetic  11.3 us (3%)
    all_gather x1, waiting for transfers between devices, on_device(): lax.all_gather(rows_wide, 'dp', axis=0, tiled=True)  170 us
    all_to_all x1, blocking collectives, on_device(): lax.all_to_all(normed_group, 'seq', split_axis=0, concat_axis=1, tiled=True)  52.4 us
    all_to_all x1, waiting for transfers between devices, on_device(): lax.all_to_all(key_heads, 'seq', split_axis=1, concat_axis=0, tiled=True)  28.8 us
    all_to_all x1, waiting for transfers between devices, on_device(): lax.all_to_all(query_heads, 'seq', split_axis=1, concat_axis=0, tiled=True)  26 us
    all_to_all x1, waiting for transfers between devices, on_device(): lax.all_to_all(value_heads, 'seq', split_axis=1, concat_axis=0, tiled=True)  24.8 us
    dot_general x1, matrix products, on_device(): jnp.dot(normed, lax.all_gather(rows_wide, 'dp', axis=0, tiled=True), pref...  13.9 us
    all_gather x1, blocking collectives, on_device(): rows_wide = lax.all_gather(weights, 'seq', axis=1, tiled=True)  12.1 us
  transfers between devices with their start and end apart: 4, of which 4 were waited for; matrix products, arithmetic and copies ran while one was open for 8% of the time, Pallas kernels for 0%

commit v1 on v0

--- a/solution.py
+++ b/solution.py
@@ -97,15 +97,12 @@
         head_gain, lax.axis_index("seq") * heads_here, heads_here, 0
     )
     normed_group = normalize(attended, gain_rows)
-    normed_heads = lax.all_to_all(normed_group, "seq", split_axis=0, concat_axis=1, tiled=True)
-    normed = normed_heads.reshape(tokens_here, H * HEAD)
-    rows_wide = lax.all_gather(weights, "seq", axis=1, tiled=True)
-    projected = jnp.dot(
-        normed,
-        lax.all_gather(rows_wide, "dp", axis=0, tiled=True),
-        preferred_element_type=jnp.float32,
-    )
-    layer_out = projected.astype(jnp.bfloat16)[None]
+    normed_all = lax.all_gather(normed_group, "seq", axis=1, tiled=True)
+    normed_all = normed_all.reshape(normed_all.shape[0], H * HEAD)
+    cols = lax.all_gather(weights, "dp", axis=0, tiled=True)
+    part = jnp.dot(normed_all, cols, preferred_element_type=jnp.float32).astype(jnp.bfloat16)
+    projected = lax.all_to_all(part, "seq", split_axis=0, concat_axis=1, tiled=True)
+    layer_out = projected[None]
     return (layer_out, updated, moment_one, moment_two)
 
 

time: 395 us -> 369 us (0.934)
  waiting for transfers between devices: 249 us -> 223 us
  local copies, waits for them, and re-layouts: 16 us -> 28 us
  blocking collectives: 64.5 us -> 56.4 us
    all_to_all x1, waiting for transfers between devices: 24.8 us -> 10.6 us  [on_device(): lax.all_to_all(value_heads, 'seq', split_axis=1, concat_axis=0, tiled=True)]
    all_to_all x1, waiting for transfers between devices: 28.8 us -> 15.5 us  [on_device(): lax.all_to_all(key_heads, 'seq', split_axis=1, concat_axis=0, tiled=True)]
    all_gather x1 -> x0, blocking collectives: 12.1 us -> none  [on_device(): rows_wide = lax.all_gather(weights, 'seq', axis=1, tiled=True)]
    all_gather x1 -> x2, waiting for transfers between devices: 170 us -> 180 us  [the longest x1 137 us: on_device(): cols = lax.all_gather(weights, 'dp', axis=0, tiled=True)]
    all_to_all x1, waiting for transfers between devices: 26 us -> 16.5 us  [on_device(): lax.all_to_all(query_heads, 'seq', split_axis=1, concat_axis=0, tiled=True)]
    all_gather x0 -> x1, local copies, waits for them, and re-layouts: none -> 7.92 us  [on_device(): normed_all = lax.all_gather(normed_group, 'seq', axis=1, tiled=True)]
    all_to_all x1, blocking collectives: 52.4 us -> 56.4 us  [on_device(): lax.all_to_all(part, 'seq', split_axis=0, concat_axis=1, tiled=True)]
    unnamed x23 -> x29, local copies, waits for them, and re-layouts: 6.89 us -> 7.91 us
  transfers between devices with their start and end apart: 4 -> 5, of which waited for: 4 -> 5; matrix products, arithmetic and copies ran while one was open for 8% -> 6% of each run, Pallas kernels for 0% -> 0%
where the time goes in v1:
time: 369 us
  waiting for transfers between devices  223 us (60%)
  blocking collectives  56.4 us (15%)
  local copies, waits for them, and re-layouts  28 us (8%)
  matrix products  20.9 us (6%)
  starting transfers between devices  15.3 us (4%)
  between operations  14.2 us (4%)
  other arithmetic  10.7 us (3%)
    all_gather x1, waiting for transfers between devices, on_device(): cols = lax.all_gather(weights, 'dp', axis=0, tiled=True)  137 us
    all_to_all x1, blocking collectives, on_device(): lax.all_to_all(part, 'seq', split_axis=0, concat_axis=1, tiled=True)  56.4 us
    all_gather x1, waiting for transfers between devices, on_device(): normed_all = lax.all_gather(normed_group, 'seq', axis=1, tiled=True)  43.9 us
    all_to_all x1, waiting for transfers between devices, on_device(): lax.all_to_all(query_heads, 'seq', split_axis=1, concat_axis=0, tiled=True)  16.5 us
    all_to_all x1, waiting for transfers between devices, on_device(): lax.all_to_all(key_heads, 'seq', split_axis=1, concat_axis=0, tiled=True)  15.5 us
    dot_general x1, matrix products, on_device(): jnp.dot(normed_all, cols, preferred_element_type=jnp.float32)  10.9 us
    all_to_all x1, waiting for transfers between devices, on_device(): lax.all_to_all(value_heads, 'seq', split_axis=1, concat_axis=0, tiled=True)  10.6 us
    all_gather x1, local copies, waits for them, and re-layouts, on_device(): normed_all = lax.all_gather(normed_group, 'seq', axis=1, tiled=True)  7.92 us
  transfers between devices with their start and end apart: 5, of which 5 were waited for; matrix products, arithmetic and copies ran while one was open for 6% of the time, Pallas kernels for 0%

profile of v1, /device:TPU:1, one launch (start us, length us, event | category | flops | bytes accessed | tf_op | source)
XLA Modules:
  0.0 368.6 jit_solution(1960539132442733777)
XLA Ops:
  7.2 2.5 copy.30
  9.7 5.8 %all-to-all-start = ((bf16[256,20,128]{0,2,1:T(8,128)(2,1)}), bf16[256,20,128]{0,2,1:T(8,128)(2,1)S(1)}, u32[]{:S(2)}, u32[]{:S(2)}) async-start(bf16[256,20,128]{0,2,1:T(8,128)(2,1)} %bitcast), calls=%async_computation | async-start | bytes 2621440 | tf_op jit(solution)/shard_map/all_to_all | solution.py:87
  17.0 16.5 %all-to-all-done = bf16[256,20,128]{0,2,1:T(8,128)(2,1)S(1)} async-done(((bf16[256,20,128]{0,2,1:T(8,128)(2,1)}), bf16[256,20,128]{0,2,1:T(8,128)(2,1)S(1)}, u32[]{:S(2)}, u32[]{:S(2)}) %all-to-all-start) | async-done | bytes 1310752 | tf_op jit(solution)/shard_map/all_to_all | solution.py:87
  33.4 4.4 %all-to-all-start.1 = ((bf16[256,20,128]{0,2,1:T(8,128)(2,1)}), bf16[256,20,128]{0,2,1:T(8,128)(2,1)S(1)}, u32[]{:S(2)}, u32[]{:S(2)}) async-start(bf16[256,20,128]{0,2,1:T(8,128)(2,1)} %bitcast.5), calls=%async_computation.1 | async-start | bytes 2621440 | tf_op jit(solution)/shard_map/all_to_all | solution.py:88
  37.8 2.4 copy.40
  40.2 15.5 %all-to-all-done.1 = bf16[256,20,128]{0,2,1:T(8,128)(2,1)S(1)} async-done(((bf16[256,20,128]{0,2,1:T(8,128)(2,1)}), bf16[256,20,128]{0,2,1:T(8,128)(2,1)S(1)}, u32[]{:S(2)}, u32[]{:S(2)}) %all-to-all-start.1) | async-done | bytes 1310752 | tf_op jit(solution)/shard_map/all_to_all | solution.py:88
  55.7 5.1 %all-to-all-start.2 = ((bf16[256,20,128]{0,2,1:T(8,128)(2,1)}), bf16[256,20,128]{0,2,1:T(8,128)(2,1)}, u32[]{:S(2)}, u32[]{:S(2)}) async-start(bf16[256,20,128]{0,2,1:T(8,128)(2,1)} %bitcast.10), calls=%async_computation.2 | async-start | bytes 2621440 | tf_op jit(solution)/shard_map/all_to_all | solution.py:89
  60.9 1.6 convert_maximum_fusion.1
  62.5 2.1 copy.32
  64.6 1.6 convert_maximum_fusion
  66.2 2.1 copy.37
  68.3 10.6 %all-to-all-done.2 = bf16[256,20,128]{0,2,1:T(8,128)(2,1)} async-done(((bf16[256,20,128]{0,2,1:T(8,128)(2,1)}), bf16[256,20,128]{0,2,1:T(8,128)(2,1)}, u32[]{:S(2)}, u32[]{:S(2)}) %all-to-all-start.2) | async-done | bytes 1310752 | tf_op jit(solution)/shard_map/all_to_all | solution.py:89
  78.9 2.4 copy.42
  81.3 3.7 multiply_convert_fusion.1
  88.1 5.6 %fusion.7 = f32[8,5,128,128]{3,2,1,0:T(8,128)} fusion(bf16[8,128,5,128]{3,1,2,0:T(8,128)(2,1)} %copy-done.4, bf16[8,128,5,128]{3,1,2,0:T(8,128)(2,1)} %copy-done.3, bf16[8,128,5,128]{3,1,2,0:T(8,128)(2,1)} %get-tuple-element.12, bf16[8,128,5,128]{3,1,2,0:T(8,128)(2,1)} %get-tuple-element.13, pred[128,128]{1,0:T(8,128)(4,1)S(1)} %iota_compare_fusion, ...), kind=kOutput, calls=%fused_computation.19 | convolution fusion | flops 515112960 | bytes 9191424 | tf_op jit(solution)/shard_map/chij,cjhe->cihe/dot_general | solution.py:52
  93.7 3.5 multiply_reduce_fusion
  97.6 1.9 fusion.1
  100.9 43.9 %all-gather.3.cloned.1.call-done = bf16[1024,20,128]{2,0,1:T(8,128)(2,1)} async-done(((bf16[1024,5,128]{2,0,1:T(8,128)(2,1)}), bf16[1024,20,128]{2,0,1:T(8,128)(2,1)}) %all-gather.3.cloned.1.call-update) | async-done | bytes 5242896 | tf_op jit(solution)/shard_map/all_gather | solution.py:100
  144.8 7.9 %copy.47 = bf16[1024,20,128]{0,2,1:T(8,128)(2,1)} copy(bf16[1024,20,128]{2,0,1:T(8,128)(2,1)} %all-gather.3.cloned.1.call-done) | data formatting | bytes 10485760 | tf_op jit(solution)/shard_map/all_gather | solution.py:100
  152.7 136.5 %all-gather.5.cloned.1.call-done = bf16[2560,1280]{1,0:T(8,128)(2,1)} async-done(((bf16[80,1280]{1,0:T(8,128)(2,1)}), bf16[2560,1280]{1,0:T(8,128)(2,1)}) %all-gather.5.cloned.1.call-update) | async-done | bytes 6553616 | tf_op jit(solution)/shard_map/all_gather | solution.py:102
  289.2 10.9 %convolution_convert_fusion = bf16[1024,1280]{1,0:T(8,128)(2,1)S(1)} fusion(bf16[1024,2560]{0,1:T(8,128)(2,1)} %bitcast.40, bf16[2560,1280]{1,0:T(8,128)(2,1)} %all-gather.5.cloned.1.call-done), kind=kOutput, calls=%fused_computation.1 | convolution fusion | flops 6712197120 | bytes 14417920 | tf_op jit(solution)/shard_map/dot_general | solution.py:103
  300.2 56.4 %all_to_all.49 = bf16[4,256,1280]{2,1,0:T(8,128)(2,1)S(1)} all-to-all(bf16[4,256,1280]{2,1,0:T(8,128)(2,1)S(1)} %bitcast.41), channel_id=1, replica_groups=mesh['dp'=32,'seq'=4] {'seq'}, dimensions={0} | all-to-all | bytes 5242880 | tf_op jit(solution)/shard_map/all_to_all | solution.py:104
  356.6 2.0 copy.48
  358.6 3.2 broadcast_in_dim.16
  (40 shorter events, 6.3 us)
Async XLA Ops:
  7.2 53.7 %copy-start = (f32[20,128]{1,0:T(8,128)S(1)}, f32[20,128]{1,0:T(8,128)}, u32[]{:S(2)}) copy-start(f32[20,128]{1,0:T(8,128)} %param.11) | copy-start | bytes 30724
  7.2 8.3 %copy-start.8 = (bf16[1,256,2560]{2,1,0:T(8,128)(2,1)S(1)}, bf16[1,256,2560]{2,1,0:T(8,128)(2,1)}, u32[]{:S(2)}) copy-start(bf16[1,256,2560]{2,1,0:T(8,128)(2,1)} %param.9) | copy-start | bytes 3932164
  9.7 23.7 %all-to-all-start = ((bf16[256,20,128]{0,2,1:T(8,128)(2,1)}), bf16[256,20,128]{0,2,1:T(8,128)(2,1)S(1)}, u32[]{:S(2)}, u32[]{:S(2)}) async-start(bf16[256,20,128]{0,2,1:T(8,128)(2,1)} %bitcast), calls=%async_computation | async-start | bytes 2621440 | tf_op jit(solution)/shard_map/all_to_all | solution.py:87
  33.4 6.8 %copy-start.6 = (bf16[256,20,128]{0,2,1:T(8,128)(2,1)}, bf16[256,20,128]{0,2,1:T(8,128)(2,1)S(1)}, u32[]{:S(2)}) copy-start(bf16[256,20,128]{0,2,1:T(8,128)(2,1)S(1)} %all-to-all-done) | copy-start | bytes 3932164
  33.4 22.3 %all-to-all-start.1 = ((bf16[256,20,128]{0,2,1:T(8,128)(2,1)}), bf16[256,20,128]{0,2,1:T(8,128)(2,1)S(1)}, u32[]{:S(2)}, u32[]{:S(2)}) async-start(bf16[256,20,128]{0,2,1:T(8,128)(2,1)} %bitcast.5), calls=%async_computation.1 | async-start | bytes 2621440 | tf_op jit(solution)/shard_map/all_to_all | solution.py:88
  55.7 5.2 %copy-start.7 = (bf16[256,20,128]{0,2,1:T(8,128)(2,1)}, bf16[256,20,128]{0,2,1:T(8,128)(2,1)S(1)}, u32[]{:S(2)}) copy-start(bf16[256,20,128]{0,2,1:T(8,128)(2,1)S(1)} %all-to-all-done.1) | copy-start | bytes 3932164
  55.7 23.1 %all-to-all-start.2 = ((bf16[256,20,128]{0,2,1:T(8,128)(2,1)}), bf16[256,20,128]{0,2,1:T(8,128)(2,1)}, u32[]{:S(2)}, u32[]{:S(2)}) async-start(bf16[256,20,128]{0,2,1:T(8,128)(2,1)} %bitcast.10), calls=%async_computation.2 | async-start | bytes 2621440 | tf_op jit(solution)/shard_map/all_to_all | solution.py:89
  60.9 83.9 %all-gather.3.cloned.1.call-start = ((), (), s32[]{:S(2)}) async-start(), calls=%async_computation.4 | async-start | bytes 6553600 | tf_op jit(solution)/shard_map/all_gather | solution.py:100
  68.3 13.0 %copy-start.2 = (f32[4,256,5,128]{3,1,0,2:T(8,128)S(1)}, f32[4,256,5,128]{3,1,0,2:T(8,128)}, u32[]{:S(2)}) copy-start(f32[4,256,5,128]{3,1,0,2:T(8,128)} %copy.32) | copy-start | bytes 7864324
  81.3 5.2 %copy-start.5 = (bf16[4,256,5,128]{3,1,0,2:T(8,128)(2,1)S(1)}, bf16[4,256,5,128]{3,1,0,2:T(8,128)(2,1)}, u32[]{:S(2)}) copy-start(bf16[4,256,5,128]{3,1,0,2:T(8,128)(2,1)} %copy.42) | copy-start | bytes 3932164
  85.0 1.1 copy-start.3
  85.0 1.5 copy-start.4
  97.6 2.0 copy-start.9
  97.6 2.0 copy-start.10
  97.6 2.0 copy-start.11
  97.6 2.0 copy-start.12
  99.5 189.7 %all-gather.5.cloned.1.call-start = ((), (), s32[]{:S(2)}) async-start(), calls=%async_computation.5 | async-start | bytes 6758400 | tf_op jit(solution)/shard_map/all_gather | solution.py:102
  356.6 5.2 %copy-start.1 = (f32[20,128]{1,0:T(8,128)S(1)}, f32[20,128]{1,0:T(8,128)}, u32[]{:S(2)}) copy-start(f32[20,128]{1,0:T(8,128)} %param.11) | copy-start | bytes 30724
Sparse Core Ops, SparseCore 0:
  99.6 45.1 all-gather.2
  146.4 142.7 all-gather.4

commit v2 on v1

--- a/solution.py
+++ b/solution.py
@@ -3,9 +3,11 @@
 import jax
 import jax.numpy as jnp
 from jax import lax
-from jax.sharding import PartitionSpec as P
+from jax.sharding import Mesh, PartitionSpec as P
 
 HEAD = 128
+DP = ("z", "xl", "y")
+SEQ = ("xh", "c")
 H = 20
 CH = 128
 
@@ -17,6 +19,45 @@
 adam_eps = 1e-08
 step_count = 100
 norm_eps = 1e-06
+
+
+def ring_gather(x, axis, size):
+    index = lax.axis_index(axis)
+    if size == 2:
+        other = lax.ppermute(x, axis, [(0, 1), (1, 0)])
+        stacked = jnp.stack([x, other])
+    else:
+        forward = [(k, (k + 1) % size) for k in range(size)]
+        backward = [(k, (k - 1) % size) for k in range(size)]
+        from_left = lax.ppermute(x, axis, forward)
+        from_right = lax.ppermute(x, axis, backward)
+        half = x.shape[0] // 2
+        far = jnp.concatenate(
+            [
+                lax.ppermute(from_left[:half], axis, forward),
+                lax.ppermute(from_right[half:], axis, backward),
+            ],
+            axis=0,
+        )
+        stacked = jnp.stack([x, from_left, far, from_right])
+    order = (index - jnp.arange(size)) % size
+    return jnp.take(stacked, order, axis=0)
+
+
+def gather_rows(weights):
+    width = weights.shape[1] // 2
+    pieces = []
+    for first, second in (("y", "z"), ("z", "y")):
+        part = weights[:, width * len(pieces) : width * (len(pieces) + 1)]
+        part = ring_gather(part, "xl", 2)
+        part = ring_gather(part, first, 4)
+        part = ring_gather(part, second, 4)
+        if first == "y":
+            part = jnp.transpose(part, (0, 2, 1, 3, 4))
+        else:
+            part = jnp.transpose(part, (1, 2, 0, 3, 4))
+        pieces.append(part.reshape(-1, width))
+    return jnp.concatenate(pieces, axis=1)
 
 
 def featurize(block, seq_length):
@@ -79,14 +120,14 @@
     updated = master_weight - learn_rate * (corrected + decay_rate * master_weight)
     weights = updated.astype(jnp.bfloat16)
     tokens_here = queries.shape[1]
-    seq_length = tokens_here * lax.axis_size("seq")
+    seq_length = tokens_here * lax.axis_size(SEQ)
     query_heads = queries[0].reshape(tokens_here, H, HEAD)
     key_heads = keys_in[0].reshape(tokens_here, H, HEAD)
     value_heads = values_in[0].reshape(tokens_here, H, HEAD)
     query_group, key_group, value_group = (
-        lax.all_to_all(query_heads, "seq", split_axis=1, concat_axis=0, tiled=True),
-        lax.all_to_all(key_heads, "seq", split_axis=1, concat_axis=0, tiled=True),
-        lax.all_to_all(value_heads, "seq", split_axis=1, concat_axis=0, tiled=True),
+        lax.all_to_all(query_heads, SEQ, split_axis=1, concat_axis=0, tiled=True),
+        lax.all_to_all(key_heads, SEQ, split_axis=1, concat_axis=0, tiled=True),
+        lax.all_to_all(value_heads, SEQ, split_axis=1, concat_axis=0, tiled=True),
     )
     heads_here = query_group.shape[1]
     query_feat = featurize(query_group, seq_length)
@@ -94,30 +135,24 @@
     states = block_states(key_feat, value_group)
     attended = attend(query_feat, key_feat, value_group, states)
     gain_rows = lax.dynamic_slice_in_dim(
-        head_gain, lax.axis_index("seq") * heads_here, heads_here, 0
+        head_gain, lax.axis_index(SEQ) * heads_here, heads_here, 0
     )
     normed_group = normalize(attended, gain_rows)
-    normed_all = lax.all_gather(normed_group, "seq", axis=1, tiled=True)
+    normed_all = lax.all_gather(normed_group, SEQ, axis=1, tiled=True)
     normed_all = normed_all.reshape(normed_all.shape[0], H * HEAD)
-    cols = lax.all_gather(weights, "dp", axis=0, tiled=True)
+    cols = gather_rows(weights)
     part = jnp.dot(normed_all, cols, preferred_element_type=jnp.float32).astype(jnp.bfloat16)
-    projected = lax.all_to_all(part, "seq", split_axis=0, concat_axis=1, tiled=True)
+    projected = lax.all_to_all(part, SEQ, split_axis=0, concat_axis=1, tiled=True)
     layer_out = projected[None]
     return (layer_out, updated, moment_one, moment_two)
 
 
 def solution(mesh):
-    in_specs = (
-        P("dp", "seq", None),
-        P("dp", "seq", None),
-        P("dp", "seq", None),
-        P(),
-        P("dp", "seq"),
-        P("dp", "seq"),
-        P("dp", "seq"),
-        P("dp", "seq"),
+    fine = Mesh(mesh.devices.reshape(4, 2, 4, 2, 2), DP + SEQ)
+    data = P(DP, SEQ, None)
+    blocks = P(DP, SEQ)
+    in_specs = (data, data, data, P(), blocks, blocks, blocks, blocks)
+    out_specs = (data, blocks, blocks, blocks)
+    return jax.shard_map(
+        on_device, mesh=fine, in_specs=in_specs, out_specs=out_specs, check_vma=False
     )
-    out_specs = (P("dp", "seq", None), P("dp", "seq"), P("dp", "seq"), P("dp", "seq"))
-    return jax.shard_map(
-        on_device, mesh=mesh, in_specs=in_specs, out_specs=out_specs, check_vma=False
-    )

time: 369 us -> 243 us (0.66)
  waiting for transfers between devices: 223 us -> 59.1 us
  starting transfers between devices: 15.3 us -> 40.1 us
  local copies, waits for them, and re-layouts: 28 us -> 44.7 us
  blocking collectives: 56.4 us -> 40.1 us
  other arithmetic: 10.7 us -> 23.6 us
    all_gather x2 -> x1, waiting for transfers between devices: 180 us -> 0.01 us  [on_device(): normed_all = lax.all_gather(normed_group, SEQ, axis=1, tiled=True)]
    ppermute x0 -> x18, starting transfers between devices: none -> 24.8 us  [the longest x4 11.8 us: ring_gather(): from_right = lax.ppermute(x, axis, backward)]
    ppermute x0 -> x18, waiting for transfers between devices: none -> 16.5 us  [the longest x4 8.74 us: ring_gather(): from_right = lax.ppermute(x, axis, backward)]
    all_to_all x1, blocking collectives: 56.4 us -> 40.1 us  [on_device(): lax.all_to_all(part, SEQ, split_axis=0, concat_axis=1, tiled=True)]
    gather x0 -> x6, local copies, waits for them, and re-layouts: none -> 7.91 us  [ring_gather(): return jnp.take(stacked, order, axis=0)]
    another operation x1 -> x13, other arithmetic: 3.68 us -> 10.6 us  [the longest x10 6.88 us: ring_gather(): stacked = jnp.stack([x, from_left, far, from_right])]
    transpose x0 -> x2, other arithmetic: none -> 4.67 us  [the longest x1 2.33 us: gather_rows(): part = jnp.transpose(part, (0, 2, 1, 3, 4))]
    slice x0 -> x8, local copies, waits for them, and re-layouts: none -> 4.16 us  [the longest x4 2.56 us: ring_gather(): from_left[:half]]
  transfers between devices with their start and end apart: 5 -> 22, of which waited for: 5 -> 9; matrix products, arithmetic and copies ran while one was open for 6% -> 17% of each run, Pallas kernels for 0% -> 0%
where the time goes in v2:
time: 243 us; the launch traced here: 242 us
  waiting for transfers between devices  59.1 us (24%)
  local copies, waits for them, and re-layouts  44.7 us (18%)
  starting transfers between devices  40.1 us (17%)
  blocking collectives  40.1 us (17%)
  other arithmetic  23.6 us (10%)
  matrix products  20.2 us (8%)
  between operations  14.5 us (6%)
    all_to_all x1, blocking collectives, on_device(): lax.all_to_all(part, SEQ, split_axis=0, concat_axis=1, tiled=True)  40.1 us
    all_to_all x1, waiting for transfers between devices, on_device(): lax.all_to_all(key_heads, SEQ, split_axis=1, concat_axis=0, tiled=True)  16.5 us
    all_to_all x1, waiting for transfers between devices, on_device(): lax.all_to_all(query_heads, SEQ, split_axis=1, concat_axis=0, tiled=True)  15.5 us
    ppermute x4, starting transfers between devices, ring_gather(): from_right = lax.ppermute(x, axis, backward)  11.8 us
    ppermute x4, starting transfers between devices, ring_gather(): lax.ppermute(from_right[half:], axis, backward)  11.3 us
    all_to_all x1, waiting for transfers between devices, on_device(): lax.all_to_all(value_heads, SEQ, split_axis=1, concat_axis=0, tiled=True)  10.6 us
    dot_general x1, matrix products, on_device(): jnp.dot(normed_all, cols, preferred_element_type=jnp.float32)  10.2 us
    ppermute x4, waiting for transfers between devices, ring_gather(): from_right = lax.ppermute(x, axis, backward)  8.74 us
  transfers between devices with their start and end apart: 22, of which 9 were waited for; matrix products, arithmetic and copies ran while one was open for 17% of the time, Pallas kernels for 0%

profile of v2, /device:TPU:1, one launch (start us, length us, event | category | flops | bytes accessed | tf_op | source)
XLA Modules:
  0.0 242.3 jit_solution(7159415101594072108)
XLA Ops:
  7.2 2.5 %copy.56 = bf16[1,256,2560]{1,2,0:T(8,128)(2,1)} copy(bf16[1,256,2560]{2,1,0:T(8,128)(2,1)} %param.15) | data formatting | bytes 2621440 | tf_op args[1]
  9.7 5.8 %all-to-all-start.1 = ((bf16[256,20,128]{0,2,1:T(8,128)(2,1)}), bf16[256,20,128]{0,2,1:T(8,128)(2,1)S(1)}, u32[]{:S(2)}, u32[]{:S(2)}) async-start(bf16[256,20,128]{0,2,1:T(8,128)(2,1)} %bitcast.5), calls=%async_computation.1 | async-start | bytes 2621440 | tf_op jit(solution)/shard_map/all_to_all | solution.py:129
  17.0 16.5 %all-to-all-done.1 = bf16[256,20,128]{0,2,1:T(8,128)(2,1)S(1)} async-done(((bf16[256,20,128]{0,2,1:T(8,128)(2,1)}), bf16[256,20,128]{0,2,1:T(8,128)(2,1)S(1)}, u32[]{:S(2)}, u32[]{:S(2)}) %all-to-all-start.1) | async-done | bytes 1310752 | tf_op jit(solution)/shard_map/all_to_all | solution.py:129
  33.4 4.4 %all-to-all-start = ((bf16[256,20,128]{0,2,1:T(8,128)(2,1)}), bf16[256,20,128]{0,2,1:T(8,128)(2,1)S(1)}, u32[]{:S(2)}, u32[]{:S(2)}) async-start(bf16[256,20,128]{0,2,1:T(8,128)(2,1)} %bitcast), calls=%async_computation | async-start | bytes 2621440 | tf_op jit(solution)/shard_map/all_to_all | solution.py:128
  40.2 15.5 %all-to-all-done = bf16[256,20,128]{0,2,1:T(8,128)(2,1)S(1)} async-done(((bf16[256,20,128]{0,2,1:T(8,128)(2,1)}), bf16[256,20,128]{0,2,1:T(8,128)(2,1)S(1)}, u32[]{:S(2)}, u32[]{:S(2)}) %all-to-all-start) | async-done | bytes 1310752 | tf_op jit(solution)/shard_map/all_to_all | solution.py:128
  55.7 5.1 %all-to-all-start.2 = ((bf16[256,20,128]{0,2,1:T(8,128)(2,1)}), bf16[256,20,128]{0,2,1:T(8,128)(2,1)}, u32[]{:S(2)}, u32[]{:S(2)}) async-start(bf16[256,20,128]{0,2,1:T(8,128)(2,1)} %bitcast.10), calls=%async_computation.2 | async-start | bytes 2621440 | tf_op jit(solution)/shard_map/all_to_all | solution.py:130
  68.3 10.6 %all-to-all-done.2 = bf16[256,20,128]{0,2,1:T(8,128)(2,1)} async-done(((bf16[256,20,128]{0,2,1:T(8,128)(2,1)}), bf16[256,20,128]{0,2,1:T(8,128)(2,1)}, u32[]{:S(2)}, u32[]{:S(2)}) %all-to-all-start.2) | async-done | bytes 1310752 | tf_op jit(solution)/shard_map/all_to_all | solution.py:130
  81.3 3.7 %multiply_convert_fusion.1 = (bf16[8,128,5,128]{3,1,2,0:T(8,128)(2,1)S(1)}, bf16[8,128,5,128]{3,1,2,0:T(8,128)(2,1)S(1)}, bf16[8,128,5,128]{3,1,2,0:T(8,128)(2,1)}, bf16[8,128,5,128]{3,1,2,0:T(8,128)(2,1)}) fusion(f32[8,128,5,128]{3,1,0,2:T(8,128)S(1)} %bitcast.69, f32[8,128]{1,0:T(8,128)S(1)} %get-tuple-element.26, f32[8,128]{1,0:T(8,128)S(1)} %get-tuple-element.25, ...), kind=kLoop, calls=%fused_computation.27 | loop fusion | flops 5242880 | bytes 10493952 | tf_op jit(solution)/shard_map/convert.3
  88.2 5.6 %fusion.14 = f32[8,5,128,128]{3,2,1,0:T(8,128)} fusion(bf16[8,128,5,128]{3,1,2,0:T(8,128)(2,1)} %copy-done.4, bf16[8,128,5,128]{3,1,2,0:T(8,128)(2,1)} %copy-done.3, bf16[8,128,5,128]{3,1,2,0:T(8,128)(2,1)} %get-tuple-element.19, bf16[8,128,5,128]{3,1,2,0:T(8,128)(2,1)} %get-tuple-element.20, pred[128,128]{1,0:T(8,128)(4,1)S(1)} %iota_compare_fusion, ...), kind=kOutput, calls=%fused_computation.33 | convolution fusion | flops 515112960 | bytes 9191424 | tf_op jit(solution)/shard_map/chij,cjhe->cihe/dot_general | solution.py:93
  93.8 3.6 %multiply_reduce_fusion = (f32[8,128,5]{1,2,0:T(8,128)S(1)}, f32[8,128,5,128]{3,1,2,0:T(8,128)S(1)}) fusion(bf16[7,5,256,128]{3,2,1,0:T(8,128)(2,1)S(1)} %slice.71, bf16[8,128,5,128]{3,1,2,0:T(8,128)(2,1)} %get-tuple-element.19, bf16[8,128,5,128]{3,1,2,0:T(8,128)(2,1)} %get-tuple-element.20, f32[8,5,128,128]{3,2,1,0:T(8,128)} %fusion.14), kind=kOutput, calls=%fused_computation.22 | convolution fusion | flops 342748160 | bytes 10178560 | tf_op jit(solution)/shard_map/cihf,chfe->cihe/dot_general | solution.py:99
  107.4 3.8 %collective-permute-start.12 = (bf16[2,80,640]{2,1,0:T(8,128)(2,1)S(1)}, bf16[2,80,640]{2,1,0:T(8,128)(2,1)S(1)}, u32[]{:S(2)}, u32[]{:S(2)}) collective-permute-start(bf16[2,80,640]{2,1,0:T(8,128)(2,1)S(1)} %get-tuple-element.22), channel_id=1, source_target_pairs={{0,96},{32,0},{64,32},{96,64},{1,97},{33,1},{65,33},{97,65},{2,98}... | collective-permute-start | bytes 614408 | tf_op jit(solution)/shard_map/ppermute | solution.py:33
  111.3 2.8 %collective-permute-start.3 = (bf16[2,80,640]{2,1,0:T(8,128)(2,1)S(1)}, bf16[2,80,640]{2,1,0:T(8,128)(2,1)S(1)}, u32[]{:S(2)}, u32[]{:S(2)}) collective-permute-start(bf16[2,80,640]{2,1,0:T(8,128)(2,1)S(1)} %get-tuple-element.21), channel_id=1, source_target_pairs={{0,12},{4,0},{8,4},{12,8},{1,13},{5,1},{9,5},{13,9},{2,14},{6,2},{... | collective-permute-start | bytes 614408 | tf_op jit(solution)/shard_map/ppermute | solution.py:33
  114.1 3.0 %collective-permute-start.13 = (bf16[1,80,640]{2,1,0:T(8,128)(2,1)S(1)}, bf16[1,80,640]{2,1,0:T(8,128)(2,1)S(1)}, u32[]{:S(2)}, u32[]{:S(2)}) collective-permute-start(bf16[1,80,640]{2,1,0:T(8,128)(2,1)S(1)} %slice.65), channel_id=1, source_target_pairs={{0,96},{32,0},{64,32},{96,64},{1,97},{33,1},{65,33},{97,65},{2,98}... | collective-permute-start | bytes 307208 | tf_op jit(solution)/shard_map/ppermute | solution.py:38
  118.3 2.7 %collective-permute-start.4 = (bf16[1,80,640]{2,1,0:T(8,128)(2,1)}, bf16[1,80,640]{2,1,0:T(8,128)(2,1)}, u32[]{:S(2)}, u32[]{:S(2)}) collective-permute-start(bf16[1,80,640]{2,1,0:T(8,128)(2,1)} %slice.60), channel_id=1, source_target_pairs={{0,12},{4,0},{8,4},{12,8},{1,13},{5,1},{9,5},{13,9},{2,14},{6,2},{... | collective-permute-start | bytes 307208 | tf_op jit(solution)/shard_map/ppermute | solution.py:38
  124.6 2.7 %collective-permute-start.16 = (bf16[4,2,80,640]{3,2,1,0:T(8,128)(2,1)}, bf16[4,2,80,640]{3,2,1,0:T(8,128)(2,1)S(1)}, u32[]{:S(2)}, u32[]{:S(2)}) collective-permute-start(bf16[4,2,80,640]{3,2,1,0:T(8,128)(2,1)} %broadcast_select_fusion), channel_id=1, source_target_pairs={{0,12},{4,0},{8,4},{12,8},{1,13},{5,1},{9,5},{13,9},{2,14},{6,2},{... | collective-permute-start | bytes 2457608 | tf_op jit(solution)/shard_map/ppermute | solution.py:33
  132.8 8.7 %collective-permute-done.16 = bf16[4,2,80,640]{3,2,1,0:T(8,128)(2,1)S(1)} collective-permute-done((bf16[4,2,80,640]{3,2,1,0:T(8,128)(2,1)}, bf16[4,2,80,640]{3,2,1,0:T(8,128)(2,1)S(1)}, u32[]{:S(2)}, u32[]{:S(2)}) %collective-permute-start.16) | collective-permute-done | bytes 819232 | tf_op jit(solution)/shard_map/ppermute | solution.py:33
  141.6 3.5 %collective-permute-start.17 = (bf16[2,2,80,640]{3,2,1,0:T(8,128)(2,1)S(1)}, bf16[2,2,80,640]{3,2,1,0:T(8,128)(2,1)S(1)}, u32[]{:S(2)}, u32[]{:S(2)}) collective-permute-start(bf16[2,2,80,640]{3,2,1,0:T(8,128)(2,1)S(1)} %slice.67), channel_id=1, source_target_pairs={{0,12},{4,0},{8,4},{12,8},{1,13},{5,1},{9,5},{13,9},{2,14},{6,2},{... | collective-permute-start | bytes 1228808 | tf_op jit(solution)/shard_map/ppermute | solution.py:38
  151.3 3.0 %collective-permute-done.15 = bf16[2,2,80,640]{3,2,1,0:T(8,128)(2,1)S(1)} collective-permute-done((bf16[2,2,80,640]{3,2,1,0:T(8,128)(2,1)S(1)}, bf16[2,2,80,640]{3,2,1,0:T(8,128)(2,1)S(1)}, u32[]{:S(2)}, u32[]{:S(2)}) %collective-permute-start.15) | collective-permute-done | bytes 409632 | tf_op jit(solution)/shard_map/ppermute | solution.py:37
  155.9 2.7 %gather_fusion.5 = bf16[4,4,2,80,640]{4,3,2,1,0:T(8,128)(2,1)} fusion(bf16[4,4,2,80,640]{4,3,2,1,0:T(8,128)(2,1)S(1)} %pad_maximum_fusion.1, s32[1024]{0:T(1024)S(1)} %pad_clamp_fusion.1), kind=kCustom, calls=%fused_computation.5.clone | custom fusion | bytes 6553616 | tf_op jit(solution)/shard_map/jit(_take)/gather | solution.py:44
  164.9 2.7 %gather_fusion.2 = bf16[4,4,2,80,640]{4,3,2,1,0:T(8,128)(2,1)} fusion(bf16[4,4,2,80,640]{4,3,2,1,0:T(8,128)(2,1)S(1)} %pad_maximum_fusion, s32[1024]{0:T(1024)S(1)} %pad_clamp_fusion), kind=kCustom, calls=%fused_computation.2.clone | custom fusion | bytes 6553616 | tf_op jit(solution)/shard_map/jit(_take)/gather | solution.py:44
  171.9 8.1 %copy.68 = bf16[1024,20,128]{0,2,1:T(8,128)(2,1)} copy(bf16[1024,20,128]{2,0,1:T(8,128)(2,1)} %all-gather.2.cloned.1.call-done) | data formatting | bytes 10485760 | tf_op jit(solution)/shard_map/all_gather | solution.py:141
  180.0 10.2 %fusion.4 = bf16[1024,1280]{1,0:T(8,128)(2,1)S(1)} fusion(bf16[1024,2560]{0,1:T(8,128)(2,1)} %bitcast.73, bf16[2560,640]{1,0:T(8,128)(2,1)S(1)} %bitcast.74, bf16[2560,640]{1,0:T(8,128)(2,1)} %bitcast.75), kind=kOutput, calls=%fused_computation.11 | convolution fusion | flops 6725304320 | bytes 14417920 | tf_op jit(solution)/shard_map/dot_general | solution.py:144
  190.2 40.1 %all_to_all.49 = bf16[4,256,1280]{2,1,0:T(8,128)(2,1)S(1)} all-to-all(bf16[4,256,1280]{2,1,0:T(8,128)(2,1)S(1)} %bitcast.76), channel_id=1, replica_groups=mesh['z'=4,'xl'=2,'y'=4,'xh'=2,'c'=2] {'xh','c'}, dimensions={0} | all-to-all | bytes 5242880 | tf_op jit(solution)/shard_map/all_to_all | solution.py:145
  232.3 3.2 %broadcast_in_dim.54 = bf16[1,256,5120]{2,1,0:T(8,128)(2,1)} reshape(bf16[256,4,1280]{2,1,0:T(4,128)(2,1)S(1)} %copy.71) | data formatting | bytes 5242880 | tf_op jit(solution)/shard_map/broadcast_in_dim | solution.py:146
  (136 shorter events, 57.5 us)
Async XLA Ops:
  7.2 53.7 %copy-start = (f32[20,128]{1,0:T(8,128)S(1)}, f32[20,128]{1,0:T(8,128)}, u32[]{:S(2)}) copy-start(f32[20,128]{1,0:T(8,128)} %param.17) | copy-start | bytes 30724
  9.7 23.7 %all-to-all-start.1 = ((bf16[256,20,128]{0,2,1:T(8,128)(2,1)}), bf16[256,20,128]{0,2,1:T(8,128)(2,1)S(1)}, u32[]{:S(2)}, u32[]{:S(2)}) async-start(bf16[256,20,128]{0,2,1:T(8,128)(2,1)} %bitcast.5), calls=%async_computation.1 | async-start | bytes 2621440 | tf_op jit(solution)/shard_map/all_to_all | solution.py:129
  33.4 22.3 %all-to-all-start = ((bf16[256,20,128]{0,2,1:T(8,128)(2,1)}), bf16[256,20,128]{0,2,1:T(8,128)(2,1)S(1)}, u32[]{:S(2)}, u32[]{:S(2)}) async-start(bf16[256,20,128]{0,2,1:T(8,128)(2,1)} %bitcast), calls=%async_computation | async-start | bytes 2621440 | tf_op jit(solution)/shard_map/all_to_all | solution.py:128
  55.7 23.2 %all-to-all-start.2 = ((bf16[256,20,128]{0,2,1:T(8,128)(2,1)}), bf16[256,20,128]{0,2,1:T(8,128)(2,1)}, u32[]{:S(2)}, u32[]{:S(2)}) async-start(bf16[256,20,128]{0,2,1:T(8,128)(2,1)} %bitcast.10), calls=%async_computation.2 | async-start | bytes 2621440 | tf_op jit(solution)/shard_map/all_to_all | solution.py:130
  60.9 111.1 %all-gather.2.cloned.1.call-start = ((), (), s32[]{:S(2)}) async-start(), calls=%async_computation.4 | async-start | bytes 6553600 | tf_op jit(solution)/shard_map/all_gather | solution.py:141
  68.3 13.0 %copy-start.2 = (f32[4,256,5,128]{3,1,0,2:T(8,128)S(1)}, f32[4,256,5,128]{3,1,0,2:T(8,128)}, u32[]{:S(2)}) copy-start(f32[4,256,5,128]{3,1,0,2:T(8,128)} %copy.58) | copy-start | bytes 7864324
  100.9 3.6 %collective-permute-start = (bf16[80,640]{1,0:T(8,128)(2,1)S(1)}, bf16[80,640]{1,0:T(8,128)(2,1)S(1)}, u32[]{:S(2)}, u32[]{:S(2)}) collective-permute-start(bf16[80,640]{1,0:T(8,128)(2,1)S(1)} %get-tuple-element.18), channel_id=1, source_target_pairs={{0,16},{16,0},{1,17},{17,1},{2,18},{18,2},{3,19},{19,3},{4,20},{20... | collective-permute-start | bytes 307208 | tf_op jit(solution)/shard_map/ppermute | solution.py:27
  101.4 5.3 %collective-permute-start.9 = (bf16[80,640]{1,0:T(8,128)(2,1)S(1)}, bf16[80,640]{1,0:T(8,128)(2,1)S(1)}, u32[]{:S(2)}, u32[]{:S(2)}) collective-permute-start(bf16[80,640]{1,0:T(8,128)(2,1)S(1)} %get-tuple-element.17), channel_id=1, source_target_pairs={{0,16},{16,0},{1,17},{17,1},{2,18},{18,2},{3,19},{19,3},{4,20},{20... | collective-permute-start | bytes 307208 | tf_op jit(solution)/shard_map/ppermute | solution.py:27
  107.4 6.7 %collective-permute-start.12 = (bf16[2,80,640]{2,1,0:T(8,128)(2,1)S(1)}, bf16[2,80,640]{2,1,0:T(8,128)(2,1)S(1)}, u32[]{:S(2)}, u32[]{:S(2)}) collective-permute-start(bf16[2,80,640]{2,1,0:T(8,128)(2,1)S(1)} %get-tuple-element.22), channel_id=1, source_target_pairs={{0,96},{32,0},{64,32},{96,64},{1,97},{33,1},{65,33},{97,65},{2,98}... | collective-permute-start | bytes 614408 | tf_op jit(solution)/shard_map/ppermute | solution.py:33
  111.3 6.2 %collective-permute-start.10 = (bf16[2,80,640]{2,1,0:T(8,128)(2,1)S(1)}, bf16[2,80,640]{2,1,0:T(8,128)(2,1)S(1)}, u32[]{:S(2)}, u32[]{:S(2)}) collective-permute-start(bf16[2,80,640]{2,1,0:T(8,128)(2,1)S(1)} %get-tuple-element.22), channel_id=1, source_target_pairs={{0,32},{32,64},{64,96},{96,0},{1,33},{33,65},{65,97},{97,1},{2,34}... | collective-permute-start | bytes 614408 | tf_op jit(solution)/shard_map/ppermute | solution.py:32
  111.3 6.3 %collective-permute-start.3 = (bf16[2,80,640]{2,1,0:T(8,128)(2,1)S(1)}, bf16[2,80,640]{2,1,0:T(8,128)(2,1)S(1)}, u32[]{:S(2)}, u32[]{:S(2)}) collective-permute-start(bf16[2,80,640]{2,1,0:T(8,128)(2,1)S(1)} %get-tuple-element.21), channel_id=1, source_target_pairs={{0,12},{4,0},{8,4},{12,8},{1,13},{5,1},{9,5},{13,9},{2,14},{6,2},{... | collective-permute-start | bytes 614408 | tf_op jit(solution)/shard_map/ppermute | solution.py:33
  114.1 7.0 %collective-permute-start.1 = (bf16[2,80,640]{2,1,0:T(8,128)(2,1)S(1)}, bf16[2,80,640]{2,1,0:T(8,128)(2,1)S(1)}, u32[]{:S(2)}, u32[]{:S(2)}) collective-permute-start(bf16[2,80,640]{2,1,0:T(8,128)(2,1)S(1)} %get-tuple-element.21), channel_id=1, source_target_pairs={{0,4},{4,8},{8,12},{12,0},{1,5},{5,9},{9,13},{13,1},{2,6},{6,10},{... | collective-permute-start | bytes 614408 | tf_op jit(solution)/shard_map/ppermute | solution.py:32
  114.1 7.6 %collective-permute-start.13 = (bf16[1,80,640]{2,1,0:T(8,128)(2,1)S(1)}, bf16[1,80,640]{2,1,0:T(8,128)(2,1)S(1)}, u32[]{:S(2)}, u32[]{:S(2)}) collective-permute-start(bf16[1,80,640]{2,1,0:T(8,128)(2,1)S(1)} %slice.65), channel_id=1, source_target_pairs={{0,96},{32,0},{64,32},{96,64},{1,97},{33,1},{65,33},{97,65},{2,98}... | collective-permute-start | bytes 307208 | tf_op jit(solution)/shard_map/ppermute | solution.py:38
  117.5 5.2 %collective-permute-start.11 = (bf16[1,80,640]{2,1,0:T(8,128)(2,1)S(1)}, bf16[1,80,640]{2,1,0:T(8,128)(2,1)S(1)}, u32[]{:S(2)}, u32[]{:S(2)}) collective-permute-start(bf16[1,80,640]{2,1,0:T(8,128)(2,1)S(1)} %slice.64), channel_id=1, source_target_pairs={{0,32},{32,64},{64,96},{96,0},{1,33},{33,65},{65,97},{97,1},{2,34}... | collective-permute-start | bytes 307208 | tf_op jit(solution)/shard_map/ppermute | solution.py:37
  118.3 9.0 %collective-permute-start.4 = (bf16[1,80,640]{2,1,0:T(8,128)(2,1)}, bf16[1,80,640]{2,1,0:T(8,128)(2,1)}, u32[]{:S(2)}, u32[]{:S(2)}) collective-permute-start(bf16[1,80,640]{2,1,0:T(8,128)(2,1)} %slice.60), channel_id=1, source_target_pairs={{0,12},{4,0},{8,4},{12,8},{1,13},{5,1},{9,5},{13,9},{2,14},{6,2},{... | collective-permute-start | bytes 307208 | tf_op jit(solution)/shard_map/ppermute | solution.py:38
  121.8 5.6 %collective-permute-start.2 = (bf16[1,80,640]{2,1,0:T(8,128)(2,1)}, bf16[1,80,640]{2,1,0:T(8,128)(2,1)}, u32[]{:S(2)}, u32[]{:S(2)}) collective-permute-start(bf16[1,80,640]{2,1,0:T(8,128)(2,1)} %slice.59), channel_id=1, source_target_pairs={{0,4},{4,8},{8,12},{12,0},{1,5},{5,9},{9,13},{13,1},{2,6},{6,10},{... | collective-permute-start | bytes 307208 | tf_op jit(solution)/shard_map/ppermute | solution.py:37
  124.6 16.9 %collective-permute-start.16 = (bf16[4,2,80,640]{3,2,1,0:T(8,128)(2,1)}, bf16[4,2,80,640]{3,2,1,0:T(8,128)(2,1)S(1)}, u32[]{:S(2)}, u32[]{:S(2)}) collective-permute-start(bf16[4,2,80,640]{3,2,1,0:T(8,128)(2,1)} %broadcast_select_fusion), channel_id=1, source_target_pairs={{0,12},{4,0},{8,4},{12,8},{1,13},{5,1},{9,5},{13,9},{2,14},{6,2},{... | collective-permute-start | bytes 2457608 | tf_op jit(solution)/shard_map/ppermute | solution.py:33
  127.3 17.7 %collective-permute-start.14 = (bf16[4,2,80,640]{3,2,1,0:T(8,128)(2,1)}, bf16[4,2,80,640]{3,2,1,0:T(8,128)(2,1)}, u32[]{:S(2)}, u32[]{:S(2)}) collective-permute-start(bf16[4,2,80,640]{3,2,1,0:T(8,128)(2,1)} %broadcast_select_fusion), channel_id=1, source_target_pairs={{0,4},{4,8},{8,12},{12,0},{1,5},{5,9},{9,13},{13,1},{2,6},{6,10},{... | collective-permute-start | bytes 2457608 | tf_op jit(solution)/shard_map/ppermute | solution.py:32
  130.4 17.1 %collective-permute-start.7 = (bf16[4,2,80,640]{3,2,1,0:T(8,128)(2,1)S(1)}, bf16[4,2,80,640]{3,2,1,0:T(8,128)(2,1)S(1)}, u32[]{:S(2)}, u32[]{:S(2)}) collective-permute-start(bf16[4,2,80,640]{3,2,1,0:T(8,128)(2,1)S(1)} %broadcast_select_fusion.1), channel_id=1, source_target_pairs={{0,96},{32,0},{64,32},{96,64},{1,97},{33,1},{65,33},{97,65},{2,98}... | collective-permute-start | bytes 2457608 | tf_op jit(solution)/shard_map/ppermute | solution.py:33
  132.8 17.5 %collective-permute-start.5 = (bf16[4,2,80,640]{3,2,1,0:T(8,128)(2,1)S(1)}, bf16[4,2,80,640]{3,2,1,0:T(8,128)(2,1)S(1)}, u32[]{:S(2)}, u32[]{:S(2)}) collective-permute-start(bf16[4,2,80,640]{3,2,1,0:T(8,128)(2,1)S(1)} %broadcast_select_fusion.1), channel_id=1, source_target_pairs={{0,32},{32,64},{64,96},{96,0},{1,33},{33,65},{65,97},{97,1},{2,34}... | collective-permute-start | bytes 2457608 | tf_op jit(solution)/shard_map/ppermute | solution.py:32
  141.6 9.5 %collective-permute-start.17 = (bf16[2,2,80,640]{3,2,1,0:T(8,128)(2,1)S(1)}, bf16[2,2,80,640]{3,2,1,0:T(8,128)(2,1)S(1)}, u32[]{:S(2)}, u32[]{:S(2)}) collective-permute-start(bf16[2,2,80,640]{3,2,1,0:T(8,128)(2,1)S(1)} %slice.67), channel_id=1, source_target_pairs={{0,12},{4,0},{8,4},{12,8},{1,13},{5,1},{9,5},{13,9},{2,14},{6,2},{... | collective-permute-start | bytes 1228808 | tf_op jit(solution)/shard_map/ppermute | solution.py:38
  146.1 8.2 %collective-permute-start.15 = (bf16[2,2,80,640]{3,2,1,0:T(8,128)(2,1)S(1)}, bf16[2,2,80,640]{3,2,1,0:T(8,128)(2,1)S(1)}, u32[]{:S(2)}, u32[]{:S(2)}) collective-permute-start(bf16[2,2,80,640]{3,2,1,0:T(8,128)(2,1)S(1)} %slice.66), channel_id=1, source_target_pairs={{0,4},{4,8},{8,12},{12,0},{1,5},{5,9},{9,13},{13,1},{2,6},{6,10},{... | collective-permute-start | bytes 1228808 | tf_op jit(solution)/shard_map/ppermute | solution.py:37
  148.3 14.8 %collective-permute-start.8 = (bf16[2,2,80,640]{3,2,1,0:T(8,128)(2,1)}, bf16[2,2,80,640]{3,2,1,0:T(8,128)(2,1)}, u32[]{:S(2)}, u32[]{:S(2)}) collective-permute-start(bf16[2,2,80,640]{3,2,1,0:T(8,128)(2,1)} %slice.62), channel_id=1, source_target_pairs={{0,96},{32,0},{64,32},{96,64},{1,97},{33,1},{65,33},{97,65},{2,98}... | collective-permute-start | bytes 1228808 | tf_op jit(solution)/shard_map/ppermute | solution.py:38
  151.1 12.0 %collective-permute-start.6 = (bf16[2,2,80,640]{3,2,1,0:T(8,128)(2,1)}, bf16[2,2,80,640]{3,2,1,0:T(8,128)(2,1)}, u32[]{:S(2)}, u32[]{:S(2)}) collective-permute-start(bf16[2,2,80,640]{3,2,1,0:T(8,128)(2,1)} %slice.61), channel_id=1, source_target_pairs={{0,32},{32,64},{64,96},{96,0},{1,33},{33,65},{65,97},{97,1},{2,34}... | collective-permute-start | bytes 1228808 | tf_op jit(solution)/shard_map/ppermute | solution.py:37
  (21 other events, 88.6 us)
Sparse Core Ops, SparseCore 0:
  99.7 45.1 all-gather.1

commit v3 on v2

--- a/solution.py
+++ b/solution.py
@@ -21,44 +21,65 @@
 norm_eps = 1e-06
 
 
-def ring_gather(x, axis, size):
+def ring_send(x, axis, size):
+    if size == 2:
+        return (lax.ppermute(x, axis, [(0, 1), (1, 0)]),)
+    forward = [(k, (k + 1) % size) for k in range(size)]
+    backward = [(k, (k - 1) % size) for k in range(size)]
+    return (lax.ppermute(x, axis, forward), lax.ppermute(x, axis, backward))
+
+
+def ring_far(received, axis, size):
+    if size == 2:
+        return received
+    forward = [(k, (k + 1) % size) for k in range(size)]
+    backward = [(k, (k - 1) % size) for k in range(size)]
+    from_left, from_right = received
+    half = from_left.shape[0] // 2
+    far = jnp.concatenate(
+        [
+            lax.ppermute(from_left[:half], axis, forward),
+            lax.ppermute(from_right[half:], axis, backward),
+        ],
+        axis=0,
+    )
+    return (from_left, far, from_right)
+
+
+def ring_finish(x, received, axis, size):
     index = lax.axis_index(axis)
-    if size == 2:
-        other = lax.ppermute(x, axis, [(0, 1), (1, 0)])
-        stacked = jnp.stack([x, other])
-    else:
-        forward = [(k, (k + 1) % size) for k in range(size)]
-        backward = [(k, (k - 1) % size) for k in range(size)]
-        from_left = lax.ppermute(x, axis, forward)
-        from_right = lax.ppermute(x, axis, backward)
-        half = x.shape[0] // 2
-        far = jnp.concatenate(
-            [
-                lax.ppermute(from_left[:half], axis, forward),
-                lax.ppermute(from_right[half:], axis, backward),
-            ],
-            axis=0,
-        )
-        stacked = jnp.stack([x, from_left, far, from_right])
+    stacked = jnp.stack((x,) + tuple(received))
     order = (index - jnp.arange(size)) % size
     return jnp.take(stacked, order, axis=0)
 
 
-def gather_rows(weights):
+def ring_gather(x, axis, size):
+    return ring_finish(x, ring_far(ring_send(x, axis, size), axis, size), axis, size)
+
+
+STAGES = (("y", "z"), ("z", "y"))
+
+
+def gather_start(weights):
     width = weights.shape[1] // 2
+    parts = []
+    for number, (first, _) in enumerate(STAGES):
+        part = weights[:, width * number : width * (number + 1)]
+        part = ring_gather(part, "xl", 2)
+        parts.append(ring_gather(part, first, 4))
+    return parts
+
+
+def gather_finish(parts, sent):
     pieces = []
-    for first, second in (("y", "z"), ("z", "y")):
-        part = weights[:, width * len(pieces) : width * (len(pieces) + 1)]
-        part = ring_gather(part, "xl", 2)
-        part = ring_gather(part, first, 4)
-        part = ring_gather(part, second, 4)
+    for part, received, (first, second) in zip(parts, sent, STAGES):
+        part = ring_finish(part, received, second, 4)
         if first == "y":
             part = jnp.transpose(part, (0, 2, 1, 3, 4))
         else:
             part = jnp.transpose(part, (1, 2, 0, 3, 4))
-        pieces.append(part.reshape(-1, width))
+        pieces.append(part.reshape(-1, part.shape[-1]))
     return jnp.concatenate(pieces, axis=1)
-
 
 def featurize(block, seq_length):
     positions = jnp.arange(block.shape[0], dtype=jnp.int32).astype(jnp.float32)
@@ -121,14 +142,19 @@
     weights = updated.astype(jnp.bfloat16)
     tokens_here = queries.shape[1]
     seq_length = tokens_here * lax.axis_size(SEQ)
-    query_heads = queries[0].reshape(tokens_here, H, HEAD)
-    key_heads = keys_in[0].reshape(tokens_here, H, HEAD)
-    value_heads = values_in[0].reshape(tokens_here, H, HEAD)
-    query_group, key_group, value_group = (
-        lax.all_to_all(query_heads, SEQ, split_axis=1, concat_axis=0, tiled=True),
-        lax.all_to_all(key_heads, SEQ, split_axis=1, concat_axis=0, tiled=True),
-        lax.all_to_all(value_heads, SEQ, split_axis=1, concat_axis=0, tiled=True),
+    parts = gather_start(weights)
+    parts, query_heads = lax.optimization_barrier(
+        (parts, queries[0].reshape(tokens_here, H, HEAD))
     )
+    query_group = lax.all_to_all(query_heads, SEQ, split_axis=1, concat_axis=0, tiled=True)
+    sent = [ring_send(part, second, 4) for part, (_, second) in zip(parts, STAGES)]
+    sent, key_heads = lax.optimization_barrier((sent, keys_in[0].reshape(tokens_here, H, HEAD)))
+    key_group = lax.all_to_all(key_heads, SEQ, split_axis=1, concat_axis=0, tiled=True)
+    sent = [ring_far(received, second, 4) for received, (_, second) in zip(sent, STAGES)]
+    sent, value_heads = lax.optimization_barrier(
+        (sent, values_in[0].reshape(tokens_here, H, HEAD))
+    )
+    value_group = lax.all_to_all(value_heads, SEQ, split_axis=1, concat_axis=0, tiled=True)
     heads_here = query_group.shape[1]
     query_feat = featurize(query_group, seq_length)
     key_feat = featurize(key_group, seq_length)
@@ -140,7 +166,7 @@
     normed_group = normalize(attended, gain_rows)
     normed_all = lax.all_gather(normed_group, SEQ, axis=1, tiled=True)
     normed_all = normed_all.reshape(normed_all.shape[0], H * HEAD)
-    cols = gather_rows(weights)
+    cols = gather_finish(parts, sent)
     part = jnp.dot(normed_all, cols, preferred_element_type=jnp.float32).astype(jnp.bfloat16)
     projected = lax.all_to_all(part, SEQ, split_axis=0, concat_axis=1, tiled=True)
     layer_out = projected[None]

time: 243 us -> 247 us (1.016)
  blocking collectives: 40.1 us -> 34.5 us
  starting transfers between devices: 40.1 us -> 45.5 us
  other arithmetic: 23.6 us -> 26.5 us
  waiting for transfers between devices: 59.1 us -> 56.4 us
    all_gather x1, waiting for transfers between devices: 0.01 us -> 25.3 us  [on_device(): normed_all = lax.all_gather(normed_group, SEQ, axis=1, tiled=True)]
    all_to_all x1, waiting for transfers between devices: 16.5 us -> 0.01 us  [on_device(): lax.all_to_all(key_heads, SEQ, split_axis=1, concat_axis=0, tiled=True)]
    all_to_all x1, waiting for transfers between devices: 15.5 us -> 0.01 us  [on_device(): lax.all_to_all(query_heads, SEQ, split_axis=1, concat_axis=0, tiled=True)]
    ppermute x18, waiting for transfers between devices: 16.5 us -> 24.8 us  [the longest x8 16.4 us: ring_send(): return (lax.ppermute(x, axis, forward), lax.ppermute(x, axis, backward))]
    all_to_all x1, blocking collectives: 40.1 us -> 34.5 us  [on_device(): lax.all_to_all(part, SEQ, split_axis=0, concat_axis=1, tiled=True)]
    all_to_all x1, waiting for transfers between devices: 10.6 us -> 6.29 us  [on_device(): lax.all_to_all(value_heads, SEQ, split_axis=1, concat_axis=0, tiled=True)]
    all_to_all x1, starting transfers between devices: 4.38 us -> 7.85 us  [on_device(): lax.all_to_all(query_heads, SEQ, split_axis=1, concat_axis=0, tiled=True)]
    concatenate x0 -> x2, other arithmetic: none -> 3.12 us  [ring_far(): jnp.concatenate([lax.ppermute(from_left[:half], axis, forward), lax.pperm...]
  transfers between devices with their start and end apart: 22 -> 22, of which waited for: 9 -> 11; matrix products, arithmetic and copies ran while one was open for 17% -> 20% of each run, Pallas kernels for 0% -> 0%
where the time goes in v3:
time: 247 us; the launch traced here: 246 us
  waiting for transfers between devices  56.4 us (23%)
  local copies, waits for them, and re-layouts  46.7 us (19%)
  starting transfers between devices  45.5 us (18%)
  blocking collectives  34.5 us (14%)
  other arithmetic  26.5 us (11%)
  matrix products  21.5 us (9%)
  between operations  14.4 us (6%)
    all_to_all x1, blocking collectives, on_device(): lax.all_to_all(part, SEQ, split_axis=0, concat_axis=1, tiled=True)  34.5 us
    all_gather x1, waiting for transfers between devices, on_device(): normed_all = lax.all_gather(normed_group, SEQ, axis=1, tiled=True)  25.3 us
    ppermute x8, waiting for transfers between devices, ring_send(): return (lax.ppermute(x, axis, forward), lax.ppermute(x, axis, backward))  16.4 us
    ppermute x8, starting transfers between devices, ring_send(): return (lax.ppermute(x, axis, forward), lax.ppermute(x, axis, backward))  12.4 us
    ppermute x4, starting transfers between devices, ring_far(): lax.ppermute(from_right[half:], axis, backward)  10.3 us
    dot_general x1, matrix products, on_device(): jnp.dot(normed_all, cols, preferred_element_type=jnp.float32)  10.2 us
    gather x6, local copies, waits for them, and re-layouts, ring_finish(): return jnp.take(stacked, order, axis=0)  8.81 us
    all_gather x1, local copies, waits for them, and re-layouts, on_device(): normed_all = lax.all_gather(normed_group, SEQ, axis=1, tiled=True)  7.94 us
  transfers between devices with their start and end apart: 22, of which 11 were waited for; matrix products, arithmetic and copies ran while one was open for 20% of the time, Pallas kernels for 0%

profile of v3, /device:TPU:1, one launch (start us, length us, event | category | flops | bytes accessed | tf_op | source)
XLA Modules:
  0.0 245.6 jit_solution(2964231010953412978)
XLA Ops:
  7.2 2.7 %fusion.32 = (bf16[80,1280]{1,0:T(8,128)(2,1)S(1)}, f32[80,1280]{1,0:T(8,128)}, f32[80,1280]{1,0:T(8,128)}, f32[80,1280]{1,0:T(8,128)}) fusion(f32[80,1280]{1,0:T(8,128)} %param.18, f32[80,1280]{1,0:T(8,128)} %param.19, f32[80,1280]{1,0:T(8,128)} %param.20, f32[80,1280]{1,0:T(8,128)} %param.21), kind=kLoop, calls=%fused_computation.89 | loop fusion | flops 1638400 | bytes 3072000 | tf_op jit(solution)/shard_map/convert_element_type | solution.py:142
  24.6 2.7 %collective-permute-start.4 = (bf16[1,80,640]{2,1,0:T(8,128)(2,1)S(1)}, bf16[1,80,640]{2,1,0:T(8,128)(2,1)S(1)}, u32[]{:S(2)}, u32[]{:S(2)}) collective-permute-start(bf16[1,80,640]{2,1,0:T(8,128)(2,1)S(1)} %slice.59), channel_id=1, source_target_pairs={{0,12},{4,0},{8,4},{12,8},{1,13},{5,1},{9,5},{13,9},{2,14},{6,2},{... | collective-permute-start | bytes 307208 | tf_op jit(solution)/shard_map/ppermute | solution.py:42
  36.1 7.8 %all-to-all-start.1 = ((bf16[256,20,128]{0,2,1:T(8,128)(2,1)}), bf16[256,20,128]{0,2,1:T(8,128)(2,1)S(1)}, u32[]{:S(2)}, u32[]{:S(2)}) async-start(bf16[256,20,128]{0,2,1:T(8,128)(2,1)} %bitcast.12), calls=%async_computation.1 | async-start | bytes 2621440 | tf_op jit(solution)/shard_map/all_to_all | solution.py:149
  47.1 2.7 %collective-permute-start.13 = (bf16[4,2,80,640]{3,2,1,0:T(8,128)(2,1)S(1)}, bf16[4,2,80,640]{3,2,1,0:T(8,128)(2,1)}, u32[]{:S(2)}, u32[]{:S(2)}) collective-permute-start(bf16[4,2,80,640]{3,2,1,0:T(8,128)(2,1)S(1)} %get-tuple-element.23), channel_id=1, source_target_pairs={{0,12},{4,0},{8,4},{12,8},{1,13},{5,1},{9,5},{13,9},{2,14},{6,2},{... | collective-permute-start | bytes 2457608 | tf_op jit(solution)/shard_map/ppermute | solution.py:29
  49.7 2.4 copy.52
  52.2 13.6 %collective-permute-done.10 = bf16[4,2,80,640]{3,2,1,0:T(8,128)(2,1)} collective-permute-done((bf16[4,2,80,640]{3,2,1,0:T(8,128)(2,1)S(1)}, bf16[4,2,80,640]{3,2,1,0:T(8,128)(2,1)}, u32[]{:S(2)}, u32[]{:S(2)}) %collective-permute-start.10) | collective-permute-done | bytes 819232 | tf_op jit(solution)/shard_map/ppermute | solution.py:29
  67.9 5.6 %all-to-all-start.2 = ((bf16[256,20,128]{0,2,1:T(8,128)(2,1)}), bf16[256,20,128]{0,2,1:T(8,128)(2,1)S(1)}, u32[]{:S(2)}, u32[]{:S(2)}) async-start(bf16[256,20,128]{0,2,1:T(8,128)(2,1)} %bitcast.13), calls=%async_computation.2 | async-start | bytes 2621440 | tf_op jit(solution)/shard_map/all_to_all | solution.py:152
  77.1 2.7 %collective-permute-start.17 = (bf16[2,2,80,640]{3,2,1,0:T(8,128)(2,1)}, bf16[2,2,80,640]{3,2,1,0:T(8,128)(2,1)S(1)}, u32[]{:S(2)}, u32[]{:S(2)}) collective-permute-start(bf16[2,2,80,640]{3,2,1,0:T(8,128)(2,1)} %slice.43), channel_id=1, source_target_pairs={{0,12},{4,0},{8,4},{12,8},{1,13},{5,1},{9,5},{13,9},{2,14},{6,2},{... | collective-permute-start | bytes 1228808 | tf_op jit(solution)/shard_map/ppermute | solution.py:42
  83.4 2.6 %collective-permute-start.15 = (bf16[2,2,80,640]{3,2,1,0:T(8,128)(2,1)}, bf16[2,2,80,640]{3,2,1,0:T(8,128)(2,1)}, u32[]{:S(2)}, u32[]{:S(2)}) collective-permute-start(bf16[2,2,80,640]{3,2,1,0:T(8,128)(2,1)} %slice.41), channel_id=1, source_target_pairs={{0,96},{32,0},{64,32},{96,64},{1,97},{33,1},{65,33},{97,65},{2,98}... | collective-permute-start | bytes 1228808 | tf_op jit(solution)/shard_map/ppermute | solution.py:42
  86.1 2.4 copy.53
  89.7 3.9 %collective-permute-done.14 = bf16[2,2,80,640]{3,2,1,0:T(8,128)(2,1)} collective-permute-done((bf16[2,2,80,640]{3,2,1,0:T(8,128)(2,1)}, bf16[2,2,80,640]{3,2,1,0:T(8,128)(2,1)}, u32[]{:S(2)}, u32[]{:S(2)}) %collective-permute-start.14) | collective-permute-done | bytes 409632 | tf_op jit(solution)/shard_map/ppermute | solution.py:41
  96.4 6.2 %all-to-all-start = ((bf16[256,20,128]{0,2,1:T(8,128)(2,1)}), bf16[256,20,128]{0,2,1:T(8,128)(2,1)}, u32[]{:S(2)}, u32[]{:S(2)}) async-start(bf16[256,20,128]{0,2,1:T(8,128)(2,1)} %bitcast.14), calls=%async_computation | async-start | bytes 2621440 | tf_op jit(solution)/shard_map/all_to_all | solution.py:157
  109.9 4.4 %multiply_convert_fusion.1 = (bf16[8,128,5,128]{3,1,2,0:T(8,128)(2,1)S(1)}, bf16[8,128,5,128]{3,1,2,0:T(8,128)(2,1)S(1)}, bf16[8,128,5,128]{3,1,2,0:T(8,128)(2,1)}, bf16[8,128,5,128]{3,1,2,0:T(8,128)(2,1)}) fusion(f32[8,128,5,128]{3,1,0,2:T(8,128)} %bitcast.64, f32[8,128]{1,0:T(8,128)S(1)} %get-tuple-element.58, f32[8,128]{1,0:T(8,128)S(1)} %get-tuple-element.57, ...), kind=kLoop, calls=%fused_computation.27 | loop fusion | flops 5242880 | bytes 10493952 | tf_op jit(solution)/shard_map/convert.3
  114.3 6.3 %all-to-all-done = bf16[256,20,128]{0,2,1:T(8,128)(2,1)} async-done(((bf16[256,20,128]{0,2,1:T(8,128)(2,1)}), bf16[256,20,128]{0,2,1:T(8,128)(2,1)}, u32[]{:S(2)}, u32[]{:S(2)}) %all-to-all-start) | async-done | bytes 1310752 | tf_op jit(solution)/shard_map/all_to_all | solution.py:157
  120.6 2.4 copy.55
  126.1 5.6 %fusion.14 = f32[8,5,128,128]{2,3,1,0:T(8,128)} fusion(bf16[8,128,5,128]{3,1,2,0:T(8,128)(2,1)} %copy-done.3, bf16[8,128,5,128]{3,1,2,0:T(8,128)(2,1)} %copy-done.2, bf16[8,128,5,128]{3,1,2,0:T(8,128)(2,1)} %get-tuple-element.49, bf16[8,128,5,128]{3,1,2,0:T(8,128)(2,1)} %get-tuple-element.50, pred[128,128]{1,0:T(8,128)(4,1)S(1)} %iota_compare_fusion, ...), kind=kOutput, calls=%fused_computation.33 | convolution fusion | flops 515112960 | bytes 9191424 | tf_op jit(solution)/shard_map/chij,cjhe->cihe/dot_general | solution.py:114
  131.6 3.5 %multiply_reduce_fusion = (f32[8,128,5]{1,2,0:T(8,128)S(1)}, f32[8,128,5,128]{3,1,2,0:T(8,128)S(1)}) fusion(f32[8,5,128,128]{2,3,1,0:T(8,128)} %fusion.14, bf16[7,5,256,128]{3,2,1,0:T(8,128)(2,1)S(1)} %slice.67, bf16[8,128,5,128]{3,1,2,0:T(8,128)(2,1)} %get-tuple-element.49, bf16[8,128,5,128]{3,1,2,0:T(8,128)(2,1)} %get-tuple-element.50), kind=kOutput, calls=%fused_computation.21 | convolution fusion | flops 342748160 | bytes 10178560 | tf_op jit(solution)/shard_map/cihf,chfe->cihe/dot_general | solution.py:120
  139.5 2.7 %gather_fusion.4 = bf16[4,4,2,80,640]{4,3,2,1,0:T(8,128)(2,1)} fusion(bf16[4,4,2,80,640]{4,3,2,1,0:T(8,128)(2,1)S(1)} %pad_maximum_fusion, s32[1024]{0:T(1024)S(1)} %pad_clamp_fusion), kind=kCustom, calls=%fused_computation.2.clone | custom fusion | bytes 6553616 | tf_op jit(solution)/shard_map/jit(_take)/gather | solution.py:53
  148.6 2.7 %gather_fusion.5 = bf16[4,4,2,80,640]{4,3,2,1,0:T(8,128)(2,1)} fusion(bf16[4,4,2,80,640]{4,3,2,1,0:T(8,128)(2,1)S(1)} %pad_maximum_fusion.1, s32[1024]{0:T(1024)S(1)} %pad_clamp_fusion.1), kind=kCustom, calls=%fused_computation.5.clone | custom fusion | bytes 6553616 | tf_op jit(solution)/shard_map/jit(_take)/gather | solution.py:53
  155.6 25.3 %all-gather.2.cloned.1.call-done = bf16[1024,20,128]{2,0,1:T(8,128)(2,1)} async-done(((bf16[1024,5,128]{2,0,1:T(8,128)(2,1)}), bf16[1024,20,128]{2,0,1:T(8,128)(2,1)}) %all-gather.2.cloned.1.call-update) | async-done | bytes 5242896 | tf_op jit(solution)/shard_map/all_gather | solution.py:167
  180.9 7.9 %copy.68 = bf16[1024,20,128]{0,2,1:T(8,128)(2,1)} copy(bf16[1024,20,128]{2,0,1:T(8,128)(2,1)} %all-gather.2.cloned.1.call-done) | data formatting | bytes 10485760 | tf_op jit(solution)/shard_map/all_gather | solution.py:167
  188.8 10.2 %fusion.4 = bf16[1024,1280]{1,0:T(8,128)(2,1)S(1)} fusion(bf16[1024,2560]{0,1:T(8,128)(2,1)} %bitcast.67, bf16[2560,640]{1,0:T(8,128)(2,1)} %bitcast.73, bf16[2560,640]{1,0:T(8,128)(2,1)S(1)} %bitcast.72), kind=kOutput, calls=%fused_computation.11 | convolution fusion | flops 6725304320 | bytes 14417920 | tf_op jit(solution)/shard_map/dot_general | solution.py:170
  199.0 34.5 %all_to_all.49 = bf16[4,256,1280]{2,1,0:T(8,128)(2,1)S(1)} all-to-all(bf16[4,256,1280]{2,1,0:T(8,128)(2,1)S(1)} %bitcast.74), channel_id=1, replica_groups=mesh['z'=4,'xl'=2,'y'=4,'xh'=2,'c'=2] {'xh','c'}, dimensions={0} | all-to-all | bytes 5242880 | tf_op jit(solution)/shard_map/all_to_all | solution.py:171
  235.6 3.2 %broadcast_in_dim.54 = bf16[1,256,5120]{2,1,0:T(8,128)(2,1)} reshape(bf16[256,4,1280]{2,1,0:T(4,128)(2,1)S(1)} %copy.71) | data formatting | bytes 5242880 | tf_op jit(solution)/shard_map/broadcast_in_dim | solution.py:172
  (111 shorter events, 67.1 us)
Async XLA Ops:
  7.2 78.9 %copy-start = (f32[20,128]{1,0:T(8,128)S(1)}, f32[20,128]{1,0:T(8,128)}, u32[]{:S(2)}) copy-start(f32[20,128]{1,0:T(8,128)} %param.17) | copy-start | bytes 30724
  9.9 4.2 %collective-permute-start = (bf16[80,640]{1,0:T(8,128)(2,1)S(1)}, bf16[80,640]{1,0:T(8,128)(2,1)S(1)}, u32[]{:S(2)}, u32[]{:S(2)}) collective-permute-start(bf16[80,640]{1,0:T(8,128)(2,1)S(1)} %get-tuple-element.48), channel_id=1, source_target_pairs={{0,16},{16,0},{1,17},{17,1},{2,18},{18,2},{3,19},{19,3},{4,20},{20... | collective-permute-start | bytes 307208 | tf_op jit(solution)/shard_map/ppermute | solution.py:26
  12.0 4.9 %collective-permute-start.5 = (bf16[80,640]{1,0:T(8,128)(2,1)S(1)}, bf16[80,640]{1,0:T(8,128)(2,1)S(1)}, u32[]{:S(2)}, u32[]{:S(2)}) collective-permute-start(bf16[80,640]{1,0:T(8,128)(2,1)S(1)} %get-tuple-element.47), channel_id=1, source_target_pairs={{0,16},{16,0},{1,17},{17,1},{2,18},{18,2},{3,19},{19,3},{4,20},{20... | collective-permute-start | bytes 307208 | tf_op jit(solution)/shard_map/ppermute | solution.py:26
  17.7 6.7 %collective-permute-start.1 = (bf16[2,80,640]{2,1,0:T(8,128)(2,1)S(1)}, bf16[2,80,640]{2,1,0:T(8,128)(2,1)S(1)}, u32[]{:S(2)}, u32[]{:S(2)}) collective-permute-start(bf16[2,80,640]{2,1,0:T(8,128)(2,1)S(1)} %get-tuple-element.52), channel_id=1, source_target_pairs={{0,4},{4,8},{8,12},{12,0},{1,5},{5,9},{9,13},{13,1},{2,6},{6,10},{... | collective-permute-start | bytes 614408 | tf_op jit(solution)/shard_map/ppermute | solution.py:29
  19.0 5.5 %collective-permute-start.3 = (bf16[2,80,640]{2,1,0:T(8,128)(2,1)S(1)}, bf16[2,80,640]{2,1,0:T(8,128)(2,1)S(1)}, u32[]{:S(2)}, u32[]{:S(2)}) collective-permute-start(bf16[2,80,640]{2,1,0:T(8,128)(2,1)S(1)} %get-tuple-element.52), channel_id=1, source_target_pairs={{0,12},{4,0},{8,4},{12,8},{1,13},{5,1},{9,5},{13,9},{2,14},{6,2},{... | collective-permute-start | bytes 614408 | tf_op jit(solution)/shard_map/ppermute | solution.py:29
  20.6 7.3 %collective-permute-start.6 = (bf16[2,80,640]{2,1,0:T(8,128)(2,1)S(1)}, bf16[2,80,640]{2,1,0:T(8,128)(2,1)S(1)}, u32[]{:S(2)}, u32[]{:S(2)}) collective-permute-start(bf16[2,80,640]{2,1,0:T(8,128)(2,1)S(1)} %get-tuple-element.51), channel_id=1, source_target_pairs={{0,32},{32,64},{64,96},{96,0},{1,33},{33,65},{65,97},{97,1},{2,34}... | collective-permute-start | bytes 614408 | tf_op jit(solution)/shard_map/ppermute | solution.py:29
  22.2 6.6 %collective-permute-start.8 = (bf16[2,80,640]{2,1,0:T(8,128)(2,1)S(1)}, bf16[2,80,640]{2,1,0:T(8,128)(2,1)S(1)}, u32[]{:S(2)}, u32[]{:S(2)}) collective-permute-start(bf16[2,80,640]{2,1,0:T(8,128)(2,1)S(1)} %get-tuple-element.51), channel_id=1, source_target_pairs={{0,96},{32,0},{64,32},{96,64},{1,97},{33,1},{65,33},{97,65},{2,98}... | collective-permute-start | bytes 614408 | tf_op jit(solution)/shard_map/ppermute | solution.py:29
  24.4 6.6 %collective-permute-start.2 = (bf16[1,80,640]{2,1,0:T(8,128)(2,1)S(1)}, bf16[1,80,640]{2,1,0:T(8,128)(2,1)S(1)}, u32[]{:S(2)}, u32[]{:S(2)}) collective-permute-start(bf16[1,80,640]{2,1,0:T(8,128)(2,1)S(1)} %slice.58), channel_id=1, source_target_pairs={{0,4},{4,8},{8,12},{12,0},{1,5},{5,9},{9,13},{13,1},{2,6},{6,10},{... | collective-permute-start | bytes 307208 | tf_op jit(solution)/shard_map/ppermute | solution.py:41
  24.6 6.5 %collective-permute-start.4 = (bf16[1,80,640]{2,1,0:T(8,128)(2,1)S(1)}, bf16[1,80,640]{2,1,0:T(8,128)(2,1)S(1)}, u32[]{:S(2)}, u32[]{:S(2)}) collective-permute-start(bf16[1,80,640]{2,1,0:T(8,128)(2,1)S(1)} %slice.59), channel_id=1, source_target_pairs={{0,12},{4,0},{8,4},{12,8},{1,13},{5,1},{9,5},{13,9},{2,14},{6,2},{... | collective-permute-start | bytes 307208 | tf_op jit(solution)/shard_map/ppermute | solution.py:42
  27.9 5.1 %collective-permute-start.7 = (bf16[1,80,640]{2,1,0:T(8,128)(2,1)S(1)}, bf16[1,80,640]{2,1,0:T(8,128)(2,1)S(1)}, u32[]{:S(2)}, u32[]{:S(2)}) collective-permute-start(bf16[1,80,640]{2,1,0:T(8,128)(2,1)S(1)} %slice.61), channel_id=1, source_target_pairs={{0,32},{32,64},{64,96},{96,0},{1,33},{33,65},{65,97},{97,1},{2,34}... | collective-permute-start | bytes 307208 | tf_op jit(solution)/shard_map/ppermute | solution.py:41
  28.8 4.2 %collective-permute-start.9 = (bf16[1,80,640]{2,1,0:T(8,128)(2,1)S(1)}, bf16[1,80,640]{2,1,0:T(8,128)(2,1)S(1)}, u32[]{:S(2)}, u32[]{:S(2)}) collective-permute-start(bf16[1,80,640]{2,1,0:T(8,128)(2,1)S(1)} %slice.62), channel_id=1, source_target_pairs={{0,96},{32,0},{64,32},{96,64},{1,97},{33,1},{65,33},{97,65},{2,98}... | collective-permute-start | bytes 307208 | tf_op jit(solution)/shard_map/ppermute | solution.py:42
  36.1 31.8 %all-to-all-start.1 = ((bf16[256,20,128]{0,2,1:T(8,128)(2,1)}), bf16[256,20,128]{0,2,1:T(8,128)(2,1)S(1)}, u32[]{:S(2)}, u32[]{:S(2)}) async-start(bf16[256,20,128]{0,2,1:T(8,128)(2,1)} %bitcast.12), calls=%async_computation.1 | async-start | bytes 2621440 | tf_op jit(solution)/shard_map/all_to_all | solution.py:149
  44.0 21.8 %collective-permute-start.10 = (bf16[4,2,80,640]{3,2,1,0:T(8,128)(2,1)S(1)}, bf16[4,2,80,640]{3,2,1,0:T(8,128)(2,1)}, u32[]{:S(2)}, u32[]{:S(2)}) collective-permute-start(bf16[4,2,80,640]{3,2,1,0:T(8,128)(2,1)S(1)} %get-tuple-element.22), channel_id=1, source_target_pairs={{0,32},{32,64},{64,96},{96,0},{1,33},{33,65},{65,97},{97,1},{2,34}... | collective-permute-start | bytes 2457608 | tf_op jit(solution)/shard_map/ppermute | solution.py:29
  45.6 20.2 %collective-permute-start.11 = (bf16[4,2,80,640]{3,2,1,0:T(8,128)(2,1)S(1)}, bf16[4,2,80,640]{3,2,1,0:T(8,128)(2,1)}, u32[]{:S(2)}, u32[]{:S(2)}) collective-permute-start(bf16[4,2,80,640]{3,2,1,0:T(8,128)(2,1)S(1)} %get-tuple-element.22), channel_id=1, source_target_pairs={{0,96},{32,0},{64,32},{96,64},{1,97},{33,1},{65,33},{97,65},{2,98}... | collective-permute-start | bytes 2457608 | tf_op jit(solution)/shard_map/ppermute | solution.py:29
  47.1 20.9 %collective-permute-start.12 = (bf16[4,2,80,640]{3,2,1,0:T(8,128)(2,1)S(1)}, bf16[4,2,80,640]{3,2,1,0:T(8,128)(2,1)}, u32[]{:S(2)}, u32[]{:S(2)}) collective-permute-start(bf16[4,2,80,640]{3,2,1,0:T(8,128)(2,1)S(1)} %get-tuple-element.23), channel_id=1, source_target_pairs={{0,4},{4,8},{8,12},{12,0},{1,5},{5,9},{9,13},{13,1},{2,6},{6,10},{... | collective-permute-start | bytes 2457608 | tf_op jit(solution)/shard_map/ppermute | solution.py:29
  47.1 20.9 %collective-permute-start.13 = (bf16[4,2,80,640]{3,2,1,0:T(8,128)(2,1)S(1)}, bf16[4,2,80,640]{3,2,1,0:T(8,128)(2,1)}, u32[]{:S(2)}, u32[]{:S(2)}) collective-permute-start(bf16[4,2,80,640]{3,2,1,0:T(8,128)(2,1)S(1)} %get-tuple-element.23), channel_id=1, source_target_pairs={{0,12},{4,0},{8,4},{12,8},{1,13},{5,1},{9,5},{13,9},{2,14},{6,2},{... | collective-permute-start | bytes 2457608 | tf_op jit(solution)/shard_map/ppermute | solution.py:29
  67.9 28.5 %all-to-all-start.2 = ((bf16[256,20,128]{0,2,1:T(8,128)(2,1)}), bf16[256,20,128]{0,2,1:T(8,128)(2,1)S(1)}, u32[]{:S(2)}, u32[]{:S(2)}) async-start(bf16[256,20,128]{0,2,1:T(8,128)(2,1)} %bitcast.13), calls=%async_computation.2 | async-start | bytes 2621440 | tf_op jit(solution)/shard_map/all_to_all | solution.py:152
  75.3 13.3 %collective-permute-start.16 = (bf16[2,2,80,640]{3,2,1,0:T(8,128)(2,1)}, bf16[2,2,80,640]{3,2,1,0:T(8,128)(2,1)S(1)}, u32[]{:S(2)}, u32[]{:S(2)}) collective-permute-start(bf16[2,2,80,640]{3,2,1,0:T(8,128)(2,1)} %slice.42), channel_id=1, source_target_pairs={{0,4},{4,8},{8,12},{12,0},{1,5},{5,9},{9,13},{13,1},{2,6},{6,10},{... | collective-permute-start | bytes 1228808 | tf_op jit(solution)/shard_map/ppermute | solution.py:41
  77.1 11.6 %collective-permute-start.17 = (bf16[2,2,80,640]{3,2,1,0:T(8,128)(2,1)}, bf16[2,2,80,640]{3,2,1,0:T(8,128)(2,1)S(1)}, u32[]{:S(2)}, u32[]{:S(2)}) collective-permute-start(bf16[2,2,80,640]{3,2,1,0:T(8,128)(2,1)} %slice.43), channel_id=1, source_target_pairs={{0,12},{4,0},{8,4},{12,8},{1,13},{5,1},{9,5},{13,9},{2,14},{6,2},{... | collective-permute-start | bytes 1228808 | tf_op jit(solution)/shard_map/ppermute | solution.py:42
  81.6 12.0 %collective-permute-start.14 = (bf16[2,2,80,640]{3,2,1,0:T(8,128)(2,1)}, bf16[2,2,80,640]{3,2,1,0:T(8,128)(2,1)}, u32[]{:S(2)}, u32[]{:S(2)}) collective-permute-start(bf16[2,2,80,640]{3,2,1,0:T(8,128)(2,1)} %slice.40), channel_id=1, source_target_pairs={{0,32},{32,64},{64,96},{96,0},{1,33},{33,65},{65,97},{97,1},{2,34}... | collective-permute-start | bytes 1228808 | tf_op jit(solution)/shard_map/ppermute | solution.py:41
  83.4 10.9 %collective-permute-start.15 = (bf16[2,2,80,640]{3,2,1,0:T(8,128)(2,1)}, bf16[2,2,80,640]{3,2,1,0:T(8,128)(2,1)}, u32[]{:S(2)}, u32[]{:S(2)}) collective-permute-start(bf16[2,2,80,640]{3,2,1,0:T(8,128)(2,1)} %slice.41), channel_id=1, source_target_pairs={{0,96},{32,0},{64,32},{96,64},{1,97},{33,1},{65,33},{97,65},{2,98}... | collective-permute-start | bytes 1228808 | tf_op jit(solution)/shard_map/ppermute | solution.py:42
  96.4 24.2 %all-to-all-start = ((bf16[256,20,128]{0,2,1:T(8,128)(2,1)}), bf16[256,20,128]{0,2,1:T(8,128)(2,1)}, u32[]{:S(2)}, u32[]{:S(2)}) async-start(bf16[256,20,128]{0,2,1:T(8,128)(2,1)} %bitcast.14), calls=%async_computation | async-start | bytes 2621440 | tf_op jit(solution)/shard_map/all_to_all | solution.py:157
  102.6 78.3 %all-gather.2.cloned.1.call-start = ((), (), s32[]{:S(2)}) async-start(), calls=%async_computation.4 | async-start | bytes 6553600 | tf_op jit(solution)/shard_map/all_gather | solution.py:167
  155.6 33.2 %copy-start.10 = (bf16[4,2,4,80,640]{4,3,2,1,0:T(8,128)(2,1)S(1)}, bf16[4,2,4,80,640]{4,3,2,1,0:T(8,128)(2,1)}, u32[]{:S(2)}) copy-start(bf16[4,2,4,80,640]{4,3,2,1,0:T(8,128)(2,1)} %copy.69) | copy-start | bytes 9830404
  (10 other events, 90.1 us)
Sparse Core Ops, SparseCore 0:
  137.5 43.3 all-gather.1

commit v4 on v3

--- a/solution.py
+++ b/solution.py
@@ -46,15 +46,12 @@
     return (from_left, far, from_right)
 
 
-def ring_finish(x, received, axis, size):
-    index = lax.axis_index(axis)
-    stacked = jnp.stack((x,) + tuple(received))
-    order = (index - jnp.arange(size)) % size
-    return jnp.take(stacked, order, axis=0)
+def ring_finish(x, received):
+    return jnp.stack((x,) + tuple(received))
 
 
 def ring_gather(x, axis, size):
-    return ring_finish(x, ring_far(ring_send(x, axis, size), axis, size), axis, size)
+    return ring_finish(x, ring_far(ring_send(x, axis, size), axis, size))
 
 
 STAGES = (("y", "z"), ("z", "y"))
@@ -70,16 +67,31 @@
     return parts
 
 
-def gather_finish(parts, sent):
+def gather_finish(parts, sent, heads_order):
+    z = lax.axis_index("z")
+    xl = lax.axis_index("xl")
+    y = lax.axis_index("y")
+    blocks_per_group = 8
+    target = jnp.arange(32)
+    group = heads_order[target // blocks_per_group]
+    absolute = group * blocks_per_group + target % blocks_per_group
+    z_rel = (z - absolute // 8) % 4
+    xl_rel = (xl - (absolute // 4) % 2) % 2
+    y_rel = (y - absolute % 4) % 4
     pieces = []
-    for part, received, (first, second) in zip(parts, sent, STAGES):
-        part = ring_finish(part, received, second, 4)
+    for part, received, (first, _) in zip(parts, sent, STAGES):
+        part = ring_finish(part, received)
         if first == "y":
-            part = jnp.transpose(part, (0, 2, 1, 3, 4))
+            source = z_rel * 8 + y_rel * 2 + xl_rel
         else:
-            part = jnp.transpose(part, (1, 2, 0, 3, 4))
-        pieces.append(part.reshape(-1, part.shape[-1]))
+            source = y_rel * 8 + z_rel * 2 + xl_rel
+        flat = part.reshape((32,) + part.shape[3:])
+        pieces.append(jnp.take(flat, source, axis=0).reshape(-1, part.shape[-1]))
     return jnp.concatenate(pieces, axis=1)
+
+
+def seq_shift(x, shift):
+    return lax.ppermute(x, SEQ, [(k, (k + shift) % 4) for k in range(4)])
 
 def featurize(block, seq_length):
     positions = jnp.arange(block.shape[0], dtype=jnp.int32).astype(jnp.float32)
@@ -164,11 +176,23 @@
         head_gain, lax.axis_index(SEQ) * heads_here, heads_here, 0
     )
     normed_group = normalize(attended, gain_rows)
-    normed_all = lax.all_gather(normed_group, SEQ, axis=1, tiled=True)
-    normed_all = normed_all.reshape(normed_all.shape[0], H * HEAD)
-    cols = gather_finish(parts, sent)
-    part = jnp.dot(normed_all, cols, preferred_element_type=jnp.float32).astype(jnp.bfloat16)
-    projected = lax.all_to_all(part, SEQ, split_axis=0, concat_axis=1, tiled=True)
+    seq_index = lax.axis_index(SEQ)
+    flat_group = normed_group.reshape(normed_group.shape[0], heads_here * HEAD)
+    normed_all = jnp.concatenate(
+        [flat_group] + [seq_shift(flat_group, shift) for shift in (1, 2, 3)], axis=1
+    )
+    heads_order = (seq_index - jnp.arange(4)) % 4
+    cols = gather_finish(parts, sent, heads_order)
+    outputs = []
+    for shift in (2, 1, 3, 0):
+        chunk = lax.dynamic_slice_in_dim(
+            normed_all, ((seq_index + shift) % 4) * tokens_here, tokens_here, 0
+        )
+        part = jnp.dot(chunk, cols, preferred_element_type=jnp.float32).astype(jnp.bfloat16)
+        outputs.append((shift, part if shift == 0 else seq_shift(part, shift)))
+    by_shift = jnp.stack([part for _, part in sorted(outputs, key=lambda item: item[0])])
+    projected = jnp.take(by_shift, (seq_index - jnp.arange(4)) % 4, axis=0)
+    projected = jnp.transpose(projected, (1, 0, 2)).reshape(tokens_here, -1)
     layer_out = projected[None]
     return (layer_out, updated, moment_one, moment_two)
 

time: 247 us -> 248 us (level)
  blocking collectives: 34.5 us -> 0 us
  waiting for transfers between devices: 56.4 us -> 89.6 us
  between operations: 14.4 us -> 1.04 us
  starting transfers between devices: 45.5 us -> 57.6 us
  other arithmetic: 26.5 us -> 34.6 us
  local copies, waits for them, and re-layouts: 46.7 us -> 40.2 us
  matrix products: 21.5 us -> 24.3 us
    ppermute x0 -> x6, waiting for transfers between devices: none -> 57.4 us  [seq_shift(): return lax.ppermute(x, SEQ, [(k, (k + shift) % 4) for k in range(4)])]
    all_to_all x1 -> x0, blocking collectives: 34.5 us -> none  [on_device(): lax.all_to_all(part, SEQ, split_axis=0, concat_axis=1, tiled=True)]
    all_gather x1 -> x0, waiting for transfers between devices: 25.3 us -> none  [on_device(): normed_all = lax.all_gather(normed_group, SEQ, axis=1, tiled=True)]
    ppermute x0 -> x6, starting transfers between devices: none -> 11 us  [seq_shift(): return lax.ppermute(x, SEQ, [(k, (k + shift) % 4) for k in range(4)])]
    all_gather x1 -> x0, local copies, waits for them, and re-layouts: 7.94 us -> none  [on_device(): normed_all = lax.all_gather(normed_group, SEQ, axis=1, tiled=True)]
    unnamed x27 -> x32, local copies, waits for them, and re-layouts: 6.35 us -> 12.3 us
    ppermute x4, waiting for transfers between devices: 4.98 us -> 10.3 us  [ring_far(): lax.ppermute(from_left[:half], axis, forward)]
    transpose x2 -> x0, other arithmetic: 4.67 us -> none  [the longest x1 2.33 us: gather_finish(): part = jnp.transpose(part, (1, 2, 0, 3, 4))]
  transfers between devices with their start and end apart: 22 -> 27, of which waited for: 11 -> 15; matrix products, arithmetic and copies ran while one was open for 20% -> 22% of each run, Pallas kernels for 0% -> 0%
where the time goes in v4:
time: 248 us; the launch traced here: 247 us
  waiting for transfers between devices  89.6 us (36%)
  starting transfers between devices  57.6 us (23%)
  local copies, waits for them, and re-layouts  40.2 us (16%)
  other arithmetic  34.6 us (14%)
  matrix products  24.3 us (10%)
    ppermute x6, waiting for transfers between devices, seq_shift(): return lax.ppermute(x, SEQ, [(k, (k + shift) % 4) for k in range(4)])  57.4 us
    dot_general x4, matrix products, on_device(): jnp.dot(chunk, cols, preferred_element_type=jnp.float32)  12.7 us
    ppermute x8, starting transfers between devices, ring_send(): return (lax.ppermute(x, axis, forward), lax.ppermute(x, axis, backward))  12.5 us
    ppermute x8, waiting for transfers between devices, ring_send(): return (lax.ppermute(x, axis, forward), lax.ppermute(x, axis, backward))  12.5 us
    unnamed x32, local copies, waits for them, and re-layouts  12.3 us
    ppermute x6, starting transfers between devices, seq_shift(): return lax.ppermute(x, SEQ, [(k, (k + shift) % 4) for k in range(4)])  11 us
    ppermute x4, waiting for transfers between devices, ring_far(): lax.ppermute(from_left[:half], axis, forward)  10.3 us
    all_to_all x1, starting transfers between devices, on_device(): lax.all_to_all(query_heads, SEQ, split_axis=1, concat_axis=0, tiled=True)  10 us
  transfers between devices with their start and end apart: 27, of which 15 were waited for; matrix products, arithmetic and copies ran while one was open for 22% of the time, Pallas kernels for 0%

profile of v4, /device:TPU:1, one launch (start us, length us, event | category | flops | bytes accessed | tf_op | source)
XLA Modules:
  0.0 247.3 jit_solution(9806805085474481111)
XLA Ops:
  7.6 3.1 %collective-permute-start.3 = (bf16[2,80,640]{2,1,0:T(8,128)(2,1)S(1)}, bf16[2,80,640]{2,1,0:T(8,128)(2,1)S(1)}, u32[]{:S(2)}, u32[]{:S(2)}) collective-permute-start(bf16[2,80,640]{2,1,0:T(8,128)(2,1)S(1)} %get-tuple-element.65), channel_id=1, source_target_pairs={{0,12},{4,0},{8,4},{12,8},{1,13},{5,1},{9,5},{13,9},{2,14},{6,2},{... | collective-permute-start | bytes 614408 | tf_op jit(solution)/shard_map/ppermute | solution.py:29
  10.7 3.8 %collective-permute-start.8 = (bf16[2,80,640]{2,1,0:T(8,128)(2,1)S(1)}, bf16[2,80,640]{2,1,0:T(8,128)(2,1)S(1)}, u32[]{:S(2)}, u32[]{:S(2)}) collective-permute-start(bf16[2,80,640]{2,1,0:T(8,128)(2,1)S(1)} %get-tuple-element.59), channel_id=1, source_target_pairs={{0,96},{32,0},{64,32},{96,64},{1,97},{33,1},{65,33},{97,65},{2,98}... | collective-permute-start | bytes 614408 | tf_op jit(solution)/shard_map/ppermute | solution.py:29
  18.9 3.1 %collective-permute-start.9 = (bf16[1,80,640]{2,1,0:T(8,128)(2,1)S(1)}, bf16[1,80,640]{2,1,0:T(8,128)(2,1)S(1)}, u32[]{:S(2)}, u32[]{:S(2)}) collective-permute-start(bf16[1,80,640]{2,1,0:T(8,128)(2,1)S(1)} %slice.61), channel_id=1, source_target_pairs={{0,96},{32,0},{64,32},{96,64},{1,97},{33,1},{65,33},{97,65},{2,98}... | collective-permute-start | bytes 307208 | tf_op jit(solution)/shard_map/ppermute | solution.py:42
  23.6 3.2 %collective-permute-done.7 = bf16[1,80,640]{2,1,0:T(8,128)(2,1)S(1)} collective-permute-done((bf16[1,80,640]{2,1,0:T(8,128)(2,1)S(1)}, bf16[1,80,640]{2,1,0:T(8,128)(2,1)S(1)}, u32[]{:S(2)}, u32[]{:S(2)}) %collective-permute-start.7) | collective-permute-done | bytes 102432 | tf_op jit(solution)/shard_map/ppermute | solution.py:41
  28.0 10.0 %all-to-all-start.1 = ((bf16[256,20,128]{0,2,1:T(8,128)(2,1)}), bf16[256,20,128]{0,2,1:T(8,128)(2,1)S(1)}, u32[]{:S(2)}, u32[]{:S(2)}) async-start(bf16[256,20,128]{0,2,1:T(8,128)(2,1)} %bitcast.12), calls=%async_computation.1 | async-start | bytes 2621440 | tf_op jit(solution)/shard_map/all_to_all | solution.py:161
  40.7 2.9 %collective-permute-start.13 = (bf16[4,2,80,640]{3,2,1,0:T(8,128)(2,1)S(1)}, bf16[4,2,80,640]{3,2,1,0:T(8,128)(2,1)}, u32[]{:S(2)}, u32[]{:S(2)}) collective-permute-start(bf16[4,2,80,640]{3,2,1,0:T(8,128)(2,1)S(1)} %pad_maximum_fusion.16), channel_id=1, source_target_pairs={{0,12},{4,0},{8,4},{12,8},{1,13},{5,1},{9,5},{13,9},{2,14},{6,2},{... | collective-permute-start | bytes 2457608 | tf_op jit(solution)/shard_map/ppermute | solution.py:29
  49.3 9.9 %collective-permute-done.10 = bf16[4,2,80,640]{3,2,1,0:T(8,128)(2,1)} collective-permute-done((bf16[4,2,80,640]{3,2,1,0:T(8,128)(2,1)S(1)}, bf16[4,2,80,640]{3,2,1,0:T(8,128)(2,1)}, u32[]{:S(2)}, u32[]{:S(2)}) %collective-permute-start.10) | collective-permute-done | bytes 819232 | tf_op jit(solution)/shard_map/ppermute | solution.py:29
  61.8 5.6 %all-to-all-start.2 = ((bf16[256,20,128]{0,2,1:T(8,128)(2,1)}), bf16[256,20,128]{0,2,1:T(8,128)(2,1)S(1)}, u32[]{:S(2)}, u32[]{:S(2)}) async-start(bf16[256,20,128]{0,2,1:T(8,128)(2,1)} %bitcast.13), calls=%async_computation.2 | async-start | bytes 2621440 | tf_op jit(solution)/shard_map/all_to_all | solution.py:164
  85.5 4.9 %collective-permute-done.16 = bf16[2,2,80,640]{3,2,1,0:T(8,128)(2,1)} collective-permute-done((bf16[2,2,80,640]{3,2,1,0:T(8,128)(2,1)}, bf16[2,2,80,640]{3,2,1,0:T(8,128)(2,1)}, u32[]{:S(2)}, u32[]{:S(2)}) %collective-permute-start.16) | collective-permute-done | bytes 409632 | tf_op jit(solution)/shard_map/ppermute | solution.py:41
  93.5 6.2 %all-to-all-start = ((bf16[256,20,128]{0,2,1:T(8,128)(2,1)}), bf16[256,20,128]{0,2,1:T(8,128)(2,1)}, u32[]{:S(2)}, u32[]{:S(2)}) async-start(bf16[256,20,128]{0,2,1:T(8,128)(2,1)} %bitcast.14), calls=%async_computation | async-start | bytes 2621440 | tf_op jit(solution)/shard_map/all_to_all | solution.py:169
  107.0 4.5 %multiply_convert_fusion.1 = (bf16[8,128,5,128]{3,1,2,0:T(8,128)(2,1)}, bf16[8,128,5,128]{3,1,2,0:T(8,128)(2,1)}, bf16[8,128,5,128]{3,1,2,0:T(8,128)(2,1)S(1)}, bf16[8,128,5,128]{3,1,2,0:T(8,128)(2,1)S(1)}) fusion(f32[8,128,5,128]{3,1,0,2:T(8,128)} %bitcast.89, f32[8,128]{1,0:T(8,128)S(1)} %get-tuple-element.75, f32[8,128]{1,0:T(8,128)S(1)} %get-tuple-element.74, ...), kind=kLoop, calls=%fused_computation.21 | loop fusion | flops 5242880 | bytes 10493952 | tf_op jit(solution)/shard_map/convert.3
  111.5 6.2 %all-to-all-done = bf16[256,20,128]{0,2,1:T(8,128)(2,1)} async-done(((bf16[256,20,128]{0,2,1:T(8,128)(2,1)}), bf16[256,20,128]{0,2,1:T(8,128)(2,1)}, u32[]{:S(2)}, u32[]{:S(2)}) %all-to-all-start) | async-done | bytes 1310752 | tf_op jit(solution)/shard_map/all_to_all | solution.py:169
  120.1 3.0 %fusion.4 = f32[8,5,256,128]{3,2,1,0:T(8,128)S(1)} fusion(bf16[8,128,5,128]{3,1,2,0:T(8,128)(2,1)} %get-tuple-element.57, bf16[8,128,5,128]{3,1,2,0:T(8,128)(2,1)} %get-tuple-element.56, bf16[8,128,5,128]{3,1,0,2:T(8,128)(2,1)} %bitcast.90), kind=kOutput, calls=%fused_computation.32 | convolution fusion | flops 340787200 | bytes 9175040 | tf_op jit(solution)/shard_map/cjhf,cjhe->chfe/dot_general | solution.py:109
  126.2 6.2 %multiply_reduce_fusion = (f32[8,128,5]{1,2,0:T(8,128)S(1)}, f32[8,128,5,128]{1,3,2,0:T(8,128)}) fusion(f32[8,5,128,128]{3,2,1,0:T(8,128)} %fusion.3, bf16[8,128,5,128]{3,1,2,0:T(8,128)(2,1)} %get-tuple-element.57, bf16[8,128,5,128]{3,1,2,0:T(8,128)(2,1)} %get-tuple-element.56, bf16[8,128,5,128]{3,1,2,0:T(8,128)(2,1)S(1)} %get-tuple-element.66, ...), kind=kOutput, calls=%fused_computation.17 | convolution fusion | flops 517073920 | bytes 11833344 | tf_op jit(solution)/shard_map/chij,cjhe->cihe/dot_general | solution.py:126
  132.4 3.2 %copy.46 = f32[8,128,5,128]{1,0,3,2:T(8,128)S(1)} copy(f32[8,128,5,128]{1,3,2,0:T(8,128)} %get-tuple-element.73) | data formatting | bytes 5242880 | tf_op jit(solution)/shard_map/add | solution.py:135
  138.1 3.1 %collective-permute-start.18 = (bf16[1024,640]{0,1:T(8,128)(2,1)}, bf16[1024,640]{0,1:T(8,128)(2,1)}, u32[]{:S(2)}, u32[]{:S(2)}) collective-permute-start(bf16[1024,640]{0,1:T(8,128)(2,1)} %fusion.1), channel_id=1, source_target_pairs={{0,1},{1,2},{2,3},{3,0},{4,5},{5,6},{6,7},{7,4},{8,9},{9,10},{10,1... | collective-permute-start | bytes 3932168 | tf_op jit(solution)/shard_map/ppermute | solution.py:94
  153.6 16.1 %collective-permute-done.20 = bf16[1024,640]{0,1:T(8,128)(2,1)} collective-permute-done((bf16[1024,640]{0,1:T(8,128)(2,1)}, bf16[1024,640]{0,1:T(8,128)(2,1)}, u32[]{:S(2)}, u32[]{:S(2)}) %collective-permute-start.20) | collective-permute-done | bytes 1310752 | tf_op jit(solution)/shard_map/ppermute | solution.py:94
  170.6 24.4 %collective-permute-done.18 = bf16[1024,640]{0,1:T(8,128)(2,1)} collective-permute-done((bf16[1024,640]{0,1:T(8,128)(2,1)}, bf16[1024,640]{0,1:T(8,128)(2,1)}, u32[]{:S(2)}, u32[]{:S(2)}) %collective-permute-start.18) | collective-permute-done | bytes 1310752 | tf_op jit(solution)/shard_map/ppermute | solution.py:94
  195.0 3.5 %pad_maximum_fusion.1 = bf16[1024,2560]{0,1:T(8,128)(2,1)S(1)} fusion(bf16[1024,640]{0,1:T(8,128)(2,1)} %collective-permute-done.20, bf16[1024,640]{0,1:T(8,128)(2,1)} %collective-permute-done.19, bf16[1024,640]{0,1:T(8,128)(2,1)} %collective-permute-done.18, bf16[1024,640]{0,1:T(8,128)(2,1)} %fusion.1), kind=kLoop, calls=%fused_computation.4 | loop fusion | flops 20971520 | bytes 10485760 | tf_op jit(solution)/shard_map/concatenate | solution.py:181
  201.3 3.8 %collective-permute-start.23 = (bf16[256,1280]{1,0:T(8,128)(2,1)}, bf16[256,1280]{1,0:T(8,128)(2,1)}, u32[]{:S(2)}, u32[]{:S(2)}) collective-permute-start(bf16[256,1280]{1,0:T(8,128)(2,1)} %convolution_convert_fusion), channel_id=1, source_target_pairs={{0,3},{1,0},{2,1},{3,2},{4,7},{5,4},{6,5},{7,6},{8,11},{9,8},{10,9... | collective-permute-start | bytes 1966088 | tf_op jit(solution)/shard_map/ppermute | solution.py:94
  213.9 4.3 %fusion.2 = bf16[1,256,1280]{2,1,0:T(8,128)(2,1)S(1)} fusion(bf16[1024,2560]{0,1:T(8,128)(2,1)} %copy-done.3, s32[]{:T(128)S(6)} %select_n.146, bf16[2560,640]{1,0:T(8,128)(2,1)S(1)} %bitcast.99, bf16[2560,640]{1,0:T(8,128)(2,1)} %bitcast.103), kind=kOutput, calls=%fused_computation.30 | convolution fusion | flops 1691156480 | bytes 8519684 | tf_op jit(solution)/shard_map/dot_general | solution.py:191
  218.2 8.3 %collective-permute-done.22 = bf16[256,1280]{1,0:T(8,128)(2,1)} collective-permute-done((bf16[256,1280]{1,0:T(8,128)(2,1)}, bf16[256,1280]{1,0:T(8,128)(2,1)}, u32[]{:S(2)}, u32[]{:S(2)}) %collective-permute-start.22) | collective-permute-done | bytes 655392 | tf_op jit(solution)/shard_map/ppermute | solution.py:94
  226.5 7.7 %collective-permute-done.21 = bf16[256,1280]{1,0:T(8,128)(2,1)} collective-permute-done((bf16[256,1280]{1,0:T(8,128)(2,1)}, bf16[256,1280]{1,0:T(8,128)(2,1)}, u32[]{:S(2)}, u32[]{:S(2)}) %collective-permute-start.21) | collective-permute-done | bytes 655392 | tf_op jit(solution)/shard_map/ppermute | solution.py:94
  242.9 4.4 %copy.48 = bf16[1,256,5120]{2,1,0:T(8,128)(2,1)} copy(bf16[1,256,5120]{1,2,0:T(8,128)(2,1)} %bitcast.87) | data formatting | bytes 5242880
  (120 shorter events, 95.0 us)
Async XLA Ops:
  5.5 5.1 %collective-permute-start.5 = (bf16[80,640]{1,0:T(8,128)(2,1)S(1)}, bf16[80,640]{1,0:T(8,128)(2,1)S(1)}, u32[]{:S(2)}, u32[]{:S(2)}) collective-permute-start(bf16[80,640]{1,0:T(8,128)(2,1)S(1)} %get-tuple-element.62), channel_id=1, source_target_pairs={{0,16},{16,0},{1,17},{17,1},{2,18},{18,2},{3,19},{19,3},{4,20},{20... | collective-permute-start | bytes 307208 | tf_op jit(solution)/shard_map/ppermute | solution.py:26
  7.6 6.9 %collective-permute-start.3 = (bf16[2,80,640]{2,1,0:T(8,128)(2,1)S(1)}, bf16[2,80,640]{2,1,0:T(8,128)(2,1)S(1)}, u32[]{:S(2)}, u32[]{:S(2)}) collective-permute-start(bf16[2,80,640]{2,1,0:T(8,128)(2,1)S(1)} %get-tuple-element.65), channel_id=1, source_target_pairs={{0,12},{4,0},{8,4},{12,8},{1,13},{5,1},{9,5},{13,9},{2,14},{6,2},{... | collective-permute-start | bytes 614408 | tf_op jit(solution)/shard_map/ppermute | solution.py:29
  10.6 6.6 %collective-permute-start.1 = (bf16[2,80,640]{2,1,0:T(8,128)(2,1)S(1)}, bf16[2,80,640]{2,1,0:T(8,128)(2,1)S(1)}, u32[]{:S(2)}, u32[]{:S(2)}) collective-permute-start(bf16[2,80,640]{2,1,0:T(8,128)(2,1)S(1)} %get-tuple-element.65), channel_id=1, source_target_pairs={{0,4},{4,8},{8,12},{12,0},{1,5},{5,9},{9,13},{13,1},{2,6},{6,10},{... | collective-permute-start | bytes 614408 | tf_op jit(solution)/shard_map/ppermute | solution.py:29
  10.7 8.2 %collective-permute-start.8 = (bf16[2,80,640]{2,1,0:T(8,128)(2,1)S(1)}, bf16[2,80,640]{2,1,0:T(8,128)(2,1)S(1)}, u32[]{:S(2)}, u32[]{:S(2)}) collective-permute-start(bf16[2,80,640]{2,1,0:T(8,128)(2,1)S(1)} %get-tuple-element.59), channel_id=1, source_target_pairs={{0,96},{32,0},{64,32},{96,64},{1,97},{33,1},{65,33},{97,65},{2,98}... | collective-permute-start | bytes 614408 | tf_op jit(solution)/shard_map/ppermute | solution.py:29
  14.5 7.4 %collective-permute-start.6 = (bf16[2,80,640]{2,1,0:T(8,128)(2,1)S(1)}, bf16[2,80,640]{2,1,0:T(8,128)(2,1)S(1)}, u32[]{:S(2)}, u32[]{:S(2)}) collective-permute-start(bf16[2,80,640]{2,1,0:T(8,128)(2,1)S(1)} %get-tuple-element.59), channel_id=1, source_target_pairs={{0,32},{32,64},{64,96},{96,0},{1,33},{33,65},{65,97},{97,1},{2,34}... | collective-permute-start | bytes 614408 | tf_op jit(solution)/shard_map/ppermute | solution.py:29
  14.5 7.5 %collective-permute-start.4 = (bf16[1,80,640]{2,1,0:T(8,128)(2,1)S(1)}, bf16[1,80,640]{2,1,0:T(8,128)(2,1)S(1)}, u32[]{:S(2)}, u32[]{:S(2)}) collective-permute-start(bf16[1,80,640]{2,1,0:T(8,128)(2,1)S(1)} %slice.58), channel_id=1, source_target_pairs={{0,12},{4,0},{8,4},{12,8},{1,13},{5,1},{9,5},{13,9},{2,14},{6,2},{... | collective-permute-start | bytes 307208 | tf_op jit(solution)/shard_map/ppermute | solution.py:42
  17.3 5.1 %collective-permute-start.2 = (bf16[1,80,640]{2,1,0:T(8,128)(2,1)S(1)}, bf16[1,80,640]{2,1,0:T(8,128)(2,1)S(1)}, u32[]{:S(2)}, u32[]{:S(2)}) collective-permute-start(bf16[1,80,640]{2,1,0:T(8,128)(2,1)S(1)} %slice.57), channel_id=1, source_target_pairs={{0,4},{4,8},{8,12},{12,0},{1,5},{5,9},{9,13},{13,1},{2,6},{6,10},{... | collective-permute-start | bytes 307208 | tf_op jit(solution)/shard_map/ppermute | solution.py:41
  28.0 33.8 %all-to-all-start.1 = ((bf16[256,20,128]{0,2,1:T(8,128)(2,1)}), bf16[256,20,128]{0,2,1:T(8,128)(2,1)S(1)}, u32[]{:S(2)}, u32[]{:S(2)}) async-start(bf16[256,20,128]{0,2,1:T(8,128)(2,1)} %bitcast.12), calls=%async_computation.1 | async-start | bytes 2621440 | tf_op jit(solution)/shard_map/all_to_all | solution.py:161
  38.0 21.2 %collective-permute-start.10 = (bf16[4,2,80,640]{3,2,1,0:T(8,128)(2,1)S(1)}, bf16[4,2,80,640]{3,2,1,0:T(8,128)(2,1)}, u32[]{:S(2)}, u32[]{:S(2)}) collective-permute-start(bf16[4,2,80,640]{3,2,1,0:T(8,128)(2,1)S(1)} %pad_maximum_fusion.15), channel_id=1, source_target_pairs={{0,32},{32,64},{64,96},{96,0},{1,33},{33,65},{65,97},{97,1},{2,34}... | collective-permute-start | bytes 2457608 | tf_op jit(solution)/shard_map/ppermute | solution.py:29
  38.0 21.2 %collective-permute-start.11 = (bf16[4,2,80,640]{3,2,1,0:T(8,128)(2,1)S(1)}, bf16[4,2,80,640]{3,2,1,0:T(8,128)(2,1)}, u32[]{:S(2)}, u32[]{:S(2)}) collective-permute-start(bf16[4,2,80,640]{3,2,1,0:T(8,128)(2,1)S(1)} %pad_maximum_fusion.15), channel_id=1, source_target_pairs={{0,96},{32,0},{64,32},{96,64},{1,97},{33,1},{65,33},{97,65},{2,98}... | collective-permute-start | bytes 2457608 | tf_op jit(solution)/shard_map/ppermute | solution.py:29
  40.7 21.1 %collective-permute-start.12 = (bf16[4,2,80,640]{3,2,1,0:T(8,128)(2,1)S(1)}, bf16[4,2,80,640]{3,2,1,0:T(8,128)(2,1)}, u32[]{:S(2)}, u32[]{:S(2)}) collective-permute-start(bf16[4,2,80,640]{3,2,1,0:T(8,128)(2,1)S(1)} %pad_maximum_fusion.16), channel_id=1, source_target_pairs={{0,4},{4,8},{8,12},{12,0},{1,5},{5,9},{9,13},{13,1},{2,6},{6,10},{... | collective-permute-start | bytes 2457608 | tf_op jit(solution)/shard_map/ppermute | solution.py:29
  40.7 21.1 %collective-permute-start.13 = (bf16[4,2,80,640]{3,2,1,0:T(8,128)(2,1)S(1)}, bf16[4,2,80,640]{3,2,1,0:T(8,128)(2,1)}, u32[]{:S(2)}, u32[]{:S(2)}) collective-permute-start(bf16[4,2,80,640]{3,2,1,0:T(8,128)(2,1)S(1)} %pad_maximum_fusion.16), channel_id=1, source_target_pairs={{0,12},{4,0},{8,4},{12,8},{1,13},{5,1},{9,5},{13,9},{2,14},{6,2},{... | collective-permute-start | bytes 2457608 | tf_op jit(solution)/shard_map/ppermute | solution.py:29
  61.8 30.6 %all-to-all-start.2 = ((bf16[256,20,128]{0,2,1:T(8,128)(2,1)}), bf16[256,20,128]{0,2,1:T(8,128)(2,1)S(1)}, u32[]{:S(2)}, u32[]{:S(2)}) async-start(bf16[256,20,128]{0,2,1:T(8,128)(2,1)} %bitcast.13), calls=%async_computation.2 | async-start | bytes 2621440 | tf_op jit(solution)/shard_map/all_to_all | solution.py:164
  69.2 12.2 %collective-permute-start.15 = (bf16[2,2,80,640]{3,2,1,0:T(8,128)(2,1)}, bf16[2,2,80,640]{3,2,1,0:T(8,128)(2,1)S(1)}, u32[]{:S(2)}, u32[]{:S(2)}) collective-permute-start(bf16[2,2,80,640]{3,2,1,0:T(8,128)(2,1)} %slice.41), channel_id=1, source_target_pairs={{0,96},{32,0},{64,32},{96,64},{1,97},{33,1},{65,33},{97,65},{2,98}... | collective-permute-start | bytes 1228808 | tf_op jit(solution)/shard_map/ppermute | solution.py:42
  71.0 12.3 %collective-permute-start.14 = (bf16[2,2,80,640]{3,2,1,0:T(8,128)(2,1)}, bf16[2,2,80,640]{3,2,1,0:T(8,128)(2,1)}, u32[]{:S(2)}, u32[]{:S(2)}) collective-permute-start(bf16[2,2,80,640]{3,2,1,0:T(8,128)(2,1)} %slice.40), channel_id=1, source_target_pairs={{0,32},{32,64},{64,96},{96,0},{1,33},{33,65},{65,97},{97,1},{2,34}... | collective-permute-start | bytes 1228808 | tf_op jit(solution)/shard_map/ppermute | solution.py:41
  74.3 11.2 %collective-permute-start.17 = (bf16[2,2,80,640]{3,2,1,0:T(8,128)(2,1)}, bf16[2,2,80,640]{3,2,1,0:T(8,128)(2,1)S(1)}, u32[]{:S(2)}, u32[]{:S(2)}) collective-permute-start(bf16[2,2,80,640]{3,2,1,0:T(8,128)(2,1)} %slice.43), channel_id=1, source_target_pairs={{0,12},{4,0},{8,4},{12,8},{1,13},{5,1},{9,5},{13,9},{2,14},{6,2},{... | collective-permute-start | bytes 1228808 | tf_op jit(solution)/shard_map/ppermute | solution.py:42
  78.8 11.7 %collective-permute-start.16 = (bf16[2,2,80,640]{3,2,1,0:T(8,128)(2,1)}, bf16[2,2,80,640]{3,2,1,0:T(8,128)(2,1)}, u32[]{:S(2)}, u32[]{:S(2)}) collective-permute-start(bf16[2,2,80,640]{3,2,1,0:T(8,128)(2,1)} %slice.42), channel_id=1, source_target_pairs={{0,4},{4,8},{8,12},{12,0},{1,5},{5,9},{9,13},{13,1},{2,6},{6,10},{... | collective-permute-start | bytes 1228808 | tf_op jit(solution)/shard_map/ppermute | solution.py:41
  93.5 24.2 %all-to-all-start = ((bf16[256,20,128]{0,2,1:T(8,128)(2,1)}), bf16[256,20,128]{0,2,1:T(8,128)(2,1)}, u32[]{:S(2)}, u32[]{:S(2)}) async-start(bf16[256,20,128]{0,2,1:T(8,128)(2,1)} %bitcast.14), calls=%async_computation | async-start | bytes 2621440 | tf_op jit(solution)/shard_map/all_to_all | solution.py:169
  137.2 32.6 %collective-permute-start.20 = (bf16[1024,640]{0,1:T(8,128)(2,1)}, bf16[1024,640]{0,1:T(8,128)(2,1)}, u32[]{:S(2)}, u32[]{:S(2)}) collective-permute-start(bf16[1024,640]{0,1:T(8,128)(2,1)} %fusion.1), channel_id=1, source_target_pairs={{0,3},{1,0},{2,1},{3,2},{4,7},{5,4},{6,5},{7,6},{8,11},{9,8},{10,9... | collective-permute-start | bytes 3932168 | tf_op jit(solution)/shard_map/ppermute | solution.py:94
  138.0 32.6 %collective-permute-start.19 = (bf16[1024,640]{0,1:T(8,128)(2,1)}, bf16[1024,640]{0,1:T(8,128)(2,1)}, u32[]{:S(2)}, u32[]{:S(2)}) collective-permute-start(bf16[1024,640]{0,1:T(8,128)(2,1)} %fusion.1), channel_id=1, source_target_pairs={{0,2},{1,3},{2,0},{3,1},{4,6},{5,7},{6,4},{7,5},{8,10},{9,11},{10,... | collective-permute-start | bytes 3932168 | tf_op jit(solution)/shard_map/ppermute | solution.py:94
  138.1 56.9 %collective-permute-start.18 = (bf16[1024,640]{0,1:T(8,128)(2,1)}, bf16[1024,640]{0,1:T(8,128)(2,1)}, u32[]{:S(2)}, u32[]{:S(2)}) collective-permute-start(bf16[1024,640]{0,1:T(8,128)(2,1)} %fusion.1), channel_id=1, source_target_pairs={{0,1},{1,2},{2,3},{3,0},{4,5},{5,6},{6,7},{7,4},{8,9},{9,10},{10,1... | collective-permute-start | bytes 3932168 | tf_op jit(solution)/shard_map/ppermute | solution.py:94
  201.3 16.9 %collective-permute-start.23 = (bf16[256,1280]{1,0:T(8,128)(2,1)}, bf16[256,1280]{1,0:T(8,128)(2,1)}, u32[]{:S(2)}, u32[]{:S(2)}) collective-permute-start(bf16[256,1280]{1,0:T(8,128)(2,1)} %convolution_convert_fusion), channel_id=1, source_target_pairs={{0,3},{1,0},{2,1},{3,2},{4,7},{5,4},{6,5},{7,6},{8,11},{9,8},{10,9... | collective-permute-start | bytes 1966088 | tf_op jit(solution)/shard_map/ppermute | solution.py:94
  207.9 18.6 %collective-permute-start.22 = (bf16[256,1280]{1,0:T(8,128)(2,1)}, bf16[256,1280]{1,0:T(8,128)(2,1)}, u32[]{:S(2)}, u32[]{:S(2)}) collective-permute-start(bf16[256,1280]{1,0:T(8,128)(2,1)} %convolution_convert_fusion.1), channel_id=1, source_target_pairs={{0,2},{1,3},{2,0},{3,1},{4,6},{5,7},{6,4},{7,5},{8,10},{9,11},{10,... | collective-permute-start | bytes 1966088 | tf_op jit(solution)/shard_map/ppermute | solution.py:94
  211.1 23.1 %collective-permute-start.21 = (bf16[256,1280]{1,0:T(8,128)(2,1)}, bf16[256,1280]{1,0:T(8,128)(2,1)}, u32[]{:S(2)}, u32[]{:S(2)}) collective-permute-start(bf16[256,1280]{1,0:T(8,128)(2,1)} %convolution_convert_fusion.2), channel_id=1, source_target_pairs={{0,1},{1,2},{2,3},{3,0},{4,5},{5,6},{6,7},{7,4},{8,9},{9,10},{10,1... | collective-permute-start | bytes 1966088 | tf_op jit(solution)/shard_map/ppermute | solution.py:94
  (17 other events, 264.0 us)

commit v5 on v4

--- a/solution.py
+++ b/solution.py
@@ -93,8 +93,8 @@
 def seq_shift(x, shift):
     return lax.ppermute(x, SEQ, [(k, (k + shift) % 4) for k in range(4)])
 
-def featurize(block, seq_length):
-    positions = jnp.arange(block.shape[0], dtype=jnp.int32).astype(jnp.float32)
+def featurize(block, offset, seq_length):
+    positions = (offset + jnp.arange(block.shape[0], dtype=jnp.int32)).astype(jnp.float32)
     angles = positions * (math.pi / (2.0 * seq_length))
     rectified = jnp.maximum(block.astype(jnp.float32), 0.0)
     cosine = rectified * jnp.cos(angles)[:, None, None]
@@ -102,42 +102,17 @@
     return jnp.concatenate([cosine, sine], axis=2).astype(jnp.bfloat16)
 
 
-def block_states(key_feat, value_heads):
-    blocks = key_feat.shape[0] // CH
-    key_blocks = key_feat.reshape(blocks, CH, key_feat.shape[1], key_feat.shape[2])
-    value_blocks = value_heads.reshape(blocks, CH, value_heads.shape[1], value_heads.shape[2])
-    return jnp.einsum(
-        "cjhf,cjhe->chfe", key_blocks, value_blocks, preferred_element_type=jnp.float32
-    )
-
-
-def attend(query_feat, key_feat, value_heads, states):
-    count = query_feat.shape[0]
-    heads_here = query_feat.shape[1]
-    blocks = count // CH
-    query_blocks = query_feat.reshape(blocks, CH, heads_here, 2 * HEAD)
-    key_blocks = key_feat.reshape(blocks, CH, heads_here, 2 * HEAD)
-    value_blocks = value_heads.reshape(blocks, CH, heads_here, HEAD)
-    scores = jnp.einsum(
-        "cihf,cjhf->chij", query_blocks, key_blocks, preferred_element_type=jnp.float32
-    )
-    causal_mask = jnp.arange(CH)[:, None] >= jnp.arange(CH)[None, :]
-    scores = jnp.where(causal_mask[None, None], scores, 0.0).astype(jnp.bfloat16)
-    inside_block = jnp.einsum(
-        "chij,cjhe->cihe", scores, value_blocks, preferred_element_type=jnp.float32
-    )
-    running = jnp.cumsum(states, axis=0)
-    before = jnp.concatenate([jnp.zeros_like(states[:1]), running[:-1]], axis=0)
-    before = before.astype(jnp.bfloat16)
-    from_before = jnp.einsum(
-        "cihf,chfe->cihe", query_blocks, before, preferred_element_type=jnp.float32
-    )
-    return (inside_block + from_before).reshape(count, heads_here, HEAD)
+def to_blocks(x):
+    return x.reshape((x.shape[0] // CH, CH) + x.shape[1:])
 
 
 def normalize(attended, gain_rows):
     mean_square = jnp.mean(attended * attended, axis=2, keepdims=True)
     return (attended * lax.rsqrt(mean_square + norm_eps) * gain_rows[None]).astype(jnp.bfloat16)
+
+
+def swap(x, axis):
+    return lax.ppermute(x, axis, [(0, 1), (1, 0)])
 
 
 def on_device(
@@ -154,44 +129,74 @@
     weights = updated.astype(jnp.bfloat16)
     tokens_here = queries.shape[1]
     seq_length = tokens_here * lax.axis_size(SEQ)
+    half = lax.axis_index("xh")
+    core = lax.axis_index("c")
+    heads_here = H // 2
     parts = gather_start(weights)
     parts, query_heads = lax.optimization_barrier(
         (parts, queries[0].reshape(tokens_here, H, HEAD))
     )
-    query_group = lax.all_to_all(query_heads, SEQ, split_axis=1, concat_axis=0, tiled=True)
+    query_group = lax.all_to_all(query_heads, "c", split_axis=1, concat_axis=0, tiled=True)
     sent = [ring_send(part, second, 4) for part, (_, second) in zip(parts, STAGES)]
     sent, key_heads = lax.optimization_barrier((sent, keys_in[0].reshape(tokens_here, H, HEAD)))
-    key_group = lax.all_to_all(key_heads, SEQ, split_axis=1, concat_axis=0, tiled=True)
+    key_group = lax.all_to_all(key_heads, "c", split_axis=1, concat_axis=0, tiled=True)
     sent = [ring_far(received, second, 4) for received, (_, second) in zip(sent, STAGES)]
     sent, value_heads = lax.optimization_barrier(
         (sent, values_in[0].reshape(tokens_here, H, HEAD))
     )
-    value_group = lax.all_to_all(value_heads, SEQ, split_axis=1, concat_axis=0, tiled=True)
-    heads_here = query_group.shape[1]
-    query_feat = featurize(query_group, seq_length)
-    key_feat = featurize(key_group, seq_length)
-    states = block_states(key_feat, value_group)
-    attended = attend(query_feat, key_feat, value_group, states)
-    gain_rows = lax.dynamic_slice_in_dim(
-        head_gain, lax.axis_index(SEQ) * heads_here, heads_here, 0
-    )
+    value_group = lax.all_to_all(value_heads, "c", split_axis=1, concat_axis=0, tiled=True)
+    span = query_group.shape[0]
+    offset = half * span
+    query_blocks = to_blocks(featurize(query_group, offset, seq_length))
+    key_blocks = to_blocks(featurize(key_group, offset, seq_length))
+    value_blocks = to_blocks(value_group)
+    states = jnp.einsum(
+        "cjhf,cjhe->chfe", key_blocks, value_blocks, preferred_element_type=jnp.float32
+    )
+    chip_total = jnp.sum(states, axis=0)
+    earlier = lax.ppermute(chip_total, "xh", [(0, 1)])
+    scores = jnp.einsum(
+        "cihf,cjhf->chij", query_blocks, key_blocks, preferred_element_type=jnp.float32
+    )
+    causal_mask = jnp.arange(CH)[:, None] >= jnp.arange(CH)[None, :]
+    scores = jnp.where(causal_mask[None, None], scores, 0.0).astype(jnp.bfloat16)
+    inside_block = jnp.einsum(
+        "chij,cjhe->cihe", scores, value_blocks, preferred_element_type=jnp.float32
+    )
+    running = jnp.cumsum(states, axis=0)
+    local_before = jnp.concatenate([jnp.zeros_like(states[:1]), running[:-1]], axis=0)
+    before = (earlier[None] + local_before).astype(jnp.bfloat16)
+    from_before = jnp.einsum(
+        "cihf,chfe->cihe", query_blocks, before, preferred_element_type=jnp.float32
+    )
+    attended = (inside_block + from_before).reshape(span, heads_here, HEAD)
+    gain_rows = lax.dynamic_slice_in_dim(head_gain, core * heads_here, heads_here, 0)
     normed_group = normalize(attended, gain_rows)
-    seq_index = lax.axis_index(SEQ)
-    flat_group = normed_group.reshape(normed_group.shape[0], heads_here * HEAD)
-    normed_all = jnp.concatenate(
-        [flat_group] + [seq_shift(flat_group, shift) for shift in (1, 2, 3)], axis=1
-    )
-    heads_order = (seq_index - jnp.arange(4)) % 4
-    cols = gather_finish(parts, sent, heads_order)
-    outputs = []
-    for shift in (2, 1, 3, 0):
-        chunk = lax.dynamic_slice_in_dim(
-            normed_all, ((seq_index + shift) % 4) * tokens_here, tokens_here, 0
-        )
-        part = jnp.dot(chunk, cols, preferred_element_type=jnp.float32).astype(jnp.bfloat16)
-        outputs.append((shift, part if shift == 0 else seq_shift(part, shift)))
-    by_shift = jnp.stack([part for _, part in sorted(outputs, key=lambda item: item[0])])
-    projected = jnp.take(by_shift, (seq_index - jnp.arange(4)) % 4, axis=0)
+    normed_own = lax.all_to_all(normed_group, "c", split_axis=0, concat_axis=1, tiled=True)
+    normed_own = normed_own.reshape(tokens_here, H * HEAD)
+    normed_peer = swap(normed_own, "xh")
+    mine = gather_finish(parts, sent, jnp.arange(4))
+    partner = swap(mine, "c")
+    tokens = jnp.concatenate([normed_peer, normed_own], axis=0)
+    wide = jnp.concatenate(
+        [
+            jnp.dot(tokens, mine, preferred_element_type=jnp.float32),
+            jnp.dot(tokens, partner, preferred_element_type=jnp.float32),
+        ],
+        axis=1,
+    ).astype(jnp.bfloat16)
+    returned = swap(wide[:tokens_here], "xh")
+    by_offset = jnp.stack(
+        [
+            wide[tokens_here:, : wide.shape[1] // 2],
+            wide[tokens_here:, wide.shape[1] // 2 :],
+            returned[:, : wide.shape[1] // 2],
+            returned[:, wide.shape[1] // 2 :],
+        ]
+    )
+    block = jnp.arange(4)
+    offsets = ((block // 2 - half) % 2) * 2 + (block % 2 - core) % 2
+    projected = jnp.take(by_offset, offsets, axis=0)
     projected = jnp.transpose(projected, (1, 0, 2)).reshape(tokens_here, -1)
     layer_out = projected[None]
     return (layer_out, updated, moment_one, moment_two)

time: 248 us -> 278 us (1.12)
  blocking collectives: 0 us -> 29.9 us
  starting transfers between devices: 57.6 us -> 44 us
  matrix products: 24.3 us -> 29.6 us
  local copies, waits for them, and re-layouts: 40.2 us -> 45.4 us
    all_to_all x0 -> x4, blocking collectives: none -> 29.9 us  [the longest x1 11.3 us: on_device(): lax.all_to_all(query_heads, 'c', split_axis=1, concat_axis=0, tiled=True)]
    all_to_all x3 -> x0, starting transfers between devices: 21.8 us -> none  [the longest x1 10 us: on_device(): lax.all_to_all(query_heads, SEQ, split_axis=1, concat_axis=0, tiled=True)]
    ppermute x6 -> x4, waiting for transfers between devices: 57.4 us -> 73.4 us  [the longest x3 57.3 us: swap(): return lax.ppermute(x, axis, [(0, 1), (1, 0)])]
    ppermute x6 -> x4, starting transfers between devices: 11 us -> 20.8 us  [the longest x3 15.2 us: swap(): return lax.ppermute(x, axis, [(0, 1), (1, 0)])]
    all_to_all x3 -> x0, waiting for transfers between devices: 6.18 us -> none  [the longest x1 6.18 us: on_device(): lax.all_to_all(value_heads, SEQ, split_axis=1, concat_axis=0, tiled=True)]
    dot_general x7 -> x5, matrix products: 24.3 us -> 29.6 us  [the longest x1 6.51 us: on_device(): jnp.einsum('cjhf,cjhe->chfe', key_blocks, value_blocks, preferred_element...]
    ppermute x4, waiting for transfers between devices: 10.3 us -> 5.24 us  [ring_far(): lax.ppermute(from_left[:half], axis, forward)]
    all_to_all x1 -> x2, local copies, waits for them, and re-layouts: 2.46 us -> 6.6 us  [the longest x1 4.15 us: on_device(): lax.all_to_all(normed_group, 'c', split_axis=0, concat_axis=1, tiled=True)]
  transfers between devices with their start and end apart: 27 -> 22, of which waited for: 15 -> 12; matrix products, arithmetic and copies ran while one was open for 22% -> 24% of each run, Pallas kernels for 0% -> 0%
where the time goes in v5:
time: 278 us; the launch traced here: 276 us
  waiting for transfers between devices  90.5 us (33%)
  local copies, waits for them, and re-layouts  45.4 us (16%)
  starting transfers between devices  44 us (16%)
  other arithmetic  36.2 us (13%)
  blocking collectives  29.9 us (11%)
  matrix products  29.6 us (11%)
    ppermute x3, waiting for transfers between devices, swap(): return lax.ppermute(x, axis, [(0, 1), (1, 0)])  57.3 us
    ppermute x1, waiting for transfers between devices, on_device(): earlier = lax.ppermute(chip_total, 'xh', [(0, 1)])  16.1 us
    ppermute x3, starting transfers between devices, swap(): return lax.ppermute(x, axis, [(0, 1), (1, 0)])  15.2 us
    unnamed x36, local copies, waits for them, and re-layouts  11.4 us
    ppermute x8, starting transfers between devices, ring_send(): return (lax.ppermute(x, axis, forward), lax.ppermute(x, axis, backward))  11.3 us
    all_to_all x1, blocking collectives, on_device(): lax.all_to_all(query_heads, 'c', split_axis=1, concat_axis=0, tiled=True)  11.3 us
    ppermute x8, waiting for transfers between devices, ring_send(): return (lax.ppermute(x, axis, forward), lax.ppermute(x, axis, backward))  9.24 us
    gather x2, local copies, waits for them, and re-layouts, gather_finish(): pieces.append(jnp.take(flat, source, axis=0).reshape(-1, part.shape[-1]))  7.21 us
  transfers between devices with their start and end apart: 22, of which 12 were waited for; matrix products, arithmetic and copies ran while one was open for 24% of the time, Pallas kernels for 0%

profile of v5, /device:TPU:1, one launch (start us, length us, event | category | flops | bytes accessed | tf_op | source)
XLA Modules:
  0.0 276.5 jit_solution(8791544084510969865)
XLA Ops:
  34.1 3.5 %collective-permute-done.11 = bf16[4,2,80,640]{3,2,1,0:T(8,128)(2,1)} collective-permute-done((bf16[4,2,80,640]{3,2,1,0:T(8,128)(2,1)S(1)}, bf16[4,2,80,640]{3,2,1,0:T(8,128)(2,1)}, u32[]{:S(2)}, u32[]{:S(2)}) %collective-permute-start.11) | collective-permute-done | bytes 819232 | tf_op jit(solution)/shard_map/ppermute | solution.py:29
  69.5 4.6 %gather_fusion.2 = bf16[32,80,640]{2,1,0:T(8,128)(2,1)} fusion(bf16[32,80,640]{2,1,0:T(8,128)(2,1)} %bitcast.92, s32[1024]{0:T(1024)S(1)} %pad_clamp_fusion.1), kind=kCustom, calls=%fused_computation.1.clone | custom fusion | bytes 6553728 | tf_op jit(solution)/shard_map/jit(_take)/gather | solution.py:89
  76.5 3.5 %pad_maximum_fusion = bf16[2560,1280]{1,0:T(8,128)(2,1)} fusion(bf16[2560,640]{1,0:T(8,128)(2,1)S(1)} %bitcast.89, bf16[2560,640]{1,0:T(8,128)(2,1)S(1)} %bitcast.87), kind=kLoop, calls=%fused_computation.3 | loop fusion | flops 13107200 | bytes 13107200 | tf_op jit(solution)/shard_map/concatenate | solution.py:90
  80.2 8.8 %collective-permute-start.20 = (bf16[2560,1280]{1,0:T(8,128)(2,1)}, bf16[2560,1280]{1,0:T(8,128)(2,1)}, u32[]{:S(2)}, u32[]{:S(2)}) collective-permute-start(bf16[2560,1280]{1,0:T(8,128)(2,1)} %pad_maximum_fusion), channel_id=1, source_target_pairs={{0,1},{1,0},{2,3},{3,2},{4,5},{5,4},{6,7},{7,6},{8,9},{9,8},{10,11... | collective-permute-start | bytes 19660808 | tf_op jit(solution)/shard_map/ppermute | solution.py:115
  89.1 11.3 %all_to_all.48 = bf16[256,20,128]{0,2,1:T(8,128)(2,1)S(1)} all-to-all(bf16[256,20,128]{0,2,1:T(8,128)(2,1)} %bitcast.101), channel_id=1, replica_groups=mesh['z'=4,'xl'=2,'y'=4,'xh'=2,'c'=2] {'c'}, dimensions={1} | all-to-all | bytes 2621440 | tf_op jit(solution)/shard_map/all_to_all | solution.py:139
  102.1 3.2 %copy.59 = f32[2,256,10,128]{3,1,0,2:T(8,128)} copy(f32[2,256,10,128]{1,3,2,0:T(8,128)} %bitcast.93) | data formatting | bytes 5242880 | tf_op jit(solution)/shard_map/max | solution.py:99
  105.3 5.9 %all_to_all.49 = bf16[256,20,128]{0,2,1:T(8,128)(2,1)S(1)} all-to-all(bf16[256,20,128]{0,2,1:T(8,128)(2,1)} %bitcast.102), channel_id=1, replica_groups=mesh['z'=4,'xl'=2,'y'=4,'xh'=2,'c'=2] {'c'}, dimensions={1} | all-to-all | bytes 2621440 | tf_op jit(solution)/shard_map/all_to_all | solution.py:142
  113.0 3.2 %copy.63 = f32[2,256,10,128]{3,1,0,2:T(8,128)} copy(f32[2,256,10,128]{1,3,2,0:T(8,128)} %bitcast.94) | data formatting | bytes 5242880 | tf_op jit(solution)/shard_map/max | solution.py:99
  116.2 6.4 %multiply_convert_fusion.1 = (bf16[4,128,10,128]{3,1,2,0:T(8,128)(2,1)}, bf16[4,128,10,128]{3,1,2,0:T(8,128)(2,1)}, bf16[4,128,10,128]{3,1,2,0:T(8,128)(2,1)}, bf16[4,128,10,128]{3,1,2,0:T(8,128)(2,1)}) fusion(f32[4,128,10,128]{3,1,0,2:T(8,128)} %bitcast.97, f32[4,128]{1,0:T(4,128)S(1)} %get-tuple-element.83, f32[4,128]{1,0:T(4,128)S(1)} %get-tuple-element.82, ...), kind=kLoop, calls=%fused_computation.25 | loop fusion | flops 5242880 | bytes 10489856 | tf_op jit(solution)/shard_map/convert.2
  122.7 5.6 %all_to_all.50 = bf16[256,20,128]{0,2,1:T(8,128)(2,1)} all-to-all(bf16[256,20,128]{0,2,1:T(8,128)(2,1)S(1)} %bitcast.103), channel_id=1, replica_groups=mesh['z'=4,'xl'=2,'y'=4,'xh'=2,'c'=2] {'c'}, dimensions={1} | all-to-all | bytes 2621440 | tf_op jit(solution)/shard_map/all_to_all | solution.py:147
  130.7 6.5 %fusion.48 = (f32[10,256,128]{2,1,0:T(8,128)}, f32[4,10,256,128]{3,2,1,0:T(8,128)}) fusion(bf16[4,128,10,128]{3,1,0,2:T(8,128)(2,1)} %bitcast.99, bf16[4,128,10,128]{3,1,2,0:T(8,128)(2,1)} %get-tuple-element.61, bf16[4,128,10,128]{3,1,2,0:T(8,128)(2,1)} %get-tuple-element.60), kind=kOutput, calls=%fused_computation.157 | convolution fusion | flops 341770240 | bytes 10485760 | tf_op jit(solution)/shard_map/cjhf,cjhe->chfe/dot_general | solution.py:153
  137.2 5.6 %collective-permute-start.18 = (f32[10,256,128]{2,1,0:T(8,128)}, f32[10,256,128]{2,1,0:T(8,128)}, u32[]{:S(2)}, u32[]{:S(2)}) collective-permute-start(f32[10,256,128]{2,1,0:T(8,128)} %get-tuple-element.78), channel_id=1, source_target_pairs={{0,2},{1,3},{4,6},{5,7},{8,10},{9,11},{12,14},{13,15},{16,18},{17,... | collective-permute-start | bytes 3932168 | tf_op jit(solution)/shard_map/ppermute | solution.py:157
  142.8 3.0 %fusion.49 = f32[4,10,256,128]{3,2,1,0:T(8,128)S(1)} fusion(f32[4,10,256,128]{3,2,1,0:T(8,128)} %get-tuple-element.79), kind=kOutput, calls=%fused_computation.158 | output fusion | flops 3932160 | bytes 10485760 | tf_op jit(solution)/shard_map/jit(cumsum)/reduce_window_sum | solution.py:166
  148.1 5.6 %fusion.5 = f32[4,10,128,128]{2,3,1,0:T(8,128)} fusion(bf16[4,128,10,128]{3,1,2,0:T(8,128)(2,1)} %get-tuple-element.61, bf16[4,128,10,128]{3,1,2,0:T(8,128)(2,1)} %get-tuple-element.60, bf16[4,128,10,128]{3,1,2,0:T(8,128)(2,1)} %get-tuple-element.72, bf16[4,128,10,128]{3,1,2,0:T(8,128)(2,1)} %get-tuple-element.73, ...), kind=kOutput, calls=%fused_computation.31 | convolution fusion | flops 515112960 | bytes 9191424 | tf_op jit(solution)/shard_map/chij,cjhe->cihe/dot_general | solution.py:163
  153.7 16.1 %collective-permute-done.18 = f32[10,256,128]{2,1,0:T(8,128)} collective-permute-done((f32[10,256,128]{2,1,0:T(8,128)}, f32[10,256,128]{2,1,0:T(8,128)}, u32[]{:S(2)}, u32[]{:S(2)}) %collective-permute-start.18) | collective-permute-done | bytes 1310752 | tf_op jit(solution)/shard_map/ppermute | solution.py:157
  169.8 5.0 %multiply_reduce_fusion = (f32[4,128,10]{1,2,0:T(8,128)S(1)}, f32[4,128,10,128]{3,1,2,0:T(8,128)S(1)}) fusion(f32[4,10,128,128]{2,3,1,0:T(8,128)} %fusion.5, f32[3,10,256,128]{3,2,1,0:T(8,128)} %slice.83, f32[10,256,128]{2,1,0:T(8,128)} %collective-permute-done.18, bf16[4,128,10,128]{3,1,2,0:T(8,128)(2,1)} %get-tuple-element.72, ...), kind=kOutput, calls=%fused_computation.20 | convolution fusion | flops 345369600 | bytes 13127680 | tf_op jit(solution)/shard_map/cihf,chfe->cihe/dot_general | solution.py:169
  177.1 7.1 %all_to_all.51 = bf16[512,10,128]{2,1,0:T(8,128)(2,1)} all-to-all(bf16[512,10,128]{2,1,0:T(8,128)(2,1)S(1)} %copy.71), channel_id=1, replica_groups=mesh['z'=4,'xl'=2,'y'=4,'xh'=2,'c'=2] {'c'}, dimensions={0} | all-to-all | bytes 2621440 | tf_op jit(solution)/shard_map/all_to_all | solution.py:175
  184.2 4.2 %copy.73 = bf16[256,2,10,128]{0,3,2,1:T(8,128)(2,1)} copy(bf16[256,2,10,128]{3,2,0,1:T(8,128)(2,1)} %bitcast.98) | data formatting | bytes 2621440 | tf_op jit(solution)/shard_map/all_to_all | solution.py:175
  188.4 3.7 %collective-permute-start.19 = (bf16[256,2560]{0,1:T(8,128)(2,1)}, bf16[256,2560]{0,1:T(8,128)(2,1)S(1)}, u32[]{:S(2)}, u32[]{:S(2)}) collective-permute-start(bf16[256,2560]{0,1:T(8,128)(2,1)} %bitcast.111), channel_id=1, source_target_pairs={{0,2},{2,0},{1,3},{3,1},{4,6},{6,4},{5,7},{7,5},{8,10},{10,8},{9,1... | collective-permute-start | bytes 3932168 | tf_op jit(solution)/shard_map/ppermute | solution.py:115
  192.1 29.1 %collective-permute-done.19 = bf16[256,2560]{0,1:T(8,128)(2,1)S(1)} collective-permute-done((bf16[256,2560]{0,1:T(8,128)(2,1)}, bf16[256,2560]{0,1:T(8,128)(2,1)S(1)}, u32[]{:S(2)}, u32[]{:S(2)}) %collective-permute-start.19) | collective-permute-done | bytes 1310752 | tf_op jit(solution)/shard_map/ppermute | solution.py:115
  221.2 6.0 %convolution_convert_fusion.1 = bf16[512,1280]{1,0:T(8,128)(2,1)S(1)} fusion(bf16[256,2560]{0,1:T(8,128)(2,1)} %bitcast.112, bf16[256,2560]{0,1:T(8,128)(2,1)S(1)} %collective-permute-done.19, bf16[2560,640]{1,0:T(8,128)(2,1)} %bitcast.90, bf16[2560,640]{1,0:T(8,128)(2,1)S(1)} %bitcast.88), kind=kOutput, calls=%fused_computation.10 | convolution fusion | flops 3374448640 | bytes 10485760 | tf_op jit(solution)/shard_map/dot_general | solution.py:183
  227.2 6.5 %convolution_convert_fusion = bf16[512,1280]{1,0:T(8,128)(2,1)S(1)} fusion(bf16[2560,1280]{1,0:T(8,128)(2,1)} %collective-permute-done.20, bf16[256,2560]{0,1:T(8,128)(2,1)S(1)} %bitcast.113, bf16[256,2560]{0,1:T(8,128)(2,1)S(1)} %collective-permute-done.19), kind=kOutput, calls=%fused_computation.9 | convolution fusion | flops 3361341440 | bytes 10485760 | tf_op jit(solution)/shard_map/dot_general | solution.py:184
  236.6 28.2 %collective-permute-done.21 = bf16[256,2560]{1,0:T(8,128)(2,1)S(1)} collective-permute-done((bf16[256,2560]{1,0:T(8,128)(2,1)S(1)}, bf16[256,2560]{1,0:T(8,128)(2,1)S(1)}, u32[]{:S(2)}, u32[]{:S(2)}) %collective-permute-start.21) | collective-permute-done | bytes 1310752 | tf_op jit(solution)/shard_map/ppermute | solution.py:115
  272.1 4.4 %copy.75 = bf16[1,256,5120]{2,1,0:T(8,128)(2,1)} copy(bf16[1,256,5120]{1,2,0:T(8,128)(2,1)} %bitcast.95) | data formatting | bytes 5242880
  (124 shorter events, 88.4 us)
Async XLA Ops:
  0.6 142.2 %copy-start = (f32[20,128]{1,0:T(8,128)S(1)}, f32[20,128]{1,0:T(8,128)}, u32[]{:S(2)}) copy-start(f32[20,128]{1,0:T(8,128)} %param.13) | copy-start | bytes 30724
  3.4 4.2 %collective-permute-start.5 = (bf16[80,640]{1,0:T(8,128)(2,1)S(1)}, bf16[80,640]{1,0:T(8,128)(2,1)S(1)}, u32[]{:S(2)}, u32[]{:S(2)}) collective-permute-start(bf16[80,640]{1,0:T(8,128)(2,1)S(1)} %get-tuple-element.68), channel_id=1, source_target_pairs={{0,16},{16,0},{1,17},{17,1},{2,18},{18,2},{3,19},{19,3},{4,20},{20... | collective-permute-start | bytes 307208 | tf_op jit(solution)/shard_map/ppermute | solution.py:26
  5.5 6.2 %collective-permute-start = (bf16[80,640]{1,0:T(8,128)(2,1)S(1)}, bf16[80,640]{1,0:T(8,128)(2,1)S(1)}, u32[]{:S(2)}, u32[]{:S(2)}) collective-permute-start(bf16[80,640]{1,0:T(8,128)(2,1)S(1)} %get-tuple-element.69), channel_id=1, source_target_pairs={{0,16},{16,0},{1,17},{17,1},{2,18},{18,2},{3,19},{19,3},{4,20},{20... | collective-permute-start | bytes 307208 | tf_op jit(solution)/shard_map/ppermute | solution.py:26
  7.6 7.2 %collective-permute-start.6 = (bf16[2,80,640]{2,1,0:T(8,128)(2,1)S(1)}, bf16[2,80,640]{2,1,0:T(8,128)(2,1)S(1)}, u32[]{:S(2)}, u32[]{:S(2)}) collective-permute-start(bf16[2,80,640]{2,1,0:T(8,128)(2,1)S(1)} %get-tuple-element.65), channel_id=1, source_target_pairs={{0,32},{32,64},{64,96},{96,0},{1,33},{33,65},{65,97},{97,1},{2,34}... | collective-permute-start | bytes 614408 | tf_op jit(solution)/shard_map/ppermute | solution.py:29
  9.6 5.5 %collective-permute-start.8 = (bf16[2,80,640]{2,1,0:T(8,128)(2,1)S(1)}, bf16[2,80,640]{2,1,0:T(8,128)(2,1)S(1)}, u32[]{:S(2)}, u32[]{:S(2)}) collective-permute-start(bf16[2,80,640]{2,1,0:T(8,128)(2,1)S(1)} %get-tuple-element.65), channel_id=1, source_target_pairs={{0,96},{32,0},{64,32},{96,64},{1,97},{33,1},{65,33},{97,65},{2,98}... | collective-permute-start | bytes 614408 | tf_op jit(solution)/shard_map/ppermute | solution.py:29
  11.8 7.3 %collective-permute-start.1 = (bf16[2,80,640]{2,1,0:T(8,128)(2,1)S(1)}, bf16[2,80,640]{2,1,0:T(8,128)(2,1)S(1)}, u32[]{:S(2)}, u32[]{:S(2)}) collective-permute-start(bf16[2,80,640]{2,1,0:T(8,128)(2,1)S(1)} %get-tuple-element.71), channel_id=1, source_target_pairs={{0,4},{4,8},{8,12},{12,0},{1,5},{5,9},{9,13},{13,1},{2,6},{6,10},{... | collective-permute-start | bytes 614408 | tf_op jit(solution)/shard_map/ppermute | solution.py:29
  13.2 7.3 %collective-permute-start.3 = (bf16[2,80,640]{2,1,0:T(8,128)(2,1)S(1)}, bf16[2,80,640]{2,1,0:T(8,128)(2,1)S(1)}, u32[]{:S(2)}, u32[]{:S(2)}) collective-permute-start(bf16[2,80,640]{2,1,0:T(8,128)(2,1)S(1)} %get-tuple-element.71), channel_id=1, source_target_pairs={{0,12},{4,0},{8,4},{12,8},{1,13},{5,1},{9,5},{13,9},{2,14},{6,2},{... | collective-permute-start | bytes 614408 | tf_op jit(solution)/shard_map/ppermute | solution.py:29
  14.8 7.2 %collective-permute-start.7 = (bf16[1,80,640]{2,1,0:T(8,128)(2,1)S(1)}, bf16[1,80,640]{2,1,0:T(8,128)(2,1)S(1)}, u32[]{:S(2)}, u32[]{:S(2)}) collective-permute-start(bf16[1,80,640]{2,1,0:T(8,128)(2,1)S(1)} %slice.81), channel_id=1, source_target_pairs={{0,32},{32,64},{64,96},{96,0},{1,33},{33,65},{65,97},{97,1},{2,34}... | collective-permute-start | bytes 307208 | tf_op jit(solution)/shard_map/ppermute | solution.py:41
  15.1 7.0 %collective-permute-start.9 = (bf16[1,80,640]{2,1,0:T(8,128)(2,1)S(1)}, bf16[1,80,640]{2,1,0:T(8,128)(2,1)S(1)}, u32[]{:S(2)}, u32[]{:S(2)}) collective-permute-start(bf16[1,80,640]{2,1,0:T(8,128)(2,1)S(1)} %slice.82), channel_id=1, source_target_pairs={{0,96},{32,0},{64,32},{96,64},{1,97},{33,1},{65,33},{97,65},{2,98}... | collective-permute-start | bytes 307208 | tf_op jit(solution)/shard_map/ppermute | solution.py:42
  19.1 5.0 %collective-permute-start.2 = (bf16[1,80,640]{2,1,0:T(8,128)(2,1)S(1)}, bf16[1,80,640]{2,1,0:T(8,128)(2,1)S(1)}, u32[]{:S(2)}, u32[]{:S(2)}) collective-permute-start(bf16[1,80,640]{2,1,0:T(8,128)(2,1)S(1)} %slice.78), channel_id=1, source_target_pairs={{0,4},{4,8},{8,12},{12,0},{1,5},{5,9},{9,13},{13,1},{2,6},{6,10},{... | collective-permute-start | bytes 307208 | tf_op jit(solution)/shard_map/ppermute | solution.py:41
  20.5 3.6 %collective-permute-start.4 = (bf16[1,80,640]{2,1,0:T(8,128)(2,1)S(1)}, bf16[1,80,640]{2,1,0:T(8,128)(2,1)S(1)}, u32[]{:S(2)}, u32[]{:S(2)}) collective-permute-start(bf16[1,80,640]{2,1,0:T(8,128)(2,1)S(1)} %slice.79), channel_id=1, source_target_pairs={{0,12},{4,0},{8,4},{12,8},{1,13},{5,1},{9,5},{13,9},{2,14},{6,2},{... | collective-permute-start | bytes 307208 | tf_op jit(solution)/shard_map/ppermute | solution.py:42
  24.3 13.4 %collective-permute-start.11 = (bf16[4,2,80,640]{3,2,1,0:T(8,128)(2,1)S(1)}, bf16[4,2,80,640]{3,2,1,0:T(8,128)(2,1)}, u32[]{:S(2)}, u32[]{:S(2)}) collective-permute-start(bf16[4,2,80,640]{3,2,1,0:T(8,128)(2,1)S(1)} %pad_maximum_fusion.18), channel_id=1, source_target_pairs={{0,96},{32,0},{64,32},{96,64},{1,97},{33,1},{65,33},{97,65},{2,98}... | collective-permute-start | bytes 2457608 | tf_op jit(solution)/shard_map/ppermute | solution.py:29
  25.5 15.0 %collective-permute-start.10 = (bf16[4,2,80,640]{3,2,1,0:T(8,128)(2,1)S(1)}, bf16[4,2,80,640]{3,2,1,0:T(8,128)(2,1)}, u32[]{:S(2)}, u32[]{:S(2)}) collective-permute-start(bf16[4,2,80,640]{3,2,1,0:T(8,128)(2,1)S(1)} %pad_maximum_fusion.18), channel_id=1, source_target_pairs={{0,32},{32,64},{64,96},{96,0},{1,33},{33,65},{65,97},{97,1},{2,34}... | collective-permute-start | bytes 2457608 | tf_op jit(solution)/shard_map/ppermute | solution.py:29
  25.8 14.7 %collective-permute-start.13 = (bf16[4,2,80,640]{3,2,1,0:T(8,128)(2,1)S(1)}, bf16[4,2,80,640]{3,2,1,0:T(8,128)(2,1)S(1)}, u32[]{:S(2)}, u32[]{:S(2)}) collective-permute-start(bf16[4,2,80,640]{3,2,1,0:T(8,128)(2,1)S(1)} %pad_maximum_fusion.19), channel_id=1, source_target_pairs={{0,12},{4,0},{8,4},{12,8},{1,13},{5,1},{9,5},{13,9},{2,14},{6,2},{... | collective-permute-start | bytes 2457608 | tf_op jit(solution)/shard_map/ppermute | solution.py:29
  28.5 14.7 %collective-permute-start.12 = (bf16[4,2,80,640]{3,2,1,0:T(8,128)(2,1)S(1)}, bf16[4,2,80,640]{3,2,1,0:T(8,128)(2,1)S(1)}, u32[]{:S(2)}, u32[]{:S(2)}) collective-permute-start(bf16[4,2,80,640]{3,2,1,0:T(8,128)(2,1)S(1)} %pad_maximum_fusion.19), channel_id=1, source_target_pairs={{0,4},{4,8},{8,12},{12,0},{1,5},{5,9},{9,13},{13,1},{2,6},{6,10},{... | collective-permute-start | bytes 2457608 | tf_op jit(solution)/shard_map/ppermute | solution.py:29
  47.9 7.1 %collective-permute-start.17 = (bf16[2,2,80,640]{3,2,1,0:T(8,128)(2,1)}, bf16[2,2,80,640]{3,2,1,0:T(8,128)(2,1)}, u32[]{:S(2)}, u32[]{:S(2)}) collective-permute-start(bf16[2,2,80,640]{3,2,1,0:T(8,128)(2,1)} %slice.59), channel_id=1, source_target_pairs={{0,12},{4,0},{8,4},{12,8},{1,13},{5,1},{9,5},{13,9},{2,14},{6,2},{... | collective-permute-start | bytes 1228808 | tf_op jit(solution)/shard_map/ppermute | solution.py:42
  48.3 8.0 %collective-permute-start.16 = (bf16[2,2,80,640]{3,2,1,0:T(8,128)(2,1)S(1)}, bf16[2,2,80,640]{3,2,1,0:T(8,128)(2,1)S(1)}, u32[]{:S(2)}, u32[]{:S(2)}) collective-permute-start(bf16[2,2,80,640]{3,2,1,0:T(8,128)(2,1)S(1)} %slice.58), channel_id=1, source_target_pairs={{0,4},{4,8},{8,12},{12,0},{1,5},{5,9},{9,13},{13,1},{2,6},{6,10},{... | collective-permute-start | bytes 1228808 | tf_op jit(solution)/shard_map/ppermute | solution.py:41
  49.3 9.0 %collective-permute-start.15 = (bf16[2,2,80,640]{3,2,1,0:T(8,128)(2,1)}, bf16[2,2,80,640]{3,2,1,0:T(8,128)(2,1)S(1)}, u32[]{:S(2)}, u32[]{:S(2)}) collective-permute-start(bf16[2,2,80,640]{3,2,1,0:T(8,128)(2,1)} %slice.57), channel_id=1, source_target_pairs={{0,96},{32,0},{64,32},{96,64},{1,97},{33,1},{65,33},{97,65},{2,98}... | collective-permute-start | bytes 1228808 | tf_op jit(solution)/shard_map/ppermute | solution.py:42
  51.8 8.5 %collective-permute-start.14 = (bf16[2,2,80,640]{3,2,1,0:T(8,128)(2,1)}, bf16[2,2,80,640]{3,2,1,0:T(8,128)(2,1)S(1)}, u32[]{:S(2)}, u32[]{:S(2)}) collective-permute-start(bf16[2,2,80,640]{3,2,1,0:T(8,128)(2,1)} %slice.56), channel_id=1, source_target_pairs={{0,32},{32,64},{64,96},{96,0},{1,33},{33,65},{65,97},{97,1},{2,34}... | collective-permute-start | bytes 1228808 | tf_op jit(solution)/shard_map/ppermute | solution.py:41
  80.2 147.0 %collective-permute-start.20 = (bf16[2560,1280]{1,0:T(8,128)(2,1)}, bf16[2560,1280]{1,0:T(8,128)(2,1)}, u32[]{:S(2)}, u32[]{:S(2)}) collective-permute-start(bf16[2560,1280]{1,0:T(8,128)(2,1)} %pad_maximum_fusion), channel_id=1, source_target_pairs={{0,1},{1,0},{2,3},{3,2},{4,5},{5,4},{6,7},{7,6},{8,9},{9,8},{10,11... | collective-permute-start | bytes 19660808 | tf_op jit(solution)/shard_map/ppermute | solution.py:115
  137.2 32.6 %collective-permute-start.18 = (f32[10,256,128]{2,1,0:T(8,128)}, f32[10,256,128]{2,1,0:T(8,128)}, u32[]{:S(2)}, u32[]{:S(2)}) collective-permute-start(f32[10,256,128]{2,1,0:T(8,128)} %get-tuple-element.78), channel_id=1, source_target_pairs={{0,2},{1,3},{4,6},{5,7},{8,10},{9,11},{12,14},{13,15},{16,18},{17,... | collective-permute-start | bytes 3932168 | tf_op jit(solution)/shard_map/ppermute | solution.py:157
  188.4 38.9 %copy-start.14 = (bf16[256,2,10,128]{0,3,2,1:T(8,128)(2,1)S(1)}, bf16[256,2,10,128]{0,3,2,1:T(8,128)(2,1)}, u32[]{:S(2)}) copy-start(bf16[256,2,10,128]{0,3,2,1:T(8,128)(2,1)} %copy.73) | copy-start | bytes 3932164
  188.4 32.8 %collective-permute-start.19 = (bf16[256,2560]{0,1:T(8,128)(2,1)}, bf16[256,2560]{0,1:T(8,128)(2,1)S(1)}, u32[]{:S(2)}, u32[]{:S(2)}) collective-permute-start(bf16[256,2560]{0,1:T(8,128)(2,1)} %bitcast.111), channel_id=1, source_target_pairs={{0,2},{2,0},{1,3},{3,1},{4,6},{6,4},{5,7},{7,5},{8,10},{10,8},{9,1... | collective-permute-start | bytes 3932168 | tf_op jit(solution)/shard_map/ppermute | solution.py:115
  233.8 31.0 %collective-permute-start.21 = (bf16[256,2560]{1,0:T(8,128)(2,1)S(1)}, bf16[256,2560]{1,0:T(8,128)(2,1)S(1)}, u32[]{:S(2)}, u32[]{:S(2)}) collective-permute-start(bf16[256,2560]{1,0:T(8,128)(2,1)S(1)} %pad_maximum_fusion.17), channel_id=1, source_target_pairs={{0,2},{2,0},{1,3},{3,1},{4,6},{6,4},{5,7},{7,5},{8,10},{10,8},{9,1... | collective-permute-start | bytes 3932168 | tf_op jit(solution)/shard_map/ppermute | solution.py:115
  (13 other events, 119.9 us)

commit v6 on v5

--- a/solution.py
+++ b/solution.py
@@ -115,6 +115,18 @@
     return lax.ppermute(x, axis, [(0, 1), (1, 0)])
 
 
+def pair_exchange(x, core, keep_axis, join_axis):
+    size = x.shape[keep_axis] // 2
+    mine = lax.dynamic_slice_in_dim(x, core * size, size, keep_axis)
+    theirs = lax.dynamic_slice_in_dim(x, (1 - core) * size, size, keep_axis)
+    received = swap(theirs, "c")
+    return jnp.where(
+        core == 0,
+        jnp.concatenate([mine, received], axis=join_axis),
+        jnp.concatenate([received, mine], axis=join_axis),
+    )
+
+
 def on_device(
     queries, keys_in, values_in, head_gain, master_weight, gradient, first_moment, second_moment
 ):
@@ -136,15 +148,15 @@
     parts, query_heads = lax.optimization_barrier(
         (parts, queries[0].reshape(tokens_here, H, HEAD))
     )
-    query_group = lax.all_to_all(query_heads, "c", split_axis=1, concat_axis=0, tiled=True)
+    query_group = pair_exchange(query_heads, core, 1, 0)
     sent = [ring_send(part, second, 4) for part, (_, second) in zip(parts, STAGES)]
     sent, key_heads = lax.optimization_barrier((sent, keys_in[0].reshape(tokens_here, H, HEAD)))
-    key_group = lax.all_to_all(key_heads, "c", split_axis=1, concat_axis=0, tiled=True)
+    key_group = pair_exchange(key_heads, core, 1, 0)
     sent = [ring_far(received, second, 4) for received, (_, second) in zip(sent, STAGES)]
     sent, value_heads = lax.optimization_barrier(
         (sent, values_in[0].reshape(tokens_here, H, HEAD))
     )
-    value_group = lax.all_to_all(value_heads, "c", split_axis=1, concat_axis=0, tiled=True)
+    value_group = pair_exchange(value_heads, core, 1, 0)
     span = query_group.shape[0]
     offset = half * span
     query_blocks = to_blocks(featurize(query_group, offset, seq_length))
@@ -172,26 +184,33 @@
     attended = (inside_block + from_before).reshape(span, heads_here, HEAD)
     gain_rows = lax.dynamic_slice_in_dim(head_gain, core * heads_here, heads_here, 0)
     normed_group = normalize(attended, gain_rows)
-    normed_own = lax.all_to_all(normed_group, "c", split_axis=0, concat_axis=1, tiled=True)
+    normed_own = pair_exchange(normed_group, core, 0, 1)
     normed_own = normed_own.reshape(tokens_here, H * HEAD)
     normed_peer = swap(normed_own, "xh")
     mine = gather_finish(parts, sent, jnp.arange(4))
     partner = swap(mine, "c")
-    tokens = jnp.concatenate([normed_peer, normed_own], axis=0)
-    wide = jnp.concatenate(
-        [
-            jnp.dot(tokens, mine, preferred_element_type=jnp.float32),
-            jnp.dot(tokens, partner, preferred_element_type=jnp.float32),
+    peer_wide = jnp.concatenate(
+        [
+            jnp.dot(normed_peer, mine, preferred_element_type=jnp.float32),
+            jnp.dot(normed_peer, partner, preferred_element_type=jnp.float32),
         ],
         axis=1,
     ).astype(jnp.bfloat16)
-    returned = swap(wide[:tokens_here], "xh")
+    returned = swap(peer_wide, "xh")
+    own_wide = jnp.concatenate(
+        [
+            jnp.dot(normed_own, mine, preferred_element_type=jnp.float32),
+            jnp.dot(normed_own, partner, preferred_element_type=jnp.float32),
+        ],
+        axis=1,
+    ).astype(jnp.bfloat16)
+    width = own_wide.shape[1] // 2
     by_offset = jnp.stack(
         [
-            wide[tokens_here:, : wide.shape[1] // 2],
-            wide[tokens_here:, wide.shape[1] // 2 :],
-            returned[:, : wide.shape[1] // 2],
-            returned[:, wide.shape[1] // 2 :],
+            own_wide[:, :width],
+            own_wide[:, width:],
+            returned[:, :width],
+            returned[:, width:],
         ]
     )
     block = jnp.arange(4)

time: 278 us -> 260 us (0.935)
  blocking collectives: 29.9 us -> 0 us
  other arithmetic: 36.2 us -> 47.6 us
  waiting for transfers between devices: 90.5 us -> 80.2 us
  starting transfers between devices: 44 us -> 50.5 us
  matrix products: 29.6 us -> 32.6 us
    all_to_all x4 -> x0, blocking collectives: 29.9 us -> none  [the longest x1 11.3 us: on_device(): lax.all_to_all(query_heads, 'c', split_axis=1, concat_axis=0, tiled=True)]
    another operation x8, other arithmetic: 3.94 us -> 10.8 us  [ring_finish(): return jnp.stack((x,) + tuple(received))]
    all_to_all x2 -> x0, local copies, waits for them, and re-layouts: 6.6 us -> none  [the longest x1 4.15 us: on_device(): lax.all_to_all(normed_group, 'c', split_axis=0, concat_axis=1, tiled=True)]
    ppermute x3 -> x7, starting transfers between devices: 15.2 us -> 20.9 us  [swap(): return lax.ppermute(x, axis, [(0, 1), (1, 0)])]
    ppermute x3 -> x7, waiting for transfers between devices: 57.3 us -> 52.3 us  [swap(): return lax.ppermute(x, axis, [(0, 1), (1, 0)])]
    select_n x0 -> x2, local copies, waits for them, and re-layouts: none -> 4.92 us  [pair_exchange(): jnp.where(core == 0, jnp.concatenate([mine, received], axis=join_axis), j...]
    select_n x0 -> x2, other arithmetic: none -> 3.95 us  [pair_exchange(): jnp.where(core == 0, jnp.concatenate([mine, received], axis=join_axis), j...]
    dynamic_slice x0 -> x4, local copies, waits for them, and re-layouts: none -> 3.63 us  [pair_exchange(): mine = lax.dynamic_slice_in_dim(x, core * size, size, keep_axis)]
  transfers between devices with their start and end apart: 22 -> 26, of which waited for: 12 -> 9; matrix products, arithmetic and copies ran while one was open for 24% -> 40% of each run, Pallas kernels for 0% -> 0%
where the time goes in v6:
time: 260 us; the launch traced here: 258 us
  waiting for transfers between devices  80.2 us (31%)
  starting transfers between devices  50.5 us (19%)
  other arithmetic  47.6 us (18%)
  local copies, waits for them, and re-layouts  46.2 us (18%)
  matrix products  32.6 us (13%)
    ppermute x7, waiting for transfers between devices, swap(): return lax.ppermute(x, axis, [(0, 1), (1, 0)])  52.3 us
    ppermute x7, starting transfers between devices, swap(): return lax.ppermute(x, axis, [(0, 1), (1, 0)])  20.9 us
    ppermute x1, waiting for transfers between devices, on_device(): earlier = lax.ppermute(chip_total, 'xh', [(0, 1)])  16 us
    ppermute x8, starting transfers between devices, ring_send(): return (lax.ppermute(x, axis, forward), lax.ppermute(x, axis, backward))  12.1 us
    another operation x8, other arithmetic, ring_finish(): return jnp.stack((x,) + tuple(received))  10.8 us
    unnamed x40, local copies, waits for them, and re-layouts  9.68 us
    ppermute x4, starting transfers between devices, ring_far(): lax.ppermute(from_right[half:], axis, backward)  8.95 us
    ppermute x8, waiting for transfers between devices, ring_send(): return (lax.ppermute(x, axis, forward), lax.ppermute(x, axis, backward))  7.52 us
  transfers between devices with their start and end apart: 26, of which 9 were waited for; matrix products, arithmetic and copies ran while one was open for 40% of the time, Pallas kernels for 0%

profile of v6, /device:TPU:1, one launch (start us, length us, event | category | flops | bytes accessed | tf_op | source)
XLA Modules:
  0.0 258.2 jit_solution(11471645338498623778)
XLA Ops:
  12.0 3.8 %collective-permute-start.8 = (bf16[2,80,640]{2,1,0:T(8,128)(2,1)}, bf16[2,80,640]{2,1,0:T(8,128)(2,1)S(1)}, u32[]{:S(2)}, u32[]{:S(2)}) collective-permute-start(bf16[2,80,640]{2,1,0:T(8,128)(2,1)} %get-tuple-element.73), channel_id=1, source_target_pairs={{0,96},{32,0},{64,32},{96,64},{1,97},{33,1},{65,33},{97,65},{2,98}... | collective-permute-start | bytes 614408 | tf_op jit(solution)/shard_map/ppermute | solution.py:29
  40.5 5.2 %collective-permute-done.10 = bf16[4,2,80,640]{3,2,1,0:T(8,128)(2,1)} collective-permute-done((bf16[4,2,80,640]{3,2,1,0:T(8,128)(2,1)S(1)}, bf16[4,2,80,640]{3,2,1,0:T(8,128)(2,1)}, u32[]{:S(2)}, u32[]{:S(2)}) %collective-permute-start.10) | collective-permute-done | bytes 819232 | tf_op jit(solution)/shard_map/ppermute | solution.py:29
  60.6 8.3 %collective-permute-start.19 = (bf16[256,10,128]{0,2,1:T(8,128)(2,1)}, bf16[256,10,128]{0,2,1:T(8,128)(2,1)}, u32[]{:S(2)}, u32[]{:S(2)}) collective-permute-start(bf16[256,10,128]{0,2,1:T(8,128)(2,1)} %get-tuple-element.69), channel_id=1, source_target_pairs={{0,1},{1,0},{2,3},{3,2},{4,5},{5,4},{6,7},{7,6},{8,9},{9,8},{10,11... | collective-permute-start | bytes 1966088 | tf_op jit(solution)/shard_map/ppermute | solution.py:115
  73.4 4.8 %collective-permute-start.18 = (bf16[256,10,128]{0,2,1:T(8,128)(2,1)}, bf16[256,10,128]{0,2,1:T(8,128)(2,1)}, u32[]{:S(2)}, u32[]{:S(2)}) collective-permute-start(bf16[256,10,128]{0,2,1:T(8,128)(2,1)} %get-tuple-element.67), channel_id=1, source_target_pairs={{0,1},{1,0},{2,3},{3,2},{4,5},{5,4},{6,7},{7,6},{8,9},{9,8},{10,11... | collective-permute-start | bytes 1966088 | tf_op jit(solution)/shard_map/ppermute | solution.py:115
  85.1 3.0 %pad_maximum_fusion.1 = bf16[4,4,2,80,640]{4,3,2,1,0:T(8,128)(2,1)} fusion(bf16[1,4,2,80,640]{4,3,2,1,0:T(8,128)(2,1)} %bitcast.29, bf16[1,4,2,80,640]{4,3,2,1,0:T(8,128)(2,1)S(1)} %bitcast.100, bf16[1,4,2,80,640]{4,3,2,1,0:T(8,128)(2,1)} %bitcast.27, bf16[1,4,2,80,640]{4,3,2,1,0:T(8,128)(2,1)S(1)} %bitcast.99), kind=kLoop, calls=%fused_computation.5 | loop fusion | flops 4915200 | bytes 6553600 | tf_op jit(solution)/shard_map/stack | solution.py:50
  88.2 4.6 %gather_fusion.1 = bf16[32,80,640]{2,1,0:T(8,128)(2,1)} fusion(bf16[32,80,640]{2,1,0:T(8,128)(2,1)} %bitcast.87, s32[1024]{0:T(1024)S(1)} %pad_clamp_fusion.2), kind=kCustom, calls=%fused_computation.clone | custom fusion | bytes 6553728 | tf_op jit(solution)/shard_map/jit(_take)/gather | solution.py:89
  95.1 3.3 %pad_maximum_fusion = bf16[2560,1280]{1,0:T(8,128)(2,1)} fusion(bf16[2560,640]{1,0:T(8,128)(2,1)S(1)} %bitcast.80, bf16[2560,640]{1,0:T(8,128)(2,1)S(1)} %bitcast.83), kind=kLoop, calls=%fused_computation.3 | loop fusion | flops 13107200 | bytes 13107200 | tf_op jit(solution)/shard_map/concatenate | solution.py:90
  99.0 4.5 %convert_maximum_fusion = (f32[512,10,128]{0,2,1:T(8,128)}, f32[512,10,128]{0,2,1:T(8,128)}) fusion(bf16[256,10,128]{0,2,1:T(8,128)(2,1)} %collective-permute-done.20, bf16[256,10,128]{0,2,1:T(8,128)(2,1)S(1)} %copy-done.11, pred[]{:T(512)S(6)} %eq.17, bf16[256,10,128]{0,2,1:T(8,128)(2,1)S(1)} %copy-done.10, bf16[256,10,128]{0,2,1:T(8,128)(2,1)} %collective-permute-done.19), kind=kLoop, calls=%fused_computation.23 | loop fusion | flops 14417920 | bytes 7864321 | tf_op jit(solution)/shard_map/max | solution.py:99
  103.5 3.2 %copy.54 = f32[512,10,128]{2,0,1:T(8,128)} copy(f32[512,10,128]{0,2,1:T(8,128)} %get-tuple-element.90) | data formatting | bytes 5242880 | tf_op jit(solution)/shard_map/max | solution.py:99
  106.7 3.2 %copy.51 = f32[512,10,128]{2,0,1:T(8,128)} copy(f32[512,10,128]{0,2,1:T(8,128)} %get-tuple-element.91) | data formatting | bytes 5242880 | tf_op jit(solution)/shard_map/max | solution.py:99
  109.9 6.4 %multiply_convert_fusion.1 = (bf16[4,128,10,128]{3,1,2,0:T(8,128)(2,1)}, bf16[4,128,10,128]{3,1,2,0:T(8,128)(2,1)}, bf16[4,128,10,128]{3,1,2,0:T(8,128)(2,1)}, bf16[4,128,10,128]{3,1,2,0:T(8,128)(2,1)}) fusion(f32[4,128,10,128]{3,1,0,2:T(8,128)} %bitcast.92, f32[4,128]{1,0:T(4,128)S(1)} %get-tuple-element.93, f32[4,128]{1,0:T(4,128)S(1)} %get-tuple-element.92, ...), kind=kLoop, calls=%fused_computation.22 | loop fusion | flops 5242880 | bytes 10489856 | tf_op jit(solution)/shard_map/convert.4
  121.5 6.5 %fusion.48 = (f32[10,256,128]{2,1,0:T(8,128)}, f32[4,10,256,128]{3,2,1,0:T(8,128)}) fusion(bf16[4,128,10,128]{3,1,0,2:T(8,128)(2,1)} %bitcast.94, bf16[4,128,10,128]{3,1,2,0:T(8,128)(2,1)} %get-tuple-element.61, bf16[4,128,10,128]{3,1,2,0:T(8,128)(2,1)} %get-tuple-element.60), kind=kOutput, calls=%fused_computation.168 | convolution fusion | flops 341770240 | bytes 10485760 | tf_op jit(solution)/shard_map/cjhf,cjhe->chfe/dot_general | solution.py:165
  128.0 5.7 %collective-permute-start.21 = (f32[10,256,128]{2,1,0:T(8,128)}, f32[10,256,128]{2,1,0:T(8,128)}, u32[]{:S(2)}, u32[]{:S(2)}) collective-permute-start(f32[10,256,128]{2,1,0:T(8,128)} %get-tuple-element.86), channel_id=1, source_target_pairs={{0,2},{1,3},{4,6},{5,7},{8,10},{9,11},{12,14},{13,15},{16,18},{17,... | collective-permute-start | bytes 3932168 | tf_op jit(solution)/shard_map/ppermute | solution.py:169
  133.7 3.0 %fusion.49 = f32[4,10,256,128]{3,2,1,0:T(8,128)S(1)} fusion(f32[4,10,256,128]{3,2,1,0:T(8,128)} %get-tuple-element.87), kind=kOutput, calls=%fused_computation.169 | output fusion | flops 3932160 | bytes 10485760 | tf_op jit(solution)/shard_map/jit(cumsum)/reduce_window_sum | solution.py:178
  139.0 5.6 %fusion.7 = f32[4,10,128,128]{2,3,1,0:T(8,128)} fusion(bf16[4,128,10,128]{3,1,2,0:T(8,128)(2,1)} %get-tuple-element.61, bf16[4,128,10,128]{3,1,2,0:T(8,128)(2,1)} %get-tuple-element.60, bf16[4,128,10,128]{3,1,2,0:T(8,128)(2,1)} %get-tuple-element.80, bf16[4,128,10,128]{3,1,2,0:T(8,128)(2,1)} %get-tuple-element.81, ...), kind=kOutput, calls=%fused_computation.34 | convolution fusion | flops 515112960 | bytes 9191424 | tf_op jit(solution)/shard_map/chij,cjhe->cihe/dot_general | solution.py:175
  144.6 16.0 %collective-permute-done.21 = f32[10,256,128]{2,1,0:T(8,128)} collective-permute-done((f32[10,256,128]{2,1,0:T(8,128)}, f32[10,256,128]{2,1,0:T(8,128)}, u32[]{:S(2)}, u32[]{:S(2)}) %collective-permute-start.21) | collective-permute-done | bytes 1310752 | tf_op jit(solution)/shard_map/ppermute | solution.py:169
  160.6 5.0 %multiply_reduce_fusion = (f32[4,128,10]{1,2,0:T(8,128)S(1)}, f32[4,128,10,128]{3,1,2,0:T(8,128)S(1)}) fusion(f32[4,10,128,128]{2,3,1,0:T(8,128)} %fusion.7, f32[3,10,256,128]{3,2,1,0:T(8,128)} %slice.77, f32[10,256,128]{2,1,0:T(8,128)} %collective-permute-done.21, bf16[4,128,10,128]{3,1,2,0:T(8,128)(2,1)} %get-tuple-element.80, ...), kind=kOutput, calls=%fused_computation.17 | convolution fusion | flops 345369600 | bytes 13127680 | tf_op jit(solution)/shard_map/cihf,chfe->cihe/dot_general | solution.py:181
  173.8 3.7 %collective-permute-start.24 = (bf16[256,2560]{0,1:T(8,128)(2,1)}, bf16[256,2560]{0,1:T(8,128)(2,1)S(1)}, u32[]{:S(2)}, u32[]{:S(2)}) collective-permute-start(bf16[256,2560]{0,1:T(8,128)(2,1)} %bitcast.88), channel_id=1, source_target_pairs={{0,2},{2,0},{1,3},{3,1},{4,6},{6,4},{5,7},{7,5},{8,10},{10,8},{9,1... | collective-permute-start | bytes 3932168 | tf_op jit(solution)/shard_map/ppermute | solution.py:115
  177.6 29.0 %collective-permute-done.24 = bf16[256,2560]{0,1:T(8,128)(2,1)S(1)} collective-permute-done((bf16[256,2560]{0,1:T(8,128)(2,1)}, bf16[256,2560]{0,1:T(8,128)(2,1)S(1)}, u32[]{:S(2)}, u32[]{:S(2)}) %collective-permute-start.24) | collective-permute-done | bytes 1310752 | tf_op jit(solution)/shard_map/ppermute | solution.py:115
  206.6 3.9 %convolution_convert_fusion.1 = bf16[256,1280]{1,0:T(8,128)(2,1)S(1)} fusion(bf16[256,2560]{0,1:T(8,128)(2,1)S(1)} %collective-permute-done.24, bf16[2560,640]{1,0:T(8,128)(2,1)S(1)} %bitcast.81, bf16[2560,640]{1,0:T(8,128)(2,1)} %bitcast.84), kind=kOutput, calls=%fused_computation.28 | convolution fusion | flops 1691156480 | bytes 8519680 | tf_op jit(solution)/shard_map/dot_general | solution.py:194
  210.5 4.9 %convolution_convert_fusion = bf16[256,1280]{1,0:T(8,128)(2,1)S(1)} fusion(bf16[256,2560]{0,1:T(8,128)(2,1)S(1)} %collective-permute-done.24, bf16[2560,1280]{1,0:T(8,128)(2,1)} %collective-permute-done.23), kind=kOutput, calls=%fused_computation.27 | convolution fusion | flops 1678049280 | bytes 8519680 | tf_op jit(solution)/shard_map/dot_general | solution.py:195
  220.2 4.8 %fusion.5 = bf16[1,256,1280]{2,1,0:T(8,128)(2,1)S(1)} fusion(bf16[256,2560]{0,1:T(8,128)(2,1)S(1)} %bitcast.90, bf16[2560,1280]{1,0:T(8,128)(2,1)} %collective-permute-done.23), kind=kOutput, calls=%fused_computation.32 | convolution fusion | flops 1678049280 | bytes 8519680 | tf_op jit(solution)/shard_map/dot_general | solution.py:203
  225.0 21.5 %collective-permute-done.25 = bf16[256,2560]{1,0:T(8,128)(2,1)S(1)} collective-permute-done((bf16[256,2560]{1,0:T(8,128)(2,1)S(1)}, bf16[256,2560]{1,0:T(8,128)(2,1)S(1)}, u32[]{:S(2)}, u32[]{:S(2)}) %collective-permute-start.25) | collective-permute-done | bytes 1310752 | tf_op jit(solution)/shard_map/ppermute | solution.py:115
  253.8 4.4 %copy.64 = bf16[1,256,5120]{2,1,0:T(8,128)(2,1)} copy(bf16[1,256,5120]{1,2,0:T(8,128)(2,1)} %bitcast.91) | data formatting | bytes 5242880
  (136 shorter events, 92.9 us)
Async XLA Ops:
  5.5 5.8 %collective-permute-start.5 = (bf16[80,640]{1,0:T(8,128)(2,1)S(1)}, bf16[80,640]{1,0:T(8,128)(2,1)S(1)}, u32[]{:S(2)}, u32[]{:S(2)}) collective-permute-start(bf16[80,640]{1,0:T(8,128)(2,1)S(1)} %get-tuple-element.76), channel_id=1, source_target_pairs={{0,16},{16,0},{1,17},{17,1},{2,18},{18,2},{3,19},{19,3},{4,20},{20... | collective-permute-start | bytes 307208 | tf_op jit(solution)/shard_map/ppermute | solution.py:26
  8.3 7.5 %collective-permute-start.3 = (bf16[2,80,640]{2,1,0:T(8,128)(2,1)S(1)}, bf16[2,80,640]{2,1,0:T(8,128)(2,1)S(1)}, u32[]{:S(2)}, u32[]{:S(2)}) collective-permute-start(bf16[2,80,640]{2,1,0:T(8,128)(2,1)S(1)} %get-tuple-element.79), channel_id=1, source_target_pairs={{0,12},{4,0},{8,4},{12,8},{1,13},{5,1},{9,5},{13,9},{2,14},{6,2},{... | collective-permute-start | bytes 614408 | tf_op jit(solution)/shard_map/ppermute | solution.py:29
  11.3 7.9 %collective-permute-start.1 = (bf16[2,80,640]{2,1,0:T(8,128)(2,1)S(1)}, bf16[2,80,640]{2,1,0:T(8,128)(2,1)S(1)}, u32[]{:S(2)}, u32[]{:S(2)}) collective-permute-start(bf16[2,80,640]{2,1,0:T(8,128)(2,1)S(1)} %get-tuple-element.79), channel_id=1, source_target_pairs={{0,4},{4,8},{8,12},{12,0},{1,5},{5,9},{9,13},{13,1},{2,6},{6,10},{... | collective-permute-start | bytes 614408 | tf_op jit(solution)/shard_map/ppermute | solution.py:29
  12.0 8.5 %collective-permute-start.8 = (bf16[2,80,640]{2,1,0:T(8,128)(2,1)}, bf16[2,80,640]{2,1,0:T(8,128)(2,1)S(1)}, u32[]{:S(2)}, u32[]{:S(2)}) collective-permute-start(bf16[2,80,640]{2,1,0:T(8,128)(2,1)} %get-tuple-element.73), channel_id=1, source_target_pairs={{0,96},{32,0},{64,32},{96,64},{1,97},{33,1},{65,33},{97,65},{2,98}... | collective-permute-start | bytes 614408 | tf_op jit(solution)/shard_map/ppermute | solution.py:29
  15.8 7.5 %collective-permute-start.6 = (bf16[2,80,640]{2,1,0:T(8,128)(2,1)}, bf16[2,80,640]{2,1,0:T(8,128)(2,1)S(1)}, u32[]{:S(2)}, u32[]{:S(2)}) collective-permute-start(bf16[2,80,640]{2,1,0:T(8,128)(2,1)} %get-tuple-element.73), channel_id=1, source_target_pairs={{0,32},{32,64},{64,96},{96,0},{1,33},{33,65},{65,97},{97,1},{2,34}... | collective-permute-start | bytes 614408 | tf_op jit(solution)/shard_map/ppermute | solution.py:29
  16.5 6.9 %collective-permute-start.4 = (bf16[1,80,640]{2,1,0:T(8,128)(2,1)}, bf16[1,80,640]{2,1,0:T(8,128)(2,1)S(1)}, u32[]{:S(2)}, u32[]{:S(2)}) collective-permute-start(bf16[1,80,640]{2,1,0:T(8,128)(2,1)} %slice.73), channel_id=1, source_target_pairs={{0,12},{4,0},{8,4},{12,8},{1,13},{5,1},{9,5},{13,9},{2,14},{6,2},{... | collective-permute-start | bytes 307208 | tf_op jit(solution)/shard_map/ppermute | solution.py:42
  19.9 5.2 %collective-permute-start.2 = (bf16[1,80,640]{2,1,0:T(8,128)(2,1)}, bf16[1,80,640]{2,1,0:T(8,128)(2,1)}, u32[]{:S(2)}, u32[]{:S(2)}) collective-permute-start(bf16[1,80,640]{2,1,0:T(8,128)(2,1)} %slice.72), channel_id=1, source_target_pairs={{0,4},{4,8},{8,12},{12,0},{1,5},{5,9},{9,13},{13,1},{2,6},{6,10},{... | collective-permute-start | bytes 307208 | tf_op jit(solution)/shard_map/ppermute | solution.py:41
  20.5 6.8 %collective-permute-start.9 = (bf16[1,80,640]{2,1,0:T(8,128)(2,1)S(1)}, bf16[1,80,640]{2,1,0:T(8,128)(2,1)S(1)}, u32[]{:S(2)}, u32[]{:S(2)}) collective-permute-start(bf16[1,80,640]{2,1,0:T(8,128)(2,1)S(1)} %slice.76), channel_id=1, source_target_pairs={{0,96},{32,0},{64,32},{96,64},{1,97},{33,1},{65,33},{97,65},{2,98}... | collective-permute-start | bytes 307208 | tf_op jit(solution)/shard_map/ppermute | solution.py:42
  23.3 4.8 %collective-permute-start.7 = (bf16[1,80,640]{2,1,0:T(8,128)(2,1)S(1)}, bf16[1,80,640]{2,1,0:T(8,128)(2,1)S(1)}, u32[]{:S(2)}, u32[]{:S(2)}) collective-permute-start(bf16[1,80,640]{2,1,0:T(8,128)(2,1)S(1)} %slice.75), channel_id=1, source_target_pairs={{0,32},{32,64},{64,96},{96,0},{1,33},{33,65},{65,97},{97,1},{2,34}... | collective-permute-start | bytes 307208 | tf_op jit(solution)/shard_map/ppermute | solution.py:41
  30.3 15.4 %collective-permute-start.10 = (bf16[4,2,80,640]{3,2,1,0:T(8,128)(2,1)S(1)}, bf16[4,2,80,640]{3,2,1,0:T(8,128)(2,1)}, u32[]{:S(2)}, u32[]{:S(2)}) collective-permute-start(bf16[4,2,80,640]{3,2,1,0:T(8,128)(2,1)S(1)} %pad_maximum_fusion.15), channel_id=1, source_target_pairs={{0,32},{32,64},{64,96},{96,0},{1,33},{33,65},{65,97},{97,1},{2,34}... | collective-permute-start | bytes 2457608 | tf_op jit(solution)/shard_map/ppermute | solution.py:29
  30.3 15.4 %collective-permute-start.11 = (bf16[4,2,80,640]{3,2,1,0:T(8,128)(2,1)S(1)}, bf16[4,2,80,640]{3,2,1,0:T(8,128)(2,1)}, u32[]{:S(2)}, u32[]{:S(2)}) collective-permute-start(bf16[4,2,80,640]{3,2,1,0:T(8,128)(2,1)S(1)} %pad_maximum_fusion.15), channel_id=1, source_target_pairs={{0,96},{32,0},{64,32},{96,64},{1,97},{33,1},{65,33},{97,65},{2,98}... | collective-permute-start | bytes 2457608 | tf_op jit(solution)/shard_map/ppermute | solution.py:29
  32.9 15.0 %collective-permute-start.12 = (bf16[4,2,80,640]{3,2,1,0:T(8,128)(2,1)}, bf16[4,2,80,640]{3,2,1,0:T(8,128)(2,1)}, u32[]{:S(2)}, u32[]{:S(2)}) collective-permute-start(bf16[4,2,80,640]{3,2,1,0:T(8,128)(2,1)} %pad_maximum_fusion.16), channel_id=1, source_target_pairs={{0,4},{4,8},{8,12},{12,0},{1,5},{5,9},{9,13},{13,1},{2,6},{6,10},{... | collective-permute-start | bytes 2457608 | tf_op jit(solution)/shard_map/ppermute | solution.py:29
  32.9 15.0 %collective-permute-start.13 = (bf16[4,2,80,640]{3,2,1,0:T(8,128)(2,1)}, bf16[4,2,80,640]{3,2,1,0:T(8,128)(2,1)}, u32[]{:S(2)}, u32[]{:S(2)}) collective-permute-start(bf16[4,2,80,640]{3,2,1,0:T(8,128)(2,1)} %pad_maximum_fusion.16), channel_id=1, source_target_pairs={{0,12},{4,0},{8,4},{12,8},{1,13},{5,1},{9,5},{13,9},{2,14},{6,2},{... | collective-permute-start | bytes 2457608 | tf_op jit(solution)/shard_map/ppermute | solution.py:29
  49.8 20.2 %collective-permute-start.15 = (bf16[2,2,80,640]{3,2,1,0:T(8,128)(2,1)}, bf16[2,2,80,640]{3,2,1,0:T(8,128)(2,1)}, u32[]{:S(2)}, u32[]{:S(2)}) collective-permute-start(bf16[2,2,80,640]{3,2,1,0:T(8,128)(2,1)} %slice.52), channel_id=1, source_target_pairs={{0,96},{32,0},{64,32},{96,64},{1,97},{33,1},{65,33},{97,65},{2,98}... | collective-permute-start | bytes 1228808 | tf_op jit(solution)/shard_map/ppermute | solution.py:42
  51.9 18.1 %collective-permute-start.14 = (bf16[2,2,80,640]{3,2,1,0:T(8,128)(2,1)S(1)}, bf16[2,2,80,640]{3,2,1,0:T(8,128)(2,1)S(1)}, u32[]{:S(2)}, u32[]{:S(2)}) collective-permute-start(bf16[2,2,80,640]{3,2,1,0:T(8,128)(2,1)S(1)} %slice.51), channel_id=1, source_target_pairs={{0,32},{32,64},{64,96},{96,0},{1,33},{33,65},{65,97},{97,1},{2,34}... | collective-permute-start | bytes 1228808 | tf_op jit(solution)/shard_map/ppermute | solution.py:41
  55.8 16.2 %collective-permute-start.17 = (bf16[2,2,80,640]{3,2,1,0:T(8,128)(2,1)S(1)}, bf16[2,2,80,640]{3,2,1,0:T(8,128)(2,1)S(1)}, u32[]{:S(2)}, u32[]{:S(2)}) collective-permute-start(bf16[2,2,80,640]{3,2,1,0:T(8,128)(2,1)S(1)} %slice.54), channel_id=1, source_target_pairs={{0,12},{4,0},{8,4},{12,8},{1,13},{5,1},{9,5},{13,9},{2,14},{6,2},{... | collective-permute-start | bytes 1228808 | tf_op jit(solution)/shard_map/ppermute | solution.py:42
  59.3 12.7 %collective-permute-start.16 = (bf16[2,2,80,640]{3,2,1,0:T(8,128)(2,1)S(1)}, bf16[2,2,80,640]{3,2,1,0:T(8,128)(2,1)S(1)}, u32[]{:S(2)}, u32[]{:S(2)}) collective-permute-start(bf16[2,2,80,640]{3,2,1,0:T(8,128)(2,1)S(1)} %slice.53), channel_id=1, source_target_pairs={{0,4},{4,8},{8,12},{12,0},{1,5},{5,9},{9,13},{13,1},{2,6},{6,10},{... | collective-permute-start | bytes 1228808 | tf_op jit(solution)/shard_map/ppermute | solution.py:41
  60.6 38.4 %collective-permute-start.19 = (bf16[256,10,128]{0,2,1:T(8,128)(2,1)}, bf16[256,10,128]{0,2,1:T(8,128)(2,1)}, u32[]{:S(2)}, u32[]{:S(2)}) collective-permute-start(bf16[256,10,128]{0,2,1:T(8,128)(2,1)} %get-tuple-element.69), channel_id=1, source_target_pairs={{0,1},{1,0},{2,3},{3,2},{4,5},{5,4},{6,7},{7,6},{8,9},{9,8},{10,11... | collective-permute-start | bytes 1966088 | tf_op jit(solution)/shard_map/ppermute | solution.py:115
  70.0 29.0 %collective-permute-start.20 = (bf16[256,10,128]{0,2,1:T(8,128)(2,1)}, bf16[256,10,128]{0,2,1:T(8,128)(2,1)}, u32[]{:S(2)}, u32[]{:S(2)}) collective-permute-start(bf16[256,10,128]{0,2,1:T(8,128)(2,1)} %get-tuple-element.71), channel_id=1, source_target_pairs={{0,1},{1,0},{2,3},{3,2},{4,5},{5,4},{6,7},{7,6},{8,9},{9,8},{10,11... | collective-permute-start | bytes 1966088 | tf_op jit(solution)/shard_map/ppermute | solution.py:115
  73.4 42.9 %collective-permute-start.18 = (bf16[256,10,128]{0,2,1:T(8,128)(2,1)}, bf16[256,10,128]{0,2,1:T(8,128)(2,1)}, u32[]{:S(2)}, u32[]{:S(2)}) collective-permute-start(bf16[256,10,128]{0,2,1:T(8,128)(2,1)} %get-tuple-element.67), channel_id=1, source_target_pairs={{0,1},{1,0},{2,3},{3,2},{4,5},{5,4},{6,7},{7,6},{8,9},{9,8},{10,11... | collective-permute-start | bytes 1966088 | tf_op jit(solution)/shard_map/ppermute | solution.py:115
  99.0 111.5 %collective-permute-start.23 = (bf16[2560,1280]{1,0:T(8,128)(2,1)}, bf16[2560,1280]{1,0:T(8,128)(2,1)}, u32[]{:S(2)}, u32[]{:S(2)}) collective-permute-start(bf16[2560,1280]{1,0:T(8,128)(2,1)} %pad_maximum_fusion), channel_id=1, source_target_pairs={{0,1},{1,0},{2,3},{3,2},{4,5},{5,4},{6,7},{7,6},{8,9},{9,8},{10,11... | collective-permute-start | bytes 19660808 | tf_op jit(solution)/shard_map/ppermute | solution.py:115
  128.0 32.6 %collective-permute-start.21 = (f32[10,256,128]{2,1,0:T(8,128)}, f32[10,256,128]{2,1,0:T(8,128)}, u32[]{:S(2)}, u32[]{:S(2)}) collective-permute-start(f32[10,256,128]{2,1,0:T(8,128)} %get-tuple-element.86), channel_id=1, source_target_pairs={{0,2},{1,3},{4,6},{5,7},{8,10},{9,11},{12,14},{13,15},{16,18},{17,... | collective-permute-start | bytes 3932168 | tf_op jit(solution)/shard_map/ppermute | solution.py:169
  173.8 32.8 %collective-permute-start.24 = (bf16[256,2560]{0,1:T(8,128)(2,1)}, bf16[256,2560]{0,1:T(8,128)(2,1)S(1)}, u32[]{:S(2)}, u32[]{:S(2)}) collective-permute-start(bf16[256,2560]{0,1:T(8,128)(2,1)} %bitcast.88), channel_id=1, source_target_pairs={{0,2},{2,0},{1,3},{3,1},{4,6},{6,4},{5,7},{7,5},{8,10},{10,8},{9,1... | collective-permute-start | bytes 3932168 | tf_op jit(solution)/shard_map/ppermute | solution.py:115
  215.5 31.0 %collective-permute-start.25 = (bf16[256,2560]{1,0:T(8,128)(2,1)S(1)}, bf16[256,2560]{1,0:T(8,128)(2,1)S(1)}, u32[]{:S(2)}, u32[]{:S(2)}) collective-permute-start(bf16[256,2560]{1,0:T(8,128)(2,1)S(1)} %pad_maximum_fusion.14), channel_id=1, source_target_pairs={{0,2},{2,0},{1,3},{3,1},{4,6},{6,4},{5,7},{7,5},{8,10},{10,8},{9,1... | collective-permute-start | bytes 3932168 | tf_op jit(solution)/shard_map/ppermute | solution.py:115
  (19 other events, 257.1 us)

commit v7 on v6

--- a/solution.py
+++ b/solution.py
@@ -144,7 +144,8 @@
     half = lax.axis_index("xh")
     core = lax.axis_index("c")
     heads_here = H // 2
-    parts = gather_start(weights)
+    both = jnp.concatenate([weights, swap(weights, "xh")], axis=1)
+    parts = gather_start(both)
     parts, query_heads = lax.optimization_barrier(
         (parts, queries[0].reshape(tokens_here, H, HEAD))
     )
@@ -186,30 +187,17 @@
     normed_group = normalize(attended, gain_rows)
     normed_own = pair_exchange(normed_group, core, 0, 1)
     normed_own = normed_own.reshape(tokens_here, H * HEAD)
-    normed_peer = swap(normed_own, "xh")
-    mine = gather_finish(parts, sent, jnp.arange(4))
-    partner = swap(mine, "c")
-    peer_wide = jnp.concatenate(
-        [
-            jnp.dot(normed_peer, mine, preferred_element_type=jnp.float32),
-            jnp.dot(normed_peer, partner, preferred_element_type=jnp.float32),
-        ],
-        axis=1,
-    ).astype(jnp.bfloat16)
-    returned = swap(peer_wide, "xh")
-    own_wide = jnp.concatenate(
-        [
-            jnp.dot(normed_own, mine, preferred_element_type=jnp.float32),
-            jnp.dot(normed_own, partner, preferred_element_type=jnp.float32),
-        ],
-        axis=1,
-    ).astype(jnp.bfloat16)
+    columns = gather_finish(parts, sent, jnp.arange(4))
+    tokens = jnp.concatenate([normed_own, swap(normed_own, "c")], axis=0)
+    wide = jnp.dot(tokens, columns, preferred_element_type=jnp.float32).astype(jnp.bfloat16)
+    own_wide = wide[:tokens_here]
+    returned = swap(wide[tokens_here:], "c")
     width = own_wide.shape[1] // 2
     by_offset = jnp.stack(
         [
             own_wide[:, :width],
+            returned[:, :width],
             own_wide[:, width:],
-            returned[:, :width],
             returned[:, width:],
         ]
     )

time: 260 us -> 237 us (0.912)
  waiting for transfers between devices: 80.2 us -> 46.7 us
  local copies, waits for them, and re-layouts: 46.2 us -> 55.5 us
  other arithmetic: 47.6 us -> 54.4 us
  matrix products: 32.6 us -> 28.6 us
    ppermute x7, waiting for transfers between devices: 52.3 us -> 6.52 us  [swap(): return lax.ppermute(x, axis, [(0, 1), (1, 0)])]
    ppermute x8, waiting for transfers between devices: 7.52 us -> 27 us  [ring_send(): return (lax.ppermute(x, axis, forward), lax.ppermute(x, axis, backward))]
    ppermute x1, waiting for transfers between devices: 16 us -> 4.44 us  [on_device(): earlier = lax.ppermute(chip_total, 'xh', [(0, 1)])]
    gather x2, local copies, waits for them, and re-layouts: 7.19 us -> 13.2 us  [gather_finish(): pieces.append(jnp.take(flat, source, axis=0).reshape(-1, part.shape[-1]))]
    select_n x2, other arithmetic: 4.78 us -> 9.78 us  [gather_finish(): pieces.append(jnp.take(flat, source, axis=0).reshape(-1, part.shape[-1]))]
    another operation x8, other arithmetic: 10.8 us -> 15.1 us  [ring_finish(): return jnp.stack((x,) + tuple(received))]
    dot_general x4 -> x1, matrix products: 15.5 us -> 12 us  [on_device(): jnp.dot(tokens, columns, preferred_element_type=jnp.float32)]
    concatenate x2 -> x0, other arithmetic: 3.37 us -> none  [the longest x1 3.28 us: gather_finish(): return jnp.concatenate(pieces, axis=1)]
  transfers between devices with their start and end apart: 26 -> 26, of which waited for: 9 -> 12; matrix products, arithmetic and copies ran while one was open for 40% -> 36% of each run, Pallas kernels for 0% -> 0%
where the time goes in v7:
time: 237 us; the launch traced here: 236 us
  local copies, waits for them, and re-layouts  55.5 us (23%)
  other arithmetic  54.4 us (23%)
  starting transfers between devices  49.3 us (21%)
  waiting for transfers between devices  46.7 us (20%)
  matrix products  28.6 us (12%)
    ppermute x8, waiting for transfers between devices, ring_send(): return (lax.ppermute(x, axis, forward), lax.ppermute(x, axis, backward))  27 us
    ppermute x7, starting transfers between devices, swap(): return lax.ppermute(x, axis, [(0, 1), (1, 0)])  21.2 us
    another operation x8, other arithmetic, ring_finish(): return jnp.stack((x,) + tuple(received))  15.1 us
    gather x2, local copies, waits for them, and re-layouts, gather_finish(): pieces.append(jnp.take(flat, source, axis=0).reshape(-1, part.shape[-1]))  13.2 us
    ppermute x8, starting transfers between devices, ring_send(): return (lax.ppermute(x, axis, forward), lax.ppermute(x, axis, backward))  12 us
    dot_general x1, matrix products, on_device(): jnp.dot(tokens, columns, preferred_element_type=jnp.float32)  12 us
    unnamed x54, local copies, waits for them, and re-layouts  11.6 us
    select_n x2, other arithmetic, gather_finish(): pieces.append(jnp.take(flat, source, axis=0).reshape(-1, part.shape[-1]))  9.78 us
  transfers between devices with their start and end apart: 26, of which 12 were waited for; matrix products, arithmetic and copies ran while one was open for 36% of the time, Pallas kernels for 0%

profile of v7, /device:TPU:1, one launch (start us, length us, event | category | flops | bytes accessed | tf_op | source)
XLA Modules:
  0.0 235.5 jit_solution(9665450258924325576)
XLA Ops:
  3.4 3.6 %collective-permute-start.5 = (bf16[80,1280]{1,0:T(8,128)(2,1)S(1)}, bf16[80,1280]{1,0:T(8,128)(2,1)S(1)}, u32[]{:S(2)}, u32[]{:S(2)}) collective-permute-start(bf16[80,1280]{1,0:T(8,128)(2,1)S(1)} %get-tuple-element.54), channel_id=1, source_target_pairs={{0,2},{2,0},{1,3},{3,1},{4,6},{6,4},{5,7},{7,5},{8,10},{10,8},{9,1... | collective-permute-start | bytes 614408 | tf_op jit(solution)/shard_map/ppermute | solution.py:115
  7.2 4.0 %collective-permute-done.5 = bf16[80,1280]{1,0:T(8,128)(2,1)S(1)} collective-permute-done((bf16[80,1280]{1,0:T(8,128)(2,1)S(1)}, bf16[80,1280]{1,0:T(8,128)(2,1)S(1)}, u32[]{:S(2)}, u32[]{:S(2)}) %collective-permute-start.5) | collective-permute-done | bytes 204832 | tf_op jit(solution)/shard_map/ppermute | solution.py:115
  12.8 3.3 %collective-permute-done = bf16[80,1280]{1,0:T(8,128)(2,1)S(1)} collective-permute-done((bf16[80,1280]{1,0:T(8,128)(2,1)S(1)}, bf16[80,1280]{1,0:T(8,128)(2,1)S(1)}, u32[]{:S(2)}, u32[]{:S(2)}) %collective-permute-start) | collective-permute-done | bytes 204832 | tf_op jit(solution)/shard_map/ppermute | solution.py:26
  21.4 3.8 %collective-permute-start.9 = (bf16[2,80,1280]{2,1,0:T(8,128)(2,1)}, bf16[2,80,1280]{2,1,0:T(8,128)(2,1)S(1)}, u32[]{:S(2)}, u32[]{:S(2)}) collective-permute-start(bf16[2,80,1280]{2,1,0:T(8,128)(2,1)} %get-tuple-element.75), channel_id=1, source_target_pairs={{0,96},{32,0},{64,32},{96,64},{1,97},{33,1},{65,33},{97,65},{2,98}... | collective-permute-start | bytes 1228808 | tf_op jit(solution)/shard_map/ppermute | solution.py:29
  25.2 3.3 %collective-permute-start.4 = (bf16[1,80,1280]{2,1,0:T(8,128)(2,1)S(1)}, bf16[1,80,1280]{2,1,0:T(8,128)(2,1)S(1)}, u32[]{:S(2)}, u32[]{:S(2)}) collective-permute-start(bf16[1,80,1280]{2,1,0:T(8,128)(2,1)S(1)} %slice.71), channel_id=1, source_target_pairs={{0,12},{4,0},{8,4},{12,8},{1,13},{5,1},{9,5},{13,9},{2,14},{6,2},{... | collective-permute-start | bytes 614408 | tf_op jit(solution)/shard_map/ppermute | solution.py:42
  32.8 3.4 %collective-permute-start.10 = (bf16[1,80,1280]{2,1,0:T(8,128)(2,1)S(1)}, bf16[1,80,1280]{2,1,0:T(8,128)(2,1)S(1)}, u32[]{:S(2)}, u32[]{:S(2)}) collective-permute-start(bf16[1,80,1280]{2,1,0:T(8,128)(2,1)S(1)} %slice.73), channel_id=1, source_target_pairs={{0,96},{32,0},{64,32},{96,64},{1,97},{33,1},{65,33},{97,65},{2,98}... | collective-permute-start | bytes 614408 | tf_op jit(solution)/shard_map/ppermute | solution.py:42
  54.5 23.2 %collective-permute-done.11 = bf16[4,2,80,1280]{3,2,1,0:T(8,128)(2,1)} collective-permute-done((bf16[4,2,80,1280]{3,2,1,0:T(8,128)(2,1)S(1)}, bf16[4,2,80,1280]{3,2,1,0:T(8,128)(2,1)}, u32[]{:S(2)}, u32[]{:S(2)}) %collective-permute-start.11) | collective-permute-done | bytes 1638432 | tf_op jit(solution)/shard_map/ppermute | solution.py:29
  95.0 7.2 %collective-permute-start.20 = (bf16[256,10,128]{0,2,1:T(8,128)(2,1)S(1)}, bf16[256,10,128]{0,2,1:T(8,128)(2,1)S(1)}, u32[]{:S(2)}, u32[]{:S(2)}) collective-permute-start(bf16[256,10,128]{0,2,1:T(8,128)(2,1)S(1)} %get-tuple-element.71), channel_id=1, source_target_pairs={{0,1},{1,0},{2,3},{3,2},{4,5},{5,4},{6,7},{7,6},{8,9},{9,8},{10,11... | collective-permute-start | bytes 1966088 | tf_op jit(solution)/shard_map/ppermute | solution.py:115
  109.9 8.0 %collective-permute-start.19 = (bf16[256,10,128]{0,2,1:T(8,128)(2,1)}, bf16[256,10,128]{0,2,1:T(8,128)(2,1)}, u32[]{:S(2)}, u32[]{:S(2)}) collective-permute-start(bf16[256,10,128]{0,2,1:T(8,128)(2,1)} %get-tuple-element.69), channel_id=1, source_target_pairs={{0,1},{1,0},{2,3},{3,2},{4,5},{5,4},{6,7},{7,6},{8,9},{9,8},{10,11... | collective-permute-start | bytes 1966088 | tf_op jit(solution)/shard_map/ppermute | solution.py:115
  125.2 5.5 %multiply_convert_fusion.1 = (bf16[4,128,10,128]{3,1,2,0:T(8,128)(2,1)S(1)}, bf16[4,128,10,128]{3,1,2,0:T(8,128)(2,1)S(1)}, bf16[4,128,10,128]{3,1,2,0:T(8,128)(2,1)}, bf16[4,128,10,128]{3,1,2,0:T(8,128)(2,1)}) fusion(f32[4,128,10,128]{3,1,0,2:T(8,128)} %bitcast.77, f32[4,128]{1,0:T(4,128)S(1)} %get-tuple-element.91, f32[4,128]{1,0:T(4,128)S(1)} %get-tuple-element.90, ...), kind=kLoop, calls=%fused_computation.29 | loop fusion | flops 5242880 | bytes 10489856 | tf_op jit(solution)/shard_map/convert
  130.7 3.6 %maximum_select_fusion.2 = bf16[512,10,128]{0,2,1:T(8,128)(2,1)} fusion(bf16[256,10,128]{0,2,1:T(8,128)(2,1)} %collective-permute-done.19, bf16[256,10,128]{0,2,1:T(8,128)(2,1)S(1)} %get-tuple-element.68, pred[]{:T(512)S(6)} %eq.17), kind=kLoop, calls=%fused_computation.42 | loop fusion | flops 5898240 | bytes 2621441 | tf_op jit(solution)/shard_map/jit(_where)/select_n | solution.py:123
  136.8 5.9 %fusion.57 = (f32[10,256,128]{2,1,0:T(8,128)}, f32[4,10,256,128]{3,2,1,0:T(8,128)}) fusion(bf16[4,128,10,128]{3,1,0,2:T(8,128)(2,1)} %bitcast.87, bf16[4,128,10,128]{3,1,2,0:T(8,128)(2,1)S(1)} %get-tuple-element.63, bf16[4,128,10,128]{3,1,2,0:T(8,128)(2,1)S(1)} %get-tuple-element.62), kind=kOutput, calls=%fused_computation.169 | convolution fusion | flops 341770240 | bytes 10485760 | tf_op jit(solution)/shard_map/cjhf,cjhe->chfe/dot_general | solution.py:166
  142.7 4.0 %collective-permute-start.22 = (f32[10,256,128]{2,1,0:T(8,128)}, f32[10,256,128]{2,1,0:T(8,128)}, u32[]{:S(2)}, u32[]{:S(2)}) collective-permute-start(f32[10,256,128]{2,1,0:T(8,128)} %get-tuple-element.84), channel_id=1, source_target_pairs={{0,2},{1,3},{4,6},{5,7},{8,10},{9,11},{12,14},{13,15},{16,18},{17,... | collective-permute-start | bytes 3932168 | tf_op jit(solution)/shard_map/ppermute | solution.py:170
  146.7 5.3 %pad_maximum_fusion.1 = bf16[4,4,2,80,1280]{4,3,2,1,0:T(8,128)(2,1)} fusion(bf16[1,4,2,80,1280]{4,3,2,1,0:T(8,128)(2,1)} %bitcast.35, bf16[1,4,2,80,1280]{4,3,2,1,0:T(8,128)(2,1)S(1)} %bitcast.82, bf16[1,4,2,80,1280]{4,3,2,1,0:T(8,128)(2,1)} %bitcast.33, bf16[1,4,2,80,1280]{4,3,2,1,0:T(8,128)(2,1)S(1)} %bitcast.80), kind=kLoop, calls=%fused_computation.8 | loop fusion | flops 9830400 | bytes 13107200 | tf_op jit(solution)/shard_map/stack | solution.py:50
  152.0 6.5 %gather_fusion.2 = bf16[32,80,1280]{2,1,0:T(8,128)(2,1)} fusion(bf16[32,80,1280]{2,1,0:T(8,128)(2,1)} %bitcast.74, s32[1024]{0:T(1024)S(1)} %pad_clamp_fusion.1), kind=kCustom, calls=%fused_computation.1.clone | custom fusion | bytes 13107328 | tf_op jit(solution)/shard_map/jit(_take)/gather | solution.py:89
  164.0 5.7 %fusion.15 = f32[4,10,128,128]{2,3,1,0:T(8,128)} fusion(bf16[4,128,10,128]{3,1,2,0:T(8,128)(2,1)} %copy-done.9, bf16[4,128,10,128]{3,1,2,0:T(8,128)(2,1)} %copy-done.8, bf16[4,128,10,128]{3,1,2,0:T(8,128)(2,1)} %get-tuple-element.78, bf16[4,128,10,128]{3,1,2,0:T(8,128)(2,1)} %get-tuple-element.79, pred[128,128]{1,0:T(8,128)(4,1)S(1)} %iota_compare_fusion, ...), kind=kOutput, calls=%fused_computation.39 | convolution fusion | flops 515112960 | bytes 9191424 | tf_op jit(solution)/shard_map/chij,cjhe->cihe/dot_general | solution.py:176
  169.7 4.4 %collective-permute-done.22 = f32[10,256,128]{2,1,0:T(8,128)} collective-permute-done((f32[10,256,128]{2,1,0:T(8,128)}, f32[10,256,128]{2,1,0:T(8,128)}, u32[]{:S(2)}, u32[]{:S(2)}) %collective-permute-start.22) | collective-permute-done | bytes 1310752 | tf_op jit(solution)/shard_map/ppermute | solution.py:170
  174.1 5.0 %multiply_reduce_fusion = (f32[4,128,10]{1,2,0:T(8,128)S(1)}, f32[4,128,10,128]{3,1,2,0:T(8,128)S(1)}) fusion(f32[4,10,128,128]{2,3,1,0:T(8,128)} %fusion.15, f32[3,10,256,128]{3,2,1,0:T(8,128)} %slice.74, f32[10,256,128]{2,1,0:T(8,128)} %collective-permute-done.22, bf16[4,128,10,128]{3,1,2,0:T(8,128)(2,1)} %get-tuple-element.78, ...), kind=kOutput, calls=%fused_computation.24 | convolution fusion | flops 345369600 | bytes 13127680 | tf_op jit(solution)/shard_map/cihf,chfe->cihe/dot_general | solution.py:182
  181.5 3.4 %broadcast_select_fusion = bf16[32,80,1280]{2,1,0:T(8,128)(2,1)} fusion(bf16[32,80,1280]{2,1,0:T(8,128)(2,1)S(1)} %bitcast.73, pred[32]{0:T(512)(128)(4,1)S(1)} %get-tuple-element.52), kind=kLoop, calls=%fused_computation.9 | loop fusion | flops 3276800 | bytes 13107232 | tf_op jit(solution)/shard_map/jit(_take)/select_n | solution.py:89
  188.8 5.3 %pad_maximum_fusion = bf16[4,4,2,80,1280]{4,3,2,1,0:T(8,128)(2,1)} fusion(bf16[1,4,2,80,1280]{4,3,2,1,0:T(8,128)(2,1)} %bitcast.29, bf16[1,4,2,80,1280]{4,3,2,1,0:T(8,128)(2,1)S(1)} %bitcast.81, bf16[1,4,2,80,1280]{4,3,2,1,0:T(8,128)(2,1)} %bitcast.27, bf16[1,4,2,80,1280]{4,3,2,1,0:T(8,128)(2,1)S(1)} %bitcast.79), kind=kLoop, calls=%fused_computation.7 | loop fusion | flops 9830400 | bytes 13107200 | tf_op jit(solution)/shard_map/stack | solution.py:50
  194.1 6.6 %gather_fusion.1 = bf16[32,80,1280]{2,1,0:T(8,128)(2,1)} fusion(bf16[32,80,1280]{2,1,0:T(8,128)(2,1)} %bitcast.75, s32[1024]{0:T(1024)S(1)} %pad_clamp_fusion.2), kind=kCustom, calls=%fused_computation.clone | custom fusion | bytes 13107328 | tf_op jit(solution)/shard_map/jit(_take)/gather | solution.py:89
  200.7 6.4 %broadcast_select_fusion.1 = bf16[32,80,1280]{2,1,0:T(8,128)(2,1)} fusion(bf16[32,80,1280]{2,1,0:T(8,128)(2,1)} %gather_fusion.1, pred[32]{0:T(512)(128)(4,1)S(1)} %get-tuple-element.47), kind=kLoop, calls=%fused_computation.10 | loop fusion | flops 3276800 | bytes 13107232 | tf_op jit(solution)/shard_map/jit(_take)/select_n | solution.py:89
  207.1 12.0 %fusion.4 = bf16[512,2560]{1,0:T(8,128)(2,1)} fusion(bf16[2560,1280]{1,0:T(8,128)(2,1)S(1)} %bitcast.85, bf16[2560,1280]{1,0:T(8,128)(2,1)} %bitcast.86, bf16[256,2560]{0,1:T(8,128)(2,1)} %collective-permute-done.24, bf16[256,2560]{0,1:T(8,128)(2,1)S(1)} %bitcast.93), kind=kOutput, calls=%fused_computation.12 | convolution fusion | flops 6743654400 | bytes 18350080 | tf_op jit(solution)/shard_map/dot_general | solution.py:192
  231.1 4.4 %copy.64 = bf16[1,256,5120]{2,1,0:T(8,128)(2,1)} copy(bf16[1,256,5120]{1,2,0:T(8,128)(2,1)} %bitcast.76) | data formatting | bytes 5242880
  (148 shorter events, 90.7 us)
Async XLA Ops:
  3.4 7.9 %collective-permute-start.5 = (bf16[80,1280]{1,0:T(8,128)(2,1)S(1)}, bf16[80,1280]{1,0:T(8,128)(2,1)S(1)}, u32[]{:S(2)}, u32[]{:S(2)}) collective-permute-start(bf16[80,1280]{1,0:T(8,128)(2,1)S(1)} %get-tuple-element.54), channel_id=1, source_target_pairs={{0,2},{2,0},{1,3},{3,1},{4,6},{6,4},{5,7},{7,5},{8,10},{10,8},{9,1... | collective-permute-start | bytes 614408 | tf_op jit(solution)/shard_map/ppermute | solution.py:115
  6.9 9.2 %collective-permute-start = (bf16[80,1280]{1,0:T(8,128)(2,1)S(1)}, bf16[80,1280]{1,0:T(8,128)(2,1)S(1)}, u32[]{:S(2)}, u32[]{:S(2)}) collective-permute-start(bf16[80,1280]{1,0:T(8,128)(2,1)S(1)} %get-tuple-element.54), channel_id=1, source_target_pairs={{0,16},{16,0},{1,17},{17,1},{2,18},{18,2},{3,19},{19,3},{4,20},{20... | collective-permute-start | bytes 614408 | tf_op jit(solution)/shard_map/ppermute | solution.py:26
  11.2 9.3 %collective-permute-start.6 = (bf16[80,1280]{1,0:T(8,128)(2,1)S(1)}, bf16[80,1280]{1,0:T(8,128)(2,1)S(1)}, u32[]{:S(2)}, u32[]{:S(2)}) collective-permute-start(bf16[80,1280]{1,0:T(8,128)(2,1)S(1)} %collective-permute-done.5), channel_id=1, source_target_pairs={{0,16},{16,0},{1,17},{17,1},{2,18},{18,2},{3,19},{19,3},{4,20},{20... | collective-permute-start | bytes 614408 | tf_op jit(solution)/shard_map/ppermute | solution.py:26
  16.2 9.0 %collective-permute-start.3 = (bf16[2,80,1280]{2,1,0:T(8,128)(2,1)S(1)}, bf16[2,80,1280]{2,1,0:T(8,128)(2,1)S(1)}, u32[]{:S(2)}, u32[]{:S(2)}) collective-permute-start(bf16[2,80,1280]{2,1,0:T(8,128)(2,1)S(1)} %get-tuple-element.77), channel_id=1, source_target_pairs={{0,12},{4,0},{8,4},{12,8},{1,13},{5,1},{9,5},{13,9},{2,14},{6,2},{... | collective-permute-start | bytes 1228808 | tf_op jit(solution)/shard_map/ppermute | solution.py:29
  19.0 9.6 %collective-permute-start.1 = (bf16[2,80,1280]{2,1,0:T(8,128)(2,1)S(1)}, bf16[2,80,1280]{2,1,0:T(8,128)(2,1)S(1)}, u32[]{:S(2)}, u32[]{:S(2)}) collective-permute-start(bf16[2,80,1280]{2,1,0:T(8,128)(2,1)S(1)} %get-tuple-element.77), channel_id=1, source_target_pairs={{0,4},{4,8},{8,12},{12,0},{1,5},{5,9},{9,13},{13,1},{2,6},{6,10},{... | collective-permute-start | bytes 1228808 | tf_op jit(solution)/shard_map/ppermute | solution.py:29
  21.4 11.3 %collective-permute-start.9 = (bf16[2,80,1280]{2,1,0:T(8,128)(2,1)}, bf16[2,80,1280]{2,1,0:T(8,128)(2,1)S(1)}, u32[]{:S(2)}, u32[]{:S(2)}) collective-permute-start(bf16[2,80,1280]{2,1,0:T(8,128)(2,1)} %get-tuple-element.75), channel_id=1, source_target_pairs={{0,96},{32,0},{64,32},{96,64},{1,97},{33,1},{65,33},{97,65},{2,98}... | collective-permute-start | bytes 1228808 | tf_op jit(solution)/shard_map/ppermute | solution.py:29
  25.2 10.9 %collective-permute-start.7 = (bf16[2,80,1280]{2,1,0:T(8,128)(2,1)}, bf16[2,80,1280]{2,1,0:T(8,128)(2,1)S(1)}, u32[]{:S(2)}, u32[]{:S(2)}) collective-permute-start(bf16[2,80,1280]{2,1,0:T(8,128)(2,1)} %get-tuple-element.75), channel_id=1, source_target_pairs={{0,32},{32,64},{64,96},{96,0},{1,33},{33,65},{65,97},{97,1},{2,34}... | collective-permute-start | bytes 1228808 | tf_op jit(solution)/shard_map/ppermute | solution.py:29
  25.2 11.0 %collective-permute-start.4 = (bf16[1,80,1280]{2,1,0:T(8,128)(2,1)S(1)}, bf16[1,80,1280]{2,1,0:T(8,128)(2,1)S(1)}, u32[]{:S(2)}, u32[]{:S(2)}) collective-permute-start(bf16[1,80,1280]{2,1,0:T(8,128)(2,1)S(1)} %slice.71), channel_id=1, source_target_pairs={{0,12},{4,0},{8,4},{12,8},{1,13},{5,1},{9,5},{13,9},{2,14},{6,2},{... | collective-permute-start | bytes 614408 | tf_op jit(solution)/shard_map/ppermute | solution.py:42
  30.0 6.3 %collective-permute-start.2 = (bf16[1,80,1280]{2,1,0:T(8,128)(2,1)}, bf16[1,80,1280]{2,1,0:T(8,128)(2,1)}, u32[]{:S(2)}, u32[]{:S(2)}) collective-permute-start(bf16[1,80,1280]{2,1,0:T(8,128)(2,1)} %slice.70), channel_id=1, source_target_pairs={{0,4},{4,8},{8,12},{12,0},{1,5},{5,9},{9,13},{13,1},{2,6},{6,10},{... | collective-permute-start | bytes 614408 | tf_op jit(solution)/shard_map/ppermute | solution.py:41
  32.8 6.1 %collective-permute-start.10 = (bf16[1,80,1280]{2,1,0:T(8,128)(2,1)S(1)}, bf16[1,80,1280]{2,1,0:T(8,128)(2,1)S(1)}, u32[]{:S(2)}, u32[]{:S(2)}) collective-permute-start(bf16[1,80,1280]{2,1,0:T(8,128)(2,1)S(1)} %slice.73), channel_id=1, source_target_pairs={{0,96},{32,0},{64,32},{96,64},{1,97},{33,1},{65,33},{97,65},{2,98}... | collective-permute-start | bytes 614408 | tf_op jit(solution)/shard_map/ppermute | solution.py:42
  36.2 5.9 %collective-permute-start.8 = (bf16[1,80,1280]{2,1,0:T(8,128)(2,1)S(1)}, bf16[1,80,1280]{2,1,0:T(8,128)(2,1)S(1)}, u32[]{:S(2)}, u32[]{:S(2)}) collective-permute-start(bf16[1,80,1280]{2,1,0:T(8,128)(2,1)S(1)} %slice.72), channel_id=1, source_target_pairs={{0,32},{32,64},{64,96},{96,0},{1,33},{33,65},{65,97},{97,1},{2,34}... | collective-permute-start | bytes 614408 | tf_op jit(solution)/shard_map/ppermute | solution.py:41
  43.5 34.2 %collective-permute-start.11 = (bf16[4,2,80,1280]{3,2,1,0:T(8,128)(2,1)S(1)}, bf16[4,2,80,1280]{3,2,1,0:T(8,128)(2,1)}, u32[]{:S(2)}, u32[]{:S(2)}) collective-permute-start(bf16[4,2,80,1280]{3,2,1,0:T(8,128)(2,1)S(1)} %pad_maximum_fusion.9), channel_id=1, source_target_pairs={{0,32},{32,64},{64,96},{96,0},{1,33},{33,65},{65,97},{97,1},{2,34}... | collective-permute-start | bytes 4915208 | tf_op jit(solution)/shard_map/ppermute | solution.py:29
  43.5 34.1 %collective-permute-start.12 = (bf16[4,2,80,1280]{3,2,1,0:T(8,128)(2,1)S(1)}, bf16[4,2,80,1280]{3,2,1,0:T(8,128)(2,1)}, u32[]{:S(2)}, u32[]{:S(2)}) collective-permute-start(bf16[4,2,80,1280]{3,2,1,0:T(8,128)(2,1)S(1)} %pad_maximum_fusion.9), channel_id=1, source_target_pairs={{0,96},{32,0},{64,32},{96,64},{1,97},{33,1},{65,33},{97,65},{2,98}... | collective-permute-start | bytes 4915208 | tf_op jit(solution)/shard_map/ppermute | solution.py:29
  46.2 33.6 %collective-permute-start.13 = (bf16[4,2,80,1280]{3,2,1,0:T(8,128)(2,1)S(1)}, bf16[4,2,80,1280]{3,2,1,0:T(8,128)(2,1)}, u32[]{:S(2)}, u32[]{:S(2)}) collective-permute-start(bf16[4,2,80,1280]{3,2,1,0:T(8,128)(2,1)S(1)} %pad_maximum_fusion.10), channel_id=1, source_target_pairs={{0,4},{4,8},{8,12},{12,0},{1,5},{5,9},{9,13},{13,1},{2,6},{6,10},{... | collective-permute-start | bytes 4915208 | tf_op jit(solution)/shard_map/ppermute | solution.py:29
  47.5 32.7 %collective-permute-start.14 = (bf16[4,2,80,1280]{3,2,1,0:T(8,128)(2,1)S(1)}, bf16[4,2,80,1280]{3,2,1,0:T(8,128)(2,1)}, u32[]{:S(2)}, u32[]{:S(2)}) collective-permute-start(bf16[4,2,80,1280]{3,2,1,0:T(8,128)(2,1)S(1)} %pad_maximum_fusion.10), channel_id=1, source_target_pairs={{0,12},{4,0},{8,4},{12,8},{1,13},{5,1},{9,5},{13,9},{2,14},{6,2},{... | collective-permute-start | bytes 4915208 | tf_op jit(solution)/shard_map/ppermute | solution.py:29
  82.3 20.0 %collective-permute-start.16 = (bf16[2,2,80,1280]{3,2,1,0:T(8,128)(2,1)}, bf16[2,2,80,1280]{3,2,1,0:T(8,128)(2,1)}, u32[]{:S(2)}, u32[]{:S(2)}) collective-permute-start(bf16[2,2,80,1280]{3,2,1,0:T(8,128)(2,1)} %slice.50), channel_id=1, source_target_pairs={{0,96},{32,0},{64,32},{96,64},{1,97},{33,1},{65,33},{97,65},{2,98}... | collective-permute-start | bytes 2457608 | tf_op jit(solution)/shard_map/ppermute | solution.py:42
  84.7 18.6 %collective-permute-start.15 = (bf16[2,2,80,1280]{3,2,1,0:T(8,128)(2,1)}, bf16[2,2,80,1280]{3,2,1,0:T(8,128)(2,1)}, u32[]{:S(2)}, u32[]{:S(2)}) collective-permute-start(bf16[2,2,80,1280]{3,2,1,0:T(8,128)(2,1)} %slice.49), channel_id=1, source_target_pairs={{0,32},{32,64},{64,96},{96,0},{1,33},{33,65},{65,97},{97,1},{2,34}... | collective-permute-start | bytes 2457608 | tf_op jit(solution)/shard_map/ppermute | solution.py:41
  88.1 18.0 %collective-permute-start.18 = (bf16[2,2,80,1280]{3,2,1,0:T(8,128)(2,1)}, bf16[2,2,80,1280]{3,2,1,0:T(8,128)(2,1)S(1)}, u32[]{:S(2)}, u32[]{:S(2)}) collective-permute-start(bf16[2,2,80,1280]{3,2,1,0:T(8,128)(2,1)} %slice.52), channel_id=1, source_target_pairs={{0,12},{4,0},{8,4},{12,8},{1,13},{5,1},{9,5},{13,9},{2,14},{6,2},{... | collective-permute-start | bytes 2457608 | tf_op jit(solution)/shard_map/ppermute | solution.py:42
  92.2 14.2 %collective-permute-start.17 = (bf16[2,2,80,1280]{3,2,1,0:T(8,128)(2,1)}, bf16[2,2,80,1280]{3,2,1,0:T(8,128)(2,1)}, u32[]{:S(2)}, u32[]{:S(2)}) collective-permute-start(bf16[2,2,80,1280]{3,2,1,0:T(8,128)(2,1)} %slice.51), channel_id=1, source_target_pairs={{0,4},{4,8},{8,12},{12,0},{1,5},{5,9},{9,13},{13,1},{2,6},{6,10},{... | collective-permute-start | bytes 2457608 | tf_op jit(solution)/shard_map/ppermute | solution.py:41
  95.0 22.9 %collective-permute-start.20 = (bf16[256,10,128]{0,2,1:T(8,128)(2,1)S(1)}, bf16[256,10,128]{0,2,1:T(8,128)(2,1)S(1)}, u32[]{:S(2)}, u32[]{:S(2)}) collective-permute-start(bf16[256,10,128]{0,2,1:T(8,128)(2,1)S(1)} %get-tuple-element.71), channel_id=1, source_target_pairs={{0,1},{1,0},{2,3},{3,2},{4,5},{5,4},{6,7},{7,6},{8,9},{9,8},{10,11... | collective-permute-start | bytes 1966088 | tf_op jit(solution)/shard_map/ppermute | solution.py:115
  102.3 15.6 %collective-permute-start.21 = (bf16[256,10,128]{0,2,1:T(8,128)(2,1)S(1)}, bf16[256,10,128]{0,2,1:T(8,128)(2,1)S(1)}, u32[]{:S(2)}, u32[]{:S(2)}) collective-permute-start(bf16[256,10,128]{0,2,1:T(8,128)(2,1)S(1)} %get-tuple-element.73), channel_id=1, source_target_pairs={{0,1},{1,0},{2,3},{3,2},{4,5},{5,4},{6,7},{7,6},{8,9},{9,8},{10,11... | collective-permute-start | bytes 1966088 | tf_op jit(solution)/shard_map/ppermute | solution.py:115
  109.9 20.8 %collective-permute-start.19 = (bf16[256,10,128]{0,2,1:T(8,128)(2,1)}, bf16[256,10,128]{0,2,1:T(8,128)(2,1)}, u32[]{:S(2)}, u32[]{:S(2)}) collective-permute-start(bf16[256,10,128]{0,2,1:T(8,128)(2,1)} %get-tuple-element.69), channel_id=1, source_target_pairs={{0,1},{1,0},{2,3},{3,2},{4,5},{5,4},{6,7},{7,6},{8,9},{9,8},{10,11... | collective-permute-start | bytes 1966088 | tf_op jit(solution)/shard_map/ppermute | solution.py:115
  142.7 31.5 %collective-permute-start.22 = (f32[10,256,128]{2,1,0:T(8,128)}, f32[10,256,128]{2,1,0:T(8,128)}, u32[]{:S(2)}, u32[]{:S(2)}) collective-permute-start(f32[10,256,128]{2,1,0:T(8,128)} %get-tuple-element.84), channel_id=1, source_target_pairs={{0,2},{1,3},{4,6},{5,7},{8,10},{9,11},{12,14},{13,15},{16,18},{17,... | collective-permute-start | bytes 3932168 | tf_op jit(solution)/shard_map/ppermute | solution.py:170
  188.8 18.4 %collective-permute-start.24 = (bf16[256,2560]{0,1:T(8,128)(2,1)}, bf16[256,2560]{0,1:T(8,128)(2,1)}, u32[]{:S(2)}, u32[]{:S(2)}) collective-permute-start(bf16[256,2560]{0,1:T(8,128)(2,1)} %bitcast.92), channel_id=1, source_target_pairs={{0,1},{1,0},{2,3},{3,2},{4,5},{5,4},{6,7},{7,6},{8,9},{9,8},{10,11... | collective-permute-start | bytes 3932168 | tf_op jit(solution)/shard_map/ppermute | solution.py:115
  (26 other events, 337.6 us)

commit v8 on v7

--- a/solution.py
+++ b/solution.py
@@ -67,27 +67,19 @@
     return parts
 
 
-def gather_finish(parts, sent, heads_order):
+def gather_finish(parts, sent):
     z = lax.axis_index("z")
     xl = lax.axis_index("xl")
     y = lax.axis_index("y")
-    blocks_per_group = 8
-    target = jnp.arange(32)
-    group = heads_order[target // blocks_per_group]
-    absolute = group * blocks_per_group + target % blocks_per_group
-    z_rel = (z - absolute // 8) % 4
-    xl_rel = (xl - (absolute // 4) % 2) % 2
-    y_rel = (y - absolute % 4) % 4
+    stacked = jnp.arange(32)
     pieces = []
     for part, received, (first, _) in zip(parts, sent, STAGES):
         part = ring_finish(part, received)
-        if first == "y":
-            source = z_rel * 8 + y_rel * 2 + xl_rel
-        else:
-            source = y_rel * 8 + z_rel * 2 + xl_rel
-        flat = part.reshape((32,) + part.shape[3:])
-        pieces.append(jnp.take(flat, source, axis=0).reshape(-1, part.shape[-1]))
-    return jnp.concatenate(pieces, axis=1)
+        outer, inner, xl_rel = stacked // 8, (stacked // 2) % 4, stacked % 2
+        z_rel, y_rel = (outer, inner) if first == "y" else (inner, outer)
+        source = ((z - z_rel) % 4) * 8 + ((xl - xl_rel) % 2) * 4 + (y - y_rel) % 4
+        pieces.append((part.reshape(-1, part.shape[-1]), source))
+    return pieces
 
 
 def seq_shift(x, shift):
@@ -187,24 +179,27 @@
     normed_group = normalize(attended, gain_rows)
     normed_own = pair_exchange(normed_group, core, 0, 1)
     normed_own = normed_own.reshape(tokens_here, H * HEAD)
-    columns = gather_finish(parts, sent, jnp.arange(4))
     tokens = jnp.concatenate([normed_own, swap(normed_own, "c")], axis=0)
-    wide = jnp.dot(tokens, columns, preferred_element_type=jnp.float32).astype(jnp.bfloat16)
-    own_wide = wide[:tokens_here]
-    returned = swap(wide[tokens_here:], "c")
-    width = own_wide.shape[1] // 2
-    by_offset = jnp.stack(
-        [
-            own_wide[:, :width],
-            returned[:, :width],
-            own_wide[:, width:],
-            returned[:, width:],
-        ]
-    )
-    block = jnp.arange(4)
-    offsets = ((block // 2 - half) % 2) * 2 + (block % 2 - core) % 2
-    projected = jnp.take(by_offset, offsets, axis=0)
-    projected = jnp.transpose(projected, (1, 0, 2)).reshape(tokens_here, -1)
+    by_block = tokens.reshape(tokens.shape[0], 32, -1)
+    wide = []
+    for rows, source in gather_finish(parts, sent):
+        features = jnp.take(by_block, source, axis=1).reshape(tokens.shape)
+        wide.append(
+            jnp.dot(features, rows, preferred_element_type=jnp.float32).astype(jnp.bfloat16)
+        )
+    own = [piece[:tokens_here] for piece in wide]
+    returned = [swap(piece[tokens_here:], "c") for piece in wide]
+    candidates = own + returned
+
+    def place(chip, side):
+        order = []
+        for block in range(4):
+            from_partner = (block % 2 - side) % 2
+            order.append(2 * from_partner + (block // 2 - chip) % 2)
+        return lambda *pieces: jnp.concatenate([pieces[i] for i in order], axis=1)
+
+    branches = [place(chip, side) for chip in (0, 1) for side in (0, 1)]
+    projected = lax.switch(half * 2 + core, branches, *candidates)
     layer_out = projected[None]
     return (layer_out, updated, moment_one, moment_two)
 

time: 237 us -> 230 us (0.970)
  local copies, waits for them, and re-layouts: 55.5 us -> 38.2 us
  waiting for transfers between devices: 46.7 us -> 63.4 us
  other arithmetic: 54.4 us -> 47.7 us
    ppermute x1, waiting for transfers between devices: 4.44 us -> 17.1 us  [on_device(): earlier = lax.ppermute(chip_total, 'xh', [(0, 1)])]
    gather x4 -> x2, local copies, waits for them, and re-layouts: 16.1 us -> 4.42 us  [on_device(): features = jnp.take(by_block, source, axis=1).reshape(tokens.shape)]
    select_n x4 -> x2, other arithmetic: 11.9 us -> 4.07 us  [on_device(): features = jnp.take(by_block, source, axis=1).reshape(tokens.shape)]
    ppermute x8, waiting for transfers between devices: 27 us -> 30.2 us  [ring_send(): return (lax.ppermute(x, axis, forward), lax.ppermute(x, axis, backward))]
    unnamed x54 -> x41, local copies, waits for them, and re-layouts: 11.6 us -> 8.77 us
    broadcast_in_dim x0 -> x1, other arithmetic: none -> 2.59 us  [on_device(): layer_out = projected[None]]
    select_n x1 -> x0, local copies, waits for them, and re-layouts: 2.56 us -> none  [on_device(): projected = jnp.take(by_offset, offsets, axis=0)]
    and x3 -> x1, other arithmetic: 2.54 us -> 0.02 us  [on_device(): features = jnp.take(by_block, source, axis=1).reshape(tokens.shape)]
  transfers between devices with their start and end apart: 26 -> 27, of which waited for: 12 -> 13; matrix products, arithmetic and copies ran while one was open for 36% -> 30% of each run, Pallas kernels for 0% -> 0%
where the time goes in v8:
time: 230 us; the launch traced here: 229 us
  waiting for transfers between devices  63.4 us (28%)
  starting transfers between devices  49.9 us (22%)
  other arithmetic  47.7 us (21%)
  local copies, waits for them, and re-layouts  38.2 us (17%)
  matrix products  28.8 us (13%)
    ppermute x8, waiting for transfers between devices, ring_send(): return (lax.ppermute(x, axis, forward), lax.ppermute(x, axis, backward))  30.2 us
    ppermute x8, starting transfers between devices, swap(): return lax.ppermute(x, axis, [(0, 1), (1, 0)])  21.6 us
    ppermute x1, waiting for transfers between devices, on_device(): earlier = lax.ppermute(chip_total, 'xh', [(0, 1)])  17.1 us
    another operation x8, other arithmetic, ring_finish(): return jnp.stack((x,) + tuple(received))  15.5 us
    dot_general x2, matrix products, on_device(): jnp.dot(features, rows, preferred_element_type=jnp.float32)  13 us
    ppermute x8, starting transfers between devices, ring_send(): return (lax.ppermute(x, axis, forward), lax.ppermute(x, axis, backward))  12 us
    ppermute x4, starting transfers between devices, ring_far(): lax.ppermute(from_right[half:], axis, backward)  8.96 us
    unnamed x41, local copies, waits for them, and re-layouts  8.77 us
  transfers between devices with their start and end apart: 27, of which 13 were waited for; matrix products, arithmetic and copies ran while one was open for 30% of the time, Pallas kernels for 0%

profile of v8, /device:TPU:1, one launch (start us, length us, event | category | flops | bytes accessed | tf_op | source)
XLA Modules:
  0.0 228.9 jit_solution(6589392577143374451)
XLA Ops:
  3.4 3.6 %collective-permute-start.5 = (bf16[80,1280]{1,0:T(8,128)(2,1)S(1)}, bf16[80,1280]{1,0:T(8,128)(2,1)S(1)}, u32[]{:S(2)}, u32[]{:S(2)}) collective-permute-start(bf16[80,1280]{1,0:T(8,128)(2,1)S(1)} %get-tuple-element.93), channel_id=1, source_target_pairs={{0,2},{2,0},{1,3},{3,1},{4,6},{6,4},{5,7},{7,5},{8,10},{10,8},{9,1... | collective-permute-start | bytes 614408 | tf_op jit(solution)/shard_map/ppermute | solution.py:107
  7.2 4.0 %collective-permute-done.5 = bf16[80,1280]{1,0:T(8,128)(2,1)S(1)} collective-permute-done((bf16[80,1280]{1,0:T(8,128)(2,1)S(1)}, bf16[80,1280]{1,0:T(8,128)(2,1)S(1)}, u32[]{:S(2)}, u32[]{:S(2)}) %collective-permute-start.5) | collective-permute-done | bytes 204832 | tf_op jit(solution)/shard_map/ppermute | solution.py:107
  12.8 3.3 %collective-permute-done = bf16[80,1280]{1,0:T(8,128)(2,1)S(1)} collective-permute-done((bf16[80,1280]{1,0:T(8,128)(2,1)S(1)}, bf16[80,1280]{1,0:T(8,128)(2,1)S(1)}, u32[]{:S(2)}, u32[]{:S(2)}) %collective-permute-start) | collective-permute-done | bytes 204832 | tf_op jit(solution)/shard_map/ppermute | solution.py:26
  16.2 2.8 %collective-permute-start.3 = (bf16[2,80,1280]{2,1,0:T(8,128)(2,1)S(1)}, bf16[2,80,1280]{2,1,0:T(8,128)(2,1)S(1)}, u32[]{:S(2)}, u32[]{:S(2)}) collective-permute-start(bf16[2,80,1280]{2,1,0:T(8,128)(2,1)S(1)} %get-tuple-element.116), channel_id=1, source_target_pairs={{0,12},{4,0},{8,4},{12,8},{1,13},{5,1},{9,5},{13,9},{2,14},{6,2},{... | collective-permute-start | bytes 1228808 | tf_op jit(solution)/shard_map/ppermute | solution.py:29
  21.5 3.8 %collective-permute-start.9 = (bf16[2,80,1280]{2,1,0:T(8,128)(2,1)}, bf16[2,80,1280]{2,1,0:T(8,128)(2,1)S(1)}, u32[]{:S(2)}, u32[]{:S(2)}) collective-permute-start(bf16[2,80,1280]{2,1,0:T(8,128)(2,1)} %get-tuple-element.114), channel_id=1, source_target_pairs={{0,96},{32,0},{64,32},{96,64},{1,97},{33,1},{65,33},{97,65},{2,98}... | collective-permute-start | bytes 1228808 | tf_op jit(solution)/shard_map/ppermute | solution.py:29
  25.2 3.3 %collective-permute-start.4 = (bf16[1,80,1280]{2,1,0:T(8,128)(2,1)S(1)}, bf16[1,80,1280]{2,1,0:T(8,128)(2,1)S(1)}, u32[]{:S(2)}, u32[]{:S(2)}) collective-permute-start(bf16[1,80,1280]{2,1,0:T(8,128)(2,1)S(1)} %slice.57), channel_id=1, source_target_pairs={{0,12},{4,0},{8,4},{12,8},{1,13},{5,1},{9,5},{13,9},{2,14},{6,2},{... | collective-permute-start | bytes 614408 | tf_op jit(solution)/shard_map/ppermute | solution.py:42
  32.8 3.4 %collective-permute-start.10 = (bf16[1,80,1280]{2,1,0:T(8,128)(2,1)S(1)}, bf16[1,80,1280]{2,1,0:T(8,128)(2,1)S(1)}, u32[]{:S(2)}, u32[]{:S(2)}) collective-permute-start(bf16[1,80,1280]{2,1,0:T(8,128)(2,1)S(1)} %slice.59), channel_id=1, source_target_pairs={{0,96},{32,0},{64,32},{96,64},{1,97},{33,1},{65,33},{97,65},{2,98}... | collective-permute-start | bytes 614408 | tf_op jit(solution)/shard_map/ppermute | solution.py:42
  38.8 3.2 %collective-permute-done.8 = bf16[1,80,1280]{2,1,0:T(8,128)(2,1)S(1)} collective-permute-done((bf16[1,80,1280]{2,1,0:T(8,128)(2,1)S(1)}, bf16[1,80,1280]{2,1,0:T(8,128)(2,1)S(1)}, u32[]{:S(2)}, u32[]{:S(2)}) %collective-permute-start.8) | collective-permute-done | bytes 204832 | tf_op jit(solution)/shard_map/ppermute | solution.py:41
  51.3 26.4 %collective-permute-done.11 = bf16[4,2,80,1280]{3,2,1,0:T(8,128)(2,1)} collective-permute-done((bf16[4,2,80,1280]{3,2,1,0:T(8,128)(2,1)S(1)}, bf16[4,2,80,1280]{3,2,1,0:T(8,128)(2,1)}, u32[]{:S(2)}, u32[]{:S(2)}) %collective-permute-start.11) | collective-permute-done | bytes 1638432 | tf_op jit(solution)/shard_map/ppermute | solution.py:29
  94.8 7.2 %collective-permute-start.20 = (bf16[256,10,128]{0,2,1:T(8,128)(2,1)S(1)}, bf16[256,10,128]{0,2,1:T(8,128)(2,1)S(1)}, u32[]{:S(2)}, u32[]{:S(2)}) collective-permute-start(bf16[256,10,128]{0,2,1:T(8,128)(2,1)S(1)} %get-tuple-element.110), channel_id=1, source_target_pairs={{0,1},{1,0},{2,3},{3,2},{4,5},{5,4},{6,7},{7,6},{8,9},{9,8},{10,11... | collective-permute-start | bytes 1966088 | tf_op jit(solution)/shard_map/ppermute | solution.py:107
  109.7 8.0 %collective-permute-start.19 = (bf16[256,10,128]{0,2,1:T(8,128)(2,1)}, bf16[256,10,128]{0,2,1:T(8,128)(2,1)}, u32[]{:S(2)}, u32[]{:S(2)}) collective-permute-start(bf16[256,10,128]{0,2,1:T(8,128)(2,1)} %get-tuple-element.108), channel_id=1, source_target_pairs={{0,1},{1,0},{2,3},{3,2},{4,5},{5,4},{6,7},{7,6},{8,9},{9,8},{10,11... | collective-permute-start | bytes 1966088 | tf_op jit(solution)/shard_map/ppermute | solution.py:107
  119.7 3.2 %copy.52 = f32[512,10,128]{2,0,1:T(8,128)} copy(f32[512,10,128]{0,2,1:T(8,128)} %get-tuple-element.125) | data formatting | bytes 5242880 | tf_op jit(solution)/shard_map/max | solution.py:91
  125.0 5.5 %multiply_convert_fusion.1 = (bf16[4,128,10,128]{3,1,2,0:T(8,128)(2,1)}, bf16[4,128,10,128]{3,1,2,0:T(8,128)(2,1)}, bf16[4,128,10,128]{3,1,2,0:T(8,128)(2,1)S(1)}, bf16[4,128,10,128]{3,1,2,0:T(8,128)(2,1)S(1)}) fusion(f32[4,128,10,128]{3,1,0,2:T(8,128)} %bitcast.69, f32[4,128]{1,0:T(4,128)S(1)} %get-tuple-element.128, f32[4,128]{1,0:T(4,128)S(1)} %get-tuple-element.127, ...), kind=kLoop, calls=%fused_computation.23 | loop fusion | flops 5242880 | bytes 10489856 | tf_op jit(solution)/shard_map/convert
  135.6 6.5 %fusion.39 = (f32[10,256,128]{2,1,0:T(8,128)}, f32[4,10,256,128]{3,2,1,0:T(8,128)}) fusion(bf16[4,128,10,128]{3,1,0,2:T(8,128)(2,1)} %bitcast.77, bf16[4,128,10,128]{3,1,2,0:T(8,128)(2,1)} %get-tuple-element.100, bf16[4,128,10,128]{3,1,2,0:T(8,128)(2,1)} %get-tuple-element.99), kind=kOutput, calls=%fused_computation.122 | convolution fusion | flops 341770240 | bytes 10485760 | tf_op jit(solution)/shard_map/cjhf,cjhe->chfe/dot_general | solution.py:158
  142.1 4.1 %collective-permute-start.22 = (f32[10,256,128]{2,1,0:T(8,128)}, f32[10,256,128]{2,1,0:T(8,128)}, u32[]{:S(2)}, u32[]{:S(2)}) collective-permute-start(f32[10,256,128]{2,1,0:T(8,128)} %get-tuple-element.119), channel_id=1, source_target_pairs={{0,2},{1,3},{4,6},{5,7},{8,10},{9,11},{12,14},{13,15},{16,18},{17,... | collective-permute-start | bytes 3932168 | tf_op jit(solution)/shard_map/ppermute | solution.py:162
  146.3 3.0 %fusion.40 = f32[4,10,256,128]{3,2,1,0:T(8,128)S(1)} fusion(f32[4,10,256,128]{3,2,1,0:T(8,128)} %get-tuple-element.120), kind=kOutput, calls=%fused_computation.123 | output fusion | flops 3932160 | bytes 10485760 | tf_op jit(solution)/shard_map/jit(cumsum)/reduce_window_sum | solution.py:171
  151.6 4.9 %fusion.5 = f32[4,10,128,128]{2,3,1,0:T(8,128)} fusion(bf16[4,128,10,128]{3,1,2,0:T(8,128)(2,1)} %get-tuple-element.100, bf16[4,128,10,128]{3,1,2,0:T(8,128)(2,1)} %get-tuple-element.99, bf16[4,128,10,128]{3,1,2,0:T(8,128)(2,1)S(1)} %get-tuple-element.117, bf16[4,128,10,128]{3,1,2,0:T(8,128)(2,1)S(1)} %get-tuple-element.118, ...), kind=kOutput, calls=%fused_computation.35 | convolution fusion | flops 515112960 | bytes 9191424 | tf_op jit(solution)/shard_map/chij,cjhe->cihe/dot_general | solution.py:168
  156.5 17.1 %collective-permute-done.22 = f32[10,256,128]{2,1,0:T(8,128)} collective-permute-done((f32[10,256,128]{2,1,0:T(8,128)}, f32[10,256,128]{2,1,0:T(8,128)}, u32[]{:S(2)}, u32[]{:S(2)}) %collective-permute-start.22) | collective-permute-done | bytes 1310752 | tf_op jit(solution)/shard_map/ppermute | solution.py:162
  173.6 4.4 %multiply_reduce_fusion = (f32[4,128,10]{1,2,0:T(8,128)S(1)}, f32[4,128,10,128]{3,1,2,0:T(8,128)S(1)}) fusion(f32[4,10,128,128]{2,3,1,0:T(8,128)} %fusion.5, f32[3,10,256,128]{3,2,1,0:T(8,128)} %slice.60, f32[10,256,128]{2,1,0:T(8,128)} %collective-permute-done.22, bf16[4,128,10,128]{3,1,2,0:T(8,128)(2,1)S(1)} %get-tuple-element.117, ...), kind=kOutput, calls=%fused_computation.18 | convolution fusion | flops 345369600 | bytes 13127680 | tf_op jit(solution)/shard_map/cihf,chfe->cihe/dot_general | solution.py:174
  183.7 3.1 %maximum_select_fusion.3 = bf16[256,20,128]{2,0,1:T(8,128)(2,1)} fusion(bf16[256,10,128]{2,0,1:T(8,128)(2,1)} %copy-done.17, bf16[256,10,128]{2,0,1:T(8,128)(2,1)} %get-tuple-element.105, pred[]{:T(512)S(6)} %eq.17), kind=kLoop, calls=%fused_computation.39 | loop fusion | flops 1966080 | bytes 2621441 | tf_op jit(solution)/shard_map/jit(_where)/select_n | solution.py:115
  189.6 5.4 %pad_maximum_fusion = bf16[4,4,2,80,1280]{4,3,2,1,0:T(8,128)(2,1)} fusion(bf16[1,4,2,80,1280]{4,3,2,1,0:T(8,128)(2,1)} %bitcast.32, bf16[1,4,2,80,1280]{4,3,2,1,0:T(8,128)(2,1)S(1)} %bitcast.73, bf16[1,4,2,80,1280]{4,3,2,1,0:T(8,128)(2,1)} %bitcast.30, bf16[1,4,2,80,1280]{4,3,2,1,0:T(8,128)(2,1)S(1)} %bitcast.71), kind=kLoop, calls=%fused_computation.6 | loop fusion | flops 9830400 | bytes 13107200 | tf_op jit(solution)/shard_map/stack | solution.py:50
  195.0 5.4 %pad_maximum_fusion.1 = bf16[4,4,2,80,1280]{4,3,2,1,0:T(8,128)(2,1)} fusion(bf16[1,4,2,80,1280]{4,3,2,1,0:T(8,128)(2,1)} %bitcast.39, bf16[1,4,2,80,1280]{4,3,2,1,0:T(8,128)(2,1)S(1)} %bitcast.74, bf16[1,4,2,80,1280]{4,3,2,1,0:T(8,128)(2,1)} %bitcast.37, bf16[1,4,2,80,1280]{4,3,2,1,0:T(8,128)(2,1)S(1)} %bitcast.72), kind=kLoop, calls=%fused_computation.7 | loop fusion | flops 9830400 | bytes 13107200 | tf_op jit(solution)/shard_map/stack | solution.py:50
  205.1 6.5 %convolution_convert_fusion.1 = bf16[512,1280]{1,0:T(8,128)(2,1)S(1)} fusion(bf16[512,2560]{0,1:T(8,128)(2,1)S(1)} %bitcast.84, bf16[2560,1280]{1,0:T(8,128)(2,1)} %bitcast.76), kind=kOutput, calls=%fused_computation.10 | convolution fusion | flops 3356098560 | bytes 10485760 | tf_op jit(solution)/shard_map/dot_general | solution.py:188
  216.9 6.5 %convolution_convert_fusion = bf16[512,1280]{1,0:T(8,128)(2,1)S(1)} fusion(bf16[512,2560]{0,1:T(8,128)(2,1)S(1)} %bitcast.85, bf16[2560,1280]{1,0:T(8,128)(2,1)} %bitcast.75), kind=kOutput, calls=%fused_computation.9 | convolution fusion | flops 3356098560 | bytes 10485760 | tf_op jit(solution)/shard_map/dot_general | solution.py:188
  (128 shorter events, 86.1 us)
Async XLA Ops:
  3.4 7.9 %collective-permute-start.5 = (bf16[80,1280]{1,0:T(8,128)(2,1)S(1)}, bf16[80,1280]{1,0:T(8,128)(2,1)S(1)}, u32[]{:S(2)}, u32[]{:S(2)}) collective-permute-start(bf16[80,1280]{1,0:T(8,128)(2,1)S(1)} %get-tuple-element.93), channel_id=1, source_target_pairs={{0,2},{2,0},{1,3},{3,1},{4,6},{6,4},{5,7},{7,5},{8,10},{10,8},{9,1... | collective-permute-start | bytes 614408 | tf_op jit(solution)/shard_map/ppermute | solution.py:107
  6.9 9.2 %collective-permute-start = (bf16[80,1280]{1,0:T(8,128)(2,1)S(1)}, bf16[80,1280]{1,0:T(8,128)(2,1)S(1)}, u32[]{:S(2)}, u32[]{:S(2)}) collective-permute-start(bf16[80,1280]{1,0:T(8,128)(2,1)S(1)} %get-tuple-element.93), channel_id=1, source_target_pairs={{0,16},{16,0},{1,17},{17,1},{2,18},{18,2},{3,19},{19,3},{4,20},{20... | collective-permute-start | bytes 614408 | tf_op jit(solution)/shard_map/ppermute | solution.py:26
  11.2 9.3 %collective-permute-start.6 = (bf16[80,1280]{1,0:T(8,128)(2,1)S(1)}, bf16[80,1280]{1,0:T(8,128)(2,1)S(1)}, u32[]{:S(2)}, u32[]{:S(2)}) collective-permute-start(bf16[80,1280]{1,0:T(8,128)(2,1)S(1)} %collective-permute-done.5), channel_id=1, source_target_pairs={{0,16},{16,0},{1,17},{17,1},{2,18},{18,2},{3,19},{19,3},{4,20},{20... | collective-permute-start | bytes 614408 | tf_op jit(solution)/shard_map/ppermute | solution.py:26
  16.2 9.1 %collective-permute-start.3 = (bf16[2,80,1280]{2,1,0:T(8,128)(2,1)S(1)}, bf16[2,80,1280]{2,1,0:T(8,128)(2,1)S(1)}, u32[]{:S(2)}, u32[]{:S(2)}) collective-permute-start(bf16[2,80,1280]{2,1,0:T(8,128)(2,1)S(1)} %get-tuple-element.116), channel_id=1, source_target_pairs={{0,12},{4,0},{8,4},{12,8},{1,13},{5,1},{9,5},{13,9},{2,14},{6,2},{... | collective-permute-start | bytes 1228808 | tf_op jit(solution)/shard_map/ppermute | solution.py:29
  19.0 9.6 %collective-permute-start.1 = (bf16[2,80,1280]{2,1,0:T(8,128)(2,1)S(1)}, bf16[2,80,1280]{2,1,0:T(8,128)(2,1)S(1)}, u32[]{:S(2)}, u32[]{:S(2)}) collective-permute-start(bf16[2,80,1280]{2,1,0:T(8,128)(2,1)S(1)} %get-tuple-element.116), channel_id=1, source_target_pairs={{0,4},{4,8},{8,12},{12,0},{1,5},{5,9},{9,13},{13,1},{2,6},{6,10},{... | collective-permute-start | bytes 1228808 | tf_op jit(solution)/shard_map/ppermute | solution.py:29
  21.5 11.3 %collective-permute-start.9 = (bf16[2,80,1280]{2,1,0:T(8,128)(2,1)}, bf16[2,80,1280]{2,1,0:T(8,128)(2,1)S(1)}, u32[]{:S(2)}, u32[]{:S(2)}) collective-permute-start(bf16[2,80,1280]{2,1,0:T(8,128)(2,1)} %get-tuple-element.114), channel_id=1, source_target_pairs={{0,96},{32,0},{64,32},{96,64},{1,97},{33,1},{65,33},{97,65},{2,98}... | collective-permute-start | bytes 1228808 | tf_op jit(solution)/shard_map/ppermute | solution.py:29
  25.2 10.9 %collective-permute-start.7 = (bf16[2,80,1280]{2,1,0:T(8,128)(2,1)}, bf16[2,80,1280]{2,1,0:T(8,128)(2,1)S(1)}, u32[]{:S(2)}, u32[]{:S(2)}) collective-permute-start(bf16[2,80,1280]{2,1,0:T(8,128)(2,1)} %get-tuple-element.114), channel_id=1, source_target_pairs={{0,32},{32,64},{64,96},{96,0},{1,33},{33,65},{65,97},{97,1},{2,34}... | collective-permute-start | bytes 1228808 | tf_op jit(solution)/shard_map/ppermute | solution.py:29
  25.2 11.0 %collective-permute-start.4 = (bf16[1,80,1280]{2,1,0:T(8,128)(2,1)S(1)}, bf16[1,80,1280]{2,1,0:T(8,128)(2,1)S(1)}, u32[]{:S(2)}, u32[]{:S(2)}) collective-permute-start(bf16[1,80,1280]{2,1,0:T(8,128)(2,1)S(1)} %slice.57), channel_id=1, source_target_pairs={{0,12},{4,0},{8,4},{12,8},{1,13},{5,1},{9,5},{13,9},{2,14},{6,2},{... | collective-permute-start | bytes 614408 | tf_op jit(solution)/shard_map/ppermute | solution.py:42
  30.0 6.3 %collective-permute-start.2 = (bf16[1,80,1280]{2,1,0:T(8,128)(2,1)}, bf16[1,80,1280]{2,1,0:T(8,128)(2,1)}, u32[]{:S(2)}, u32[]{:S(2)}) collective-permute-start(bf16[1,80,1280]{2,1,0:T(8,128)(2,1)} %slice.56), channel_id=1, source_target_pairs={{0,4},{4,8},{8,12},{12,0},{1,5},{5,9},{9,13},{13,1},{2,6},{6,10},{... | collective-permute-start | bytes 614408 | tf_op jit(solution)/shard_map/ppermute | solution.py:41
  32.8 6.1 %collective-permute-start.10 = (bf16[1,80,1280]{2,1,0:T(8,128)(2,1)S(1)}, bf16[1,80,1280]{2,1,0:T(8,128)(2,1)S(1)}, u32[]{:S(2)}, u32[]{:S(2)}) collective-permute-start(bf16[1,80,1280]{2,1,0:T(8,128)(2,1)S(1)} %slice.59), channel_id=1, source_target_pairs={{0,96},{32,0},{64,32},{96,64},{1,97},{33,1},{65,33},{97,65},{2,98}... | collective-permute-start | bytes 614408 | tf_op jit(solution)/shard_map/ppermute | solution.py:42
  43.5 34.2 %collective-permute-start.11 = (bf16[4,2,80,1280]{3,2,1,0:T(8,128)(2,1)S(1)}, bf16[4,2,80,1280]{3,2,1,0:T(8,128)(2,1)}, u32[]{:S(2)}, u32[]{:S(2)}) collective-permute-start(bf16[4,2,80,1280]{3,2,1,0:T(8,128)(2,1)S(1)} %pad_maximum_fusion.9), channel_id=1, source_target_pairs={{0,32},{32,64},{64,96},{96,0},{1,33},{33,65},{65,97},{97,1},{2,34}... | collective-permute-start | bytes 4915208 | tf_op jit(solution)/shard_map/ppermute | solution.py:29
  43.6 34.1 %collective-permute-start.12 = (bf16[4,2,80,1280]{3,2,1,0:T(8,128)(2,1)S(1)}, bf16[4,2,80,1280]{3,2,1,0:T(8,128)(2,1)}, u32[]{:S(2)}, u32[]{:S(2)}) collective-permute-start(bf16[4,2,80,1280]{3,2,1,0:T(8,128)(2,1)S(1)} %pad_maximum_fusion.9), channel_id=1, source_target_pairs={{0,96},{32,0},{64,32},{96,64},{1,97},{33,1},{65,33},{97,65},{2,98}... | collective-permute-start | bytes 4915208 | tf_op jit(solution)/shard_map/ppermute | solution.py:29
  46.2 33.6 %collective-permute-start.13 = (bf16[4,2,80,1280]{3,2,1,0:T(8,128)(2,1)S(1)}, bf16[4,2,80,1280]{3,2,1,0:T(8,128)(2,1)}, u32[]{:S(2)}, u32[]{:S(2)}) collective-permute-start(bf16[4,2,80,1280]{3,2,1,0:T(8,128)(2,1)S(1)} %pad_maximum_fusion.10), channel_id=1, source_target_pairs={{0,4},{4,8},{8,12},{12,0},{1,5},{5,9},{9,13},{13,1},{2,6},{6,10},{... | collective-permute-start | bytes 4915208 | tf_op jit(solution)/shard_map/ppermute | solution.py:29
  47.5 32.7 %collective-permute-start.14 = (bf16[4,2,80,1280]{3,2,1,0:T(8,128)(2,1)S(1)}, bf16[4,2,80,1280]{3,2,1,0:T(8,128)(2,1)}, u32[]{:S(2)}, u32[]{:S(2)}) collective-permute-start(bf16[4,2,80,1280]{3,2,1,0:T(8,128)(2,1)S(1)} %pad_maximum_fusion.10), channel_id=1, source_target_pairs={{0,12},{4,0},{8,4},{12,8},{1,13},{5,1},{9,5},{13,9},{2,14},{6,2},{... | collective-permute-start | bytes 4915208 | tf_op jit(solution)/shard_map/ppermute | solution.py:29
  82.3 19.8 %collective-permute-start.16 = (bf16[2,2,80,1280]{3,2,1,0:T(8,128)(2,1)}, bf16[2,2,80,1280]{3,2,1,0:T(8,128)(2,1)}, u32[]{:S(2)}, u32[]{:S(2)}) collective-permute-start(bf16[2,2,80,1280]{3,2,1,0:T(8,128)(2,1)} %slice.44), channel_id=1, source_target_pairs={{0,96},{32,0},{64,32},{96,64},{1,97},{33,1},{65,33},{97,65},{2,98}... | collective-permute-start | bytes 2457608 | tf_op jit(solution)/shard_map/ppermute | solution.py:42
  84.7 18.6 %collective-permute-start.15 = (bf16[2,2,80,1280]{3,2,1,0:T(8,128)(2,1)}, bf16[2,2,80,1280]{3,2,1,0:T(8,128)(2,1)}, u32[]{:S(2)}, u32[]{:S(2)}) collective-permute-start(bf16[2,2,80,1280]{3,2,1,0:T(8,128)(2,1)} %slice.43), channel_id=1, source_target_pairs={{0,32},{32,64},{64,96},{96,0},{1,33},{33,65},{65,97},{97,1},{2,34}... | collective-permute-start | bytes 2457608 | tf_op jit(solution)/shard_map/ppermute | solution.py:41
  88.0 18.0 %collective-permute-start.18 = (bf16[2,2,80,1280]{3,2,1,0:T(8,128)(2,1)}, bf16[2,2,80,1280]{3,2,1,0:T(8,128)(2,1)S(1)}, u32[]{:S(2)}, u32[]{:S(2)}) collective-permute-start(bf16[2,2,80,1280]{3,2,1,0:T(8,128)(2,1)} %slice.46), channel_id=1, source_target_pairs={{0,12},{4,0},{8,4},{12,8},{1,13},{5,1},{9,5},{13,9},{2,14},{6,2},{... | collective-permute-start | bytes 2457608 | tf_op jit(solution)/shard_map/ppermute | solution.py:42
  92.1 14.2 %collective-permute-start.17 = (bf16[2,2,80,1280]{3,2,1,0:T(8,128)(2,1)}, bf16[2,2,80,1280]{3,2,1,0:T(8,128)(2,1)}, u32[]{:S(2)}, u32[]{:S(2)}) collective-permute-start(bf16[2,2,80,1280]{3,2,1,0:T(8,128)(2,1)} %slice.45), channel_id=1, source_target_pairs={{0,4},{4,8},{8,12},{12,0},{1,5},{5,9},{9,13},{13,1},{2,6},{6,10},{... | collective-permute-start | bytes 2457608 | tf_op jit(solution)/shard_map/ppermute | solution.py:41
  94.8 22.9 %collective-permute-start.20 = (bf16[256,10,128]{0,2,1:T(8,128)(2,1)S(1)}, bf16[256,10,128]{0,2,1:T(8,128)(2,1)S(1)}, u32[]{:S(2)}, u32[]{:S(2)}) collective-permute-start(bf16[256,10,128]{0,2,1:T(8,128)(2,1)S(1)} %get-tuple-element.110), channel_id=1, source_target_pairs={{0,1},{1,0},{2,3},{3,2},{4,5},{5,4},{6,7},{7,6},{8,9},{9,8},{10,11... | collective-permute-start | bytes 1966088 | tf_op jit(solution)/shard_map/ppermute | solution.py:107
  102.1 15.6 %collective-permute-start.21 = (bf16[256,10,128]{0,2,1:T(8,128)(2,1)S(1)}, bf16[256,10,128]{0,2,1:T(8,128)(2,1)S(1)}, u32[]{:S(2)}, u32[]{:S(2)}) collective-permute-start(bf16[256,10,128]{0,2,1:T(8,128)(2,1)S(1)} %get-tuple-element.112), channel_id=1, source_target_pairs={{0,1},{1,0},{2,3},{3,2},{4,5},{5,4},{6,7},{7,6},{8,9},{9,8},{10,11... | collective-permute-start | bytes 1966088 | tf_op jit(solution)/shard_map/ppermute | solution.py:107
  109.7 20.8 %collective-permute-start.19 = (bf16[256,10,128]{0,2,1:T(8,128)(2,1)}, bf16[256,10,128]{0,2,1:T(8,128)(2,1)}, u32[]{:S(2)}, u32[]{:S(2)}) collective-permute-start(bf16[256,10,128]{0,2,1:T(8,128)(2,1)} %get-tuple-element.108), channel_id=1, source_target_pairs={{0,1},{1,0},{2,3},{3,2},{4,5},{5,4},{6,7},{7,6},{8,9},{9,8},{10,11... | collective-permute-start | bytes 1966088 | tf_op jit(solution)/shard_map/ppermute | solution.py:107
  142.1 31.5 %collective-permute-start.22 = (f32[10,256,128]{2,1,0:T(8,128)}, f32[10,256,128]{2,1,0:T(8,128)}, u32[]{:S(2)}, u32[]{:S(2)}) collective-permute-start(f32[10,256,128]{2,1,0:T(8,128)} %get-tuple-element.119), channel_id=1, source_target_pairs={{0,2},{1,3},{4,6},{5,7},{8,10},{9,11},{12,14},{13,15},{16,18},{17,... | collective-permute-start | bytes 3932168 | tf_op jit(solution)/shard_map/ppermute | solution.py:162
  189.2 11.3 %collective-permute-start.24 = (bf16[256,2560]{0,1:T(8,128)(2,1)}, bf16[256,2560]{0,1:T(8,128)(2,1)S(1)}, u32[]{:S(2)}, u32[]{:S(2)}) collective-permute-start(bf16[256,2560]{0,1:T(8,128)(2,1)} %bitcast.79), channel_id=1, source_target_pairs={{0,1},{1,0},{2,3},{3,2},{4,5},{5,4},{6,7},{7,6},{8,9},{9,8},{10,11... | collective-permute-start | bytes 3932168 | tf_op jit(solution)/shard_map/ppermute | solution.py:107
  212.5 11.4 %collective-permute-start.25 = (bf16[256,1280]{1,0:T(8,128)(2,1)}, bf16[256,1280]{1,0:T(8,128)(2,1)}, u32[]{:S(2)}, u32[]{:S(2)}) collective-permute-start(bf16[256,1280]{1,0:T(8,128)(2,1)} %get-tuple-element.103), channel_id=1, source_target_pairs={{0,1},{1,0},{2,3},{3,2},{4,5},{5,4},{6,7},{7,6},{8,9},{9,8},{10,11... | collective-permute-start | bytes 1966088 | tf_op jit(solution)/shard_map/ppermute | solution.py:107
  (21 other events, 321.2 us)

commit v9 on v8

--- a/solution.py
+++ b/solution.py
@@ -143,13 +143,8 @@
     )
     query_group = pair_exchange(query_heads, core, 1, 0)
     sent = [ring_send(part, second, 4) for part, (_, second) in zip(parts, STAGES)]
-    sent, key_heads = lax.optimization_barrier((sent, keys_in[0].reshape(tokens_here, H, HEAD)))
-    key_group = pair_exchange(key_heads, core, 1, 0)
-    sent = [ring_far(received, second, 4) for received, (_, second) in zip(sent, STAGES)]
-    sent, value_heads = lax.optimization_barrier(
-        (sent, values_in[0].reshape(tokens_here, H, HEAD))
-    )
-    value_group = pair_exchange(value_heads, core, 1, 0)
+    key_group = pair_exchange(keys_in[0].reshape(tokens_here, H, HEAD), core, 1, 0)
+    value_group = pair_exchange(values_in[0].reshape(tokens_here, H, HEAD), core, 1, 0)
     span = query_group.shape[0]
     offset = half * span
     query_blocks = to_blocks(featurize(query_group, offset, seq_length))
@@ -159,6 +154,8 @@
         "cjhf,cjhe->chfe", key_blocks, value_blocks, preferred_element_type=jnp.float32
     )
     chip_total = jnp.sum(states, axis=0)
+    sent, chip_total = lax.optimization_barrier((sent, chip_total))
+    sent = [ring_far(received, second, 4) for received, (_, second) in zip(sent, STAGES)]
     earlier = lax.ppermute(chip_total, "xh", [(0, 1)])
     scores = jnp.einsum(
         "cihf,cjhf->chij", query_blocks, key_blocks, preferred_element_type=jnp.float32
@@ -175,6 +172,7 @@
         "cihf,chfe->cihe", query_blocks, before, preferred_element_type=jnp.float32
     )
     attended = (inside_block + from_before).reshape(span, heads_here, HEAD)
+    sent, attended = lax.optimization_barrier((sent, attended))
     gain_rows = lax.dynamic_slice_in_dim(head_gain, core * heads_here, heads_here, 0)
     normed_group = normalize(attended, gain_rows)
     normed_own = pair_exchange(normed_group, core, 0, 1)

time: 230 us -> 193 us (0.84)
  waiting for transfers between devices: 63.4 us -> 28.4 us
  local copies, waits for them, and re-layouts: 38.2 us -> 46.5 us
  starting transfers between devices: 49.9 us -> 44.2 us
  matrix products: 28.8 us -> 23.3 us
    ppermute x8, waiting for transfers between devices: 30.2 us -> 10.3 us  [ring_send(): return (lax.ppermute(x, axis, forward), lax.ppermute(x, axis, backward))]
    ppermute x1, waiting for transfers between devices: 17.1 us -> 0.01 us  [on_device(): earlier = lax.ppermute(chip_total, 'xh', [(0, 1)])]
    ppermute x8, starting transfers between devices: 21.6 us -> 13.8 us  [swap(): return lax.ppermute(x, axis, [(0, 1), (1, 0)])]
    max x2 -> x4, local copies, waits for them, and re-layouts: 5.28 us -> 12 us  [featurize(): rectified = jnp.maximum(block.astype(jnp.float32), 0.0)]
    dot_general x1, matrix products: 6.55 us -> 1.94 us  [on_device(): jnp.einsum('cjhf,cjhe->chfe', key_blocks, value_blocks, preferred_element...]
    another operation x8, other arithmetic: 15.5 us -> 18.6 us  [ring_finish(): return jnp.stack((x,) + tuple(received))]
    ppermute x4, starting transfers between devices: 8.96 us -> 11.6 us  [ring_far(): lax.ppermute(from_right[half:], axis, backward)]
    unnamed x41 -> x49, local copies, waits for them, and re-layouts: 8.77 us -> 8.89 us
  transfers between devices with their start and end apart: 27 -> 27, of which waited for: 13 -> 12; matrix products, arithmetic and copies ran while one was open for 30% -> 43% of each run, Pallas kernels for 0% -> 0%
where the time goes in v9:
time: 193 us; the launch traced here: 192 us
  other arithmetic  48.7 us (25%)
  local copies, waits for them, and re-layouts  46.5 us (24%)
  starting transfers between devices  44.2 us (23%)
  waiting for transfers between devices  28.4 us (15%)
  matrix products  23.3 us (12%)
    another operation x8, other arithmetic, ring_finish(): return jnp.stack((x,) + tuple(received))  18.6 us
    ppermute x8, starting transfers between devices, swap(): return lax.ppermute(x, axis, [(0, 1), (1, 0)])  13.8 us
    dot_general x2, matrix products, on_device(): jnp.dot(features, rows, preferred_element_type=jnp.float32)  13 us
    max x4, local copies, waits for them, and re-layouts, featurize(): rectified = jnp.maximum(block.astype(jnp.float32), 0.0)  12 us
    ppermute x8, starting transfers between devices, ring_send(): return (lax.ppermute(x, axis, forward), lax.ppermute(x, axis, backward))  11.8 us
    ppermute x4, starting transfers between devices, ring_far(): lax.ppermute(from_right[half:], axis, backward)  11.6 us
    ppermute x8, waiting for transfers between devices, ring_send(): return (lax.ppermute(x, axis, forward), lax.ppermute(x, axis, backward))  10.3 us
    unnamed x49, local copies, waits for them, and re-layouts  8.89 us
  transfers between devices with their start and end apart: 27, of which 12 were waited for; matrix products, arithmetic and copies ran while one was open for 43% of the time, Pallas kernels for 0%

profile of v9, /device:TPU:1, one launch (start us, length us, event | category | flops | bytes accessed | tf_op | source)
XLA Modules:
  0.0 192.2 jit_solution(10571343403883161800)
XLA Ops:
  3.4 3.6 %collective-permute-start.5 = (bf16[80,1280]{1,0:T(8,128)(2,1)S(1)}, bf16[80,1280]{1,0:T(8,128)(2,1)S(1)}, u32[]{:S(2)}, u32[]{:S(2)}) collective-permute-start(bf16[80,1280]{1,0:T(8,128)(2,1)S(1)} %get-tuple-element.93), channel_id=1, source_target_pairs={{0,2},{2,0},{1,3},{3,1},{4,6},{6,4},{5,7},{7,5},{8,10},{10,8},{9,1... | collective-permute-start | bytes 614408 | tf_op jit(solution)/shard_map/ppermute | solution.py:107
  7.2 4.0 %collective-permute-done.5 = bf16[80,1280]{1,0:T(8,128)(2,1)S(1)} collective-permute-done((bf16[80,1280]{1,0:T(8,128)(2,1)S(1)}, bf16[80,1280]{1,0:T(8,128)(2,1)S(1)}, u32[]{:S(2)}, u32[]{:S(2)}) %collective-permute-start.5) | collective-permute-done | bytes 204832 | tf_op jit(solution)/shard_map/ppermute | solution.py:107
  12.8 3.3 %collective-permute-done = bf16[80,1280]{1,0:T(8,128)(2,1)S(1)} collective-permute-done((bf16[80,1280]{1,0:T(8,128)(2,1)S(1)}, bf16[80,1280]{1,0:T(8,128)(2,1)S(1)}, u32[]{:S(2)}, u32[]{:S(2)}) %collective-permute-start) | collective-permute-done | bytes 204832 | tf_op jit(solution)/shard_map/ppermute | solution.py:26
  21.5 3.8 %collective-permute-start.9 = (bf16[2,80,1280]{2,1,0:T(8,128)(2,1)}, bf16[2,80,1280]{2,1,0:T(8,128)(2,1)}, u32[]{:S(2)}, u32[]{:S(2)}) collective-permute-start(bf16[2,80,1280]{2,1,0:T(8,128)(2,1)} %get-tuple-element.114), channel_id=1, source_target_pairs={{0,96},{32,0},{64,32},{96,64},{1,97},{33,1},{65,33},{97,65},{2,98}... | collective-permute-start | bytes 1228808 | tf_op jit(solution)/shard_map/ppermute | solution.py:29
  32.2 4.1 %collective-permute-start.15 = (bf16[256,10,128]{0,2,1:T(8,128)(2,1)}, bf16[256,10,128]{0,2,1:T(8,128)(2,1)}, u32[]{:S(2)}, u32[]{:S(2)}) collective-permute-start(bf16[256,10,128]{0,2,1:T(8,128)(2,1)} %get-tuple-element.112), channel_id=1, source_target_pairs={{0,1},{1,0},{2,3},{3,2},{4,5},{5,4},{6,7},{7,6},{8,9},{9,8},{10,11... | collective-permute-start | bytes 1966088 | tf_op jit(solution)/shard_map/ppermute | solution.py:107
  40.5 3.8 %collective-permute-start.10 = (bf16[1,80,1280]{2,1,0:T(8,128)(2,1)S(1)}, bf16[1,80,1280]{2,1,0:T(8,128)(2,1)S(1)}, u32[]{:S(2)}, u32[]{:S(2)}) collective-permute-start(bf16[1,80,1280]{2,1,0:T(8,128)(2,1)S(1)} %slice.59), channel_id=1, source_target_pairs={{0,96},{32,0},{64,32},{96,64},{1,97},{33,1},{65,33},{97,65},{2,98}... | collective-permute-start | bytes 614408 | tf_op jit(solution)/shard_map/ppermute | solution.py:42
  48.3 4.1 %collective-permute-done.8 = bf16[1,80,1280]{2,1,0:T(8,128)(2,1)S(1)} collective-permute-done((bf16[1,80,1280]{2,1,0:T(8,128)(2,1)S(1)}, bf16[1,80,1280]{2,1,0:T(8,128)(2,1)S(1)}, u32[]{:S(2)}, u32[]{:S(2)}) %collective-permute-start.8) | collective-permute-done | bytes 204832 | tf_op jit(solution)/shard_map/ppermute | solution.py:41
  67.0 3.9 %convert_maximum_fusion = (f32[512,10,128]{0,2,1:T(8,128)S(1)}, f32[512,10,128]{0,2,1:T(8,128)}) fusion(bf16[256,10,128]{0,2,1:T(8,128)(2,1)} %copy-done.22, bf16[256,10,128]{0,2,1:T(8,128)(2,1)} %get-tuple-element.107, pred[]{:T(512)S(6)} %eq.17, bf16[256,10,128]{0,2,1:T(8,128)(2,1)S(1)} %copy-done.12, bf16[256,10,128]{0,2,1:T(8,128)(2,1)} %collective-permute-done.15), kind=kLoop, calls=%fused_computation.22 | loop fusion | flops 14417920 | bytes 7864321 | tf_op jit(solution)/shard_map/max | solution.py:91
  70.9 3.3 %copy.15 = f32[512,10,128]{2,0,1:T(8,128)} copy(f32[512,10,128]{0,2,1:T(8,128)} %get-tuple-element.124) | data formatting | bytes 5242880 | tf_op jit(solution)/shard_map/max | solution.py:91
  74.2 3.2 %copy.16 = f32[4,128,10,128]{1,3,2,0:T(8,128)} copy(f32[4,128,10,128]{3,1,0,2:T(8,128)} %bitcast.59) | data formatting | bytes 5242880 | tf_op jit(solution)/shard_map/max | solution.py:91
  79.6 3.3 %copy.22 = f32[4,128,10,128]{1,3,2,0:T(8,128)} copy(f32[4,128,10,128]{3,1,0,2:T(8,128)} %bitcast.60) | data formatting | bytes 5242880 | tf_op jit(solution)/shard_map/max | solution.py:91
  83.0 4.4 %multiply_convert_fusion.4 = (bf16[4,128,10,128]{1,3,2,0:T(8,128)(2,1)S(1)}, bf16[4,128,10,128]{1,3,2,0:T(8,128)(2,1)S(1)}, bf16[4,128,10,128]{1,3,2,0:T(8,128)(2,1)}, bf16[4,128,10,128]{1,3,2,0:T(8,128)(2,1)}) fusion(f32[4,128,10,128]{1,3,2,0:T(8,128)S(1)} %copy-done.3, f32[4,128]{1,0:T(4,128)S(1)} %get-tuple-element.126, ...), kind=kLoop, calls=%fused_computation.24 | loop fusion | flops 5242880 | bytes 10489856 | tf_op jit(solution)/shard_map/convert.2
  89.4 7.2 %collective-permute-done.11 = bf16[4,2,80,1280]{3,2,1,0:T(8,128)(2,1)} collective-permute-done((bf16[4,2,80,1280]{3,2,1,0:T(8,128)(2,1)}, bf16[4,2,80,1280]{3,2,1,0:T(8,128)(2,1)}, u32[]{:S(2)}, u32[]{:S(2)}) %collective-permute-start.11) | collective-permute-done | bytes 1638432 | tf_op jit(solution)/shard_map/ppermute | solution.py:29
  98.6 4.7 %collective-permute-start.22 = (f32[10,256,128]{2,1,0:T(8,128)}, f32[10,256,128]{2,1,0:T(8,128)}, u32[]{:S(2)}, u32[]{:S(2)}) collective-permute-start(f32[10,256,128]{2,1,0:T(8,128)} %get-tuple-element.81), channel_id=1, source_target_pairs={{0,2},{1,3},{4,6},{5,7},{8,10},{9,11},{12,14},{13,15},{16,18},{17,... | collective-permute-start | bytes 3932168 | tf_op jit(solution)/shard_map/ppermute | solution.py:159
  123.1 4.9 %fusion.3 = f32[4,10,128,128]{2,3,1,0:T(8,128)} fusion(bf16[4,128,10,128]{1,3,2,0:T(8,128)(2,1)S(1)} %copy-done.4, bf16[4,128,10,128]{1,3,2,0:T(8,128)(2,1)S(1)} %copy-done.6, bf16[4,128,10,128]{1,3,2,0:T(8,128)(2,1)} %copy-done.9, bf16[4,128,10,128]{1,3,2,0:T(8,128)(2,1)} %copy-done.8, pred[128,128]{1,0:T(8,128)(4,1)S(1)} %iota_compare_fusion, ...), kind=kOutput, calls=%fused_computation.33 | convolution fusion | flops 515112960 | bytes 9191424 | tf_op jit(solution)/shard_map/chij,cjhe->cihe/dot_general | solution.py:165
  134.1 3.5 %add_bitcast_fusion = f32[4,128,10,128]{3,1,2,0:T(8,128)S(1)} fusion(f32[4,10,128,128]{2,3,1,0:T(8,128)} %fusion.3, f32[3,10,256,128]{3,2,1,0:T(8,128)S(1)} %slice-done, f32[10,256,128]{2,1,0:T(8,128)} %collective-permute-done.22, bf16[4,128,10,128]{1,3,2,0:T(8,128)(2,1)S(1)} %copy-done.5, bf16[4,128,10,128]{1,3,2,0:T(8,128)(2,1)S(1)} %copy-done.7), kind=kOutput, calls=%fused_computation.17 | convolution fusion | flops 344064000 | bytes 13107200 | tf_op jit(solution)/shard_map/cihf,chfe->cihe/dot_general | solution.py:171
  140.6 3.5 %collective-permute-start.23 = (bf16[256,10,128]{2,0,1:T(8,128)(2,1)}, bf16[256,10,128]{2,0,1:T(8,128)(2,1)}, u32[]{:S(2)}, u32[]{:S(2)}) collective-permute-start(bf16[256,10,128]{2,0,1:T(8,128)(2,1)} %get-tuple-element.106), channel_id=1, source_target_pairs={{0,1},{1,0},{2,3},{3,2},{4,5},{5,4},{6,7},{7,6},{8,9},{9,8},{10,11... | collective-permute-start | bytes 1966088 | tf_op jit(solution)/shard_map/ppermute | solution.py:107
  146.2 2.9 %maximum_select_fusion.3 = bf16[256,20,128]{2,0,1:T(8,128)(2,1)} fusion(bf16[256,10,128]{2,0,1:T(8,128)(2,1)} %collective-permute-done.23, bf16[256,10,128]{2,0,1:T(8,128)(2,1)} %get-tuple-element.105, pred[]{:T(512)S(6)} %eq.17), kind=kLoop, calls=%fused_computation.37 | loop fusion | flops 1966080 | bytes 2621441 | tf_op jit(solution)/shard_map/jit(_where)/select_n | solution.py:115
  151.9 5.7 %pad_maximum_fusion.1 = bf16[4,4,2,80,1280]{4,3,2,1,0:T(8,128)(2,1)} fusion(bf16[1,4,2,80,1280]{4,3,2,1,0:T(8,128)(2,1)} %bitcast.39, bf16[1,4,2,80,1280]{4,3,2,1,0:T(8,128)(2,1)S(1)} %bitcast.61, bf16[1,4,2,80,1280]{4,3,2,1,0:T(8,128)(2,1)} %bitcast.37, bf16[1,4,2,80,1280]{4,3,2,1,0:T(8,128)(2,1)} %bitcast.36), kind=kLoop, calls=%fused_computation.7 | loop fusion | flops 9830400 | bytes 13107200 | tf_op jit(solution)/shard_map/stack | solution.py:50
  157.6 5.9 %pad_maximum_fusion = bf16[4,4,2,80,1280]{4,3,2,1,0:T(8,128)(2,1)} fusion(bf16[1,4,2,80,1280]{4,3,2,1,0:T(8,128)(2,1)} %bitcast.32, bf16[1,4,2,80,1280]{4,3,2,1,0:T(8,128)(2,1)S(1)} %bitcast.62, bf16[1,4,2,80,1280]{4,3,2,1,0:T(8,128)(2,1)} %bitcast.30, bf16[1,4,2,80,1280]{4,3,2,1,0:T(8,128)(2,1)} %bitcast.29), kind=kLoop, calls=%fused_computation.6 | loop fusion | flops 9830400 | bytes 13107200 | tf_op jit(solution)/shard_map/stack | solution.py:50
  168.1 6.5 %convolution_convert_fusion = bf16[512,1280]{1,0:T(8,128)(2,1)S(1)} fusion(bf16[512,2560]{0,1:T(8,128)(2,1)S(1)} %bitcast.72, bf16[2560,1280]{1,0:T(8,128)(2,1)} %bitcast.64), kind=kOutput, calls=%fused_computation.9 | convolution fusion | flops 3356098560 | bytes 10485760 | tf_op jit(solution)/shard_map/dot_general | solution.py:186
  179.9 6.5 %convolution_convert_fusion.1 = bf16[512,1280]{1,0:T(8,128)(2,1)S(1)} fusion(bf16[512,2560]{0,1:T(8,128)(2,1)S(1)} %bitcast.73, bf16[2560,1280]{1,0:T(8,128)(2,1)} %bitcast.63), kind=kOutput, calls=%fused_computation.10 | convolution fusion | flops 3356098560 | bytes 10485760 | tf_op jit(solution)/shard_map/dot_general | solution.py:186
  188.6 2.9 %conditional.1 = (bf16[1,256,5120]{2,1,0:T(8,128)(2,1)}) conditional(s32[]{:T(128)} %clamp.3, (bf16[256,1280]{1,0:T(8,128)(2,1)S(1)}, bf16[256,1280]{1,0:T(8,128)(2,1)S(1)}, bf16[256,1280]{1,0:T(8,128)(2,1)S(1)}, bf16[256,1280]{1,0:T(8,128)(2,1)}) %tuple.31, (bf16[256,1280]{1,0:T(8,128)(2,1)S(1)}, ...), branch_computations={%region_3.5_spmd, %region_4.6_spmd, %region_5.7_spmd, %region_6.8_... | conditional | flops 10485760 | bytes 5242888 | solution.py:200
  188.6 2.9 %maximum_bitcast_fusion.1 = bf16[1,256,5120]{2,1,0:T(8,128)(2,1)} fusion(bf16[256,1280]{1,0:T(8,128)(2,1)S(1)} %get-tuple-element.46, bf16[256,1280]{1,0:T(8,128)(2,1)} %get-tuple-element.45, bf16[256,1280]{1,0:T(8,128)(2,1)S(1)} %get-tuple-element.44, bf16[256,1280]{1,0:T(8,128)(2,1)S(1)} %get-tuple-element.43), kind=kLoop, calls=%fused_computation.3 | loop fusion | flops 10485760 | bytes 5242880 | tf_op jit(solution)/shard_map/broadcast_in_dim | solution.py:201
  (139 shorter events, 92.1 us)
Async XLA Ops:
  3.4 7.9 %collective-permute-start.5 = (bf16[80,1280]{1,0:T(8,128)(2,1)S(1)}, bf16[80,1280]{1,0:T(8,128)(2,1)S(1)}, u32[]{:S(2)}, u32[]{:S(2)}) collective-permute-start(bf16[80,1280]{1,0:T(8,128)(2,1)S(1)} %get-tuple-element.93), channel_id=1, source_target_pairs={{0,2},{2,0},{1,3},{3,1},{4,6},{6,4},{5,7},{7,5},{8,10},{10,8},{9,1... | collective-permute-start | bytes 614408 | tf_op jit(solution)/shard_map/ppermute | solution.py:107
  6.9 9.2 %collective-permute-start = (bf16[80,1280]{1,0:T(8,128)(2,1)S(1)}, bf16[80,1280]{1,0:T(8,128)(2,1)S(1)}, u32[]{:S(2)}, u32[]{:S(2)}) collective-permute-start(bf16[80,1280]{1,0:T(8,128)(2,1)S(1)} %get-tuple-element.93), channel_id=1, source_target_pairs={{0,16},{16,0},{1,17},{17,1},{2,18},{18,2},{3,19},{19,3},{4,20},{20... | collective-permute-start | bytes 614408 | tf_op jit(solution)/shard_map/ppermute | solution.py:26
  11.2 9.3 %collective-permute-start.6 = (bf16[80,1280]{1,0:T(8,128)(2,1)S(1)}, bf16[80,1280]{1,0:T(8,128)(2,1)S(1)}, u32[]{:S(2)}, u32[]{:S(2)}) collective-permute-start(bf16[80,1280]{1,0:T(8,128)(2,1)S(1)} %collective-permute-done.5), channel_id=1, source_target_pairs={{0,16},{16,0},{1,17},{17,1},{2,18},{18,2},{3,19},{19,3},{4,20},{20... | collective-permute-start | bytes 614408 | tf_op jit(solution)/shard_map/ppermute | solution.py:26
  17.1 9.8 %collective-permute-start.1 = (bf16[2,80,1280]{2,1,0:T(8,128)(2,1)}, bf16[2,80,1280]{2,1,0:T(8,128)(2,1)S(1)}, u32[]{:S(2)}, u32[]{:S(2)}) collective-permute-start(bf16[2,80,1280]{2,1,0:T(8,128)(2,1)} %get-tuple-element.116), channel_id=1, source_target_pairs={{0,4},{4,8},{8,12},{12,0},{1,5},{5,9},{9,13},{13,1},{2,6},{6,10},{... | collective-permute-start | bytes 1228808 | tf_op jit(solution)/shard_map/ppermute | solution.py:29
  18.4 9.5 %collective-permute-start.3 = (bf16[2,80,1280]{2,1,0:T(8,128)(2,1)}, bf16[2,80,1280]{2,1,0:T(8,128)(2,1)S(1)}, u32[]{:S(2)}, u32[]{:S(2)}) collective-permute-start(bf16[2,80,1280]{2,1,0:T(8,128)(2,1)} %get-tuple-element.116), channel_id=1, source_target_pairs={{0,12},{4,0},{8,4},{12,8},{1,13},{5,1},{9,5},{13,9},{2,14},{6,2},{... | collective-permute-start | bytes 1228808 | tf_op jit(solution)/shard_map/ppermute | solution.py:29
  21.5 18.1 %collective-permute-start.9 = (bf16[2,80,1280]{2,1,0:T(8,128)(2,1)}, bf16[2,80,1280]{2,1,0:T(8,128)(2,1)}, u32[]{:S(2)}, u32[]{:S(2)}) collective-permute-start(bf16[2,80,1280]{2,1,0:T(8,128)(2,1)} %get-tuple-element.114), channel_id=1, source_target_pairs={{0,96},{32,0},{64,32},{96,64},{1,97},{33,1},{65,33},{97,65},{2,98}... | collective-permute-start | bytes 1228808 | tf_op jit(solution)/shard_map/ppermute | solution.py:29
  25.2 15.3 %collective-permute-start.7 = (bf16[2,80,1280]{2,1,0:T(8,128)(2,1)}, bf16[2,80,1280]{2,1,0:T(8,128)(2,1)}, u32[]{:S(2)}, u32[]{:S(2)}) collective-permute-start(bf16[2,80,1280]{2,1,0:T(8,128)(2,1)} %get-tuple-element.114), channel_id=1, source_target_pairs={{0,32},{32,64},{64,96},{96,0},{1,33},{33,65},{65,97},{97,1},{2,34}... | collective-permute-start | bytes 1228808 | tf_op jit(solution)/shard_map/ppermute | solution.py:29
  27.6 17.7 %collective-permute-start.2 = (bf16[1,80,1280]{2,1,0:T(8,128)(2,1)}, bf16[1,80,1280]{2,1,0:T(8,128)(2,1)}, u32[]{:S(2)}, u32[]{:S(2)}) collective-permute-start(bf16[1,80,1280]{2,1,0:T(8,128)(2,1)} %slice.56), channel_id=1, source_target_pairs={{0,4},{4,8},{8,12},{12,0},{1,5},{5,9},{9,13},{13,1},{2,6},{6,10},{... | collective-permute-start | bytes 614408 | tf_op jit(solution)/shard_map/ppermute | solution.py:41
  28.6 16.8 %collective-permute-start.4 = (bf16[1,80,1280]{2,1,0:T(8,128)(2,1)}, bf16[1,80,1280]{2,1,0:T(8,128)(2,1)}, u32[]{:S(2)}, u32[]{:S(2)}) collective-permute-start(bf16[1,80,1280]{2,1,0:T(8,128)(2,1)} %slice.57), channel_id=1, source_target_pairs={{0,12},{4,0},{8,4},{12,8},{1,13},{5,1},{9,5},{13,9},{2,14},{6,2},{... | collective-permute-start | bytes 614408 | tf_op jit(solution)/shard_map/ppermute | solution.py:42
  32.2 28.1 %collective-permute-start.15 = (bf16[256,10,128]{0,2,1:T(8,128)(2,1)}, bf16[256,10,128]{0,2,1:T(8,128)(2,1)}, u32[]{:S(2)}, u32[]{:S(2)}) collective-permute-start(bf16[256,10,128]{0,2,1:T(8,128)(2,1)} %get-tuple-element.112), channel_id=1, source_target_pairs={{0,1},{1,0},{2,3},{3,2},{4,5},{5,4},{6,7},{7,6},{8,9},{9,8},{10,11... | collective-permute-start | bytes 1966088 | tf_op jit(solution)/shard_map/ppermute | solution.py:107
  39.6 20.7 %collective-permute-start.16 = (bf16[256,10,128]{0,2,1:T(8,128)(2,1)}, bf16[256,10,128]{0,2,1:T(8,128)(2,1)}, u32[]{:S(2)}, u32[]{:S(2)}) collective-permute-start(bf16[256,10,128]{0,2,1:T(8,128)(2,1)} %get-tuple-element.110), channel_id=1, source_target_pairs={{0,1},{1,0},{2,3},{3,2},{4,5},{5,4},{6,7},{7,6},{8,9},{9,8},{10,11... | collective-permute-start | bytes 1966088 | tf_op jit(solution)/shard_map/ppermute | solution.py:107
  40.5 7.8 %collective-permute-start.10 = (bf16[1,80,1280]{2,1,0:T(8,128)(2,1)S(1)}, bf16[1,80,1280]{2,1,0:T(8,128)(2,1)S(1)}, u32[]{:S(2)}, u32[]{:S(2)}) collective-permute-start(bf16[1,80,1280]{2,1,0:T(8,128)(2,1)S(1)} %slice.59), channel_id=1, source_target_pairs={{0,96},{32,0},{64,32},{96,64},{1,97},{33,1},{65,33},{97,65},{2,98}... | collective-permute-start | bytes 614408 | tf_op jit(solution)/shard_map/ppermute | solution.py:42
  56.0 10.2 %collective-permute-start.21 = (bf16[256,10,128]{0,2,1:T(8,128)(2,1)S(1)}, bf16[256,10,128]{0,2,1:T(8,128)(2,1)S(1)}, u32[]{:S(2)}, u32[]{:S(2)}) collective-permute-start(bf16[256,10,128]{0,2,1:T(8,128)(2,1)S(1)} %get-tuple-element.108), channel_id=1, source_target_pairs={{0,1},{1,0},{2,3},{3,2},{4,5},{5,4},{6,7},{7,6},{8,9},{9,8},{10,11... | collective-permute-start | bytes 1966088 | tf_op jit(solution)/shard_map/ppermute | solution.py:107
  57.6 39.0 %collective-permute-start.11 = (bf16[4,2,80,1280]{3,2,1,0:T(8,128)(2,1)}, bf16[4,2,80,1280]{3,2,1,0:T(8,128)(2,1)}, u32[]{:S(2)}, u32[]{:S(2)}) collective-permute-start(bf16[4,2,80,1280]{3,2,1,0:T(8,128)(2,1)} %pad_maximum_fusion.9), channel_id=1, source_target_pairs={{0,32},{32,64},{64,96},{96,0},{1,33},{33,65},{65,97},{97,1},{2,34}... | collective-permute-start | bytes 4915208 | tf_op jit(solution)/shard_map/ppermute | solution.py:29
  57.6 39.0 %collective-permute-start.12 = (bf16[4,2,80,1280]{3,2,1,0:T(8,128)(2,1)}, bf16[4,2,80,1280]{3,2,1,0:T(8,128)(2,1)}, u32[]{:S(2)}, u32[]{:S(2)}) collective-permute-start(bf16[4,2,80,1280]{3,2,1,0:T(8,128)(2,1)} %pad_maximum_fusion.9), channel_id=1, source_target_pairs={{0,96},{32,0},{64,32},{96,64},{1,97},{33,1},{65,33},{97,65},{2,98}... | collective-permute-start | bytes 4915208 | tf_op jit(solution)/shard_map/ppermute | solution.py:29
  60.3 38.3 %collective-permute-start.13 = (bf16[4,2,80,1280]{3,2,1,0:T(8,128)(2,1)}, bf16[4,2,80,1280]{3,2,1,0:T(8,128)(2,1)}, u32[]{:S(2)}, u32[]{:S(2)}) collective-permute-start(bf16[4,2,80,1280]{3,2,1,0:T(8,128)(2,1)} %pad_maximum_fusion.10), channel_id=1, source_target_pairs={{0,4},{4,8},{8,12},{12,0},{1,5},{5,9},{9,13},{13,1},{2,6},{6,10},{... | collective-permute-start | bytes 4915208 | tf_op jit(solution)/shard_map/ppermute | solution.py:29
  60.3 38.3 %collective-permute-start.14 = (bf16[4,2,80,1280]{3,2,1,0:T(8,128)(2,1)}, bf16[4,2,80,1280]{3,2,1,0:T(8,128)(2,1)}, u32[]{:S(2)}, u32[]{:S(2)}) collective-permute-start(bf16[4,2,80,1280]{3,2,1,0:T(8,128)(2,1)} %pad_maximum_fusion.10), channel_id=1, source_target_pairs={{0,12},{4,0},{8,4},{12,8},{1,13},{5,1},{9,5},{13,9},{2,14},{6,2},{... | collective-permute-start | bytes 4915208 | tf_op jit(solution)/shard_map/ppermute | solution.py:29
  98.6 35.4 %collective-permute-start.22 = (f32[10,256,128]{2,1,0:T(8,128)}, f32[10,256,128]{2,1,0:T(8,128)}, u32[]{:S(2)}, u32[]{:S(2)}) collective-permute-start(f32[10,256,128]{2,1,0:T(8,128)} %get-tuple-element.81), channel_id=1, source_target_pairs={{0,2},{1,3},{4,6},{5,7},{8,10},{9,11},{12,14},{13,15},{16,18},{17,... | collective-permute-start | bytes 3932168 | tf_op jit(solution)/shard_map/ppermute | solution.py:159
  105.5 22.5 %collective-permute-start.19 = (bf16[2,2,80,1280]{3,2,1,0:T(8,128)(2,1)}, bf16[2,2,80,1280]{3,2,1,0:T(8,128)(2,1)}, u32[]{:S(2)}, u32[]{:S(2)}) collective-permute-start(bf16[2,2,80,1280]{3,2,1,0:T(8,128)(2,1)} %slice.45), channel_id=1, source_target_pairs={{0,4},{4,8},{8,12},{12,0},{1,5},{5,9},{9,13},{13,1},{2,6},{6,10},{... | collective-permute-start | bytes 2457608 | tf_op jit(solution)/shard_map/ppermute | solution.py:41
  107.6 20.4 %collective-permute-start.20 = (bf16[2,2,80,1280]{3,2,1,0:T(8,128)(2,1)}, bf16[2,2,80,1280]{3,2,1,0:T(8,128)(2,1)}, u32[]{:S(2)}, u32[]{:S(2)}) collective-permute-start(bf16[2,2,80,1280]{3,2,1,0:T(8,128)(2,1)} %slice.46), channel_id=1, source_target_pairs={{0,12},{4,0},{8,4},{12,8},{1,13},{5,1},{9,5},{13,9},{2,14},{6,2},{... | collective-permute-start | bytes 2457608 | tf_op jit(solution)/shard_map/ppermute | solution.py:42
  112.4 18.9 %collective-permute-start.17 = (bf16[2,2,80,1280]{3,2,1,0:T(8,128)(2,1)}, bf16[2,2,80,1280]{3,2,1,0:T(8,128)(2,1)S(1)}, u32[]{:S(2)}, u32[]{:S(2)}) collective-permute-start(bf16[2,2,80,1280]{3,2,1,0:T(8,128)(2,1)} %slice.43), channel_id=1, source_target_pairs={{0,32},{32,64},{64,96},{96,0},{1,33},{33,65},{65,97},{97,1},{2,34}... | collective-permute-start | bytes 2457608 | tf_op jit(solution)/shard_map/ppermute | solution.py:41
  114.5 18.0 %collective-permute-start.18 = (bf16[2,2,80,1280]{3,2,1,0:T(8,128)(2,1)}, bf16[2,2,80,1280]{3,2,1,0:T(8,128)(2,1)}, u32[]{:S(2)}, u32[]{:S(2)}) collective-permute-start(bf16[2,2,80,1280]{3,2,1,0:T(8,128)(2,1)} %slice.44), channel_id=1, source_target_pairs={{0,96},{32,0},{64,32},{96,64},{1,97},{33,1},{65,33},{97,65},{2,98}... | collective-permute-start | bytes 2457608 | tf_op jit(solution)/shard_map/ppermute | solution.py:42
  151.5 12.0 %collective-permute-start.24 = (bf16[256,2560]{0,1:T(8,128)(2,1)}, bf16[256,2560]{0,1:T(8,128)(2,1)S(1)}, u32[]{:S(2)}, u32[]{:S(2)}) collective-permute-start(bf16[256,2560]{0,1:T(8,128)(2,1)} %bitcast.67), channel_id=1, source_target_pairs={{0,1},{1,0},{2,3},{3,2},{4,5},{5,4},{6,7},{7,6},{8,9},{9,8},{10,11... | collective-permute-start | bytes 3932168 | tf_op jit(solution)/shard_map/ppermute | solution.py:107
  175.5 11.4 %collective-permute-start.26 = (bf16[256,1280]{1,0:T(8,128)(2,1)}, bf16[256,1280]{1,0:T(8,128)(2,1)}, u32[]{:S(2)}, u32[]{:S(2)}) collective-permute-start(bf16[256,1280]{1,0:T(8,128)(2,1)} %get-tuple-element.101), channel_id=1, source_target_pairs={{0,1},{1,0},{2,3},{3,2},{4,5},{5,4},{6,7},{7,6},{8,9},{9,8},{10,11... | collective-permute-start | bytes 1966088 | tf_op jit(solution)/shard_map/ppermute | solution.py:107
  (27 other events, 216.7 us)

commit v10 on v9

--- a/solution.py
+++ b/solution.py
@@ -57,14 +57,20 @@
 STAGES = (("y", "z"), ("z", "y"))
 
 
+def ring_direct(x, axis, size):
+    shifted = [
+        lax.ppermute(x, axis, [(k, (k + shift) % size) for k in range(size)])
+        for shift in (1, 2, 3)
+    ]
+    return jnp.stack([x] + shifted)
+
+
 def gather_start(weights):
-    width = weights.shape[1] // 2
-    parts = []
-    for number, (first, _) in enumerate(STAGES):
-        part = weights[:, width * number : width * (number + 1)]
-        part = ring_gather(part, "xl", 2)
-        parts.append(ring_gather(part, first, 4))
-    return parts
+    near = swap(weights, "xl")
+    peer = swap(weights, "xh")
+    diagonal = lax.ppermute(weights, ("xl", "xh"), [(k, 3 - k) for k in range(4)])
+    halves = (jnp.stack([weights, near]), jnp.stack([peer, diagonal]))
+    return [ring_direct(part, first, 4) for part, (first, _) in zip(halves, STAGES)]
 
 
 def gather_finish(parts, sent):
@@ -136,8 +142,7 @@
     half = lax.axis_index("xh")
     core = lax.axis_index("c")
     heads_here = H // 2
-    both = jnp.concatenate([weights, swap(weights, "xh")], axis=1)
-    parts = gather_start(both)
+    parts = gather_start(weights)
     parts, query_heads = lax.optimization_barrier(
         (parts, queries[0].reshape(tokens_here, H, HEAD))
     )

time: 193 us -> 188 us (0.974)
  waiting for transfers between devices: 28.4 us -> 36.8 us
  starting transfers between devices: 44.2 us -> 38.3 us
  local copies, waits for them, and re-layouts: 46.5 us -> 42.4 us
  other arithmetic: 48.7 us -> 45.4 us
    ppermute x2 -> x7, waiting for transfers between devices: 3.92 us -> 15.6 us  [the longest x6 9.95 us: ring_direct(): lax.ppermute(x, axis, [(k, (k + shift) % size) for k in range(size)])]
    ppermute x2 -> x7, starting transfers between devices: 1.91 us -> 13.1 us  [the longest x6 12.2 us: ring_direct(): lax.ppermute(x, axis, [(k, (k + shift) % size) for k in range(size)])]
    ppermute x8 -> x4, starting transfers between devices: 11.8 us -> 4.14 us  [ring_send(): return (lax.ppermute(x, axis, forward), lax.ppermute(x, axis, backward))]
    another operation x8 -> x2, other arithmetic: 18.6 us -> 11.6 us  [ring_finish(): return jnp.stack((x,) + tuple(received))]
    ppermute x4 -> x2, starting transfers between devices: 11.6 us -> 4.99 us  [ring_far(): lax.ppermute(from_right[half:], axis, backward)]
    another operation x1 -> x5, other arithmetic: 4.43 us -> 9.35 us  [the longest x4 4.93 us: ring_direct(): return jnp.stack([x] + shifted)]
    ppermute x4 -> x2, waiting for transfers between devices: 5.72 us -> 1.38 us  [ring_far(): lax.ppermute(from_left[:half], axis, forward)]
    ppermute x8 -> x9, starting transfers between devices: 13.8 us -> 11.8 us  [swap(): return lax.ppermute(x, axis, [(0, 1), (1, 0)])]
  transfers between devices with their start and end apart: 27 -> 25, of which waited for: 12 -> 11; matrix products, arithmetic and copies ran while one was open for 43% -> 41% of each run, Pallas kernels for 0% -> 0%
where the time goes in v10:
time: 188 us; the launch traced here: 187 us
  other arithmetic  45.4 us (24%)
  local copies, waits for them, and re-layouts  42.4 us (23%)
  starting transfers between devices  38.3 us (20%)
  waiting for transfers between devices  36.8 us (20%)
  matrix products  23.3 us (12%)
    dot_general x2, matrix products, on_device(): jnp.dot(features, rows, preferred_element_type=jnp.float32)  13 us
    ppermute x4, waiting for transfers between devices, ring_send(): return (lax.ppermute(x, axis, forward), lax.ppermute(x, axis, backward))  12.3 us
    ppermute x6, starting transfers between devices, ring_direct(): lax.ppermute(x, axis, [(k, (k + shift) % size) for k in range(size)])  12.2 us
    max x4, local copies, waits for them, and re-layouts, featurize(): rectified = jnp.maximum(block.astype(jnp.float32), 0.0)  12.1 us
    ppermute x9, starting transfers between devices, swap(): return lax.ppermute(x, axis, [(0, 1), (1, 0)])  11.8 us
    another operation x2, other arithmetic, ring_finish(): return jnp.stack((x,) + tuple(received))  11.6 us
    ppermute x6, waiting for transfers between devices, ring_direct(): lax.ppermute(x, axis, [(k, (k + shift) % size) for k in range(size)])  9.95 us
    unnamed x41, local copies, waits for them, and re-layouts  8.06 us
  transfers between devices with their start and end apart: 25, of which 11 were waited for; matrix products, arithmetic and copies ran while one was open for 41% of the time, Pallas kernels for 0%

profile of v10, /device:TPU:1, one launch (start us, length us, event | category | flops | bytes accessed | tf_op | source)
XLA Modules:
  0.0 187.1 jit_solution(17508890148429006225)
XLA Ops:
  0.7 2.7 %fusion.33 = (bf16[80,1280]{1,0:T(8,128)(2,1)S(1)}, f32[80,1280]{1,0:T(8,128)}, f32[80,1280]{1,0:T(8,128)}, f32[80,1280]{1,0:T(8,128)}) fusion(f32[80,1280]{1,0:T(8,128)} %param.18, f32[80,1280]{1,0:T(8,128)} %param.19, f32[80,1280]{1,0:T(8,128)} %param.20, f32[80,1280]{1,0:T(8,128)} %param.21), kind=kLoop, calls=%fused_computation.114 | loop fusion | flops 1638400 | bytes 3072000 | tf_op jit(solution)/shard_map/convert_element_type | solution.py:139
  3.4 3.6 %collective-permute-start.4 = (bf16[80,1280]{1,0:T(8,128)(2,1)S(1)}, bf16[80,1280]{1,0:T(8,128)(2,1)S(1)}, u32[]{:S(2)}, u32[]{:S(2)}) collective-permute-start(bf16[80,1280]{1,0:T(8,128)(2,1)S(1)} %get-tuple-element.93), channel_id=1, source_target_pairs={{0,2},{2,0},{1,3},{3,1},{4,6},{6,4},{5,7},{7,5},{8,10},{10,8},{9,1... | collective-permute-start | bytes 614408 | tf_op jit(solution)/shard_map/ppermute | solution.py:113
  7.8 3.5 %collective-permute-done.4 = bf16[80,1280]{1,0:T(8,128)(2,1)S(1)} collective-permute-done((bf16[80,1280]{1,0:T(8,128)(2,1)S(1)}, bf16[80,1280]{1,0:T(8,128)(2,1)S(1)}, u32[]{:S(2)}, u32[]{:S(2)}) %collective-permute-start.4) | collective-permute-done | bytes 204832 | tf_op jit(solution)/shard_map/ppermute | solution.py:113
  11.2 5.6 %collective-permute-done.5 = bf16[80,1280]{1,0:T(8,128)(2,1)S(1)} collective-permute-done((bf16[80,1280]{1,0:T(8,128)(2,1)S(1)}, bf16[80,1280]{1,0:T(8,128)(2,1)S(1)}, u32[]{:S(2)}, u32[]{:S(2)}) %collective-permute-start.5) | collective-permute-done | bytes 204832 | tf_op jit(solution)/shard_map/ppermute | solution.py:71
  20.3 3.4 %collective-permute-start.7 = (bf16[2,80,1280]{2,1,0:T(8,128)(2,1)}, bf16[2,80,1280]{2,1,0:T(8,128)(2,1)}, u32[]{:S(2)}, u32[]{:S(2)}) collective-permute-start(bf16[2,80,1280]{2,1,0:T(8,128)(2,1)} %get-tuple-element.114), channel_id=1, source_target_pairs={{0,64},{32,96},{64,0},{96,32},{1,65},{33,97},{65,1},{97,33},{2,66}... | collective-permute-start | bytes 1228808 | tf_op jit(solution)/shard_map/ppermute | solution.py:62
  35.1 6.1 %collective-permute-done.7 = bf16[2,80,1280]{2,1,0:T(8,128)(2,1)} collective-permute-done((bf16[2,80,1280]{2,1,0:T(8,128)(2,1)}, bf16[2,80,1280]{2,1,0:T(8,128)(2,1)}, u32[]{:S(2)}, u32[]{:S(2)}) %collective-permute-start.7) | collective-permute-done | bytes 409632 | tf_op jit(solution)/shard_map/ppermute | solution.py:62
  45.1 3.7 %collective-permute-done.2 = bf16[2,80,1280]{2,1,0:T(8,128)(2,1)S(1)} collective-permute-done((bf16[2,80,1280]{2,1,0:T(8,128)(2,1)S(1)}, bf16[2,80,1280]{2,1,0:T(8,128)(2,1)S(1)}, u32[]{:S(2)}, u32[]{:S(2)}) %collective-permute-start.2) | collective-permute-done | bytes 409632 | tf_op jit(solution)/shard_map/ppermute | solution.py:62
  59.5 3.9 %convert_maximum_fusion = (f32[512,10,128]{0,2,1:T(8,128)S(1)}, f32[512,10,128]{0,2,1:T(8,128)}) fusion(bf16[256,10,128]{0,2,1:T(8,128)(2,1)} %collective-permute-done.19, bf16[256,10,128]{0,2,1:T(8,128)(2,1)} %get-tuple-element.107, pred[]{:T(512)S(6)} %eq.17, bf16[256,10,128]{0,2,1:T(8,128)(2,1)S(1)} %copy-done.12, ...), kind=kLoop, calls=%fused_computation.22 | loop fusion | flops 14417920 | bytes 7864321 | tf_op jit(solution)/shard_map/max | solution.py:97
  63.5 3.3 %copy.15 = f32[512,10,128]{2,0,1:T(8,128)} copy(f32[512,10,128]{0,2,1:T(8,128)} %get-tuple-element.124) | data formatting | bytes 5242880 | tf_op jit(solution)/shard_map/max | solution.py:97
  66.8 3.2 %copy.16 = f32[4,128,10,128]{1,3,2,0:T(8,128)} copy(f32[4,128,10,128]{3,1,0,2:T(8,128)} %bitcast.57) | data formatting | bytes 5242880 | tf_op jit(solution)/shard_map/max | solution.py:97
  72.1 3.4 %copy.22 = f32[4,128,10,128]{1,3,2,0:T(8,128)} copy(f32[4,128,10,128]{3,1,0,2:T(8,128)} %bitcast.58) | data formatting | bytes 5242880 | tf_op jit(solution)/shard_map/max | solution.py:97
  75.5 4.4 %multiply_convert_fusion.4 = (bf16[4,128,10,128]{1,3,2,0:T(8,128)(2,1)S(1)}, bf16[4,128,10,128]{1,3,2,0:T(8,128)(2,1)S(1)}, bf16[4,128,10,128]{1,3,2,0:T(8,128)(2,1)}, bf16[4,128,10,128]{1,3,2,0:T(8,128)(2,1)}) fusion(f32[4,128,10,128]{1,3,2,0:T(8,128)S(1)} %copy-done.3, f32[4,128]{1,0:T(4,128)S(1)} %get-tuple-element.126, ...), kind=kLoop, calls=%fused_computation.24 | loop fusion | flops 5242880 | bytes 10489856 | tf_op jit(solution)/shard_map/convert.2
  81.9 11.3 %collective-permute-done.10 = bf16[4,2,80,1280]{3,2,1,0:T(8,128)(2,1)} collective-permute-done((bf16[4,2,80,1280]{3,2,1,0:T(8,128)(2,1)}, bf16[4,2,80,1280]{3,2,1,0:T(8,128)(2,1)}, u32[]{:S(2)}, u32[]{:S(2)}) %collective-permute-start.10) | collective-permute-done | bytes 1638432 | tf_op jit(solution)/shard_map/ppermute | solution.py:29
  94.2 4.0 %collective-permute-start.20 = (f32[10,256,128]{2,1,0:T(8,128)}, f32[10,256,128]{2,1,0:T(8,128)}, u32[]{:S(2)}, u32[]{:S(2)}) collective-permute-start(f32[10,256,128]{2,1,0:T(8,128)} %get-tuple-element.81), channel_id=1, source_target_pairs={{0,2},{1,3},{4,6},{5,7},{8,10},{9,11},{12,14},{13,15},{16,18},{17,... | collective-permute-start | bytes 3932168 | tf_op jit(solution)/shard_map/ppermute | solution.py:164
  117.9 4.9 %fusion.3 = f32[4,10,128,128]{2,3,1,0:T(8,128)} fusion(bf16[4,128,10,128]{1,3,2,0:T(8,128)(2,1)S(1)} %copy-done.4, bf16[4,128,10,128]{1,3,2,0:T(8,128)(2,1)S(1)} %copy-done.6, bf16[4,128,10,128]{1,3,2,0:T(8,128)(2,1)} %copy-done.9, bf16[4,128,10,128]{1,3,2,0:T(8,128)(2,1)} %copy-done.8, pred[128,128]{1,0:T(8,128)(4,1)S(1)} %iota_compare_fusion, ...), kind=kOutput, calls=%fused_computation.33 | convolution fusion | flops 515112960 | bytes 9191424 | tf_op jit(solution)/shard_map/chij,cjhe->cihe/dot_general | solution.py:170
  128.7 3.5 %add_bitcast_fusion = f32[4,128,10,128]{3,1,2,0:T(8,128)S(1)} fusion(f32[4,10,128,128]{2,3,1,0:T(8,128)} %fusion.3, f32[3,10,256,128]{3,2,1,0:T(8,128)S(1)} %slice-done, f32[10,256,128]{2,1,0:T(8,128)} %collective-permute-done.20, bf16[4,128,10,128]{1,3,2,0:T(8,128)(2,1)S(1)} %copy-done.5, bf16[4,128,10,128]{1,3,2,0:T(8,128)(2,1)S(1)} %copy-done.7), kind=kOutput, calls=%fused_computation.17 | convolution fusion | flops 344064000 | bytes 13107200 | tf_op jit(solution)/shard_map/cihf,chfe->cihe/dot_general | solution.py:176
  135.2 3.7 %collective-permute-start.21 = (bf16[256,10,128]{2,0,1:T(8,128)(2,1)}, bf16[256,10,128]{2,0,1:T(8,128)(2,1)}, u32[]{:S(2)}, u32[]{:S(2)}) collective-permute-start(bf16[256,10,128]{2,0,1:T(8,128)(2,1)} %get-tuple-element.106), channel_id=1, source_target_pairs={{0,1},{1,0},{2,3},{3,2},{4,5},{5,4},{6,7},{7,6},{8,9},{9,8},{10,11... | collective-permute-start | bytes 1966088 | tf_op jit(solution)/shard_map/ppermute | solution.py:113
  141.0 2.9 %maximum_select_fusion.3 = bf16[256,20,128]{2,0,1:T(8,128)(2,1)} fusion(bf16[256,10,128]{2,0,1:T(8,128)(2,1)} %collective-permute-done.21, bf16[256,10,128]{2,0,1:T(8,128)(2,1)} %get-tuple-element.105, pred[]{:T(512)S(6)} %eq.17), kind=kLoop, calls=%fused_computation.37 | loop fusion | flops 1966080 | bytes 2621441 | tf_op jit(solution)/shard_map/jit(_where)/select_n | solution.py:121
  146.8 5.7 %pad_maximum_fusion.1 = bf16[4,4,2,80,1280]{4,3,2,1,0:T(8,128)(2,1)} fusion(bf16[1,4,2,80,1280]{4,3,2,1,0:T(8,128)(2,1)} %bitcast.39, bf16[1,4,2,80,1280]{4,3,2,1,0:T(8,128)(2,1)S(1)} %bitcast.59, bf16[1,4,2,80,1280]{4,3,2,1,0:T(8,128)(2,1)} %bitcast.37, bf16[1,4,2,80,1280]{4,3,2,1,0:T(8,128)(2,1)} %bitcast.36), kind=kLoop, calls=%fused_computation.7 | loop fusion | flops 9830400 | bytes 13107200 | tf_op jit(solution)/shard_map/stack | solution.py:50
  152.5 5.9 %pad_maximum_fusion = bf16[4,4,2,80,1280]{4,3,2,1,0:T(8,128)(2,1)} fusion(bf16[1,4,2,80,1280]{4,3,2,1,0:T(8,128)(2,1)} %bitcast.32, bf16[1,4,2,80,1280]{4,3,2,1,0:T(8,128)(2,1)S(1)} %bitcast.60, bf16[1,4,2,80,1280]{4,3,2,1,0:T(8,128)(2,1)} %bitcast.30, bf16[1,4,2,80,1280]{4,3,2,1,0:T(8,128)(2,1)} %bitcast.29), kind=kLoop, calls=%fused_computation.6 | loop fusion | flops 9830400 | bytes 13107200 | tf_op jit(solution)/shard_map/stack | solution.py:50
  162.9 6.5 %convolution_convert_fusion = bf16[512,1280]{1,0:T(8,128)(2,1)S(1)} fusion(bf16[512,2560]{0,1:T(8,128)(2,1)S(1)} %bitcast.70, bf16[2560,1280]{1,0:T(8,128)(2,1)} %bitcast.62), kind=kOutput, calls=%fused_computation.9 | convolution fusion | flops 3356098560 | bytes 10485760 | tf_op jit(solution)/shard_map/dot_general | solution.py:191
  174.7 6.5 %convolution_convert_fusion.1 = bf16[512,1280]{1,0:T(8,128)(2,1)S(1)} fusion(bf16[512,2560]{0,1:T(8,128)(2,1)S(1)} %bitcast.71, bf16[2560,1280]{1,0:T(8,128)(2,1)} %bitcast.61), kind=kOutput, calls=%fused_computation.10 | convolution fusion | flops 3356098560 | bytes 10485760 | tf_op jit(solution)/shard_map/dot_general | solution.py:191
  183.5 2.9 %conditional.1 = (bf16[1,256,5120]{2,1,0:T(8,128)(2,1)}) conditional(s32[]{:T(128)} %clamp.3, (bf16[256,1280]{1,0:T(8,128)(2,1)S(1)}, bf16[256,1280]{1,0:T(8,128)(2,1)S(1)}, bf16[256,1280]{1,0:T(8,128)(2,1)S(1)}, bf16[256,1280]{1,0:T(8,128)(2,1)}) %tuple.31, (bf16[256,1280]{1,0:T(8,128)(2,1)S(1)}, ...), branch_computations={%region_3.5_spmd, %region_4.6_spmd, %region_5.7_spmd, %region_6.8_... | conditional | flops 10485760 | bytes 5242888 | solution.py:205
  183.5 2.9 %maximum_bitcast_fusion.1 = bf16[1,256,5120]{2,1,0:T(8,128)(2,1)} fusion(bf16[256,1280]{1,0:T(8,128)(2,1)S(1)} %get-tuple-element.46, bf16[256,1280]{1,0:T(8,128)(2,1)} %get-tuple-element.45, bf16[256,1280]{1,0:T(8,128)(2,1)S(1)} %get-tuple-element.44, bf16[256,1280]{1,0:T(8,128)(2,1)S(1)} %get-tuple-element.43), kind=kLoop, calls=%fused_computation.3 | loop fusion | flops 10485760 | bytes 5242880 | tf_op jit(solution)/shard_map/broadcast_in_dim | solution.py:206
  (121 shorter events, 81.8 us)
Async XLA Ops:
  3.4 7.9 %collective-permute-start.4 = (bf16[80,1280]{1,0:T(8,128)(2,1)S(1)}, bf16[80,1280]{1,0:T(8,128)(2,1)S(1)}, u32[]{:S(2)}, u32[]{:S(2)}) collective-permute-start(bf16[80,1280]{1,0:T(8,128)(2,1)S(1)} %get-tuple-element.93), channel_id=1, source_target_pairs={{0,2},{2,0},{1,3},{3,1},{4,6},{6,4},{5,7},{7,5},{8,10},{10,8},{9,1... | collective-permute-start | bytes 614408 | tf_op jit(solution)/shard_map/ppermute | solution.py:113
  6.9 9.9 %collective-permute-start.5 = (bf16[80,1280]{1,0:T(8,128)(2,1)S(1)}, bf16[80,1280]{1,0:T(8,128)(2,1)S(1)}, u32[]{:S(2)}, u32[]{:S(2)}) collective-permute-start(bf16[80,1280]{1,0:T(8,128)(2,1)S(1)} %get-tuple-element.93), channel_id=1, source_target_pairs={{0,18},{2,16},{16,2},{18,0},{1,19},{3,17},{17,3},{19,1},{4,22},{6,... | collective-permute-start | bytes 614408 | tf_op jit(solution)/shard_map/ppermute | solution.py:71
  7.8 20.0 %collective-permute-start = (bf16[80,1280]{1,0:T(8,128)(2,1)S(1)}, bf16[80,1280]{1,0:T(8,128)(2,1)S(1)}, u32[]{:S(2)}, u32[]{:S(2)}) collective-permute-start(bf16[80,1280]{1,0:T(8,128)(2,1)S(1)} %get-tuple-element.93), channel_id=1, source_target_pairs={{0,16},{16,0},{1,17},{17,1},{2,18},{18,2},{3,19},{19,3},{4,20},{20... | collective-permute-start | bytes 614408 | tf_op jit(solution)/shard_map/ppermute | solution.py:113
  17.8 14.0 %collective-permute-start.6 = (bf16[2,80,1280]{2,1,0:T(8,128)(2,1)}, bf16[2,80,1280]{2,1,0:T(8,128)(2,1)S(1)}, u32[]{:S(2)}, u32[]{:S(2)}) collective-permute-start(bf16[2,80,1280]{2,1,0:T(8,128)(2,1)} %get-tuple-element.114), channel_id=1, source_target_pairs={{0,32},{32,64},{64,96},{96,0},{1,33},{33,65},{65,97},{97,1},{2,34}... | collective-permute-start | bytes 1228808 | tf_op jit(solution)/shard_map/ppermute | solution.py:62
  20.3 20.8 %collective-permute-start.7 = (bf16[2,80,1280]{2,1,0:T(8,128)(2,1)}, bf16[2,80,1280]{2,1,0:T(8,128)(2,1)}, u32[]{:S(2)}, u32[]{:S(2)}) collective-permute-start(bf16[2,80,1280]{2,1,0:T(8,128)(2,1)} %get-tuple-element.114), channel_id=1, source_target_pairs={{0,64},{32,96},{64,0},{96,32},{1,65},{33,97},{65,1},{97,33},{2,66}... | collective-permute-start | bytes 1228808 | tf_op jit(solution)/shard_map/ppermute | solution.py:62
  23.7 18.8 %collective-permute-start.8 = (bf16[2,80,1280]{2,1,0:T(8,128)(2,1)}, bf16[2,80,1280]{2,1,0:T(8,128)(2,1)}, u32[]{:S(2)}, u32[]{:S(2)}) collective-permute-start(bf16[2,80,1280]{2,1,0:T(8,128)(2,1)} %get-tuple-element.114), channel_id=1, source_target_pairs={{0,96},{32,0},{64,32},{96,64},{1,97},{33,1},{65,33},{97,65},{2,98}... | collective-permute-start | bytes 1228808 | tf_op jit(solution)/shard_map/ppermute | solution.py:62
  27.9 17.3 %collective-permute-start.1 = (bf16[2,80,1280]{2,1,0:T(8,128)(2,1)S(1)}, bf16[2,80,1280]{2,1,0:T(8,128)(2,1)S(1)}, u32[]{:S(2)}, u32[]{:S(2)}) collective-permute-start(bf16[2,80,1280]{2,1,0:T(8,128)(2,1)S(1)} %get-tuple-element.116), channel_id=1, source_target_pairs={{0,4},{4,8},{8,12},{12,0},{1,5},{5,9},{9,13},{13,1},{2,6},{6,10},{... | collective-permute-start | bytes 1228808 | tf_op jit(solution)/shard_map/ppermute | solution.py:62
  29.2 19.6 %collective-permute-start.2 = (bf16[2,80,1280]{2,1,0:T(8,128)(2,1)S(1)}, bf16[2,80,1280]{2,1,0:T(8,128)(2,1)S(1)}, u32[]{:S(2)}, u32[]{:S(2)}) collective-permute-start(bf16[2,80,1280]{2,1,0:T(8,128)(2,1)S(1)} %get-tuple-element.116), channel_id=1, source_target_pairs={{0,8},{4,12},{8,0},{12,4},{1,9},{5,13},{9,1},{13,5},{2,10},{6,14},... | collective-permute-start | bytes 1228808 | tf_op jit(solution)/shard_map/ppermute | solution.py:62
  31.9 17.2 %collective-permute-start.3 = (bf16[2,80,1280]{2,1,0:T(8,128)(2,1)S(1)}, bf16[2,80,1280]{2,1,0:T(8,128)(2,1)S(1)}, u32[]{:S(2)}, u32[]{:S(2)}) collective-permute-start(bf16[2,80,1280]{2,1,0:T(8,128)(2,1)S(1)} %get-tuple-element.116), channel_id=1, source_target_pairs={{0,12},{4,0},{8,4},{12,8},{1,13},{5,1},{9,5},{13,9},{2,14},{6,2},{... | collective-permute-start | bytes 1228808 | tf_op jit(solution)/shard_map/ppermute | solution.py:62
  41.1 14.9 %collective-permute-start.13 = (bf16[256,10,128]{0,2,1:T(8,128)(2,1)}, bf16[256,10,128]{0,2,1:T(8,128)(2,1)}, u32[]{:S(2)}, u32[]{:S(2)}) collective-permute-start(bf16[256,10,128]{0,2,1:T(8,128)(2,1)} %get-tuple-element.112), channel_id=1, source_target_pairs={{0,1},{1,0},{2,3},{3,2},{4,5},{5,4},{6,7},{7,6},{8,9},{9,8},{10,11... | collective-permute-start | bytes 1966088 | tf_op jit(solution)/shard_map/ppermute | solution.py:113
  42.5 13.6 %collective-permute-start.14 = (bf16[256,10,128]{0,2,1:T(8,128)(2,1)}, bf16[256,10,128]{0,2,1:T(8,128)(2,1)S(1)}, u32[]{:S(2)}, u32[]{:S(2)}) collective-permute-start(bf16[256,10,128]{0,2,1:T(8,128)(2,1)} %get-tuple-element.110), channel_id=1, source_target_pairs={{0,1},{1,0},{2,3},{3,2},{4,5},{5,4},{6,7},{7,6},{8,9},{9,8},{10,11... | collective-permute-start | bytes 1966088 | tf_op jit(solution)/shard_map/ppermute | solution.py:113
  51.4 8.1 %collective-permute-start.19 = (bf16[256,10,128]{0,2,1:T(8,128)(2,1)S(1)}, bf16[256,10,128]{0,2,1:T(8,128)(2,1)}, u32[]{:S(2)}, u32[]{:S(2)}) collective-permute-start(bf16[256,10,128]{0,2,1:T(8,128)(2,1)S(1)} %get-tuple-element.108), channel_id=1, source_target_pairs={{0,1},{1,0},{2,3},{3,2},{4,5},{5,4},{6,7},{7,6},{8,9},{9,8},{10,11... | collective-permute-start | bytes 1966088 | tf_op jit(solution)/shard_map/ppermute | solution.py:113
  53.4 39.8 %collective-permute-start.11 = (bf16[4,2,80,1280]{3,2,1,0:T(8,128)(2,1)}, bf16[4,2,80,1280]{3,2,1,0:T(8,128)(2,1)}, u32[]{:S(2)}, u32[]{:S(2)}) collective-permute-start(bf16[4,2,80,1280]{3,2,1,0:T(8,128)(2,1)} %pad_maximum_fusion.10), channel_id=1, source_target_pairs={{0,4},{4,8},{8,12},{12,0},{1,5},{5,9},{9,13},{13,1},{2,6},{6,10},{... | collective-permute-start | bytes 4915208 | tf_op jit(solution)/shard_map/ppermute | solution.py:29
  55.0 38.2 %collective-permute-start.12 = (bf16[4,2,80,1280]{3,2,1,0:T(8,128)(2,1)}, bf16[4,2,80,1280]{3,2,1,0:T(8,128)(2,1)}, u32[]{:S(2)}, u32[]{:S(2)}) collective-permute-start(bf16[4,2,80,1280]{3,2,1,0:T(8,128)(2,1)} %pad_maximum_fusion.10), channel_id=1, source_target_pairs={{0,12},{4,0},{8,4},{12,8},{1,13},{5,1},{9,5},{13,9},{2,14},{6,2},{... | collective-permute-start | bytes 4915208 | tf_op jit(solution)/shard_map/ppermute | solution.py:29
  56.1 37.1 %collective-permute-start.10 = (bf16[4,2,80,1280]{3,2,1,0:T(8,128)(2,1)}, bf16[4,2,80,1280]{3,2,1,0:T(8,128)(2,1)}, u32[]{:S(2)}, u32[]{:S(2)}) collective-permute-start(bf16[4,2,80,1280]{3,2,1,0:T(8,128)(2,1)} %pad_maximum_fusion.9), channel_id=1, source_target_pairs={{0,96},{32,0},{64,32},{96,64},{1,97},{33,1},{65,33},{97,65},{2,98}... | collective-permute-start | bytes 4915208 | tf_op jit(solution)/shard_map/ppermute | solution.py:29
  56.1 38.2 %collective-permute-start.9 = (bf16[4,2,80,1280]{3,2,1,0:T(8,128)(2,1)}, bf16[4,2,80,1280]{3,2,1,0:T(8,128)(2,1)}, u32[]{:S(2)}, u32[]{:S(2)}) collective-permute-start(bf16[4,2,80,1280]{3,2,1,0:T(8,128)(2,1)} %pad_maximum_fusion.9), channel_id=1, source_target_pairs={{0,32},{32,64},{64,96},{96,0},{1,33},{33,65},{65,97},{97,1},{2,34}... | collective-permute-start | bytes 4915208 | tf_op jit(solution)/shard_map/ppermute | solution.py:29
  94.2 34.4 %collective-permute-start.20 = (f32[10,256,128]{2,1,0:T(8,128)}, f32[10,256,128]{2,1,0:T(8,128)}, u32[]{:S(2)}, u32[]{:S(2)}) collective-permute-start(f32[10,256,128]{2,1,0:T(8,128)} %get-tuple-element.81), channel_id=1, source_target_pairs={{0,2},{1,3},{4,6},{5,7},{8,10},{9,11},{12,14},{13,15},{16,18},{17,... | collective-permute-start | bytes 3932168 | tf_op jit(solution)/shard_map/ppermute | solution.py:164
  100.3 22.5 %collective-permute-start.17 = (bf16[2,2,80,1280]{3,2,1,0:T(8,128)(2,1)}, bf16[2,2,80,1280]{3,2,1,0:T(8,128)(2,1)}, u32[]{:S(2)}, u32[]{:S(2)}) collective-permute-start(bf16[2,2,80,1280]{3,2,1,0:T(8,128)(2,1)} %slice.29), channel_id=1, source_target_pairs={{0,4},{4,8},{8,12},{12,0},{1,5},{5,9},{9,13},{13,1},{2,6},{6,10},{... | collective-permute-start | bytes 2457608 | tf_op jit(solution)/shard_map/ppermute | solution.py:41
  102.7 20.1 %collective-permute-start.18 = (bf16[2,2,80,1280]{3,2,1,0:T(8,128)(2,1)}, bf16[2,2,80,1280]{3,2,1,0:T(8,128)(2,1)}, u32[]{:S(2)}, u32[]{:S(2)}) collective-permute-start(bf16[2,2,80,1280]{3,2,1,0:T(8,128)(2,1)} %slice.30), channel_id=1, source_target_pairs={{0,12},{4,0},{8,4},{12,8},{1,13},{5,1},{9,5},{13,9},{2,14},{6,2},{... | collective-permute-start | bytes 2457608 | tf_op jit(solution)/shard_map/ppermute | solution.py:42
  107.2 18.7 %collective-permute-start.15 = (bf16[2,2,80,1280]{3,2,1,0:T(8,128)(2,1)}, bf16[2,2,80,1280]{3,2,1,0:T(8,128)(2,1)S(1)}, u32[]{:S(2)}, u32[]{:S(2)}) collective-permute-start(bf16[2,2,80,1280]{3,2,1,0:T(8,128)(2,1)} %slice.27), channel_id=1, source_target_pairs={{0,32},{32,64},{64,96},{96,0},{1,33},{33,65},{65,97},{97,1},{2,34}... | collective-permute-start | bytes 2457608 | tf_op jit(solution)/shard_map/ppermute | solution.py:41
  109.4 17.6 %collective-permute-start.16 = (bf16[2,2,80,1280]{3,2,1,0:T(8,128)(2,1)}, bf16[2,2,80,1280]{3,2,1,0:T(8,128)(2,1)}, u32[]{:S(2)}, u32[]{:S(2)}) collective-permute-start(bf16[2,2,80,1280]{3,2,1,0:T(8,128)(2,1)} %slice.28), channel_id=1, source_target_pairs={{0,96},{32,0},{64,32},{96,64},{1,97},{33,1},{65,33},{97,65},{2,98}... | collective-permute-start | bytes 2457608 | tf_op jit(solution)/shard_map/ppermute | solution.py:42
  135.2 5.8 %collective-permute-start.21 = (bf16[256,10,128]{2,0,1:T(8,128)(2,1)}, bf16[256,10,128]{2,0,1:T(8,128)(2,1)}, u32[]{:S(2)}, u32[]{:S(2)}) collective-permute-start(bf16[256,10,128]{2,0,1:T(8,128)(2,1)} %get-tuple-element.106), channel_id=1, source_target_pairs={{0,1},{1,0},{2,3},{3,2},{4,5},{5,4},{6,7},{7,6},{8,9},{9,8},{10,11... | collective-permute-start | bytes 1966088 | tf_op jit(solution)/shard_map/ppermute | solution.py:113
  146.4 11.9 %collective-permute-start.22 = (bf16[256,2560]{0,1:T(8,128)(2,1)}, bf16[256,2560]{0,1:T(8,128)(2,1)S(1)}, u32[]{:S(2)}, u32[]{:S(2)}) collective-permute-start(bf16[256,2560]{0,1:T(8,128)(2,1)} %bitcast.65), channel_id=1, source_target_pairs={{0,1},{1,0},{2,3},{3,2},{4,5},{5,4},{6,7},{7,6},{8,9},{9,8},{10,11... | collective-permute-start | bytes 3932168 | tf_op jit(solution)/shard_map/ppermute | solution.py:113
  170.4 11.4 %collective-permute-start.24 = (bf16[256,1280]{1,0:T(8,128)(2,1)}, bf16[256,1280]{1,0:T(8,128)(2,1)}, u32[]{:S(2)}, u32[]{:S(2)}) collective-permute-start(bf16[256,1280]{1,0:T(8,128)(2,1)} %get-tuple-element.101), channel_id=1, source_target_pairs={{0,1},{1,0},{2,3},{3,2},{4,5},{5,4},{6,7},{7,6},{8,9},{9,8},{10,11... | collective-permute-start | bytes 1966088 | tf_op jit(solution)/shard_map/ppermute | solution.py:113
  (21 other events, 156.3 us)

commit v11 on v10

--- a/solution.py
+++ b/solution.py
@@ -146,14 +146,15 @@
     parts, query_heads = lax.optimization_barrier(
         (parts, queries[0].reshape(tokens_here, H, HEAD))
     )
-    query_group = pair_exchange(query_heads, core, 1, 0)
+    local_offset = (half * 2 + core) * tokens_here
+    query_group = pair_exchange(featurize(query_heads, local_offset, seq_length), core, 1, 0)
     sent = [ring_send(part, second, 4) for part, (_, second) in zip(parts, STAGES)]
-    key_group = pair_exchange(keys_in[0].reshape(tokens_here, H, HEAD), core, 1, 0)
+    key_heads = keys_in[0].reshape(tokens_here, H, HEAD)
+    key_group = pair_exchange(featurize(key_heads, local_offset, seq_length), core, 1, 0)
     value_group = pair_exchange(values_in[0].reshape(tokens_here, H, HEAD), core, 1, 0)
     span = query_group.shape[0]
-    offset = half * span
-    query_blocks = to_blocks(featurize(query_group, offset, seq_length))
-    key_blocks = to_blocks(featurize(key_group, offset, seq_length))
+    query_blocks = to_blocks(query_group)
+    key_blocks = to_blocks(key_group)
     value_blocks = to_blocks(value_group)
     states = jnp.einsum(
         "cjhf,cjhe->chfe", key_blocks, value_blocks, preferred_element_type=jnp.float32
@@ -186,7 +187,7 @@
     by_block = tokens.reshape(tokens.shape[0], 32, -1)
     wide = []
     for rows, source in gather_finish(parts, sent):
-        features = jnp.take(by_block, source, axis=1).reshape(tokens.shape)
+        features = jnp.take(by_block, source, axis=1, mode="clip").reshape(tokens.shape)
         wide.append(
             jnp.dot(features, rows, preferred_element_type=jnp.float32).astype(jnp.bfloat16)
         )

time: 188 us -> 205 us (1.090)
  waiting for transfers between devices: 36.8 us -> 53.3 us
  local copies, waits for them, and re-layouts: 42.4 us -> 34.2 us
  other arithmetic: 45.4 us -> 51.8 us
  matrix products: 23.3 us -> 26.3 us
    max x4 -> x0, local copies, waits for them, and re-layouts: 12.1 us -> none  [featurize(): rectified = jnp.maximum(block.astype(jnp.float32), 0.0)]
    ppermute x4, waiting for transfers between devices: 12.3 us -> 21.7 us  [ring_send(): return (lax.ppermute(x, axis, forward), lax.ppermute(x, axis, backward))]
    select_n x2 -> x3, other arithmetic: 3.32 us -> 11.1 us  [pair_exchange(): jnp.where(core == 0, jnp.concatenate([mine, received], axis=join_axis), j...]
    select_n x2 -> x4, local copies, waits for them, and re-layouts: 3.92 us -> 11.2 us  [pair_exchange(): jnp.where(core == 0, jnp.concatenate([mine, received], axis=join_axis), j...]
    ppermute x2, waiting for transfers between devices: 1.38 us -> 8.03 us  [ring_far(): lax.ppermute(from_left[:half], axis, forward)]
    select_n x2 -> x0, other arithmetic: 4.07 us -> none  [on_device(): features = jnp.take(by_block, source, axis=1).reshape(tokens.shape)]
    concatenate x0 -> x2, other arithmetic: none -> 3.5 us  [featurize(): return jnp.concatenate([cosine, sine], axis=2).astype(jnp.bfloat16)]
    another operation x4, other arithmetic: 4.93 us -> 8 us  [ring_direct(): return jnp.stack([x] + shifted)]
  transfers between devices with their start and end apart: 25 -> 25, of which waited for: 11 -> 15; matrix products, arithmetic and copies ran while one was open for 41% -> 37% of each run, Pallas kernels for 0% -> 0%
where the time goes in v11:
time: 205 us; the launch traced here: 204 us
  waiting for transfers between devices  53.3 us (26%)
  other arithmetic  51.8 us (25%)
  starting transfers between devices  37.6 us (18%)
  local copies, waits for them, and re-layouts  34.2 us (17%)
  matrix products  26.3 us (13%)
    ppermute x4, waiting for transfers between devices, ring_send(): return (lax.ppermute(x, axis, forward), lax.ppermute(x, axis, backward))  21.7 us
    dot_general x2, matrix products, on_device(): jnp.dot(features, rows, preferred_element_type=jnp.float32)  14.5 us
    ppermute x6, starting transfers between devices, ring_direct(): lax.ppermute(x, axis, [(k, (k + shift) % size) for k in range(size)])  12.4 us
    another operation x2, other arithmetic, ring_finish(): return jnp.stack((x,) + tuple(received))  11.6 us
    select_n x4, local copies, waits for them, and re-layouts, pair_exchange(): jnp.where(core == 0, jnp.concatenate([mine, received], axis=join_axis), j...  11.2 us
    select_n x3, other arithmetic, pair_exchange(): jnp.where(core == 0, jnp.concatenate([mine, received], axis=join_axis), j...  11.1 us
    ppermute x9, starting transfers between devices, swap(): return lax.ppermute(x, axis, [(0, 1), (1, 0)])  10.6 us
    ppermute x6, waiting for transfers between devices, ring_direct(): lax.ppermute(x, axis, [(k, (k + shift) % size) for k in range(size)])  9.63 us
  transfers between devices with their start and end apart: 25, of which 15 were waited for; matrix products, arithmetic and copies ran while one was open for 37% of the time, Pallas kernels for 0%

profile of v11, /device:TPU:1, one launch (start us, length us, event | category | flops | bytes accessed | tf_op | source)
XLA Modules:
  0.0 204.1 jit_solution(17824858269238173504)
XLA Ops:
  3.4 3.6 %collective-permute-start.4 = (bf16[80,1280]{1,0:T(8,128)(2,1)S(1)}, bf16[80,1280]{1,0:T(8,128)(2,1)S(1)}, u32[]{:S(2)}, u32[]{:S(2)}) collective-permute-start(bf16[80,1280]{1,0:T(8,128)(2,1)S(1)} %get-tuple-element.88), channel_id=1, source_target_pairs={{0,2},{2,0},{1,3},{3,1},{4,6},{6,4},{5,7},{7,5},{8,10},{10,8},{9,1... | collective-permute-start | bytes 614408 | tf_op jit(solution)/shard_map/ppermute | solution.py:113
  11.2 5.6 %collective-permute-done.5 = bf16[80,1280]{1,0:T(8,128)(2,1)S(1)} collective-permute-done((bf16[80,1280]{1,0:T(8,128)(2,1)S(1)}, bf16[80,1280]{1,0:T(8,128)(2,1)S(1)}, u32[]{:S(2)}, u32[]{:S(2)}) %collective-permute-start.5) | collective-permute-done | bytes 204832 | tf_op jit(solution)/shard_map/ppermute | solution.py:71
  21.0 3.4 %collective-permute-start.7 = (bf16[2,80,1280]{2,1,0:T(8,128)(2,1)}, bf16[2,80,1280]{2,1,0:T(8,128)(2,1)}, u32[]{:S(2)}, u32[]{:S(2)}) collective-permute-start(bf16[2,80,1280]{2,1,0:T(8,128)(2,1)} %get-tuple-element.109), channel_id=1, source_target_pairs={{0,64},{32,96},{64,0},{96,32},{1,65},{33,97},{65,1},{97,33},{2,66}... | collective-permute-start | bytes 1228808 | tf_op jit(solution)/shard_map/ppermute | solution.py:62
  36.6 4.4 %collective-permute-done.7 = bf16[2,80,1280]{2,1,0:T(8,128)(2,1)} collective-permute-done((bf16[2,80,1280]{2,1,0:T(8,128)(2,1)}, bf16[2,80,1280]{2,1,0:T(8,128)(2,1)}, u32[]{:S(2)}, u32[]{:S(2)}) %collective-permute-start.7) | collective-permute-done | bytes 409632 | tf_op jit(solution)/shard_map/ppermute | solution.py:62
  44.7 4.1 %collective-permute-done.2 = bf16[2,80,1280]{2,1,0:T(8,128)(2,1)} collective-permute-done((bf16[2,80,1280]{2,1,0:T(8,128)(2,1)}, bf16[2,80,1280]{2,1,0:T(8,128)(2,1)}, u32[]{:S(2)}, u32[]{:S(2)}) %collective-permute-start.2) | collective-permute-done | bytes 409632 | tf_op jit(solution)/shard_map/ppermute | solution.py:62
  72.1 6.4 %maximum_select_fusion = (bf16[512,10,256]{0,2,1:T(8,128)(2,1)}, bf16[512,10,256]{0,2,1:T(8,128)(2,1)}) fusion(bf16[256,10,256]{0,2,1:T(8,128)(2,1)} %collective-permute-done.13, bf16[256,10,256]{0,2,1:T(8,128)(2,1)} %get-tuple-element.94, pred[]{:T(512)S(6)} %eq.17, bf16[256,10,256]{0,2,1:T(8,128)(2,1)S(1)} %copy-done.8, ...), kind=kLoop, calls=%fused_computation.20 | loop fusion | flops 23592960 | bytes 10485761 | tf_op jit(solution)/shard_map/jit(_where)/select_n | solution.py:121
  78.5 3.0 %copy.14 = bf16[512,10,256]{2,0,1:T(8,128)(2,1)S(1)} copy(bf16[512,10,256]{0,2,1:T(8,128)(2,1)} %get-tuple-element.118) | data formatting | bytes 5242880 | tf_op jit(solution)/shard_map/jit(_where)/select_n | solution.py:121
  81.5 3.6 %fusion.54 = (f32[10,256,128]{2,1,0:T(8,128)}, f32[4,10,256,128]{3,2,1,0:T(8,128)S(1)}) fusion(bf16[4,128,10,128]{3,1,0,2:T(8,128)(2,1)} %bitcast.72, bf16[4,128,10,256]{3,1,0,2:T(8,128)(2,1)S(1)} %bitcast.61), kind=kOutput, calls=%fused_computation.121 | convolution fusion | flops 336527360 | bytes 10485760 | tf_op jit(solution)/shard_map/cjhf,cjhe->chfe/dot_general | solution.py:159
  85.1 15.4 %collective-permute-done.10 = bf16[4,2,80,1280]{3,2,1,0:T(8,128)(2,1)} collective-permute-done((bf16[4,2,80,1280]{3,2,1,0:T(8,128)(2,1)}, bf16[4,2,80,1280]{3,2,1,0:T(8,128)(2,1)}, u32[]{:S(2)}, u32[]{:S(2)}) %collective-permute-start.10) | collective-permute-done | bytes 1638432 | tf_op jit(solution)/shard_map/ppermute | solution.py:29
  101.4 3.2 %collective-permute-done.12 = bf16[4,2,80,1280]{3,2,1,0:T(8,128)(2,1)} collective-permute-done((bf16[4,2,80,1280]{3,2,1,0:T(8,128)(2,1)}, bf16[4,2,80,1280]{3,2,1,0:T(8,128)(2,1)}, u32[]{:S(2)}, u32[]{:S(2)}) %collective-permute-start.12) | collective-permute-done | bytes 1638432 | tf_op jit(solution)/shard_map/ppermute | solution.py:29
  106.9 4.0 %collective-permute-start.20 = (f32[10,256,128]{2,1,0:T(8,128)}, f32[10,256,128]{2,1,0:T(8,128)}, u32[]{:S(2)}, u32[]{:S(2)}) collective-permute-start(f32[10,256,128]{2,1,0:T(8,128)} %get-tuple-element.80), channel_id=1, source_target_pairs={{0,2},{1,3},{4,6},{5,7},{8,10},{9,11},{12,14},{13,15},{16,18},{17,... | collective-permute-start | bytes 3932168 | tf_op jit(solution)/shard_map/ppermute | solution.py:165
  117.7 2.9 %fusion.55 = f32[4,10,256,128]{3,2,1,0:T(8,128)} fusion(f32[4,10,256,128]{3,2,1,0:T(8,128)S(1)} %get-tuple-element.115), kind=kOutput, calls=%fused_computation.122 | output fusion | flops 3932160 | bytes 10485760 | tf_op jit(solution)/shard_map/jit(cumsum)/reduce_window_sum | solution.py:174
  120.6 4.4 %copy.19 = bf16[512,10,256]{2,0,1:T(8,128)(2,1)} copy(bf16[512,10,256]{0,2,1:T(8,128)(2,1)} %get-tuple-element.119) | data formatting | bytes 5242880 | tf_op jit(solution)/shard_map/jit(_where)/select_n | solution.py:121
  131.8 4.9 %fusion.10 = f32[4,10,128,128]{2,3,1,0:T(8,128)} fusion(bf16[4,128,10,256]{3,1,0,2:T(8,128)(2,1)S(1)} %bitcast.62, bf16[4,128,10,256]{3,1,0,2:T(8,128)(2,1)} %bitcast.64, pred[128,128]{1,0:T(8,128)(4,1)S(1)} %iota_compare_fusion, bf16[4,128,10,128]{3,1,0,2:T(8,128)(2,1)} %bitcast.73), kind=kOutput, calls=%fused_computation.44 | convolution fusion | flops 504627200 | bytes 9191424 | tf_op jit(solution)/shard_map/chij,cjhe->cihe/dot_general | solution.py:171
  138.2 8.0 %collective-permute-done.15 = bf16[2,2,80,1280]{3,2,1,0:T(8,128)(2,1)} collective-permute-done((bf16[2,2,80,1280]{3,2,1,0:T(8,128)(2,1)}, bf16[2,2,80,1280]{3,2,1,0:T(8,128)(2,1)}, u32[]{:S(2)}, u32[]{:S(2)}) %collective-permute-start.15) | collective-permute-done | bytes 819232 | tf_op jit(solution)/shard_map/ppermute | solution.py:41
  148.8 3.3 %add_bitcast_fusion = f32[4,128,10,128]{3,1,2,0:T(8,128)S(1)} fusion(f32[4,10,128,128]{2,3,1,0:T(8,128)} %fusion.10, f32[3,10,256,128]{3,2,1,0:T(8,128)S(1)} %slice-done, f32[10,256,128]{2,1,0:T(8,128)} %collective-permute-done.20, bf16[4,128,10,256]{3,1,0,2:T(8,128)(2,1)S(1)} %bitcast.65), kind=kOutput, calls=%fused_computation.25 | convolution fusion | flops 338821120 | bytes 13107200 | tf_op jit(solution)/shard_map/cihf,chfe->cihe/dot_general | solution.py:177
  155.1 3.3 %collective-permute-start.21 = (bf16[256,10,128]{2,0,1:T(8,128)(2,1)}, bf16[256,10,128]{2,0,1:T(8,128)(2,1)}, u32[]{:S(2)}, u32[]{:S(2)}) collective-permute-start(bf16[256,10,128]{2,0,1:T(8,128)(2,1)} %get-tuple-element.103), channel_id=1, source_target_pairs={{0,1},{1,0},{2,3},{3,2},{4,5},{5,4},{6,7},{7,6},{8,9},{9,8},{10,11... | collective-permute-start | bytes 1966088 | tf_op jit(solution)/shard_map/ppermute | solution.py:113
  160.5 2.9 %maximum_select_fusion.3 = bf16[256,20,128]{2,0,1:T(8,128)(2,1)} fusion(bf16[256,10,128]{2,0,1:T(8,128)(2,1)} %collective-permute-done.21, bf16[256,10,128]{2,0,1:T(8,128)(2,1)} %get-tuple-element.102, pred[]{:T(512)S(6)} %eq.17), kind=kLoop, calls=%fused_computation.50 | loop fusion | flops 1966080 | bytes 2621441 | tf_op jit(solution)/shard_map/jit(_where)/select_n | solution.py:121
  166.3 5.7 %pad_maximum_fusion.1 = bf16[4,4,2,80,1280]{4,3,2,1,0:T(8,128)(2,1)} fusion(bf16[1,4,2,80,1280]{4,3,2,1,0:T(8,128)(2,1)} %bitcast.41, bf16[1,4,2,80,1280]{4,3,2,1,0:T(8,128)(2,1)S(1)} %bitcast.68, bf16[1,4,2,80,1280]{4,3,2,1,0:T(8,128)(2,1)} %bitcast.39, bf16[1,4,2,80,1280]{4,3,2,1,0:T(8,128)(2,1)} %bitcast.38), kind=kLoop, calls=%fused_computation.7 | loop fusion | flops 9830400 | bytes 13107200 | tf_op jit(solution)/shard_map/stack | solution.py:50
  172.0 5.8 %pad_maximum_fusion = bf16[4,4,2,80,1280]{4,3,2,1,0:T(8,128)(2,1)} fusion(bf16[1,4,2,80,1280]{4,3,2,1,0:T(8,128)(2,1)} %bitcast.33, bf16[1,4,2,80,1280]{4,3,2,1,0:T(8,128)(2,1)S(1)} %bitcast.69, bf16[1,4,2,80,1280]{4,3,2,1,0:T(8,128)(2,1)} %bitcast.31, bf16[1,4,2,80,1280]{4,3,2,1,0:T(8,128)(2,1)} %bitcast.30), kind=kLoop, calls=%fused_computation.6 | loop fusion | flops 9830400 | bytes 13107200 | tf_op jit(solution)/shard_map/stack | solution.py:50
  180.4 7.3 %convolution_convert_fusion = bf16[512,1280]{1,0:T(8,128)(2,1)S(1)} fusion(bf16[512,2560]{0,1:T(8,128)(2,1)} %bitcast.67, bf16[2560,1280]{1,0:T(8,128)(2,1)} %bitcast.71), kind=kOutput, calls=%fused_computation.9 | convolution fusion | flops 3356098560 | bytes 10485760 | tf_op jit(solution)/shard_map/dot_general | solution.py:192
  190.9 7.3 %convolution_convert_fusion.1 = bf16[512,1280]{1,0:T(8,128)(2,1)S(1)} fusion(bf16[512,2560]{0,1:T(8,128)(2,1)} %bitcast.66, bf16[2560,1280]{1,0:T(8,128)(2,1)} %bitcast.70), kind=kOutput, calls=%fused_computation.10 | convolution fusion | flops 3356098560 | bytes 10485760 | tf_op jit(solution)/shard_map/dot_general | solution.py:192
  200.5 2.9 %conditional.1 = (bf16[1,256,5120]{2,1,0:T(8,128)(2,1)}) conditional(s32[]{:T(128)} %clamp.3, (bf16[256,1280]{1,0:T(8,128)(2,1)S(1)}, bf16[256,1280]{1,0:T(8,128)(2,1)S(1)}, bf16[256,1280]{1,0:T(8,128)(2,1)S(1)}, bf16[256,1280]{1,0:T(8,128)(2,1)}) %tuple.30, (bf16[256,1280]{1,0:T(8,128)(2,1)S(1)}, ...), branch_computations={%region_3.4_spmd, %region_4.5_spmd, %region_5.6_spmd, %region_6.7_... | conditional | flops 10485760 | bytes 5242888 | solution.py:206
  200.5 2.9 %maximum_bitcast_fusion.1 = bf16[1,256,5120]{2,1,0:T(8,128)(2,1)} fusion(bf16[256,1280]{1,0:T(8,128)(2,1)S(1)} %get-tuple-element.45, bf16[256,1280]{1,0:T(8,128)(2,1)} %get-tuple-element.44, bf16[256,1280]{1,0:T(8,128)(2,1)S(1)} %get-tuple-element.43, bf16[256,1280]{1,0:T(8,128)(2,1)S(1)} %get-tuple-element.42), kind=kLoop, calls=%fused_computation.3 | loop fusion | flops 10485760 | bytes 5242880 | tf_op jit(solution)/shard_map/broadcast_in_dim | solution.py:207
  (105 shorter events, 87.9 us)
Async XLA Ops:
  3.4 7.9 %collective-permute-start.4 = (bf16[80,1280]{1,0:T(8,128)(2,1)S(1)}, bf16[80,1280]{1,0:T(8,128)(2,1)S(1)}, u32[]{:S(2)}, u32[]{:S(2)}) collective-permute-start(bf16[80,1280]{1,0:T(8,128)(2,1)S(1)} %get-tuple-element.88), channel_id=1, source_target_pairs={{0,2},{2,0},{1,3},{3,1},{4,6},{6,4},{5,7},{7,5},{8,10},{10,8},{9,1... | collective-permute-start | bytes 614408 | tf_op jit(solution)/shard_map/ppermute | solution.py:113
  6.9 9.9 %collective-permute-start.5 = (bf16[80,1280]{1,0:T(8,128)(2,1)S(1)}, bf16[80,1280]{1,0:T(8,128)(2,1)S(1)}, u32[]{:S(2)}, u32[]{:S(2)}) collective-permute-start(bf16[80,1280]{1,0:T(8,128)(2,1)S(1)} %get-tuple-element.88), channel_id=1, source_target_pairs={{0,18},{2,16},{16,2},{18,0},{1,19},{3,17},{17,3},{19,1},{4,22},{6,... | collective-permute-start | bytes 614408 | tf_op jit(solution)/shard_map/ppermute | solution.py:71
  7.8 17.3 %collective-permute-start = (bf16[80,1280]{1,0:T(8,128)(2,1)S(1)}, bf16[80,1280]{1,0:T(8,128)(2,1)S(1)}, u32[]{:S(2)}, u32[]{:S(2)}) collective-permute-start(bf16[80,1280]{1,0:T(8,128)(2,1)S(1)} %get-tuple-element.88), channel_id=1, source_target_pairs={{0,16},{16,0},{1,17},{17,1},{2,18},{18,2},{3,19},{19,3},{4,20},{20... | collective-permute-start | bytes 614408 | tf_op jit(solution)/shard_map/ppermute | solution.py:113
  17.6 13.9 %collective-permute-start.6 = (bf16[2,80,1280]{2,1,0:T(8,128)(2,1)}, bf16[2,80,1280]{2,1,0:T(8,128)(2,1)}, u32[]{:S(2)}, u32[]{:S(2)}) collective-permute-start(bf16[2,80,1280]{2,1,0:T(8,128)(2,1)} %get-tuple-element.109), channel_id=1, source_target_pairs={{0,32},{32,64},{64,96},{96,0},{1,33},{33,65},{65,97},{97,1},{2,34}... | collective-permute-start | bytes 1228808 | tf_op jit(solution)/shard_map/ppermute | solution.py:62
  21.0 20.0 %collective-permute-start.7 = (bf16[2,80,1280]{2,1,0:T(8,128)(2,1)}, bf16[2,80,1280]{2,1,0:T(8,128)(2,1)}, u32[]{:S(2)}, u32[]{:S(2)}) collective-permute-start(bf16[2,80,1280]{2,1,0:T(8,128)(2,1)} %get-tuple-element.109), channel_id=1, source_target_pairs={{0,64},{32,96},{64,0},{96,32},{1,65},{33,97},{65,1},{97,33},{2,66}... | collective-permute-start | bytes 1228808 | tf_op jit(solution)/shard_map/ppermute | solution.py:62
  24.4 17.6 %collective-permute-start.8 = (bf16[2,80,1280]{2,1,0:T(8,128)(2,1)}, bf16[2,80,1280]{2,1,0:T(8,128)(2,1)}, u32[]{:S(2)}, u32[]{:S(2)}) collective-permute-start(bf16[2,80,1280]{2,1,0:T(8,128)(2,1)} %get-tuple-element.109), channel_id=1, source_target_pairs={{0,96},{32,0},{64,32},{96,64},{1,97},{33,1},{65,33},{97,65},{2,98}... | collective-permute-start | bytes 1228808 | tf_op jit(solution)/shard_map/ppermute | solution.py:62
  27.6 17.1 %collective-permute-start.1 = (bf16[2,80,1280]{2,1,0:T(8,128)(2,1)}, bf16[2,80,1280]{2,1,0:T(8,128)(2,1)}, u32[]{:S(2)}, u32[]{:S(2)}) collective-permute-start(bf16[2,80,1280]{2,1,0:T(8,128)(2,1)} %get-tuple-element.111), channel_id=1, source_target_pairs={{0,4},{4,8},{8,12},{12,0},{1,5},{5,9},{9,13},{13,1},{2,6},{6,10},{... | collective-permute-start | bytes 1228808 | tf_op jit(solution)/shard_map/ppermute | solution.py:62
  28.9 19.9 %collective-permute-start.2 = (bf16[2,80,1280]{2,1,0:T(8,128)(2,1)}, bf16[2,80,1280]{2,1,0:T(8,128)(2,1)}, u32[]{:S(2)}, u32[]{:S(2)}) collective-permute-start(bf16[2,80,1280]{2,1,0:T(8,128)(2,1)} %get-tuple-element.111), channel_id=1, source_target_pairs={{0,8},{4,12},{8,0},{12,4},{1,9},{5,13},{9,1},{13,5},{2,10},{6,14},... | collective-permute-start | bytes 1228808 | tf_op jit(solution)/shard_map/ppermute | solution.py:62
  31.6 17.4 %collective-permute-start.3 = (bf16[2,80,1280]{2,1,0:T(8,128)(2,1)}, bf16[2,80,1280]{2,1,0:T(8,128)(2,1)}, u32[]{:S(2)}, u32[]{:S(2)}) collective-permute-start(bf16[2,80,1280]{2,1,0:T(8,128)(2,1)} %get-tuple-element.111), channel_id=1, source_target_pairs={{0,12},{4,0},{8,4},{12,8},{1,13},{5,1},{9,5},{13,9},{2,14},{6,2},{... | collective-permute-start | bytes 1228808 | tf_op jit(solution)/shard_map/ppermute | solution.py:62
  56.0 12.4 %collective-permute-start.19 = (bf16[256,10,256]{0,2,1:T(8,128)(2,1)}, bf16[256,10,256]{0,2,1:T(8,128)(2,1)}, u32[]{:S(2)}, u32[]{:S(2)}) collective-permute-start(bf16[256,10,256]{0,2,1:T(8,128)(2,1)} %get-tuple-element.93), channel_id=1, source_target_pairs={{0,1},{1,0},{2,3},{3,2},{4,5},{5,4},{6,7},{7,6},{8,9},{9,8},{10,11... | collective-permute-start | bytes 3932168 | tf_op jit(solution)/shard_map/ppermute | solution.py:113
  62.2 9.9 %collective-permute-start.13 = (bf16[256,10,256]{0,2,1:T(8,128)(2,1)}, bf16[256,10,256]{0,2,1:T(8,128)(2,1)}, u32[]{:S(2)}, u32[]{:S(2)}) collective-permute-start(bf16[256,10,256]{0,2,1:T(8,128)(2,1)} %get-tuple-element.95), channel_id=1, source_target_pairs={{0,1},{1,0},{2,3},{3,2},{4,5},{5,4},{6,7},{7,6},{8,9},{9,8},{10,11... | collective-permute-start | bytes 3932168 | tf_op jit(solution)/shard_map/ppermute | solution.py:113
  62.5 3.9 %collective-permute-start.14 = (bf16[256,10,128]{0,2,1:T(8,128)(2,1)S(1)}, bf16[256,10,128]{0,2,1:T(8,128)(2,1)}, u32[]{:S(2)}, u32[]{:S(2)}) collective-permute-start(bf16[256,10,128]{0,2,1:T(8,128)(2,1)S(1)} %get-tuple-element.107), channel_id=1, source_target_pairs={{0,1},{1,0},{2,3},{3,2},{4,5},{5,4},{6,7},{7,6},{8,9},{9,8},{10,11... | collective-permute-start | bytes 1966088 | tf_op jit(solution)/shard_map/ppermute | solution.py:113
  62.9 37.6 %collective-permute-start.10 = (bf16[4,2,80,1280]{3,2,1,0:T(8,128)(2,1)}, bf16[4,2,80,1280]{3,2,1,0:T(8,128)(2,1)}, u32[]{:S(2)}, u32[]{:S(2)}) collective-permute-start(bf16[4,2,80,1280]{3,2,1,0:T(8,128)(2,1)} %pad_maximum_fusion.3), channel_id=1, source_target_pairs={{0,96},{32,0},{64,32},{96,64},{1,97},{33,1},{65,33},{97,65},{2,98}... | collective-permute-start | bytes 4915208 | tf_op jit(solution)/shard_map/ppermute | solution.py:29
  62.9 38.5 %collective-permute-start.11 = (bf16[4,2,80,1280]{3,2,1,0:T(8,128)(2,1)}, bf16[4,2,80,1280]{3,2,1,0:T(8,128)(2,1)}, u32[]{:S(2)}, u32[]{:S(2)}) collective-permute-start(bf16[4,2,80,1280]{3,2,1,0:T(8,128)(2,1)} %pad_maximum_fusion.4), channel_id=1, source_target_pairs={{0,4},{4,8},{8,12},{12,0},{1,5},{5,9},{9,13},{13,1},{2,6},{6,10},{... | collective-permute-start | bytes 4915208 | tf_op jit(solution)/shard_map/ppermute | solution.py:29
  66.3 38.2 %collective-permute-start.12 = (bf16[4,2,80,1280]{3,2,1,0:T(8,128)(2,1)}, bf16[4,2,80,1280]{3,2,1,0:T(8,128)(2,1)}, u32[]{:S(2)}, u32[]{:S(2)}) collective-permute-start(bf16[4,2,80,1280]{3,2,1,0:T(8,128)(2,1)} %pad_maximum_fusion.4), channel_id=1, source_target_pairs={{0,12},{4,0},{8,4},{12,8},{1,13},{5,1},{9,5},{13,9},{2,14},{6,2},{... | collective-permute-start | bytes 4915208 | tf_op jit(solution)/shard_map/ppermute | solution.py:29
  68.4 38.5 %collective-permute-start.9 = (bf16[4,2,80,1280]{3,2,1,0:T(8,128)(2,1)}, bf16[4,2,80,1280]{3,2,1,0:T(8,128)(2,1)}, u32[]{:S(2)}, u32[]{:S(2)}) collective-permute-start(bf16[4,2,80,1280]{3,2,1,0:T(8,128)(2,1)} %pad_maximum_fusion.3), channel_id=1, source_target_pairs={{0,32},{32,64},{64,96},{96,0},{1,33},{33,65},{65,97},{97,1},{2,34}... | collective-permute-start | bytes 4915208 | tf_op jit(solution)/shard_map/ppermute | solution.py:29
  106.9 42.0 %collective-permute-start.20 = (f32[10,256,128]{2,1,0:T(8,128)}, f32[10,256,128]{2,1,0:T(8,128)}, u32[]{:S(2)}, u32[]{:S(2)}) collective-permute-start(f32[10,256,128]{2,1,0:T(8,128)} %get-tuple-element.80), channel_id=1, source_target_pairs={{0,2},{1,3},{4,6},{5,7},{8,10},{9,11},{12,14},{13,15},{16,18},{17,... | collective-permute-start | bytes 3932168 | tf_op jit(solution)/shard_map/ppermute | solution.py:165
  112.9 23.8 %collective-permute-start.17 = (bf16[2,2,80,1280]{3,2,1,0:T(8,128)(2,1)}, bf16[2,2,80,1280]{3,2,1,0:T(8,128)(2,1)S(1)}, u32[]{:S(2)}, u32[]{:S(2)}) collective-permute-start(bf16[2,2,80,1280]{3,2,1,0:T(8,128)(2,1)} %slice.29), channel_id=1, source_target_pairs={{0,4},{4,8},{8,12},{12,0},{1,5},{5,9},{9,13},{13,1},{2,6},{6,10},{... | collective-permute-start | bytes 2457608 | tf_op jit(solution)/shard_map/ppermute | solution.py:41
  115.0 21.7 %collective-permute-start.18 = (bf16[2,2,80,1280]{3,2,1,0:T(8,128)(2,1)}, bf16[2,2,80,1280]{3,2,1,0:T(8,128)(2,1)}, u32[]{:S(2)}, u32[]{:S(2)}) collective-permute-start(bf16[2,2,80,1280]{3,2,1,0:T(8,128)(2,1)} %slice.30), channel_id=1, source_target_pairs={{0,12},{4,0},{8,4},{12,8},{1,13},{5,1},{9,5},{13,9},{2,14},{6,2},{... | collective-permute-start | bytes 2457608 | tf_op jit(solution)/shard_map/ppermute | solution.py:42
  127.0 19.2 %collective-permute-start.15 = (bf16[2,2,80,1280]{3,2,1,0:T(8,128)(2,1)}, bf16[2,2,80,1280]{3,2,1,0:T(8,128)(2,1)}, u32[]{:S(2)}, u32[]{:S(2)}) collective-permute-start(bf16[2,2,80,1280]{3,2,1,0:T(8,128)(2,1)} %slice.27), channel_id=1, source_target_pairs={{0,32},{32,64},{64,96},{96,0},{1,33},{33,65},{65,97},{97,1},{2,34}... | collective-permute-start | bytes 2457608 | tf_op jit(solution)/shard_map/ppermute | solution.py:41
  129.1 18.1 %collective-permute-start.16 = (bf16[2,2,80,1280]{3,2,1,0:T(8,128)(2,1)}, bf16[2,2,80,1280]{3,2,1,0:T(8,128)(2,1)}, u32[]{:S(2)}, u32[]{:S(2)}) collective-permute-start(bf16[2,2,80,1280]{3,2,1,0:T(8,128)(2,1)} %slice.28), channel_id=1, source_target_pairs={{0,96},{32,0},{64,32},{96,64},{1,97},{33,1},{65,33},{97,65},{2,98}... | collective-permute-start | bytes 2457608 | tf_op jit(solution)/shard_map/ppermute | solution.py:42
  155.1 5.4 %collective-permute-start.21 = (bf16[256,10,128]{2,0,1:T(8,128)(2,1)}, bf16[256,10,128]{2,0,1:T(8,128)(2,1)}, u32[]{:S(2)}, u32[]{:S(2)}) collective-permute-start(bf16[256,10,128]{2,0,1:T(8,128)(2,1)} %get-tuple-element.103), channel_id=1, source_target_pairs={{0,1},{1,0},{2,3},{3,2},{4,5},{5,4},{6,7},{7,6},{8,9},{9,8},{10,11... | collective-permute-start | bytes 1966088 | tf_op jit(solution)/shard_map/ppermute | solution.py:113
  165.9 11.9 %collective-permute-start.22 = (bf16[256,2560]{0,1:T(8,128)(2,1)}, bf16[256,2560]{0,1:T(8,128)(2,1)S(1)}, u32[]{:S(2)}, u32[]{:S(2)}) collective-permute-start(bf16[256,2560]{0,1:T(8,128)(2,1)} %bitcast.75), channel_id=1, source_target_pairs={{0,1},{1,0},{2,3},{3,2},{4,5},{5,4},{6,7},{7,6},{8,9},{9,8},{10,11... | collective-permute-start | bytes 3932168 | tf_op jit(solution)/shard_map/ppermute | solution.py:113
  188.6 10.2 %collective-permute-start.24 = (bf16[256,1280]{1,0:T(8,128)(2,1)}, bf16[256,1280]{1,0:T(8,128)(2,1)}, u32[]{:S(2)}, u32[]{:S(2)}) collective-permute-start(bf16[256,1280]{1,0:T(8,128)(2,1)} %get-tuple-element.98), channel_id=1, source_target_pairs={{0,1},{1,0},{2,3},{3,2},{4,5},{5,4},{6,7},{7,6},{8,9},{9,8},{10,11... | collective-permute-start | bytes 1966088 | tf_op jit(solution)/shard_map/ppermute | solution.py:113
  (14 other events, 150.5 us)

commit v12 on v10

--- a/solution.py
+++ b/solution.py
@@ -148,8 +148,8 @@
     )
     query_group = pair_exchange(query_heads, core, 1, 0)
     sent = [ring_send(part, second, 4) for part, (_, second) in zip(parts, STAGES)]
-    key_group = pair_exchange(keys_in[0].reshape(tokens_here, H, HEAD), core, 1, 0)
-    value_group = pair_exchange(values_in[0].reshape(tokens_here, H, HEAD), core, 1, 0)
+    key_value = jnp.stack([keys_in[0], values_in[0]]).reshape(2, tokens_here, H, HEAD)
+    key_group, value_group = pair_exchange(key_value, core, 2, 1)
     span = query_group.shape[0]
     offset = half * span
     query_blocks = to_blocks(featurize(query_group, offset, seq_length))
@@ -186,12 +186,13 @@
     by_block = tokens.reshape(tokens.shape[0], 32, -1)
     wide = []
     for rows, source in gather_finish(parts, sent):
-        features = jnp.take(by_block, source, axis=1).reshape(tokens.shape)
+        features = jnp.take(by_block, source, axis=1, mode="clip").reshape(tokens.shape)
         wide.append(
             jnp.dot(features, rows, preferred_element_type=jnp.float32).astype(jnp.bfloat16)
         )
     own = [piece[:tokens_here] for piece in wide]
-    returned = [swap(piece[tokens_here:], "c") for piece in wide]
+    returned = swap(jnp.stack([piece[tokens_here:] for piece in wide]), "c")
+    returned = [returned[0], returned[1]]
     candidates = own + returned
 
     def place(chip, side):

time: 188 us -> 190 us (1.011)
  local copies, waits for them, and re-layouts: 42.4 us -> 47.8 us
  waiting for transfers between devices: 36.8 us -> 34 us
    unnamed x41 -> x45, local copies, waits for them, and re-layouts: 8.06 us -> 12.2 us
    select_n x2 -> x0, other arithmetic: 4.07 us -> none  [on_device(): features = jnp.take(by_block, source, axis=1).reshape(tokens.shape)]
    another operation x0 -> x3, local copies, waits for them, and re-layouts: none -> 3.8 us  [the longest x2 3.72 us: on_device(): key_group, value_group = pair_exchange(key_value, core, 2, 1)]
    another operation x1 -> x3, other arithmetic: 4.42 us -> 7.41 us
    select_n x2, other arithmetic: 3.32 us -> 5.26 us  [pair_exchange(): jnp.where(core == 0, jnp.concatenate([mine, received], axis=join_axis), j...]
    max x1 -> x2, other arithmetic: 3.94 us -> 2.08 us  [featurize(): rectified = jnp.maximum(block.astype(jnp.float32), 0.0)]
    select_n x2 -> x1, local copies, waits for them, and re-layouts: 3.92 us -> 2.47 us  [pair_exchange(): jnp.where(core == 0, jnp.concatenate([mine, received], axis=join_axis), j...]
    ppermute x9 -> x7, waiting for transfers between devices: 7.21 us -> 5.85 us  [swap(): return lax.ppermute(x, axis, [(0, 1), (1, 0)])]
  transfers between devices with their start and end apart: 25 -> 23, of which waited for: 11 -> 12; matrix products, arithmetic and copies ran while one was open for 41% -> 37% of each run, Pallas kernels for 0% -> 0%
where the time goes in v12:
time: 190 us; the launch traced here: 189 us
  local copies, waits for them, and re-layouts  47.8 us (25%)
  other arithmetic  44 us (23%)
  starting transfers between devices  37.6 us (20%)
  waiting for transfers between devices  34 us (18%)
  matrix products  24.9 us (13%)
    dot_general x2, matrix products, on_device(): jnp.dot(features, rows, preferred_element_type=jnp.float32)  14.5 us
    unnamed x45, local copies, waits for them, and re-layouts  12.2 us
    ppermute x6, starting transfers between devices, ring_direct(): lax.ppermute(x, axis, [(k, (k + shift) % size) for k in range(size)])  12 us
    another operation x2, other arithmetic, ring_finish(): return jnp.stack((x,) + tuple(received))  11.6 us
    ppermute x4, waiting for transfers between devices, ring_send(): return (lax.ppermute(x, axis, forward), lax.ppermute(x, axis, backward))  11.5 us
    ppermute x7, starting transfers between devices, swap(): return lax.ppermute(x, axis, [(0, 1), (1, 0)])  11.3 us
    max x4, local copies, waits for them, and re-layouts, featurize(): rectified = jnp.maximum(block.astype(jnp.float32), 0.0)  10.7 us
    ppermute x6, waiting for transfers between devices, ring_direct(): lax.ppermute(x, axis, [(k, (k + shift) % size) for k in range(size)])  9.36 us
  transfers between devices with their start and end apart: 23, of which 12 were waited for; matrix products, arithmetic and copies ran while one was open for 37% of the time, Pallas kernels for 0%

profile of v12, /device:TPU:1, one launch (start us, length us, event | category | flops | bytes accessed | tf_op | source)
XLA Modules:
  0.0 189.3 jit_solution(979098989020098385)
XLA Ops:
  0.7 2.7 %fusion.35 = (bf16[80,1280]{1,0:T(8,128)(2,1)S(1)}, f32[80,1280]{1,0:T(8,128)}, f32[80,1280]{1,0:T(8,128)}, f32[80,1280]{1,0:T(8,128)}) fusion(f32[80,1280]{1,0:T(8,128)} %param.16, f32[80,1280]{1,0:T(8,128)} %param.17, f32[80,1280]{1,0:T(8,128)} %param.18, f32[80,1280]{1,0:T(8,128)} %param.19), kind=kLoop, calls=%fused_computation.113 | loop fusion | flops 1638400 | bytes 3072000 | tf_op jit(solution)/shard_map/convert_element_type | solution.py:139
  3.4 3.6 %collective-permute-start.4 = (bf16[80,1280]{1,0:T(8,128)(2,1)S(1)}, bf16[80,1280]{1,0:T(8,128)(2,1)S(1)}, u32[]{:S(2)}, u32[]{:S(2)}) collective-permute-start(bf16[80,1280]{1,0:T(8,128)(2,1)S(1)} %get-tuple-element.88), channel_id=1, source_target_pairs={{0,2},{2,0},{1,3},{3,1},{4,6},{6,4},{5,7},{7,5},{8,10},{10,8},{9,1... | collective-permute-start | bytes 614408 | tf_op jit(solution)/shard_map/ppermute | solution.py:113
  11.3 5.6 %collective-permute-done.5 = bf16[80,1280]{1,0:T(8,128)(2,1)S(1)} collective-permute-done((bf16[80,1280]{1,0:T(8,128)(2,1)S(1)}, bf16[80,1280]{1,0:T(8,128)(2,1)S(1)}, u32[]{:S(2)}, u32[]{:S(2)}) %collective-permute-start.5) | collective-permute-done | bytes 204832 | tf_op jit(solution)/shard_map/ppermute | solution.py:71
  25.7 3.3 %collective-permute-start.7 = (bf16[2,80,1280]{2,1,0:T(8,128)(2,1)}, bf16[2,80,1280]{2,1,0:T(8,128)(2,1)S(1)}, u32[]{:S(2)}, u32[]{:S(2)}) collective-permute-start(bf16[2,80,1280]{2,1,0:T(8,128)(2,1)} %get-tuple-element.109), channel_id=1, source_target_pairs={{0,64},{32,96},{64,0},{96,32},{1,65},{33,97},{65,1},{97,33},{2,66}... | collective-permute-start | bytes 1228808 | tf_op jit(solution)/shard_map/ppermute | solution.py:62
  31.1 2.6 %collective-permute-start.2 = (bf16[2,80,1280]{2,1,0:T(8,128)(2,1)S(1)}, bf16[2,80,1280]{2,1,0:T(8,128)(2,1)S(1)}, u32[]{:S(2)}, u32[]{:S(2)}) collective-permute-start(bf16[2,80,1280]{2,1,0:T(8,128)(2,1)S(1)} %get-tuple-element.111), channel_id=1, source_target_pairs={{0,8},{4,12},{8,0},{12,4},{1,9},{5,13},{9,1},{13,5},{2,10},{6,14},... | collective-permute-start | bytes 1228808 | tf_op jit(solution)/shard_map/ppermute | solution.py:62
  37.7 4.9 %collective-permute-done.7 = bf16[2,80,1280]{2,1,0:T(8,128)(2,1)S(1)} collective-permute-done((bf16[2,80,1280]{2,1,0:T(8,128)(2,1)}, bf16[2,80,1280]{2,1,0:T(8,128)(2,1)S(1)}, u32[]{:S(2)}, u32[]{:S(2)}) %collective-permute-start.7) | collective-permute-done | bytes 409632 | tf_op jit(solution)/shard_map/ppermute | solution.py:62
  46.5 2.5 %pad_maximum_fusion.11 = bf16[4,2,80,1280]{3,2,1,0:T(8,128)(2,1)} fusion(bf16[1,2,80,1280]{3,2,1,0:T(8,128)(2,1)S(1)} %bitcast.86, bf16[1,2,80,1280]{3,2,1,0:T(8,128)(2,1)S(1)} %bitcast.84, bf16[1,2,80,1280]{3,2,1,0:T(8,128)(2,1)} %bitcast.13, bf16[1,2,80,1280]{3,2,1,0:T(8,128)(2,1)S(1)} %get-tuple-element.108), kind=kLoop, calls=%fused_computation.30 | loop fusion | flops 2457600 | bytes 3276800 | tf_op jit(solution)/shard_map/stack | solution.py:65
  62.7 3.3 %copy.22 = f32[4,128,10,128]{1,3,2,0:T(8,128)} copy(f32[4,128,10,128]{3,1,0,2:T(8,128)} %bitcast.69) | data formatting | bytes 5242880 | tf_op jit(solution)/shard_map/max | solution.py:97
  71.9 3.2 %copy.17 = f32[4,128,10,128]{1,3,2,0:T(8,128)} copy(f32[4,128,10,128]{3,1,0,2:T(8,128)} %bitcast.70) | data formatting | bytes 5242880 | tf_op jit(solution)/shard_map/max | solution.py:97
  75.1 2.6 %copy.19 = bf16[1,512,10,128]{3,1,2,0:T(8,128)(2,1)} copy(bf16[1,512,10,128]{1,3,2,0:T(8,128)(2,1)} %unstack.10) | data formatting | bytes 2621440 | tf_op jit(solution)/shard_map/unstack | solution.py:152
  77.7 4.3 %multiply_convert_fusion.4 = (bf16[4,128,10,128]{1,3,2,0:T(8,128)(2,1)S(1)}, bf16[4,128,10,128]{1,3,2,0:T(8,128)(2,1)S(1)}, bf16[4,128,10,128]{1,3,2,0:T(8,128)(2,1)}, bf16[4,128,10,128]{1,3,2,0:T(8,128)(2,1)}) fusion(f32[4,128,10,128]{1,3,2,0:T(8,128)} %copy.17, f32[4,128]{1,0:T(4,128)S(1)} %get-tuple-element.119, f32[4,128]{1,0:T(4,128)S(1)} %get-tuple-element.118, ...), kind=kLoop, calls=%fused_computation.26 | loop fusion | flops 5242880 | bytes 10489856 | tf_op jit(solution)/shard_map/convert.2
  84.0 10.5 %collective-permute-done.10 = bf16[4,2,80,1280]{3,2,1,0:T(8,128)(2,1)} collective-permute-done((bf16[4,2,80,1280]{3,2,1,0:T(8,128)(2,1)}, bf16[4,2,80,1280]{3,2,1,0:T(8,128)(2,1)}, u32[]{:S(2)}, u32[]{:S(2)}) %collective-permute-start.10) | collective-permute-done | bytes 1638432 | tf_op jit(solution)/shard_map/ppermute | solution.py:29
  95.5 4.0 %collective-permute-start.19 = (f32[10,256,128]{2,1,0:T(8,128)}, f32[10,256,128]{2,1,0:T(8,128)}, u32[]{:S(2)}, u32[]{:S(2)}) collective-permute-start(f32[10,256,128]{2,1,0:T(8,128)} %get-tuple-element.80), channel_id=1, source_target_pairs={{0,2},{1,3},{4,6},{5,7},{8,10},{9,11},{12,14},{13,15},{16,18},{17,... | collective-permute-start | bytes 3932168 | tf_op jit(solution)/shard_map/ppermute | solution.py:164
  110.7 2.6 %collective-permute-start.15 = (bf16[2,2,80,1280]{3,2,1,0:T(8,128)(2,1)}, bf16[2,2,80,1280]{3,2,1,0:T(8,128)(2,1)}, u32[]{:S(2)}, u32[]{:S(2)}) collective-permute-start(bf16[2,2,80,1280]{3,2,1,0:T(8,128)(2,1)} %slice.34), channel_id=1, source_target_pairs={{0,96},{32,0},{64,32},{96,64},{1,97},{33,1},{65,33},{97,65},{2,98}... | collective-permute-start | bytes 2457608 | tf_op jit(solution)/shard_map/ppermute | solution.py:42
  115.6 2.6 %copy-done.2 = f32[4,10,256,128]{3,2,1,0:T(8,128)} copy-done((f32[4,10,256,128]{3,2,1,0:T(8,128)}, f32[4,10,256,128]{3,2,1,0:T(8,128)S(1)}, u32[]{:S(2)}) %copy-start.2) | copy-done | bytes 5242904
  119.2 4.8 %fusion.3 = f32[4,10,128,128]{2,3,1,0:T(8,128)} fusion(bf16[4,128,10,128]{1,3,2,0:T(8,128)(2,1)S(1)} %copy-done.4, bf16[4,128,10,128]{1,3,2,0:T(8,128)(2,1)S(1)} %copy-done.6, bf16[4,128,10,128]{1,3,2,0:T(8,128)(2,1)} %copy-done.9, bf16[4,128,10,128]{1,3,2,0:T(8,128)(2,1)} %copy-done.8, pred[128,128]{1,0:T(8,128)(4,1)S(1)} %iota_compare_fusion, ...), kind=kOutput, calls=%fused_computation.33 | convolution fusion | flops 515112960 | bytes 9191424 | tf_op jit(solution)/shard_map/chij,cjhe->cihe/dot_general | solution.py:170
  129.9 3.5 %add_bitcast_fusion = f32[4,128,10,128]{3,1,2,0:T(8,128)S(1)} fusion(f32[4,10,128,128]{2,3,1,0:T(8,128)} %fusion.3, f32[3,10,256,128]{3,2,1,0:T(8,128)S(1)} %slice-done, f32[10,256,128]{2,1,0:T(8,128)} %collective-permute-done.19, bf16[4,128,10,128]{1,3,2,0:T(8,128)(2,1)S(1)} %copy-done.5, bf16[4,128,10,128]{1,3,2,0:T(8,128)(2,1)S(1)} %copy-done.7), kind=kOutput, calls=%fused_computation.19 | convolution fusion | flops 344064000 | bytes 13107200 | tf_op jit(solution)/shard_map/cihf,chfe->cihe/dot_general | solution.py:176
  136.5 3.7 %collective-permute-start.20 = (bf16[256,10,128]{2,0,1:T(8,128)(2,1)}, bf16[256,10,128]{2,0,1:T(8,128)(2,1)}, u32[]{:S(2)}, u32[]{:S(2)}) collective-permute-start(bf16[256,10,128]{2,0,1:T(8,128)(2,1)} %get-tuple-element.105), channel_id=1, source_target_pairs={{0,1},{1,0},{2,3},{3,2},{4,5},{5,4},{6,7},{7,6},{8,9},{9,8},{10,11... | collective-permute-start | bytes 1966088 | tf_op jit(solution)/shard_map/ppermute | solution.py:113
  142.3 2.9 %maximum_select_fusion.2 = bf16[256,20,128]{2,0,1:T(8,128)(2,1)} fusion(bf16[256,10,128]{2,0,1:T(8,128)(2,1)} %collective-permute-done.20, bf16[256,10,128]{2,0,1:T(8,128)(2,1)} %get-tuple-element.104, pred[]{:T(512)S(6)} %eq.16), kind=kLoop, calls=%fused_computation.35 | loop fusion | flops 1966080 | bytes 2621441 | tf_op jit(solution)/shard_map/jit(_where)/select_n | solution.py:121
  148.1 5.7 %pad_maximum_fusion.1 = bf16[4,4,2,80,1280]{4,3,2,1,0:T(8,128)(2,1)} fusion(bf16[1,4,2,80,1280]{4,3,2,1,0:T(8,128)(2,1)} %bitcast.41, bf16[1,4,2,80,1280]{4,3,2,1,0:T(8,128)(2,1)S(1)} %bitcast.73, bf16[1,4,2,80,1280]{4,3,2,1,0:T(8,128)(2,1)} %bitcast.39, bf16[1,4,2,80,1280]{4,3,2,1,0:T(8,128)(2,1)} %bitcast.38), kind=kLoop, calls=%fused_computation.7 | loop fusion | flops 9830400 | bytes 13107200 | tf_op jit(solution)/shard_map/stack | solution.py:50
  153.8 5.8 %pad_maximum_fusion = bf16[4,4,2,80,1280]{4,3,2,1,0:T(8,128)(2,1)} fusion(bf16[1,4,2,80,1280]{4,3,2,1,0:T(8,128)(2,1)} %bitcast.32, bf16[1,4,2,80,1280]{4,3,2,1,0:T(8,128)(2,1)S(1)} %bitcast.74, bf16[1,4,2,80,1280]{4,3,2,1,0:T(8,128)(2,1)} %bitcast.30, bf16[1,4,2,80,1280]{4,3,2,1,0:T(8,128)(2,1)} %bitcast.29), kind=kLoop, calls=%fused_computation.6 | loop fusion | flops 9830400 | bytes 13107200 | tf_op jit(solution)/shard_map/stack | solution.py:50
  162.2 7.3 %convolution_convert_fusion = bf16[512,1280]{1,0:T(8,128)(2,1)S(1)} fusion(bf16[512,2560]{0,1:T(8,128)(2,1)} %bitcast.72, bf16[2560,1280]{1,0:T(8,128)(2,1)} %bitcast.76), kind=kOutput, calls=%fused_computation.9 | convolution fusion | flops 3356098560 | bytes 10485760 | tf_op jit(solution)/shard_map/dot_general | solution.py:191
  172.6 7.3 %convolution_convert_fusion.1 = bf16[512,1280]{1,0:T(8,128)(2,1)S(1)} fusion(bf16[512,2560]{0,1:T(8,128)(2,1)} %bitcast.71, bf16[2560,1280]{1,0:T(8,128)(2,1)} %bitcast.75), kind=kOutput, calls=%fused_computation.10 | convolution fusion | flops 3356098560 | bytes 10485760 | tf_op jit(solution)/shard_map/dot_general | solution.py:191
  182.3 3.2 %collective-permute-done.22 = bf16[2,256,1280]{2,1,0:T(8,128)(2,1)} collective-permute-done((bf16[2,256,1280]{2,1,0:T(8,128)(2,1)}, bf16[2,256,1280]{2,1,0:T(8,128)(2,1)}, u32[]{:S(2)}, u32[]{:S(2)}) %collective-permute-start.22) | collective-permute-done | bytes 1310752 | tf_op jit(solution)/shard_map/ppermute | solution.py:113
  (123 shorter events, 87.3 us)
Async XLA Ops:
  0.6 53.9 %copy-start = (f32[20,128]{1,0:T(8,128)S(1)}, f32[20,128]{1,0:T(8,128)}, u32[]{:S(2)}) copy-start(f32[20,128]{1,0:T(8,128)} %param.15) | copy-start | bytes 30724
  3.4 7.9 %collective-permute-start.4 = (bf16[80,1280]{1,0:T(8,128)(2,1)S(1)}, bf16[80,1280]{1,0:T(8,128)(2,1)S(1)}, u32[]{:S(2)}, u32[]{:S(2)}) collective-permute-start(bf16[80,1280]{1,0:T(8,128)(2,1)S(1)} %get-tuple-element.88), channel_id=1, source_target_pairs={{0,2},{2,0},{1,3},{3,1},{4,6},{6,4},{5,7},{7,5},{8,10},{10,8},{9,1... | collective-permute-start | bytes 614408 | tf_op jit(solution)/shard_map/ppermute | solution.py:113
  7.0 9.9 %collective-permute-start.5 = (bf16[80,1280]{1,0:T(8,128)(2,1)S(1)}, bf16[80,1280]{1,0:T(8,128)(2,1)S(1)}, u32[]{:S(2)}, u32[]{:S(2)}) collective-permute-start(bf16[80,1280]{1,0:T(8,128)(2,1)S(1)} %get-tuple-element.88), channel_id=1, source_target_pairs={{0,18},{2,16},{16,2},{18,0},{1,19},{3,17},{17,3},{19,1},{4,22},{6,... | collective-permute-start | bytes 614408 | tf_op jit(solution)/shard_map/ppermute | solution.py:71
  7.8 21.9 %collective-permute-start = (bf16[80,1280]{1,0:T(8,128)(2,1)S(1)}, bf16[80,1280]{1,0:T(8,128)(2,1)S(1)}, u32[]{:S(2)}, u32[]{:S(2)}) collective-permute-start(bf16[80,1280]{1,0:T(8,128)(2,1)S(1)} %get-tuple-element.88), channel_id=1, source_target_pairs={{0,16},{16,0},{1,17},{17,1},{2,18},{18,2},{3,19},{19,3},{4,20},{20... | collective-permute-start | bytes 614408 | tf_op jit(solution)/shard_map/ppermute | solution.py:113
  19.4 14.3 %collective-permute-start.6 = (bf16[2,80,1280]{2,1,0:T(8,128)(2,1)}, bf16[2,80,1280]{2,1,0:T(8,128)(2,1)}, u32[]{:S(2)}, u32[]{:S(2)}) collective-permute-start(bf16[2,80,1280]{2,1,0:T(8,128)(2,1)} %get-tuple-element.109), channel_id=1, source_target_pairs={{0,32},{32,64},{64,96},{96,0},{1,33},{33,65},{65,97},{97,1},{2,34}... | collective-permute-start | bytes 1228808 | tf_op jit(solution)/shard_map/ppermute | solution.py:62
  25.7 17.0 %collective-permute-start.7 = (bf16[2,80,1280]{2,1,0:T(8,128)(2,1)}, bf16[2,80,1280]{2,1,0:T(8,128)(2,1)S(1)}, u32[]{:S(2)}, u32[]{:S(2)}) collective-permute-start(bf16[2,80,1280]{2,1,0:T(8,128)(2,1)} %get-tuple-element.109), channel_id=1, source_target_pairs={{0,64},{32,96},{64,0},{96,32},{1,65},{33,97},{65,1},{97,33},{2,66}... | collective-permute-start | bytes 1228808 | tf_op jit(solution)/shard_map/ppermute | solution.py:62
  29.0 17.5 %collective-permute-start.8 = (bf16[2,80,1280]{2,1,0:T(8,128)(2,1)}, bf16[2,80,1280]{2,1,0:T(8,128)(2,1)S(1)}, u32[]{:S(2)}, u32[]{:S(2)}) collective-permute-start(bf16[2,80,1280]{2,1,0:T(8,128)(2,1)} %get-tuple-element.109), channel_id=1, source_target_pairs={{0,96},{32,0},{64,32},{96,64},{1,97},{33,1},{65,33},{97,65},{2,98}... | collective-permute-start | bytes 1228808 | tf_op jit(solution)/shard_map/ppermute | solution.py:62
  29.8 19.2 %collective-permute-start.1 = (bf16[2,80,1280]{2,1,0:T(8,128)(2,1)S(1)}, bf16[2,80,1280]{2,1,0:T(8,128)(2,1)S(1)}, u32[]{:S(2)}, u32[]{:S(2)}) collective-permute-start(bf16[2,80,1280]{2,1,0:T(8,128)(2,1)S(1)} %get-tuple-element.111), channel_id=1, source_target_pairs={{0,4},{4,8},{8,12},{12,0},{1,5},{5,9},{9,13},{13,1},{2,6},{6,10},{... | collective-permute-start | bytes 1228808 | tf_op jit(solution)/shard_map/ppermute | solution.py:62
  31.1 19.6 %collective-permute-start.2 = (bf16[2,80,1280]{2,1,0:T(8,128)(2,1)S(1)}, bf16[2,80,1280]{2,1,0:T(8,128)(2,1)S(1)}, u32[]{:S(2)}, u32[]{:S(2)}) collective-permute-start(bf16[2,80,1280]{2,1,0:T(8,128)(2,1)S(1)} %get-tuple-element.111), channel_id=1, source_target_pairs={{0,8},{4,12},{8,0},{12,4},{1,9},{5,13},{9,1},{13,5},{2,10},{6,14},... | collective-permute-start | bytes 1228808 | tf_op jit(solution)/shard_map/ppermute | solution.py:62
  33.8 17.2 %collective-permute-start.3 = (bf16[2,80,1280]{2,1,0:T(8,128)(2,1)S(1)}, bf16[2,80,1280]{2,1,0:T(8,128)(2,1)S(1)}, u32[]{:S(2)}, u32[]{:S(2)}) collective-permute-start(bf16[2,80,1280]{2,1,0:T(8,128)(2,1)S(1)} %get-tuple-element.111), channel_id=1, source_target_pairs={{0,12},{4,0},{8,4},{12,8},{1,13},{5,1},{9,5},{13,9},{2,14},{6,2},{... | collective-permute-start | bytes 1228808 | tf_op jit(solution)/shard_map/ppermute | solution.py:62
  42.6 23.4 %collective-permute-start.13 = (bf16[2,256,10,128]{1,3,2,0:T(8,128)(2,1)}, bf16[2,256,10,128]{1,3,2,0:T(8,128)(2,1)}, u32[]{:S(2)}, u32[]{:S(2)}) collective-permute-start(bf16[2,256,10,128]{1,3,2,0:T(8,128)(2,1)} %get-tuple-element.97), channel_id=1, source_target_pairs={{0,1},{1,0},{2,3},{3,2},{4,5},{5,4},{6,7},{7,6},{8,9},{9,8},{10,11... | collective-permute-start | bytes 3932168 | tf_op jit(solution)/shard_map/ppermute | solution.py:113
  52.4 5.0 %collective-permute-start.18 = (bf16[256,10,128]{0,2,1:T(8,128)(2,1)S(1)}, bf16[256,10,128]{0,2,1:T(8,128)(2,1)S(1)}, u32[]{:S(2)}, u32[]{:S(2)}) collective-permute-start(bf16[256,10,128]{0,2,1:T(8,128)(2,1)S(1)} %get-tuple-element.107), channel_id=1, source_target_pairs={{0,1},{1,0},{2,3},{3,2},{4,5},{5,4},{6,7},{7,6},{8,9},{9,8},{10,11... | collective-permute-start | bytes 1966088 | tf_op jit(solution)/shard_map/ppermute | solution.py:113
  54.6 39.8 %collective-permute-start.11 = (bf16[4,2,80,1280]{3,2,1,0:T(8,128)(2,1)}, bf16[4,2,80,1280]{3,2,1,0:T(8,128)(2,1)}, u32[]{:S(2)}, u32[]{:S(2)}) collective-permute-start(bf16[4,2,80,1280]{3,2,1,0:T(8,128)(2,1)} %pad_maximum_fusion.11), channel_id=1, source_target_pairs={{0,4},{4,8},{8,12},{12,0},{1,5},{5,9},{9,13},{13,1},{2,6},{6,10},{... | collective-permute-start | bytes 4915208 | tf_op jit(solution)/shard_map/ppermute | solution.py:29
  56.3 38.1 %collective-permute-start.12 = (bf16[4,2,80,1280]{3,2,1,0:T(8,128)(2,1)}, bf16[4,2,80,1280]{3,2,1,0:T(8,128)(2,1)}, u32[]{:S(2)}, u32[]{:S(2)}) collective-permute-start(bf16[4,2,80,1280]{3,2,1,0:T(8,128)(2,1)} %pad_maximum_fusion.11), channel_id=1, source_target_pairs={{0,12},{4,0},{8,4},{12,8},{1,13},{5,1},{9,5},{13,9},{2,14},{6,2},{... | collective-permute-start | bytes 4915208 | tf_op jit(solution)/shard_map/ppermute | solution.py:29
  57.4 37.1 %collective-permute-start.10 = (bf16[4,2,80,1280]{3,2,1,0:T(8,128)(2,1)}, bf16[4,2,80,1280]{3,2,1,0:T(8,128)(2,1)}, u32[]{:S(2)}, u32[]{:S(2)}) collective-permute-start(bf16[4,2,80,1280]{3,2,1,0:T(8,128)(2,1)} %pad_maximum_fusion.10), channel_id=1, source_target_pairs={{0,96},{32,0},{64,32},{96,64},{1,97},{33,1},{65,33},{97,65},{2,98}... | collective-permute-start | bytes 4915208 | tf_op jit(solution)/shard_map/ppermute | solution.py:29
  57.4 38.1 %collective-permute-start.9 = (bf16[4,2,80,1280]{3,2,1,0:T(8,128)(2,1)}, bf16[4,2,80,1280]{3,2,1,0:T(8,128)(2,1)}, u32[]{:S(2)}, u32[]{:S(2)}) collective-permute-start(bf16[4,2,80,1280]{3,2,1,0:T(8,128)(2,1)} %pad_maximum_fusion.10), channel_id=1, source_target_pairs={{0,32},{32,64},{64,96},{96,0},{1,33},{33,65},{65,97},{97,1},{2,34}... | collective-permute-start | bytes 4915208 | tf_op jit(solution)/shard_map/ppermute | solution.py:29
  95.5 34.4 %collective-permute-start.19 = (f32[10,256,128]{2,1,0:T(8,128)}, f32[10,256,128]{2,1,0:T(8,128)}, u32[]{:S(2)}, u32[]{:S(2)}) collective-permute-start(f32[10,256,128]{2,1,0:T(8,128)} %get-tuple-element.80), channel_id=1, source_target_pairs={{0,2},{1,3},{4,6},{5,7},{8,10},{9,11},{12,14},{13,15},{16,18},{17,... | collective-permute-start | bytes 3932168 | tf_op jit(solution)/shard_map/ppermute | solution.py:164
  101.6 22.4 %collective-permute-start.16 = (bf16[2,2,80,1280]{3,2,1,0:T(8,128)(2,1)}, bf16[2,2,80,1280]{3,2,1,0:T(8,128)(2,1)}, u32[]{:S(2)}, u32[]{:S(2)}) collective-permute-start(bf16[2,2,80,1280]{3,2,1,0:T(8,128)(2,1)} %slice.35), channel_id=1, source_target_pairs={{0,4},{4,8},{8,12},{12,0},{1,5},{5,9},{9,13},{13,1},{2,6},{6,10},{... | collective-permute-start | bytes 2457608 | tf_op jit(solution)/shard_map/ppermute | solution.py:41
  104.0 20.1 %collective-permute-start.17 = (bf16[2,2,80,1280]{3,2,1,0:T(8,128)(2,1)}, bf16[2,2,80,1280]{3,2,1,0:T(8,128)(2,1)}, u32[]{:S(2)}, u32[]{:S(2)}) collective-permute-start(bf16[2,2,80,1280]{3,2,1,0:T(8,128)(2,1)} %slice.36), channel_id=1, source_target_pairs={{0,12},{4,0},{8,4},{12,8},{1,13},{5,1},{9,5},{13,9},{2,14},{6,2},{... | collective-permute-start | bytes 2457608 | tf_op jit(solution)/shard_map/ppermute | solution.py:42
  108.5 18.6 %collective-permute-start.14 = (bf16[2,2,80,1280]{3,2,1,0:T(8,128)(2,1)}, bf16[2,2,80,1280]{3,2,1,0:T(8,128)(2,1)S(1)}, u32[]{:S(2)}, u32[]{:S(2)}) collective-permute-start(bf16[2,2,80,1280]{3,2,1,0:T(8,128)(2,1)} %slice.33), channel_id=1, source_target_pairs={{0,32},{32,64},{64,96},{96,0},{1,33},{33,65},{65,97},{97,1},{2,34}... | collective-permute-start | bytes 2457608 | tf_op jit(solution)/shard_map/ppermute | solution.py:41
  110.7 17.6 %collective-permute-start.15 = (bf16[2,2,80,1280]{3,2,1,0:T(8,128)(2,1)}, bf16[2,2,80,1280]{3,2,1,0:T(8,128)(2,1)}, u32[]{:S(2)}, u32[]{:S(2)}) collective-permute-start(bf16[2,2,80,1280]{3,2,1,0:T(8,128)(2,1)} %slice.34), channel_id=1, source_target_pairs={{0,96},{32,0},{64,32},{96,64},{1,97},{33,1},{65,33},{97,65},{2,98}... | collective-permute-start | bytes 2457608 | tf_op jit(solution)/shard_map/ppermute | solution.py:42
  136.5 5.8 %collective-permute-start.20 = (bf16[256,10,128]{2,0,1:T(8,128)(2,1)}, bf16[256,10,128]{2,0,1:T(8,128)(2,1)}, u32[]{:S(2)}, u32[]{:S(2)}) collective-permute-start(bf16[256,10,128]{2,0,1:T(8,128)(2,1)} %get-tuple-element.105), channel_id=1, source_target_pairs={{0,1},{1,0},{2,3},{3,2},{4,5},{5,4},{6,7},{7,6},{8,9},{9,8},{10,11... | collective-permute-start | bytes 1966088 | tf_op jit(solution)/shard_map/ppermute | solution.py:113
  147.7 11.9 %collective-permute-start.21 = (bf16[256,2560]{0,1:T(8,128)(2,1)}, bf16[256,2560]{0,1:T(8,128)(2,1)S(1)}, u32[]{:S(2)}, u32[]{:S(2)}) collective-permute-start(bf16[256,2560]{0,1:T(8,128)(2,1)} %bitcast.79), channel_id=1, source_target_pairs={{0,1},{1,0},{2,3},{3,2},{4,5},{5,4},{6,7},{7,6},{8,9},{9,8},{10,11... | collective-permute-start | bytes 3932168 | tf_op jit(solution)/shard_map/ppermute | solution.py:113
  182.1 3.4 %collective-permute-start.22 = (bf16[2,256,1280]{2,1,0:T(8,128)(2,1)}, bf16[2,256,1280]{2,1,0:T(8,128)(2,1)}, u32[]{:S(2)}, u32[]{:S(2)}) collective-permute-start(bf16[2,256,1280]{2,1,0:T(8,128)(2,1)} %pad_maximum_fusion.18), channel_id=1, source_target_pairs={{0,1},{1,0},{2,3},{3,2},{4,5},{5,4},{6,7},{7,6},{8,9},{9,8},{10,11... | collective-permute-start | bytes 3932168 | tf_op jit(solution)/shard_map/ppermute | solution.py:113
  (21 other events, 78.7 us)

commit v13 on v10

--- a/solution.py
+++ b/solution.py
@@ -65,11 +65,14 @@
     return jnp.stack([x] + shifted)
 
 
-def gather_start(weights):
+def gather_first(weights):
     near = swap(weights, "xl")
     peer = swap(weights, "xh")
     diagonal = lax.ppermute(weights, ("xl", "xh"), [(k, 3 - k) for k in range(4)])
-    halves = (jnp.stack([weights, near]), jnp.stack([peer, diagonal]))
+    return (jnp.stack([weights, near]), jnp.stack([peer, diagonal]))
+
+
+def gather_start(halves):
     return [ring_direct(part, first, 4) for part, (first, _) in zip(halves, STAGES)]
 
 
@@ -142,10 +145,11 @@
     half = lax.axis_index("xh")
     core = lax.axis_index("c")
     heads_here = H // 2
-    parts = gather_start(weights)
-    parts, query_heads = lax.optimization_barrier(
-        (parts, queries[0].reshape(tokens_here, H, HEAD))
-    )
+    halves = gather_first(weights)
+    halves, query_heads = lax.optimization_barrier(
+        (halves, queries[0].reshape(tokens_here, H, HEAD))
+    )
+    parts = gather_start(halves)
     query_group = pair_exchange(query_heads, core, 1, 0)
     sent = [ring_send(part, second, 4) for part, (_, second) in zip(parts, STAGES)]
     key_group = pair_exchange(keys_in[0].reshape(tokens_here, H, HEAD), core, 1, 0)
@@ -177,12 +181,12 @@
         "cihf,chfe->cihe", query_blocks, before, preferred_element_type=jnp.float32
     )
     attended = (inside_block + from_before).reshape(span, heads_here, HEAD)
-    sent, attended = lax.optimization_barrier((sent, attended))
     gain_rows = lax.dynamic_slice_in_dim(head_gain, core * heads_here, heads_here, 0)
     normed_group = normalize(attended, gain_rows)
     normed_own = pair_exchange(normed_group, core, 0, 1)
     normed_own = normed_own.reshape(tokens_here, H * HEAD)
     tokens = jnp.concatenate([normed_own, swap(normed_own, "c")], axis=0)
+    sent, tokens = lax.optimization_barrier((sent, tokens))
     by_block = tokens.reshape(tokens.shape[0], 32, -1)
     wide = []
     for rows, source in gather_finish(parts, sent):

time: 188 us -> 216 us (1.15); the launches traced: 187 us -> 212 us
  waiting for transfers between devices: 36.8 us -> 69.7 us
  local copies, waits for them, and re-layouts: 42.4 us -> 38.4 us
  other arithmetic: 45.4 us -> 42.4 us
    ppermute x1, waiting for transfers between devices: 0.01 us -> 15.2 us  [on_device(): earlier = lax.ppermute(chip_total, 'xh', [(0, 1)])]
    ppermute x2, waiting for transfers between devices: 1.38 us -> 12.4 us  [ring_far(): lax.ppermute(from_left[:half], axis, forward)]
    ppermute x6, waiting for transfers between devices: 9.95 us -> 20.4 us  [ring_direct(): lax.ppermute(x, axis, [(k, (k + shift) % size) for k in range(size)])]
    dot_general x2, matrix products: 13 us -> 7.24 us  [on_device(): jnp.dot(features, rows, preferred_element_type=jnp.float32)]
    ppermute x4, waiting for transfers between devices: 12.3 us -> 8.89 us  [ring_send(): return (lax.ppermute(x, axis, forward), lax.ppermute(x, axis, backward))]
    another operation x5 -> x3, other arithmetic: 9.35 us -> 5.99 us  [the longest x4 4.93 us: ring_direct(): return jnp.stack([x] + shifted)]
    ppermute x4, starting transfers between devices: 4.14 us -> 7.14 us  [ring_send(): return (lax.ppermute(x, axis, forward), lax.ppermute(x, axis, backward))]
    select_n x2, other arithmetic: 3.32 us -> 0.59 us  [pair_exchange(): jnp.where(core == 0, jnp.concatenate([mine, received], axis=join_axis), j...]
  transfers between devices with their start and end apart: 25 -> 25, of which waited for: 11 -> 14; matrix products, arithmetic and copies ran while one was open for 41% -> 35% of each run, Pallas kernels for 0% -> 0%
where the time goes in v13:
time: 216 us; the launch traced here: 212 us
  waiting for transfers between devices  69.7 us (32%)
  other arithmetic  42.4 us (20%)
  starting transfers between devices  39.1 us (18%)
  local copies, waits for them, and re-layouts  38.4 us (18%)
  matrix products  21.8 us (10%)
    ppermute x6, waiting for transfers between devices, ring_direct(): lax.ppermute(x, axis, [(k, (k + shift) % size) for k in range(size)])  20.4 us
    ppermute x1, waiting for transfers between devices, on_device(): earlier = lax.ppermute(chip_total, 'xh', [(0, 1)])  15.2 us
    ppermute x2, waiting for transfers between devices, ring_far(): lax.ppermute(from_left[:half], axis, forward)  12.4 us
    max x4, local copies, waits for them, and re-layouts, featurize(): rectified = jnp.maximum(block.astype(jnp.float32), 0.0)  11.9 us
    ppermute x9, starting transfers between devices, swap(): return lax.ppermute(x, axis, [(0, 1), (1, 0)])  11.9 us
    another operation x4, other arithmetic, ring_finish(): return jnp.stack((x,) + tuple(received))  11.4 us
    ppermute x6, starting transfers between devices, ring_direct(): lax.ppermute(x, axis, [(k, (k + shift) % size) for k in range(size)])  10.9 us
    ppermute x4, waiting for transfers between devices, ring_send(): return (lax.ppermute(x, axis, forward), lax.ppermute(x, axis, backward))  8.89 us
  transfers between devices with their start and end apart: 25, of which 14 were waited for; matrix products, arithmetic and copies ran while one was open for 35% of the time, Pallas kernels for 0%

profile of v13, /device:TPU:1, one launch (start us, length us, event | category | flops | bytes accessed | tf_op | source)
XLA Modules:
  0.0 212.4 jit_solution(6876470127004391649)
XLA Ops:
  3.4 3.6 %collective-permute-start.1 = (bf16[80,1280]{1,0:T(8,128)(2,1)S(1)}, bf16[80,1280]{1,0:T(8,128)(2,1)S(1)}, u32[]{:S(2)}, u32[]{:S(2)}) collective-permute-start(bf16[80,1280]{1,0:T(8,128)(2,1)S(1)} %get-tuple-element.93), channel_id=1, source_target_pairs={{0,2},{2,0},{1,3},{3,1},{4,6},{6,4},{5,7},{7,5},{8,10},{10,8},{9,1... | collective-permute-start | bytes 614408 | tf_op jit(solution)/shard_map/ppermute | solution.py:116
  11.2 5.6 %collective-permute-done.2 = bf16[80,1280]{1,0:T(8,128)(2,1)S(1)} collective-permute-done((bf16[80,1280]{1,0:T(8,128)(2,1)S(1)}, bf16[80,1280]{1,0:T(8,128)(2,1)S(1)}, u32[]{:S(2)}, u32[]{:S(2)}) %collective-permute-start.2) | collective-permute-done | bytes 204832 | tf_op jit(solution)/shard_map/ppermute | solution.py:71
  20.3 3.3 %collective-permute-start.9 = (bf16[2,80,1280]{2,1,0:T(8,128)(2,1)}, bf16[2,80,1280]{2,1,0:T(8,128)(2,1)}, u32[]{:S(2)}, u32[]{:S(2)}) collective-permute-start(bf16[2,80,1280]{2,1,0:T(8,128)(2,1)} %pad_maximum_fusion.18), channel_id=1, source_target_pairs={{0,64},{32,96},{64,0},{96,32},{1,65},{33,97},{65,1},{97,33},{2,66}... | collective-permute-start | bytes 1228808 | tf_op jit(solution)/shard_map/ppermute | solution.py:62
  33.5 8.3 %collective-permute-done.9 = bf16[2,80,1280]{2,1,0:T(8,128)(2,1)} collective-permute-done((bf16[2,80,1280]{2,1,0:T(8,128)(2,1)}, bf16[2,80,1280]{2,1,0:T(8,128)(2,1)}, u32[]{:S(2)}, u32[]{:S(2)}) %collective-permute-start.9) | collective-permute-done | bytes 409632 | tf_op jit(solution)/shard_map/ppermute | solution.py:62
  46.5 3.4 %fusion.33 = (bf16[1,4,2,80,1280]{4,3,2,1,0:T(8,128)(2,1)}, bf16[4,2,80,1280]{3,2,1,0:T(8,128)(2,1)}) fusion(bf16[1,2,80,1280]{3,2,1,0:T(8,128)(2,1)} %bitcast.16, bf16[1,2,80,1280]{3,2,1,0:T(8,128)(2,1)} %bitcast.15, bf16[1,2,80,1280]{3,2,1,0:T(8,128)(2,1)} %bitcast.14, bf16[1,2,80,1280]{3,2,1,0:T(8,128)(2,1)} %bitcast.13), kind=kLoop, calls=%fused_computation.115 | loop fusion | flops 2457600 | bytes 4915200 | tf_op jit(solution)/shard_map/stack | solution.py:50
  54.5 8.6 %collective-permute-done.5 = bf16[2,80,1280]{2,1,0:T(8,128)(2,1)S(1)} collective-permute-done((bf16[2,80,1280]{2,1,0:T(8,128)(2,1)}, bf16[2,80,1280]{2,1,0:T(8,128)(2,1)S(1)}, u32[]{:S(2)}, u32[]{:S(2)}) %collective-permute-start.5) | collective-permute-done | bytes 409632 | tf_op jit(solution)/shard_map/ppermute | solution.py:62
  63.1 3.3 %collective-permute-start.12 = (bf16[4,2,80,1280]{3,2,1,0:T(8,128)(2,1)}, bf16[4,2,80,1280]{3,2,1,0:T(8,128)(2,1)}, u32[]{:S(2)}, u32[]{:S(2)}) collective-permute-start(bf16[4,2,80,1280]{3,2,1,0:T(8,128)(2,1)} %get-tuple-element.102), channel_id=1, source_target_pairs={{0,12},{4,0},{8,4},{12,8},{1,13},{5,1},{9,5},{13,9},{2,14},{6,2},{... | collective-permute-start | bytes 4915208 | tf_op jit(solution)/shard_map/ppermute | solution.py:29
  73.0 3.9 %convert_maximum_fusion = (f32[512,10,128]{0,2,1:T(8,128)S(1)}, f32[512,10,128]{0,2,1:T(8,128)}) fusion(bf16[256,10,128]{0,2,1:T(8,128)(2,1)} %collective-permute-done.19, bf16[256,10,128]{0,2,1:T(8,128)(2,1)} %get-tuple-element.111, pred[]{:T(512)S(6)} %eq.17, bf16[256,10,128]{0,2,1:T(8,128)(2,1)S(1)} %copy-done.14, ...), kind=kLoop, calls=%fused_computation.24 | loop fusion | flops 14417920 | bytes 7864321 | tf_op jit(solution)/shard_map/max | solution.py:100
  76.9 3.2 %copy.47 = f32[512,10,128]{2,0,1:T(8,128)} copy(f32[512,10,128]{0,2,1:T(8,128)} %get-tuple-element.126) | data formatting | bytes 5242880 | tf_op jit(solution)/shard_map/max | solution.py:100
  80.1 3.2 %copy.48 = f32[4,128,10,128]{1,3,2,0:T(8,128)} copy(f32[4,128,10,128]{3,1,0,2:T(8,128)} %bitcast.68) | data formatting | bytes 5242880 | tf_op jit(solution)/shard_map/max | solution.py:100
  85.4 3.4 %copy.54 = f32[4,128,10,128]{1,3,2,0:T(8,128)} copy(f32[4,128,10,128]{3,1,0,2:T(8,128)} %bitcast.69) | data formatting | bytes 5242880 | tf_op jit(solution)/shard_map/max | solution.py:100
  88.8 4.4 %multiply_convert_fusion.3 = (bf16[4,128,10,128]{1,3,2,0:T(8,128)(2,1)S(1)}, bf16[4,128,10,128]{1,3,2,0:T(8,128)(2,1)S(1)}, bf16[4,128,10,128]{1,3,2,0:T(8,128)(2,1)}, bf16[4,128,10,128]{1,3,2,0:T(8,128)(2,1)}) fusion(f32[4,128,10,128]{1,3,2,0:T(8,128)S(1)} %copy-done.2, f32[4,128]{1,0:T(4,128)S(1)} %get-tuple-element.128, ...), kind=kLoop, calls=%fused_computation.26 | loop fusion | flops 5242880 | bytes 10489856 | tf_op jit(solution)/shard_map/convert.2
  93.2 4.5 %fusion.39 = (f32[10,256,128]{2,1,0:T(8,128)}, f32[4,10,256,128]{3,2,1,0:T(8,128)}) fusion(bf16[4,128,10,128]{3,1,0,2:T(8,128)(2,1)S(1)} %bitcast.75, bf16[4,128,10,128]{1,3,2,0:T(8,128)(2,1)S(1)} %get-tuple-element.100, bf16[4,128,10,128]{1,3,2,0:T(8,128)(2,1)S(1)} %get-tuple-element.99), kind=kOutput, calls=%fused_computation.120 | convolution fusion | flops 341770240 | bytes 10485760 | tf_op jit(solution)/shard_map/cjhf,cjhe->chfe/dot_general | solution.py:162
  97.6 3.8 %collective-permute-done.12 = bf16[4,2,80,1280]{3,2,1,0:T(8,128)(2,1)} collective-permute-done((bf16[4,2,80,1280]{3,2,1,0:T(8,128)(2,1)}, bf16[4,2,80,1280]{3,2,1,0:T(8,128)(2,1)}, u32[]{:S(2)}, u32[]{:S(2)}) %collective-permute-start.12) | collective-permute-done | bytes 1638432 | tf_op jit(solution)/shard_map/ppermute | solution.py:29
  101.4 5.1 %collective-permute-done.6 = bf16[4,2,80,1280]{3,2,1,0:T(8,128)(2,1)} collective-permute-done((bf16[4,2,80,1280]{3,2,1,0:T(8,128)(2,1)}, bf16[4,2,80,1280]{3,2,1,0:T(8,128)(2,1)}, u32[]{:S(2)}, u32[]{:S(2)}) %collective-permute-start.6) | collective-permute-done | bytes 1638432 | tf_op jit(solution)/shard_map/ppermute | solution.py:29
  106.5 3.0 %collective-permute-start.20 = (f32[10,256,128]{2,1,0:T(8,128)}, f32[10,256,128]{2,1,0:T(8,128)}, u32[]{:S(2)}, u32[]{:S(2)}) collective-permute-start(f32[10,256,128]{2,1,0:T(8,128)} %get-tuple-element.81), channel_id=1, source_target_pairs={{0,2},{1,3},{4,6},{5,7},{8,10},{9,11},{12,14},{13,15},{16,18},{17,... | collective-permute-start | bytes 3932168 | tf_op jit(solution)/shard_map/ppermute | solution.py:168
  109.6 3.0 %fusion.40 = f32[4,10,256,128]{3,2,1,0:T(8,128)S(1)} fusion(f32[4,10,256,128]{3,2,1,0:T(8,128)} %get-tuple-element.120), kind=kOutput, calls=%fused_computation.121 | output fusion | flops 3932160 | bytes 10485760 | tf_op jit(solution)/shard_map/jit(cumsum)/reduce_window_sum | solution.py:177
  115.2 4.9 %fusion.5 = f32[4,10,128,128]{2,3,1,0:T(8,128)} fusion(bf16[4,128,10,128]{1,3,2,0:T(8,128)(2,1)S(1)} %copy-done.7, bf16[4,128,10,128]{1,3,2,0:T(8,128)(2,1)S(1)} %copy-done.8, bf16[4,128,10,128]{1,3,2,0:T(8,128)(2,1)} %copy-done.10, bf16[4,128,10,128]{1,3,2,0:T(8,128)(2,1)} %copy-done.9, pred[128,128]{1,0:T(8,128)(4,1)S(1)} %iota_compare_fusion, ...), kind=kOutput, calls=%fused_computation.35 | convolution fusion | flops 515112960 | bytes 9191424 | tf_op jit(solution)/shard_map/chij,cjhe->cihe/dot_general | solution.py:174
  120.0 15.2 %collective-permute-done.20 = f32[10,256,128]{2,1,0:T(8,128)} collective-permute-done((f32[10,256,128]{2,1,0:T(8,128)}, f32[10,256,128]{2,1,0:T(8,128)}, u32[]{:S(2)}, u32[]{:S(2)}) %collective-permute-start.20) | collective-permute-done | bytes 1310752 | tf_op jit(solution)/shard_map/ppermute | solution.py:168
  135.2 5.2 %multiply_reduce_fusion = (f32[4,128,10]{1,2,0:T(8,128)S(1)}, f32[4,128,10,128]{3,1,2,0:T(8,128)S(1)}) fusion(f32[4,10,128,128]{2,3,1,0:T(8,128)} %fusion.5, bf16[4,128,10,128]{1,3,2,0:T(8,128)(2,1)S(1)} %copy-done.7, bf16[4,128,10,128]{1,3,2,0:T(8,128)(2,1)S(1)} %copy-done.8, f32[3,10,256,128]{3,2,1,0:T(8,128)} %slice.40, ...), kind=kOutput, calls=%fused_computation.18 | convolution fusion | flops 345369600 | bytes 13127680 | tf_op jit(solution)/shard_map/cihf,chfe->cihe/dot_general | solution.py:180
  159.8 8.1 %collective-permute-done.17 = bf16[2,2,80,1280]{3,2,1,0:T(8,128)(2,1)S(1)} collective-permute-done((bf16[2,2,80,1280]{3,2,1,0:T(8,128)(2,1)}, bf16[2,2,80,1280]{3,2,1,0:T(8,128)(2,1)S(1)}, u32[]{:S(2)}, u32[]{:S(2)}) %collective-permute-start.17) | collective-permute-done | bytes 819232 | tf_op jit(solution)/shard_map/ppermute | solution.py:41
  171.5 4.3 %collective-permute-done.15 = bf16[2,2,80,1280]{3,2,1,0:T(8,128)(2,1)S(1)} collective-permute-done((bf16[2,2,80,1280]{3,2,1,0:T(8,128)(2,1)}, bf16[2,2,80,1280]{3,2,1,0:T(8,128)(2,1)S(1)}, u32[]{:S(2)}, u32[]{:S(2)}) %collective-permute-start.15) | collective-permute-done | bytes 819232 | tf_op jit(solution)/shard_map/ppermute | solution.py:41
  188.9 3.6 %convolution_convert_fusion = bf16[512,1280]{1,0:T(8,128)(2,1)S(1)} fusion(bf16[512,2560]{0,1:T(8,128)(2,1)S(1)} %bitcast.81, bf16[2560,1280]{1,0:T(8,128)(2,1)S(1)} %bitcast.72), kind=kOutput, calls=%fused_computation.9 | convolution fusion | flops 3356098560 | bytes 10485760 | tf_op jit(solution)/shard_map/dot_general | solution.py:195
  202.9 3.6 %convolution_convert_fusion.1 = bf16[512,1280]{1,0:T(8,128)(2,1)S(1)} fusion(bf16[512,2560]{0,1:T(8,128)(2,1)S(1)} %bitcast.82, bf16[2560,1280]{1,0:T(8,128)(2,1)S(1)} %bitcast.73), kind=kOutput, calls=%fused_computation.10 | convolution fusion | flops 3356098560 | bytes 10485760 | tf_op jit(solution)/shard_map/dot_general | solution.py:195
  (118 shorter events, 95.8 us)
Async XLA Ops:
  3.4 7.9 %collective-permute-start.1 = (bf16[80,1280]{1,0:T(8,128)(2,1)S(1)}, bf16[80,1280]{1,0:T(8,128)(2,1)S(1)}, u32[]{:S(2)}, u32[]{:S(2)}) collective-permute-start(bf16[80,1280]{1,0:T(8,128)(2,1)S(1)} %get-tuple-element.93), channel_id=1, source_target_pairs={{0,2},{2,0},{1,3},{3,1},{4,6},{6,4},{5,7},{7,5},{8,10},{10,8},{9,1... | collective-permute-start | bytes 614408 | tf_op jit(solution)/shard_map/ppermute | solution.py:116
  6.9 9.9 %collective-permute-start.2 = (bf16[80,1280]{1,0:T(8,128)(2,1)S(1)}, bf16[80,1280]{1,0:T(8,128)(2,1)S(1)}, u32[]{:S(2)}, u32[]{:S(2)}) collective-permute-start(bf16[80,1280]{1,0:T(8,128)(2,1)S(1)} %get-tuple-element.93), channel_id=1, source_target_pairs={{0,18},{2,16},{16,2},{18,0},{1,19},{3,17},{17,3},{19,1},{4,22},{6,... | collective-permute-start | bytes 614408 | tf_op jit(solution)/shard_map/ppermute | solution.py:71
  7.8 9.9 %collective-permute-start = (bf16[80,1280]{1,0:T(8,128)(2,1)S(1)}, bf16[80,1280]{1,0:T(8,128)(2,1)S(1)}, u32[]{:S(2)}, u32[]{:S(2)}) collective-permute-start(bf16[80,1280]{1,0:T(8,128)(2,1)S(1)} %get-tuple-element.93), channel_id=1, source_target_pairs={{0,16},{16,0},{1,17},{17,1},{2,18},{18,2},{3,19},{19,3},{4,20},{20... | collective-permute-start | bytes 614408 | tf_op jit(solution)/shard_map/ppermute | solution.py:116
  18.5 13.7 %collective-permute-start.8 = (bf16[2,80,1280]{2,1,0:T(8,128)(2,1)}, bf16[2,80,1280]{2,1,0:T(8,128)(2,1)}, u32[]{:S(2)}, u32[]{:S(2)}) collective-permute-start(bf16[2,80,1280]{2,1,0:T(8,128)(2,1)} %pad_maximum_fusion.18), channel_id=1, source_target_pairs={{0,32},{32,64},{64,96},{96,0},{1,33},{33,65},{65,97},{97,1},{2,34}... | collective-permute-start | bytes 1228808 | tf_op jit(solution)/shard_map/ppermute | solution.py:62
  20.3 21.5 %collective-permute-start.9 = (bf16[2,80,1280]{2,1,0:T(8,128)(2,1)}, bf16[2,80,1280]{2,1,0:T(8,128)(2,1)}, u32[]{:S(2)}, u32[]{:S(2)}) collective-permute-start(bf16[2,80,1280]{2,1,0:T(8,128)(2,1)} %pad_maximum_fusion.18), channel_id=1, source_target_pairs={{0,64},{32,96},{64,0},{96,32},{1,65},{33,97},{65,1},{97,33},{2,66}... | collective-permute-start | bytes 1228808 | tf_op jit(solution)/shard_map/ppermute | solution.py:62
  23.6 21.1 %collective-permute-start.10 = (bf16[2,80,1280]{2,1,0:T(8,128)(2,1)}, bf16[2,80,1280]{2,1,0:T(8,128)(2,1)}, u32[]{:S(2)}, u32[]{:S(2)}) collective-permute-start(bf16[2,80,1280]{2,1,0:T(8,128)(2,1)} %pad_maximum_fusion.18), channel_id=1, source_target_pairs={{0,96},{32,0},{64,32},{96,64},{1,97},{33,1},{65,33},{97,65},{2,98}... | collective-permute-start | bytes 1228808 | tf_op jit(solution)/shard_map/ppermute | solution.py:62
  27.1 41.3 %collective-permute-start.13 = (bf16[256,10,128]{0,2,1:T(8,128)(2,1)}, bf16[256,10,128]{0,2,1:T(8,128)(2,1)}, u32[]{:S(2)}, u32[]{:S(2)}) collective-permute-start(bf16[256,10,128]{0,2,1:T(8,128)(2,1)} %get-tuple-element.116), channel_id=1, source_target_pairs={{0,1},{1,0},{2,3},{3,2},{4,5},{5,4},{6,7},{7,6},{8,9},{9,8},{10,11... | collective-permute-start | bytes 1966088 | tf_op jit(solution)/shard_map/ppermute | solution.py:116
  30.2 38.3 %collective-permute-start.14 = (bf16[256,10,128]{0,2,1:T(8,128)(2,1)S(1)}, bf16[256,10,128]{0,2,1:T(8,128)(2,1)S(1)}, u32[]{:S(2)}, u32[]{:S(2)}) collective-permute-start(bf16[256,10,128]{0,2,1:T(8,128)(2,1)S(1)} %get-tuple-element.114), channel_id=1, source_target_pairs={{0,1},{1,0},{2,3},{3,2},{4,5},{5,4},{6,7},{7,6},{8,9},{9,8},{10,11... | collective-permute-start | bytes 1966088 | tf_op jit(solution)/shard_map/ppermute | solution.py:116
  32.2 17.7 %collective-permute-start.3 = (bf16[2,80,1280]{2,1,0:T(8,128)(2,1)}, bf16[2,80,1280]{2,1,0:T(8,128)(2,1)S(1)}, u32[]{:S(2)}, u32[]{:S(2)}) collective-permute-start(bf16[2,80,1280]{2,1,0:T(8,128)(2,1)} %pad_maximum_fusion.17), channel_id=1, source_target_pairs={{0,4},{4,8},{8,12},{12,0},{1,5},{5,9},{9,13},{13,1},{2,6},{6,10},{... | collective-permute-start | bytes 1228808 | tf_op jit(solution)/shard_map/ppermute | solution.py:62
  41.8 11.5 %collective-permute-start.4 = (bf16[2,80,1280]{2,1,0:T(8,128)(2,1)}, bf16[2,80,1280]{2,1,0:T(8,128)(2,1)S(1)}, u32[]{:S(2)}, u32[]{:S(2)}) collective-permute-start(bf16[2,80,1280]{2,1,0:T(8,128)(2,1)} %pad_maximum_fusion.17), channel_id=1, source_target_pairs={{0,8},{4,12},{8,0},{12,4},{1,9},{5,13},{9,1},{13,5},{2,10},{6,14},... | collective-permute-start | bytes 1228808 | tf_op jit(solution)/shard_map/ppermute | solution.py:62
  44.7 18.4 %collective-permute-start.5 = (bf16[2,80,1280]{2,1,0:T(8,128)(2,1)}, bf16[2,80,1280]{2,1,0:T(8,128)(2,1)S(1)}, u32[]{:S(2)}, u32[]{:S(2)}) collective-permute-start(bf16[2,80,1280]{2,1,0:T(8,128)(2,1)} %pad_maximum_fusion.17), channel_id=1, source_target_pairs={{0,12},{4,0},{8,4},{12,8},{1,13},{5,1},{9,5},{13,9},{2,14},{6,2},{... | collective-permute-start | bytes 1228808 | tf_op jit(solution)/shard_map/ppermute | solution.py:62
  49.9 23.1 %collective-permute-start.19 = (bf16[256,10,128]{0,2,1:T(8,128)(2,1)S(1)}, bf16[256,10,128]{0,2,1:T(8,128)(2,1)}, u32[]{:S(2)}, u32[]{:S(2)}) collective-permute-start(bf16[256,10,128]{0,2,1:T(8,128)(2,1)S(1)} %get-tuple-element.112), channel_id=1, source_target_pairs={{0,1},{1,0},{2,3},{3,2},{4,5},{5,4},{6,7},{7,6},{8,9},{9,8},{10,11... | collective-permute-start | bytes 1966088 | tf_op jit(solution)/shard_map/ppermute | solution.py:116
  53.3 44.3 %collective-permute-start.11 = (bf16[4,2,80,1280]{3,2,1,0:T(8,128)(2,1)}, bf16[4,2,80,1280]{3,2,1,0:T(8,128)(2,1)}, u32[]{:S(2)}, u32[]{:S(2)}) collective-permute-start(bf16[4,2,80,1280]{3,2,1,0:T(8,128)(2,1)} %get-tuple-element.102), channel_id=1, source_target_pairs={{0,4},{4,8},{8,12},{12,0},{1,5},{5,9},{9,13},{13,1},{2,6},{6,10},{... | collective-permute-start | bytes 4915208 | tf_op jit(solution)/shard_map/ppermute | solution.py:29
  63.1 38.3 %collective-permute-start.12 = (bf16[4,2,80,1280]{3,2,1,0:T(8,128)(2,1)}, bf16[4,2,80,1280]{3,2,1,0:T(8,128)(2,1)}, u32[]{:S(2)}, u32[]{:S(2)}) collective-permute-start(bf16[4,2,80,1280]{3,2,1,0:T(8,128)(2,1)} %get-tuple-element.102), channel_id=1, source_target_pairs={{0,12},{4,0},{8,4},{12,8},{1,13},{5,1},{9,5},{13,9},{2,14},{6,2},{... | collective-permute-start | bytes 4915208 | tf_op jit(solution)/shard_map/ppermute | solution.py:29
  68.5 38.1 %collective-permute-start.6 = (bf16[4,2,80,1280]{3,2,1,0:T(8,128)(2,1)}, bf16[4,2,80,1280]{3,2,1,0:T(8,128)(2,1)}, u32[]{:S(2)}, u32[]{:S(2)}) collective-permute-start(bf16[4,2,80,1280]{3,2,1,0:T(8,128)(2,1)} %get-tuple-element.104), channel_id=1, source_target_pairs={{0,32},{32,64},{64,96},{96,0},{1,33},{33,65},{65,97},{97,1},{2,34}... | collective-permute-start | bytes 4915208 | tf_op jit(solution)/shard_map/ppermute | solution.py:29
  68.5 38.1 %collective-permute-start.7 = (bf16[4,2,80,1280]{3,2,1,0:T(8,128)(2,1)}, bf16[4,2,80,1280]{3,2,1,0:T(8,128)(2,1)}, u32[]{:S(2)}, u32[]{:S(2)}) collective-permute-start(bf16[4,2,80,1280]{3,2,1,0:T(8,128)(2,1)} %get-tuple-element.104), channel_id=1, source_target_pairs={{0,96},{32,0},{64,32},{96,64},{1,97},{33,1},{65,33},{97,65},{2,98}... | collective-permute-start | bytes 4915208 | tf_op jit(solution)/shard_map/ppermute | solution.py:29
  106.5 28.6 %collective-permute-start.20 = (f32[10,256,128]{2,1,0:T(8,128)}, f32[10,256,128]{2,1,0:T(8,128)}, u32[]{:S(2)}, u32[]{:S(2)}) collective-permute-start(f32[10,256,128]{2,1,0:T(8,128)} %get-tuple-element.81), channel_id=1, source_target_pairs={{0,2},{1,3},{4,6},{5,7},{8,10},{9,11},{12,14},{13,15},{16,18},{17,... | collective-permute-start | bytes 3932168 | tf_op jit(solution)/shard_map/ppermute | solution.py:168
  141.8 9.5 %collective-permute-start.21 = (bf16[256,10,128]{2,0,1:T(8,128)(2,1)S(1)}, bf16[256,10,128]{2,0,1:T(8,128)(2,1)S(1)}, u32[]{:S(2)}, u32[]{:S(2)}) collective-permute-start(bf16[256,10,128]{2,0,1:T(8,128)(2,1)S(1)} %get-tuple-element.110), channel_id=1, source_target_pairs={{0,1},{1,0},{2,3},{3,2},{4,5},{5,4},{6,7},{7,6},{8,9},{9,8},{10,11... | collective-permute-start | bytes 1966088 | tf_op jit(solution)/shard_map/ppermute | solution.py:116
  146.6 21.3 %collective-permute-start.17 = (bf16[2,2,80,1280]{3,2,1,0:T(8,128)(2,1)}, bf16[2,2,80,1280]{3,2,1,0:T(8,128)(2,1)S(1)}, u32[]{:S(2)}, u32[]{:S(2)}) collective-permute-start(bf16[2,2,80,1280]{3,2,1,0:T(8,128)(2,1)} %slice.29), channel_id=1, source_target_pairs={{0,4},{4,8},{8,12},{12,0},{1,5},{5,9},{9,13},{13,1},{2,6},{6,10},{... | collective-permute-start | bytes 2457608 | tf_op jit(solution)/shard_map/ppermute | solution.py:41
  148.7 20.3 %collective-permute-start.18 = (bf16[2,2,80,1280]{3,2,1,0:T(8,128)(2,1)}, bf16[2,2,80,1280]{3,2,1,0:T(8,128)(2,1)}, u32[]{:S(2)}, u32[]{:S(2)}) collective-permute-start(bf16[2,2,80,1280]{3,2,1,0:T(8,128)(2,1)} %slice.30), channel_id=1, source_target_pairs={{0,12},{4,0},{8,4},{12,8},{1,13},{5,1},{9,5},{13,9},{2,14},{6,2},{... | collective-permute-start | bytes 2457608 | tf_op jit(solution)/shard_map/ppermute | solution.py:42
  152.2 27.2 %collective-permute-start.22 = (bf16[256,2560]{0,1:T(8,128)(2,1)S(1)}, bf16[256,2560]{0,1:T(8,128)(2,1)}, u32[]{:S(2)}, u32[]{:S(2)}) collective-permute-start(bf16[256,2560]{0,1:T(8,128)(2,1)S(1)} %bitcast.76), channel_id=1, source_target_pairs={{0,1},{1,0},{2,3},{3,2},{4,5},{5,4},{6,7},{7,6},{8,9},{9,8},{10,11... | collective-permute-start | bytes 3932168 | tf_op jit(solution)/shard_map/ppermute | solution.py:116
  155.0 20.8 %collective-permute-start.15 = (bf16[2,2,80,1280]{3,2,1,0:T(8,128)(2,1)}, bf16[2,2,80,1280]{3,2,1,0:T(8,128)(2,1)S(1)}, u32[]{:S(2)}, u32[]{:S(2)}) collective-permute-start(bf16[2,2,80,1280]{3,2,1,0:T(8,128)(2,1)} %slice.27), channel_id=1, source_target_pairs={{0,32},{32,64},{64,96},{96,0},{1,33},{33,65},{65,97},{97,1},{2,34}... | collective-permute-start | bytes 2457608 | tf_op jit(solution)/shard_map/ppermute | solution.py:41
  157.1 19.9 %collective-permute-start.16 = (bf16[2,2,80,1280]{3,2,1,0:T(8,128)(2,1)}, bf16[2,2,80,1280]{3,2,1,0:T(8,128)(2,1)}, u32[]{:S(2)}, u32[]{:S(2)}) collective-permute-start(bf16[2,2,80,1280]{3,2,1,0:T(8,128)(2,1)} %slice.28), channel_id=1, source_target_pairs={{0,96},{32,0},{64,32},{96,64},{1,97},{33,1},{65,33},{97,65},{2,98}... | collective-permute-start | bytes 2457608 | tf_op jit(solution)/shard_map/ppermute | solution.py:42
  193.4 13.3 %collective-permute-start.24 = (bf16[256,1280]{1,0:T(8,128)(2,1)}, bf16[256,1280]{1,0:T(8,128)(2,1)}, u32[]{:S(2)}, u32[]{:S(2)}) collective-permute-start(bf16[256,1280]{1,0:T(8,128)(2,1)} %get-tuple-element.105), channel_id=1, source_target_pairs={{0,1},{1,0},{2,3},{3,2},{4,5},{5,4},{6,7},{7,6},{8,9},{9,8},{10,11... | collective-permute-start | bytes 1966088 | tf_op jit(solution)/shard_map/ppermute | solution.py:116
  (18 other events, 194.7 us)

commit v14 on v10

--- a/solution.py
+++ b/solution.py
@@ -21,37 +21,24 @@
 norm_eps = 1e-06
 
 
-def ring_send(x, axis, size):
-    if size == 2:
-        return (lax.ppermute(x, axis, [(0, 1), (1, 0)]),)
+def ring_send(halves, axis, size):
     forward = [(k, (k + 1) % size) for k in range(size)]
     backward = [(k, (k - 1) % size) for k in range(size)]
-    return (lax.ppermute(x, axis, forward), lax.ppermute(x, axis, backward))
+    return tuple(lax.ppermute(half, axis, perm) for perm in (forward, backward) for half in halves)
 
 
 def ring_far(received, axis, size):
-    if size == 2:
-        return received
     forward = [(k, (k + 1) % size) for k in range(size)]
     backward = [(k, (k - 1) % size) for k in range(size)]
-    from_left, from_right = received
-    half = from_left.shape[0] // 2
-    far = jnp.concatenate(
-        [
-            lax.ppermute(from_left[:half], axis, forward),
-            lax.ppermute(from_right[half:], axis, backward),
-        ],
-        axis=0,
-    )
-    return (from_left, far, from_right)
-
-
-def ring_finish(x, received):
-    return jnp.stack((x,) + tuple(received))
-
-
-def ring_gather(x, axis, size):
-    return ring_finish(x, ring_far(ring_send(x, axis, size), axis, size))
+    left_a, left_b, right_a, right_b = received
+    far_a = lax.ppermute(left_a, axis, forward)
+    far_b = lax.ppermute(right_b, axis, backward)
+    return (left_a, left_b, far_a, far_b, right_a, right_b)
+
+
+def ring_finish(halves, received):
+    pieces = jnp.stack(tuple(halves) + tuple(received))
+    return pieces.reshape((4, pieces.shape[1] * 2) + pieces.shape[2:])
 
 
 STAGES = (("y", "z"), ("z", "y"))
@@ -62,7 +49,7 @@
         lax.ppermute(x, axis, [(k, (k + shift) % size) for k in range(size)])
         for shift in (1, 2, 3)
     ]
-    return jnp.stack([x] + shifted)
+    return (jnp.stack([x, shifted[0]]), jnp.stack([shifted[1], shifted[2]]))
 
 
 def gather_start(weights):

time: 188 us -> 209 us (1.11)
  local copies, waits for them, and re-layouts: 42.4 us -> 57.7 us
  other arithmetic: 45.4 us -> 31.8 us
  waiting for transfers between devices: 36.8 us -> 48.1 us
  starting transfers between devices: 38.3 us -> 43.3 us
    unnamed x41 -> x48, local copies, waits for them, and re-layouts: 8.06 us -> 29.1 us
    another operation x7, other arithmetic: 20.9 us -> 11.6 us  [the longest x6 7.23 us: ring_direct(): return (jnp.stack([x, shifted[0]]), jnp.stack([shifted[1], shifted[2]]))]
    slice x4 -> x0, local copies, waits for them, and re-layouts: 8.46 us -> none  [the longest x2 4.23 us: ring_far(): from_right[half:]]
    ppermute x6, waiting for transfers between devices: 9.95 us -> 17.9 us  [ring_direct(): lax.ppermute(x, axis, [(k, (k + shift) % size) for k in range(size)])]
    ppermute x1, waiting for transfers between devices: 0.01 us -> 6.05 us  [on_device(): earlier = lax.ppermute(chip_total, 'xh', [(0, 1)])]
    ppermute x9, waiting for transfers between devices: 7.21 us -> 2.32 us  [swap(): return lax.ppermute(x, axis, [(0, 1), (1, 0)])]
    ppermute x8 -> x12, starting transfers between devices: 9.49 us -> 14 us  [the longest x8 8.68 us: ring_send(): lax.ppermute(half, axis, perm)]
    another operation x0 -> x2, local copies, waits for them, and re-layouts: none -> 4.24 us  [ring_finish(): pieces = jnp.stack(tuple(halves) + tuple(received))]
  transfers between devices with their start and end apart: 25 -> 29, of which waited for: 11 -> 13; matrix products, arithmetic and copies ran while one was open for 41% -> 44% of each run, Pallas kernels for 0% -> 0%
where the time goes in v14:
time: 209 us; the launch traced here: 206 us
  local copies, waits for them, and re-layouts  57.7 us (28%)
  waiting for transfers between devices  48.1 us (23%)
  starting transfers between devices  43.3 us (21%)
  other arithmetic  31.8 us (15%)
  matrix products  24.3 us (12%)
    unnamed x48, local copies, waits for them, and re-layouts  29.1 us
    ppermute x6, waiting for transfers between devices, ring_direct(): lax.ppermute(x, axis, [(k, (k + shift) % size) for k in range(size)])  17.9 us
    ppermute x8, waiting for transfers between devices, ring_send(): lax.ppermute(half, axis, perm)  16.2 us
    ppermute x9, starting transfers between devices, swap(): return lax.ppermute(x, axis, [(0, 1), (1, 0)])  13.9 us
    dot_general x2, matrix products, on_device(): jnp.dot(features, rows, preferred_element_type=jnp.float32)  13 us
    max x4, local copies, waits for them, and re-layouts, featurize(): rectified = jnp.maximum(block.astype(jnp.float32), 0.0)  11.9 us
    ppermute x6, starting transfers between devices, ring_direct(): lax.ppermute(x, axis, [(k, (k + shift) % size) for k in range(size)])  10.4 us
    ppermute x8, starting transfers between devices, ring_send(): lax.ppermute(half, axis, perm)  8.68 us
  transfers between devices with their start and end apart: 29, of which 13 were waited for; matrix products, arithmetic and copies ran while one was open for 44% of the time, Pallas kernels for 0%

profile of v14, /device:TPU:1, one launch (start us, length us, event | category | flops | bytes accessed | tf_op | source)
XLA Modules:
  0.0 206.3 jit_solution(15236041516374824060)
XLA Ops:
  0.7 2.7 %fusion.33 = (bf16[80,1280]{1,0:T(8,128)(2,1)S(1)}, f32[80,1280]{1,0:T(8,128)}, f32[80,1280]{1,0:T(8,128)}, f32[80,1280]{1,0:T(8,128)}) fusion(f32[80,1280]{1,0:T(8,128)} %param.18, f32[80,1280]{1,0:T(8,128)} %param.19, f32[80,1280]{1,0:T(8,128)} %param.20, f32[80,1280]{1,0:T(8,128)} %param.21), kind=kLoop, calls=%fused_computation.128 | loop fusion | flops 1638400 | bytes 3072000 | tf_op jit(solution)/shard_map/convert_element_type | solution.py:126
  3.4 3.6 %collective-permute-start.4 = (bf16[80,1280]{1,0:T(8,128)(2,1)S(1)}, bf16[80,1280]{1,0:T(8,128)(2,1)S(1)}, u32[]{:S(2)}, u32[]{:S(2)}) collective-permute-start(bf16[80,1280]{1,0:T(8,128)(2,1)S(1)} %get-tuple-element.117), channel_id=1, source_target_pairs={{0,2},{2,0},{1,3},{3,1},{4,6},{6,4},{5,7},{7,5},{8,10},{10,8},{9,1... | collective-permute-start | bytes 614408 | tf_op jit(solution)/shard_map/ppermute | solution.py:100
  11.2 5.6 %collective-permute-done.5 = bf16[80,1280]{1,0:T(8,128)(2,1)S(1)} collective-permute-done((bf16[80,1280]{1,0:T(8,128)(2,1)S(1)}, bf16[80,1280]{1,0:T(8,128)(2,1)S(1)}, u32[]{:S(2)}, u32[]{:S(2)}) %collective-permute-start.5) | collective-permute-done | bytes 204832 | tf_op jit(solution)/shard_map/ppermute | solution.py:58
  17.8 3.8 %collective-permute-start.7 = (bf16[2,80,1280]{2,1,0:T(8,128)(2,1)}, bf16[2,80,1280]{2,1,0:T(8,128)(2,1)S(1)}, u32[]{:S(2)}, u32[]{:S(2)}) collective-permute-start(bf16[2,80,1280]{2,1,0:T(8,128)(2,1)} %get-tuple-element.138), channel_id=1, source_target_pairs={{0,64},{32,96},{64,0},{96,32},{1,65},{33,97},{65,1},{97,33},{2,66}... | collective-permute-start | bytes 1228808 | tf_op jit(solution)/shard_map/ppermute | solution.py:49
  23.0 2.9 %collective-permute-start.2 = (bf16[2,80,1280]{2,1,0:T(8,128)(2,1)}, bf16[2,80,1280]{2,1,0:T(8,128)(2,1)}, u32[]{:S(2)}, u32[]{:S(2)}) collective-permute-start(bf16[2,80,1280]{2,1,0:T(8,128)(2,1)} %get-tuple-element.140), channel_id=1, source_target_pairs={{0,8},{4,12},{8,0},{12,4},{1,9},{5,13},{9,1},{13,5},{2,10},{6,14},... | collective-permute-start | bytes 1228808 | tf_op jit(solution)/shard_map/ppermute | solution.py:49
  32.2 8.3 %collective-permute-done.8 = bf16[2,80,1280]{2,1,0:T(8,128)(2,1)} collective-permute-done((bf16[2,80,1280]{2,1,0:T(8,128)(2,1)}, bf16[2,80,1280]{2,1,0:T(8,128)(2,1)}, u32[]{:S(2)}, u32[]{:S(2)}) %collective-permute-start.8) | collective-permute-done | bytes 409632 | tf_op jit(solution)/shard_map/ppermute | solution.py:49
  46.4 6.1 %collective-permute-done.6 = bf16[2,80,1280]{2,1,0:T(8,128)(2,1)S(1)} collective-permute-done((bf16[2,80,1280]{2,1,0:T(8,128)(2,1)}, bf16[2,80,1280]{2,1,0:T(8,128)(2,1)S(1)}, u32[]{:S(2)}, u32[]{:S(2)}) %collective-permute-start.6) | collective-permute-done | bytes 409632 | tf_op jit(solution)/shard_map/ppermute | solution.py:49
  55.7 2.7 %collective-permute-start.12 = (bf16[2,2,80,1280]{3,2,1,0:T(8,128)(2,1)}, bf16[2,2,80,1280]{3,2,1,0:T(8,128)(2,1)}, u32[]{:S(2)}, u32[]{:S(2)}) collective-permute-start(bf16[2,2,80,1280]{3,2,1,0:T(8,128)(2,1)} %pad_maximum_fusion.12), channel_id=1, source_target_pairs={{0,96},{32,0},{64,32},{96,64},{1,97},{33,1},{65,33},{97,65},{2,98}... | collective-permute-start | bytes 2457608 | tf_op jit(solution)/shard_map/ppermute | solution.py:27
  71.5 4.4 %convert_maximum_fusion = (f32[512,10,128]{0,2,1:T(8,128)S(1)}, f32[512,10,128]{0,2,1:T(8,128)}) fusion(bf16[256,10,128]{0,2,1:T(8,128)(2,1)} %collective-permute-done.23, bf16[256,10,128]{0,2,1:T(8,128)(2,1)} %get-tuple-element.131, pred[]{:T(512)S(6)} %eq.17, bf16[256,10,128]{0,2,1:T(8,128)(2,1)} %get-tuple-element.135, ...), kind=kLoop, calls=%fused_computation.20 | loop fusion | flops 14417920 | bytes 7864321 | tf_op jit(solution)/shard_map/max | solution.py:84
  75.9 3.2 %copy.15 = f32[512,10,128]{2,0,1:T(8,128)} copy(f32[512,10,128]{0,2,1:T(8,128)} %get-tuple-element.150) | data formatting | bytes 5242880 | tf_op jit(solution)/shard_map/max | solution.py:84
  79.1 3.2 %copy.16 = f32[4,128,10,128]{1,3,2,0:T(8,128)} copy(f32[4,128,10,128]{3,1,0,2:T(8,128)} %bitcast.81) | data formatting | bytes 5242880 | tf_op jit(solution)/shard_map/max | solution.py:84
  84.5 3.4 %copy.22 = f32[4,128,10,128]{1,3,2,0:T(8,128)} copy(f32[4,128,10,128]{3,1,0,2:T(8,128)} %bitcast.82) | data formatting | bytes 5242880 | tf_op jit(solution)/shard_map/max | solution.py:84
  87.8 5.3 %collective-permute-done.11 = bf16[2,2,80,1280]{3,2,1,0:T(8,128)(2,1)} collective-permute-done((bf16[2,2,80,1280]{3,2,1,0:T(8,128)(2,1)}, bf16[2,2,80,1280]{3,2,1,0:T(8,128)(2,1)}, u32[]{:S(2)}, u32[]{:S(2)}) %collective-permute-start.11) | collective-permute-done | bytes 819232 | tf_op jit(solution)/shard_map/ppermute | solution.py:27
  95.6 4.4 %multiply_convert_fusion.4 = (bf16[4,128,10,128]{1,3,2,0:T(8,128)(2,1)S(1)}, bf16[4,128,10,128]{1,3,2,0:T(8,128)(2,1)S(1)}, bf16[4,128,10,128]{1,3,2,0:T(8,128)(2,1)}, bf16[4,128,10,128]{1,3,2,0:T(8,128)(2,1)}) fusion(f32[4,128,10,128]{1,3,2,0:T(8,128)S(1)} %copy-done.2, f32[4,128]{1,0:T(4,128)S(1)} %get-tuple-element.152, ...), kind=kLoop, calls=%fused_computation.22 | loop fusion | flops 5242880 | bytes 10489856 | tf_op jit(solution)/shard_map/convert.2
  102.0 6.4 %collective-permute-done.14 = bf16[2,2,80,1280]{3,2,1,0:T(8,128)(2,1)S(1)} collective-permute-done((bf16[2,2,80,1280]{3,2,1,0:T(8,128)(2,1)S(1)}, bf16[2,2,80,1280]{3,2,1,0:T(8,128)(2,1)S(1)}, u32[]{:S(2)}, u32[]{:S(2)}) %collective-permute-start.14) | collective-permute-done | bytes 819232 | tf_op jit(solution)/shard_map/ppermute | solution.py:27
  112.9 4.1 %collective-permute-start.24 = (f32[10,256,128]{2,1,0:T(8,128)}, f32[10,256,128]{2,1,0:T(8,128)}, u32[]{:S(2)}, u32[]{:S(2)}) collective-permute-start(f32[10,256,128]{2,1,0:T(8,128)} %get-tuple-element.99), channel_id=1, source_target_pairs={{0,2},{1,3},{4,6},{5,7},{8,10},{9,11},{12,14},{13,15},{16,18},{17,... | collective-permute-start | bytes 3932168 | tf_op jit(solution)/shard_map/ppermute | solution.py:151
  129.4 4.9 %fusion.3 = f32[4,10,128,128]{2,3,1,0:T(8,128)} fusion(bf16[4,128,10,128]{1,3,2,0:T(8,128)(2,1)S(1)} %copy-done.3, bf16[4,128,10,128]{1,3,2,0:T(8,128)(2,1)S(1)} %copy-done.4, bf16[4,128,10,128]{1,3,2,0:T(8,128)(2,1)} %copy-done.6, bf16[4,128,10,128]{1,3,2,0:T(8,128)(2,1)} %copy-done.5, pred[128,128]{1,0:T(8,128)(4,1)S(1)} %iota_compare_fusion, ...), kind=kOutput, calls=%fused_computation.27 | convolution fusion | flops 515112960 | bytes 9191424 | tf_op jit(solution)/shard_map/chij,cjhe->cihe/dot_general | solution.py:157
  134.3 6.1 %collective-permute-done.24 = f32[10,256,128]{2,1,0:T(8,128)} collective-permute-done((f32[10,256,128]{2,1,0:T(8,128)}, f32[10,256,128]{2,1,0:T(8,128)}, u32[]{:S(2)}, u32[]{:S(2)}) %collective-permute-start.24) | collective-permute-done | bytes 1310752 | tf_op jit(solution)/shard_map/ppermute | solution.py:151
  140.3 4.6 %add_bitcast_fusion = f32[4,128,10,128]{3,1,2,0:T(8,128)S(1)} fusion(f32[4,10,128,128]{2,3,1,0:T(8,128)} %fusion.3, f32[3,10,256,128]{3,2,1,0:T(8,128)} %slice.24, f32[10,256,128]{2,1,0:T(8,128)} %collective-permute-done.24, bf16[4,128,10,128]{1,3,2,0:T(8,128)(2,1)S(1)} %copy-done.3, bf16[4,128,10,128]{1,3,2,0:T(8,128)(2,1)S(1)} %copy-done.4), kind=kOutput, calls=%fused_computation.15 | convolution fusion | flops 344064000 | bytes 13107200 | tf_op jit(solution)/shard_map/cihf,chfe->cihe/dot_general | solution.py:163
  146.9 4.8 %collective-permute-start.25 = (bf16[256,10,128]{2,0,1:T(8,128)(2,1)S(1)}, bf16[256,10,128]{2,0,1:T(8,128)(2,1)S(1)}, u32[]{:S(2)}, u32[]{:S(2)}) collective-permute-start(bf16[256,10,128]{2,0,1:T(8,128)(2,1)S(1)} %get-tuple-element.130), channel_id=1, source_target_pairs={{0,1},{1,0},{2,3},{3,2},{4,5},{5,4},{6,7},{7,6},{8,9},{9,8},{10,11... | collective-permute-start | bytes 1966088 | tf_op jit(solution)/shard_map/ppermute | solution.py:100
  181.8 6.5 %convolution_convert_fusion = bf16[512,1280]{1,0:T(8,128)(2,1)S(1)} fusion(bf16[512,2560]{0,1:T(8,128)(2,1)S(1)} %bitcast.90, bf16[2560,1280]{1,0:T(8,128)(2,1)} %bitcast.101), kind=kOutput, calls=%fused_computation.7 | convolution fusion | flops 3356098560 | bytes 10485760 | tf_op jit(solution)/shard_map/dot_general | solution.py:178
  193.9 6.5 %convolution_convert_fusion.1 = bf16[512,1280]{1,0:T(8,128)(2,1)S(1)} fusion(bf16[512,2560]{0,1:T(8,128)(2,1)S(1)} %bitcast.91, bf16[2560,1280]{1,0:T(8,128)(2,1)} %bitcast.100), kind=kOutput, calls=%fused_computation.8 | convolution fusion | flops 3356098560 | bytes 10485760 | tf_op jit(solution)/shard_map/dot_general | solution.py:178
  202.7 2.9 %conditional.1 = (bf16[1,256,5120]{2,1,0:T(8,128)(2,1)}) conditional(s32[]{:T(128)} %clamp.3, (bf16[256,1280]{1,0:T(8,128)(2,1)S(1)}, bf16[256,1280]{1,0:T(8,128)(2,1)S(1)}, bf16[256,1280]{1,0:T(8,128)(2,1)S(1)}, bf16[256,1280]{1,0:T(8,128)(2,1)}) %tuple.31, (bf16[256,1280]{1,0:T(8,128)(2,1)S(1)}, ...), branch_computations={%region_3.5_spmd, %region_4.6_spmd, %region_5.7_spmd, %region_6.8_... | conditional | flops 10485760 | bytes 5242888 | solution.py:192
  202.7 2.9 %maximum_bitcast_fusion.1 = bf16[1,256,5120]{2,1,0:T(8,128)(2,1)} fusion(bf16[256,1280]{1,0:T(8,128)(2,1)S(1)} %get-tuple-element.46, bf16[256,1280]{1,0:T(8,128)(2,1)} %get-tuple-element.45, bf16[256,1280]{1,0:T(8,128)(2,1)S(1)} %get-tuple-element.44, bf16[256,1280]{1,0:T(8,128)(2,1)S(1)} %get-tuple-element.43), kind=kLoop, calls=%fused_computation.3 | loop fusion | flops 10485760 | bytes 5242880 | tf_op jit(solution)/shard_map/broadcast_in_dim | solution.py:193
  (131 shorter events, 99.1 us)
Async XLA Ops:
  7.8 14.3 %collective-permute-start = (bf16[80,1280]{1,0:T(8,128)(2,1)S(1)}, bf16[80,1280]{1,0:T(8,128)(2,1)S(1)}, u32[]{:S(2)}, u32[]{:S(2)}) collective-permute-start(bf16[80,1280]{1,0:T(8,128)(2,1)S(1)} %get-tuple-element.117), channel_id=1, source_target_pairs={{0,16},{16,0},{1,17},{17,1},{2,18},{18,2},{3,19},{19,3},{4,20},{20... | collective-permute-start | bytes 614408 | tf_op jit(solution)/shard_map/ppermute | solution.py:100
  9.6 59.3 %collective-permute-start.17 = (bf16[256,10,128]{0,2,1:T(8,128)(2,1)}, bf16[256,10,128]{0,2,1:T(8,128)(2,1)}, u32[]{:S(2)}, u32[]{:S(2)}) collective-permute-start(bf16[256,10,128]{0,2,1:T(8,128)(2,1)} %get-tuple-element.136), channel_id=1, source_target_pairs={{0,1},{1,0},{2,3},{3,2},{4,5},{5,4},{6,7},{7,6},{8,9},{9,8},{10,11... | collective-permute-start | bytes 1966088 | tf_op jit(solution)/shard_map/ppermute | solution.py:100
  17.8 13.5 %collective-permute-start.7 = (bf16[2,80,1280]{2,1,0:T(8,128)(2,1)}, bf16[2,80,1280]{2,1,0:T(8,128)(2,1)S(1)}, u32[]{:S(2)}, u32[]{:S(2)}) collective-permute-start(bf16[2,80,1280]{2,1,0:T(8,128)(2,1)} %get-tuple-element.138), channel_id=1, source_target_pairs={{0,64},{32,96},{64,0},{96,32},{1,65},{33,97},{65,1},{97,33},{2,66}... | collective-permute-start | bytes 1228808 | tf_op jit(solution)/shard_map/ppermute | solution.py:49
  21.6 18.9 %collective-permute-start.8 = (bf16[2,80,1280]{2,1,0:T(8,128)(2,1)}, bf16[2,80,1280]{2,1,0:T(8,128)(2,1)}, u32[]{:S(2)}, u32[]{:S(2)}) collective-permute-start(bf16[2,80,1280]{2,1,0:T(8,128)(2,1)} %get-tuple-element.138), channel_id=1, source_target_pairs={{0,96},{32,0},{64,32},{96,64},{1,97},{33,1},{65,33},{97,65},{2,98}... | collective-permute-start | bytes 1228808 | tf_op jit(solution)/shard_map/ppermute | solution.py:49
  23.0 19.8 %collective-permute-start.2 = (bf16[2,80,1280]{2,1,0:T(8,128)(2,1)}, bf16[2,80,1280]{2,1,0:T(8,128)(2,1)}, u32[]{:S(2)}, u32[]{:S(2)}) collective-permute-start(bf16[2,80,1280]{2,1,0:T(8,128)(2,1)} %get-tuple-element.140), channel_id=1, source_target_pairs={{0,8},{4,12},{8,0},{12,4},{1,9},{5,13},{9,1},{13,5},{2,10},{6,14},... | collective-permute-start | bytes 1228808 | tf_op jit(solution)/shard_map/ppermute | solution.py:49
  25.9 18.4 %collective-permute-start.3 = (bf16[2,80,1280]{2,1,0:T(8,128)(2,1)}, bf16[2,80,1280]{2,1,0:T(8,128)(2,1)}, u32[]{:S(2)}, u32[]{:S(2)}) collective-permute-start(bf16[2,80,1280]{2,1,0:T(8,128)(2,1)} %get-tuple-element.140), channel_id=1, source_target_pairs={{0,12},{4,0},{8,4},{12,8},{1,13},{5,1},{9,5},{13,9},{2,14},{6,2},{... | collective-permute-start | bytes 1228808 | tf_op jit(solution)/shard_map/ppermute | solution.py:49
  31.3 31.2 %collective-permute-start.18 = (bf16[256,10,128]{0,2,1:T(8,128)(2,1)S(1)}, bf16[256,10,128]{0,2,1:T(8,128)(2,1)S(1)}, u32[]{:S(2)}, u32[]{:S(2)}) collective-permute-start(bf16[256,10,128]{0,2,1:T(8,128)(2,1)S(1)} %get-tuple-element.134), channel_id=1, source_target_pairs={{0,1},{1,0},{2,3},{3,2},{4,5},{5,4},{6,7},{7,6},{8,9},{9,8},{10,11... | collective-permute-start | bytes 1966088 | tf_op jit(solution)/shard_map/ppermute | solution.py:100
  40.5 12.0 %collective-permute-start.6 = (bf16[2,80,1280]{2,1,0:T(8,128)(2,1)}, bf16[2,80,1280]{2,1,0:T(8,128)(2,1)S(1)}, u32[]{:S(2)}, u32[]{:S(2)}) collective-permute-start(bf16[2,80,1280]{2,1,0:T(8,128)(2,1)} %get-tuple-element.138), channel_id=1, source_target_pairs={{0,32},{32,64},{64,96},{96,0},{1,33},{33,65},{65,97},{97,1},{2,34}... | collective-permute-start | bytes 1228808 | tf_op jit(solution)/shard_map/ppermute | solution.py:49
  42.9 11.8 %collective-permute-start.1 = (bf16[2,80,1280]{2,1,0:T(8,128)(2,1)}, bf16[2,80,1280]{2,1,0:T(8,128)(2,1)S(1)}, u32[]{:S(2)}, u32[]{:S(2)}) collective-permute-start(bf16[2,80,1280]{2,1,0:T(8,128)(2,1)} %get-tuple-element.140), channel_id=1, source_target_pairs={{0,4},{4,8},{8,12},{12,0},{1,5},{5,9},{9,13},{13,1},{2,6},{6,10},{... | collective-permute-start | bytes 1228808 | tf_op jit(solution)/shard_map/ppermute | solution.py:49
  55.7 32.1 %collective-permute-start.10 = (bf16[2,2,80,1280]{3,2,1,0:T(8,128)(2,1)}, bf16[2,2,80,1280]{3,2,1,0:T(8,128)(2,1)}, u32[]{:S(2)}, u32[]{:S(2)}) collective-permute-start(bf16[2,2,80,1280]{3,2,1,0:T(8,128)(2,1)} %pad_maximum_fusion.12), channel_id=1, source_target_pairs={{0,32},{32,64},{64,96},{96,0},{1,33},{33,65},{65,97},{97,1},{2,34}... | collective-permute-start | bytes 2457608 | tf_op jit(solution)/shard_map/ppermute | solution.py:27
  55.7 38.8 %collective-permute-start.12 = (bf16[2,2,80,1280]{3,2,1,0:T(8,128)(2,1)}, bf16[2,2,80,1280]{3,2,1,0:T(8,128)(2,1)}, u32[]{:S(2)}, u32[]{:S(2)}) collective-permute-start(bf16[2,2,80,1280]{3,2,1,0:T(8,128)(2,1)} %pad_maximum_fusion.12), channel_id=1, source_target_pairs={{0,96},{32,0},{64,32},{96,64},{1,97},{33,1},{65,33},{97,65},{2,98}... | collective-permute-start | bytes 2457608 | tf_op jit(solution)/shard_map/ppermute | solution.py:27
  58.4 34.8 %collective-permute-start.11 = (bf16[2,2,80,1280]{3,2,1,0:T(8,128)(2,1)}, bf16[2,2,80,1280]{3,2,1,0:T(8,128)(2,1)}, u32[]{:S(2)}, u32[]{:S(2)}) collective-permute-start(bf16[2,2,80,1280]{3,2,1,0:T(8,128)(2,1)} %pad_maximum_fusion.11), channel_id=1, source_target_pairs={{0,96},{32,0},{64,32},{96,64},{1,97},{33,1},{65,33},{97,65},{2,98}... | collective-permute-start | bytes 2457608 | tf_op jit(solution)/shard_map/ppermute | solution.py:27
  68.9 33.1 %collective-permute-start.13 = (bf16[2,2,80,1280]{3,2,1,0:T(8,128)(2,1)}, bf16[2,2,80,1280]{3,2,1,0:T(8,128)(2,1)}, u32[]{:S(2)}, u32[]{:S(2)}) collective-permute-start(bf16[2,2,80,1280]{3,2,1,0:T(8,128)(2,1)} %pad_maximum_fusion.13), channel_id=1, source_target_pairs={{0,4},{4,8},{8,12},{12,0},{1,5},{5,9},{9,13},{13,1},{2,6},{6,10},{... | collective-permute-start | bytes 2457608 | tf_op jit(solution)/shard_map/ppermute | solution.py:27
  68.9 39.5 %collective-permute-start.15 = (bf16[2,2,80,1280]{3,2,1,0:T(8,128)(2,1)}, bf16[2,2,80,1280]{3,2,1,0:T(8,128)(2,1)}, u32[]{:S(2)}, u32[]{:S(2)}) collective-permute-start(bf16[2,2,80,1280]{3,2,1,0:T(8,128)(2,1)} %pad_maximum_fusion.13), channel_id=1, source_target_pairs={{0,12},{4,0},{8,4},{12,8},{1,13},{5,1},{9,5},{13,9},{2,14},{6,2},{... | collective-permute-start | bytes 2457608 | tf_op jit(solution)/shard_map/ppermute | solution.py:27
  87.8 20.6 %collective-permute-start.14 = (bf16[2,2,80,1280]{3,2,1,0:T(8,128)(2,1)S(1)}, bf16[2,2,80,1280]{3,2,1,0:T(8,128)(2,1)S(1)}, u32[]{:S(2)}, u32[]{:S(2)}) collective-permute-start(bf16[2,2,80,1280]{3,2,1,0:T(8,128)(2,1)S(1)} %pad_maximum_fusion.14), channel_id=1, source_target_pairs={{0,4},{4,8},{8,12},{12,0},{1,5},{5,9},{9,13},{13,1},{2,6},{6,10},{... | collective-permute-start | bytes 2457608 | tf_op jit(solution)/shard_map/ppermute | solution.py:27
  93.2 17.3 %collective-permute-start.16 = (bf16[2,2,80,1280]{3,2,1,0:T(8,128)(2,1)S(1)}, bf16[2,2,80,1280]{3,2,1,0:T(8,128)(2,1)}, u32[]{:S(2)}, u32[]{:S(2)}) collective-permute-start(bf16[2,2,80,1280]{3,2,1,0:T(8,128)(2,1)S(1)} %pad_maximum_fusion.14), channel_id=1, source_target_pairs={{0,12},{4,0},{8,4},{12,8},{1,13},{5,1},{9,5},{13,9},{2,14},{6,2},{... | collective-permute-start | bytes 2457608 | tf_op jit(solution)/shard_map/ppermute | solution.py:27
  94.5 18.4 %collective-permute-start.9 = (bf16[2,2,80,1280]{3,2,1,0:T(8,128)(2,1)}, bf16[2,2,80,1280]{3,2,1,0:T(8,128)(2,1)}, u32[]{:S(2)}, u32[]{:S(2)}) collective-permute-start(bf16[2,2,80,1280]{3,2,1,0:T(8,128)(2,1)} %pad_maximum_fusion.11), channel_id=1, source_target_pairs={{0,32},{32,64},{64,96},{96,0},{1,33},{33,65},{65,97},{97,1},{2,34}... | collective-permute-start | bytes 2457608 | tf_op jit(solution)/shard_map/ppermute | solution.py:27
  112.9 27.5 %collective-permute-start.24 = (f32[10,256,128]{2,1,0:T(8,128)}, f32[10,256,128]{2,1,0:T(8,128)}, u32[]{:S(2)}, u32[]{:S(2)}) collective-permute-start(f32[10,256,128]{2,1,0:T(8,128)} %get-tuple-element.99), channel_id=1, source_target_pairs={{0,2},{1,3},{4,6},{5,7},{8,10},{9,11},{12,14},{13,15},{16,18},{17,... | collective-permute-start | bytes 3932168 | tf_op jit(solution)/shard_map/ppermute | solution.py:151
  124.0 21.0 %collective-permute-start.19 = (bf16[2,2,80,1280]{3,2,1,0:T(8,128)(2,1)}, bf16[2,2,80,1280]{3,2,1,0:T(8,128)(2,1)}, u32[]{:S(2)}, u32[]{:S(2)}) collective-permute-start(bf16[2,2,80,1280]{3,2,1,0:T(8,128)(2,1)} %collective-permute-done.9), channel_id=1, source_target_pairs={{0,32},{32,64},{64,96},{96,0},{1,33},{33,65},{65,97},{97,1},{2,34}... | collective-permute-start | bytes 2457608 | tf_op jit(solution)/shard_map/ppermute | solution.py:34
  124.0 21.0 %collective-permute-start.20 = (bf16[2,2,80,1280]{3,2,1,0:T(8,128)(2,1)}, bf16[2,2,80,1280]{3,2,1,0:T(8,128)(2,1)S(1)}, u32[]{:S(2)}, u32[]{:S(2)}) collective-permute-start(bf16[2,2,80,1280]{3,2,1,0:T(8,128)(2,1)} %collective-permute-done.12), channel_id=1, source_target_pairs={{0,96},{32,0},{64,32},{96,64},{1,97},{33,1},{65,33},{97,65},{2,98}... | collective-permute-start | bytes 2457608 | tf_op jit(solution)/shard_map/ppermute | solution.py:35
  126.7 18.4 %collective-permute-start.21 = (bf16[2,2,80,1280]{3,2,1,0:T(8,128)(2,1)}, bf16[2,2,80,1280]{3,2,1,0:T(8,128)(2,1)}, u32[]{:S(2)}, u32[]{:S(2)}) collective-permute-start(bf16[2,2,80,1280]{3,2,1,0:T(8,128)(2,1)} %collective-permute-done.13), channel_id=1, source_target_pairs={{0,4},{4,8},{8,12},{12,0},{1,5},{5,9},{9,13},{13,1},{2,6},{6,10},{... | collective-permute-start | bytes 2457608 | tf_op jit(solution)/shard_map/ppermute | solution.py:34
  126.9 18.2 %collective-permute-start.22 = (bf16[2,2,80,1280]{3,2,1,0:T(8,128)(2,1)}, bf16[2,2,80,1280]{3,2,1,0:T(8,128)(2,1)}, u32[]{:S(2)}, u32[]{:S(2)}) collective-permute-start(bf16[2,2,80,1280]{3,2,1,0:T(8,128)(2,1)} %collective-permute-done.16), channel_id=1, source_target_pairs={{0,12},{4,0},{8,4},{12,8},{1,13},{5,1},{9,5},{13,9},{2,14},{6,2},{... | collective-permute-start | bytes 2457608 | tf_op jit(solution)/shard_map/ppermute | solution.py:35
  146.9 22.6 %collective-permute-start.25 = (bf16[256,10,128]{2,0,1:T(8,128)(2,1)S(1)}, bf16[256,10,128]{2,0,1:T(8,128)(2,1)S(1)}, u32[]{:S(2)}, u32[]{:S(2)}) collective-permute-start(bf16[256,10,128]{2,0,1:T(8,128)(2,1)S(1)} %get-tuple-element.130), channel_id=1, source_target_pairs={{0,1},{1,0},{2,3},{3,2},{4,5},{5,4},{6,7},{7,6},{8,9},{9,8},{10,11... | collective-permute-start | bytes 1966088 | tf_op jit(solution)/shard_map/ppermute | solution.py:100
  189.2 11.4 %collective-permute-start.28 = (bf16[256,1280]{1,0:T(8,128)(2,1)}, bf16[256,1280]{1,0:T(8,128)(2,1)}, u32[]{:S(2)}, u32[]{:S(2)}) collective-permute-start(bf16[256,1280]{1,0:T(8,128)(2,1)} %get-tuple-element.125), channel_id=1, source_target_pairs={{0,1},{1,0},{2,3},{3,2},{4,5},{5,4},{6,7},{7,6},{8,9},{9,8},{10,11... | collective-permute-start | bytes 1966088 | tf_op jit(solution)/shard_map/ppermute | solution.py:100
  (21 other events, 186.4 us)

commit v15 on v10

--- a/solution.py
+++ b/solution.py
@@ -118,11 +118,12 @@
     mine = lax.dynamic_slice_in_dim(x, core * size, size, keep_axis)
     theirs = lax.dynamic_slice_in_dim(x, (1 - core) * size, size, keep_axis)
     received = swap(theirs, "c")
-    return jnp.where(
-        core == 0,
-        jnp.concatenate([mine, received], axis=join_axis),
-        jnp.concatenate([received, mine], axis=join_axis),
-    )
+    length = mine.shape[join_axis]
+    shape = list(mine.shape)
+    shape[join_axis] = 2 * length
+    joined = jnp.zeros(shape, mine.dtype)
+    joined = lax.dynamic_update_slice_in_dim(joined, mine, core * length, join_axis)
+    return lax.dynamic_update_slice_in_dim(joined, received, (1 - core) * length, join_axis)
 
 
 def on_device(

time: 188 us -> 207 us (1.10); the launches traced: 187 us -> 204 us
  local copies, waits for them, and re-layouts: 42.4 us -> 68.4 us
  other arithmetic: 45.4 us -> 39.3 us
  waiting for transfers between devices: 36.8 us -> 34.4 us
  starting transfers between devices: 38.3 us -> 36 us
    dynamic_update_slice x0 -> x8, local copies, waits for them, and re-layouts: none -> 15.3 us  [the longest x4 8.24 us: pair_exchange(): lax.dynamic_update_slice_in_dim(joined, received, (1 - core) * length, jo...]
    ppermute x4, waiting for transfers between devices: 12.3 us -> 0.01 us  [ring_send(): return (lax.ppermute(x, axis, forward), lax.ppermute(x, axis, backward))]
    max x4 -> x0, local copies, waits for them, and re-layouts: 12.1 us -> none  [featurize(): rectified = jnp.maximum(block.astype(jnp.float32), 0.0)]
    ppermute x2, waiting for transfers between devices: 1.38 us -> 9.33 us  [ring_far(): lax.ppermute(from_left[:half], axis, forward)]
    ppermute x0 -> x3, local copies, waits for them, and re-layouts: none -> 6.6 us  [swap(): return lax.ppermute(x, axis, [(0, 1), (1, 0)])]
    concatenate x0 -> x2, local copies, waits for them, and re-layouts: none -> 4.87 us  [featurize(): return jnp.concatenate([cosine, sine], axis=2).astype(jnp.bfloat16)]
    dynamic_slice x0 -> x4, local copies, waits for them, and re-layouts: none -> 4.23 us  [pair_exchange(): theirs = lax.dynamic_slice_in_dim(x, (1 - core) * size, size, keep_axis)]
    max x1 -> x0, other arithmetic: 3.94 us -> none  [featurize(): rectified = jnp.maximum(block.astype(jnp.float32), 0.0)]
  transfers between devices with their start and end apart: 25 -> 25, of which waited for: 11 -> 11; matrix products, arithmetic and copies ran while one was open for 41% -> 45% of each run, Pallas kernels for 0% -> 0%
where the time goes in v15:
time: 207 us; the launch traced here: 204 us
  local copies, waits for them, and re-layouts  68.4 us (33%)
  other arithmetic  39.3 us (19%)
  starting transfers between devices  36 us (17%)
  waiting for transfers between devices  34.4 us (17%)
  matrix products  24.8 us (12%)
    dot_general x2, matrix products, on_device(): jnp.dot(features, rows, preferred_element_type=jnp.float32)  13 us
    unnamed x21, local copies, waits for them, and re-layouts  11.9 us
    ppermute x6, waiting for transfers between devices, ring_direct(): lax.ppermute(x, axis, [(k, (k + shift) % size) for k in range(size)])  11.3 us
    another operation x2, other arithmetic, ring_finish(): return jnp.stack((x,) + tuple(received))  11.2 us
    ppermute x6, starting transfers between devices, ring_direct(): lax.ppermute(x, axis, [(k, (k + shift) % size) for k in range(size)])  11 us
    ppermute x9, starting transfers between devices, swap(): return lax.ppermute(x, axis, [(0, 1), (1, 0)])  10.5 us
    ppermute x2, waiting for transfers between devices, ring_far(): lax.ppermute(from_left[:half], axis, forward)  9.33 us
    dynamic_update_slice x4, local copies, waits for them, and re-layouts, pair_exchange(): lax.dynamic_update_slice_in_dim(joined, received, (1 - core) * length, jo...  8.24 us
  transfers between devices with their start and end apart: 25, of which 11 were waited for; matrix products, arithmetic and copies ran while one was open for 45% of the time, Pallas kernels for 0%

profile of v15, /device:TPU:1, one launch (start us, length us, event | category | flops | bytes accessed | tf_op | source)
XLA Modules:
  0.0 203.8 jit_solution(2989693790221516354)
XLA Ops:
  0.6 2.6 %fusion.38 = (bf16[80,1280]{1,0:T(8,128)(2,1)S(1)}, f32[80,1280]{1,0:T(8,128)}, f32[80,1280]{1,0:T(8,128)}, f32[80,1280]{1,0:T(8,128)}) fusion(f32[80,1280]{1,0:T(8,128)} %param.18, f32[80,1280]{1,0:T(8,128)} %param.19, f32[80,1280]{1,0:T(8,128)} %param.20, f32[80,1280]{1,0:T(8,128)} %param.21), kind=kLoop, calls=%fused_computation.119 | loop fusion | flops 1638400 | bytes 3072000 | tf_op jit(solution)/shard_map/convert_element_type | solution.py:140
  3.2 3.6 %collective-permute-start.4 = (bf16[80,1280]{1,0:T(8,128)(2,1)S(1)}, bf16[80,1280]{1,0:T(8,128)(2,1)S(1)}, u32[]{:S(2)}, u32[]{:S(2)}) collective-permute-start(bf16[80,1280]{1,0:T(8,128)(2,1)S(1)} %get-tuple-element.93), channel_id=1, source_target_pairs={{0,2},{2,0},{1,3},{3,1},{4,6},{6,4},{5,7},{7,5},{8,10},{10,8},{9,1... | collective-permute-start | bytes 614408 | tf_op jit(solution)/shard_map/ppermute | solution.py:113
  7.7 3.5 %collective-permute-done.4 = bf16[80,1280]{1,0:T(8,128)(2,1)S(1)} collective-permute-done((bf16[80,1280]{1,0:T(8,128)(2,1)S(1)}, bf16[80,1280]{1,0:T(8,128)(2,1)S(1)}, u32[]{:S(2)}, u32[]{:S(2)}) %collective-permute-start.4) | collective-permute-done | bytes 204832 | tf_op jit(solution)/shard_map/ppermute | solution.py:113
  11.1 5.6 %collective-permute-done.5 = bf16[80,1280]{1,0:T(8,128)(2,1)S(1)} collective-permute-done((bf16[80,1280]{1,0:T(8,128)(2,1)S(1)}, bf16[80,1280]{1,0:T(8,128)(2,1)S(1)}, u32[]{:S(2)}, u32[]{:S(2)}) %collective-permute-start.5) | collective-permute-done | bytes 204832 | tf_op jit(solution)/shard_map/ppermute | solution.py:71
  21.0 3.4 %collective-permute-start.7 = (bf16[2,80,1280]{2,1,0:T(8,128)(2,1)}, bf16[2,80,1280]{2,1,0:T(8,128)(2,1)S(1)}, u32[]{:S(2)}, u32[]{:S(2)}) collective-permute-start(bf16[2,80,1280]{2,1,0:T(8,128)(2,1)} %get-tuple-element.114), channel_id=1, source_target_pairs={{0,64},{32,96},{64,0},{96,32},{1,65},{33,97},{65,1},{97,33},{2,66}... | collective-permute-start | bytes 1228808 | tf_op jit(solution)/shard_map/ppermute | solution.py:62
  33.6 2.6 %collective-permute-start.2 = (bf16[2,80,1280]{2,1,0:T(8,128)(2,1)S(1)}, bf16[2,80,1280]{2,1,0:T(8,128)(2,1)S(1)}, u32[]{:S(2)}, u32[]{:S(2)}) collective-permute-start(bf16[2,80,1280]{2,1,0:T(8,128)(2,1)S(1)} %get-tuple-element.116), channel_id=1, source_target_pairs={{0,8},{4,12},{8,0},{12,4},{1,9},{5,13},{9,1},{13,5},{2,10},{6,14},... | collective-permute-start | bytes 1228808 | tf_op jit(solution)/shard_map/ppermute | solution.py:62
  38.2 2.6 %collective-permute-done.7 = bf16[2,80,1280]{2,1,0:T(8,128)(2,1)S(1)} collective-permute-done((bf16[2,80,1280]{2,1,0:T(8,128)(2,1)}, bf16[2,80,1280]{2,1,0:T(8,128)(2,1)S(1)}, u32[]{:S(2)}, u32[]{:S(2)}) %collective-permute-start.7) | collective-permute-done | bytes 409632 | tf_op jit(solution)/shard_map/ppermute | solution.py:62
  44.7 8.4 %collective-permute-done.2 = bf16[2,80,1280]{2,1,0:T(8,128)(2,1)S(1)} collective-permute-done((bf16[2,80,1280]{2,1,0:T(8,128)(2,1)S(1)}, bf16[2,80,1280]{2,1,0:T(8,128)(2,1)S(1)}, u32[]{:S(2)}, u32[]{:S(2)}) %collective-permute-start.2) | collective-permute-done | bytes 409632 | tf_op jit(solution)/shard_map/ppermute | solution.py:62
  88.4 5.7 %multiply_convert_fusion.4 = (bf16[512,10,128]{2,0,1:T(8,128)(2,1)}, bf16[512,10,128]{2,0,1:T(8,128)(2,1)}, bf16[512,10,128]{2,0,1:T(8,128)(2,1)}, bf16[512,10,128]{2,0,1:T(8,128)(2,1)}) fusion(bf16[512,10,128]{2,0,1:T(8,128)(2,1)} %constant_dynamic-update-slice_fusion.6, f32[512]{0:T(512)S(1)} %get-tuple-element.124, f32[512]{0:T(512)S(1)} %get-tuple-element.123, ...), kind=kLoop, calls=%fused_computation.24 | loop fusion | flops 7864320 | bytes 7868416 | tf_op jit(solution)/shard_map/convert.7
  94.0 2.4 %copy.16 = bf16[4,128,10,128]{1,3,2,0:T(8,128)(2,1)} copy(bf16[4,128,10,128]{3,1,0,2:T(8,128)(2,1)} %bitcast.70) | data formatting | bytes 2621440 | tf_op jit(solution)/shard_map/concatenate | solution.py:100
  96.5 2.4 %copy.17 = bf16[4,128,10,128]{1,3,2,0:T(8,128)(2,1)} copy(bf16[4,128,10,128]{3,1,0,2:T(8,128)(2,1)} %bitcast.69) | data formatting | bytes 2621440 | tf_op jit(solution)/shard_map/concatenate | solution.py:100
  98.9 3.1 %fusion.42 = (f32[10,256,128]{2,1,0:T(8,128)S(1)}, f32[4,10,256,128]{3,2,1,0:T(8,128)S(1)}) fusion(bf16[4,128,10,128]{3,1,0,2:T(8,128)(2,1)} %bitcast.21, bf16[4,128,10,128]{1,3,2,0:T(8,128)(2,1)} %copy.17, bf16[4,128,10,128]{1,3,2,0:T(8,128)(2,1)} %copy.16), kind=kOutput, calls=%fused_computation.122 | convolution fusion | flops 341770240 | bytes 10485760 | tf_op jit(solution)/shard_map/cjhf,cjhe->chfe/dot_general | solution.py:159
  104.5 2.7 %collective-permute-start.18 = (bf16[2,2,80,1280]{3,2,1,0:T(8,128)(2,1)S(1)}, bf16[2,2,80,1280]{3,2,1,0:T(8,128)(2,1)S(1)}, u32[]{:S(2)}, u32[]{:S(2)}) collective-permute-start(bf16[2,2,80,1280]{3,2,1,0:T(8,128)(2,1)S(1)} %slice.30), channel_id=1, source_target_pairs={{0,12},{4,0},{8,4},{12,8},{1,13},{5,1},{9,5},{13,9},{2,14},{6,2},{... | collective-permute-start | bytes 2457608 | tf_op jit(solution)/shard_map/ppermute | solution.py:42
  107.3 3.1 %collective-permute-start.20 = (f32[10,256,128]{2,1,0:T(8,128)S(1)}, f32[10,256,128]{2,1,0:T(8,128)S(1)}, u32[]{:S(2)}, u32[]{:S(2)}) collective-permute-start(f32[10,256,128]{2,1,0:T(8,128)S(1)} %get-tuple-element.81), channel_id=1, source_target_pairs={{0,2},{1,3},{4,6},{5,7},{8,10},{9,11},{12,14},{13,15},{16,18},{17,... | collective-permute-start | bytes 3932168 | tf_op jit(solution)/shard_map/ppermute | solution.py:165
  121.9 2.5 %collective-permute-done.17 = bf16[2,2,80,1280]{3,2,1,0:T(8,128)(2,1)S(1)} collective-permute-done((bf16[2,2,80,1280]{3,2,1,0:T(8,128)(2,1)S(1)}, bf16[2,2,80,1280]{3,2,1,0:T(8,128)(2,1)S(1)}, u32[]{:S(2)}, u32[]{:S(2)}) %collective-permute-start.17) | collective-permute-done | bytes 819232 | tf_op jit(solution)/shard_map/ppermute | solution.py:41
  125.9 6.9 %collective-permute-done.15 = bf16[2,2,80,1280]{3,2,1,0:T(8,128)(2,1)S(1)} collective-permute-done((bf16[2,2,80,1280]{3,2,1,0:T(8,128)(2,1)}, bf16[2,2,80,1280]{3,2,1,0:T(8,128)(2,1)S(1)}, u32[]{:S(2)}, u32[]{:S(2)}) %collective-permute-start.15) | collective-permute-done | bytes 819232 | tf_op jit(solution)/shard_map/ppermute | solution.py:41
  134.2 2.5 %pad_maximum_fusion.9 = bf16[4,2,80,1280]{3,2,1,0:T(8,128)(2,1)} fusion(bf16[2,2,80,1280]{3,2,1,0:T(8,128)(2,1)} %collective-permute-done.16, bf16[2,2,80,1280]{3,2,1,0:T(8,128)(2,1)S(1)} %collective-permute-done.15), kind=kLoop, calls=%fused_computation.34 | loop fusion | flops 819200 | bytes 3276800 | tf_op jit(solution)/shard_map/concatenate | solution.py:39
  140.1 6.4 %add_bitcast_fusion = f32[4,128,10,128]{3,1,2,0:T(8,128)} fusion(f32[4,10,128,128]{2,3,1,0:T(8,128)} %fusion, pred[128,128]{1,0:T(8,128)(4,1)S(1)} %iota_compare_fusion, bf16[4,128,10,128]{1,3,2,0:T(8,128)(2,1)} %copy.17, bf16[4,128,10,128]{1,3,2,0:T(8,128)(2,1)} %copy.16, bf16[4,128,10,128]{3,1,0,2:T(8,128)(2,1)} %bitcast.21, ...), kind=kOutput, calls=%fused_computation.17 | convolution fusion | flops 515768320 | bytes 11812864 | tf_op jit(solution)/shard_map/chij,cjhe->cihe/dot_general | solution.py:171
  162.2 5.9 %pad_maximum_fusion.1 = bf16[4,4,2,80,1280]{4,3,2,1,0:T(8,128)(2,1)} fusion(bf16[1,4,2,80,1280]{4,3,2,1,0:T(8,128)(2,1)} %bitcast.41, bf16[1,4,2,80,1280]{4,3,2,1,0:T(8,128)(2,1)} %bitcast.61, bf16[1,4,2,80,1280]{4,3,2,1,0:T(8,128)(2,1)} %bitcast.39, bf16[1,4,2,80,1280]{4,3,2,1,0:T(8,128)(2,1)S(1)} %bitcast.59), kind=kLoop, calls=%fused_computation.7 | loop fusion | flops 9830400 | bytes 13107200 | tf_op jit(solution)/shard_map/stack | solution.py:50
  168.1 5.3 %pad_maximum_fusion = bf16[4,4,2,80,1280]{4,3,2,1,0:T(8,128)(2,1)} fusion(bf16[1,4,2,80,1280]{4,3,2,1,0:T(8,128)(2,1)} %bitcast.34, bf16[1,4,2,80,1280]{4,3,2,1,0:T(8,128)(2,1)S(1)} %bitcast.62, bf16[1,4,2,80,1280]{4,3,2,1,0:T(8,128)(2,1)} %bitcast.32, bf16[1,4,2,80,1280]{4,3,2,1,0:T(8,128)(2,1)S(1)} %bitcast.60), kind=kLoop, calls=%fused_computation.6 | loop fusion | flops 9830400 | bytes 13107200 | tf_op jit(solution)/shard_map/stack | solution.py:50
  179.3 6.5 %convolution_convert_fusion = bf16[512,1280]{1,0:T(8,128)(2,1)S(1)} fusion(bf16[512,2560]{0,1:T(8,128)(2,1)S(1)} %bitcast.74, bf16[2560,1280]{1,0:T(8,128)(2,1)} %bitcast.64), kind=kOutput, calls=%fused_computation.9 | convolution fusion | flops 3356098560 | bytes 10485760 | tf_op jit(solution)/shard_map/dot_general | solution.py:192
  191.5 6.5 %convolution_convert_fusion.1 = bf16[512,1280]{1,0:T(8,128)(2,1)S(1)} fusion(bf16[512,2560]{0,1:T(8,128)(2,1)S(1)} %bitcast.75, bf16[2560,1280]{1,0:T(8,128)(2,1)} %bitcast.63), kind=kOutput, calls=%fused_computation.10 | convolution fusion | flops 3356098560 | bytes 10485760 | tf_op jit(solution)/shard_map/dot_general | solution.py:192
  200.2 2.9 %conditional.1 = (bf16[1,256,5120]{2,1,0:T(8,128)(2,1)}) conditional(s32[]{:T(128)} %clamp.3, (bf16[256,1280]{1,0:T(8,128)(2,1)S(1)}, bf16[256,1280]{1,0:T(8,128)(2,1)S(1)}, bf16[256,1280]{1,0:T(8,128)(2,1)S(1)}, bf16[256,1280]{1,0:T(8,128)(2,1)}) %tuple.31, (bf16[256,1280]{1,0:T(8,128)(2,1)S(1)}, ...), branch_computations={%region_3.5_spmd, %region_4.6_spmd, %region_5.7_spmd, %region_6.8_... | conditional | flops 10485760 | bytes 5242888 | solution.py:206
  200.2 2.9 %maximum_bitcast_fusion.1 = bf16[1,256,5120]{2,1,0:T(8,128)(2,1)} fusion(bf16[256,1280]{1,0:T(8,128)(2,1)S(1)} %get-tuple-element.46, bf16[256,1280]{1,0:T(8,128)(2,1)} %get-tuple-element.45, bf16[256,1280]{1,0:T(8,128)(2,1)S(1)} %get-tuple-element.44, bf16[256,1280]{1,0:T(8,128)(2,1)S(1)} %get-tuple-element.43), kind=kLoop, calls=%fused_computation.3 | loop fusion | flops 10485760 | bytes 5242880 | tf_op jit(solution)/shard_map/broadcast_in_dim | solution.py:207
  (112 shorter events, 105.9 us)
Async XLA Ops:
  3.2 7.9 %collective-permute-start.4 = (bf16[80,1280]{1,0:T(8,128)(2,1)S(1)}, bf16[80,1280]{1,0:T(8,128)(2,1)S(1)}, u32[]{:S(2)}, u32[]{:S(2)}) collective-permute-start(bf16[80,1280]{1,0:T(8,128)(2,1)S(1)} %get-tuple-element.93), channel_id=1, source_target_pairs={{0,2},{2,0},{1,3},{3,1},{4,6},{6,4},{5,7},{7,5},{8,10},{10,8},{9,1... | collective-permute-start | bytes 614408 | tf_op jit(solution)/shard_map/ppermute | solution.py:113
  6.8 9.9 %collective-permute-start.5 = (bf16[80,1280]{1,0:T(8,128)(2,1)S(1)}, bf16[80,1280]{1,0:T(8,128)(2,1)S(1)}, u32[]{:S(2)}, u32[]{:S(2)}) collective-permute-start(bf16[80,1280]{1,0:T(8,128)(2,1)S(1)} %get-tuple-element.93), channel_id=1, source_target_pairs={{0,18},{2,16},{16,2},{18,0},{1,19},{3,17},{17,3},{19,1},{4,22},{6,... | collective-permute-start | bytes 614408 | tf_op jit(solution)/shard_map/ppermute | solution.py:71
  7.7 23.5 %collective-permute-start = (bf16[80,1280]{1,0:T(8,128)(2,1)S(1)}, bf16[80,1280]{1,0:T(8,128)(2,1)}, u32[]{:S(2)}, u32[]{:S(2)}) collective-permute-start(bf16[80,1280]{1,0:T(8,128)(2,1)S(1)} %get-tuple-element.93), channel_id=1, source_target_pairs={{0,16},{16,0},{1,17},{17,1},{2,18},{18,2},{3,19},{19,3},{4,20},{20... | collective-permute-start | bytes 614408 | tf_op jit(solution)/shard_map/ppermute | solution.py:113
  17.6 18.6 %collective-permute-start.6 = (bf16[2,80,1280]{2,1,0:T(8,128)(2,1)}, bf16[2,80,1280]{2,1,0:T(8,128)(2,1)S(1)}, u32[]{:S(2)}, u32[]{:S(2)}) collective-permute-start(bf16[2,80,1280]{2,1,0:T(8,128)(2,1)} %get-tuple-element.114), channel_id=1, source_target_pairs={{0,32},{32,64},{64,96},{96,0},{1,33},{33,65},{65,97},{97,1},{2,34}... | collective-permute-start | bytes 1228808 | tf_op jit(solution)/shard_map/ppermute | solution.py:62
  21.0 19.8 %collective-permute-start.7 = (bf16[2,80,1280]{2,1,0:T(8,128)(2,1)}, bf16[2,80,1280]{2,1,0:T(8,128)(2,1)S(1)}, u32[]{:S(2)}, u32[]{:S(2)}) collective-permute-start(bf16[2,80,1280]{2,1,0:T(8,128)(2,1)} %get-tuple-element.114), channel_id=1, source_target_pairs={{0,64},{32,96},{64,0},{96,32},{1,65},{33,97},{65,1},{97,33},{2,66}... | collective-permute-start | bytes 1228808 | tf_op jit(solution)/shard_map/ppermute | solution.py:62
  24.4 17.7 %collective-permute-start.8 = (bf16[2,80,1280]{2,1,0:T(8,128)(2,1)}, bf16[2,80,1280]{2,1,0:T(8,128)(2,1)}, u32[]{:S(2)}, u32[]{:S(2)}) collective-permute-start(bf16[2,80,1280]{2,1,0:T(8,128)(2,1)} %get-tuple-element.114), channel_id=1, source_target_pairs={{0,96},{32,0},{64,32},{96,64},{1,97},{33,1},{65,33},{97,65},{2,98}... | collective-permute-start | bytes 1228808 | tf_op jit(solution)/shard_map/ppermute | solution.py:62
  32.2 12.5 %collective-permute-start.1 = (bf16[2,80,1280]{2,1,0:T(8,128)(2,1)S(1)}, bf16[2,80,1280]{2,1,0:T(8,128)(2,1)S(1)}, u32[]{:S(2)}, u32[]{:S(2)}) collective-permute-start(bf16[2,80,1280]{2,1,0:T(8,128)(2,1)S(1)} %get-tuple-element.116), channel_id=1, source_target_pairs={{0,4},{4,8},{8,12},{12,0},{1,5},{5,9},{9,13},{13,1},{2,6},{6,10},{... | collective-permute-start | bytes 1228808 | tf_op jit(solution)/shard_map/ppermute | solution.py:62
  33.6 19.6 %collective-permute-start.2 = (bf16[2,80,1280]{2,1,0:T(8,128)(2,1)S(1)}, bf16[2,80,1280]{2,1,0:T(8,128)(2,1)S(1)}, u32[]{:S(2)}, u32[]{:S(2)}) collective-permute-start(bf16[2,80,1280]{2,1,0:T(8,128)(2,1)S(1)} %get-tuple-element.116), channel_id=1, source_target_pairs={{0,8},{4,12},{8,0},{12,4},{1,9},{5,13},{9,1},{13,5},{2,10},{6,14},... | collective-permute-start | bytes 1228808 | tf_op jit(solution)/shard_map/ppermute | solution.py:62
  36.2 17.2 %collective-permute-start.3 = (bf16[2,80,1280]{2,1,0:T(8,128)(2,1)S(1)}, bf16[2,80,1280]{2,1,0:T(8,128)(2,1)S(1)}, u32[]{:S(2)}, u32[]{:S(2)}) collective-permute-start(bf16[2,80,1280]{2,1,0:T(8,128)(2,1)S(1)} %get-tuple-element.116), channel_id=1, source_target_pairs={{0,12},{4,0},{8,4},{12,8},{1,13},{5,1},{9,5},{13,9},{2,14},{6,2},{... | collective-permute-start | bytes 1228808 | tf_op jit(solution)/shard_map/ppermute | solution.py:62
  40.8 17.5 %collective-permute-start.13 = (bf16[256,10,128]{0,2,1:T(8,128)(2,1)S(1)}, bf16[256,10,128]{0,2,1:T(8,128)(2,1)}, u32[]{:S(2)}, u32[]{:S(2)}) collective-permute-start(bf16[256,10,128]{0,2,1:T(8,128)(2,1)S(1)} %get-tuple-element.111), channel_id=1, source_target_pairs={{0,1},{1,0},{2,3},{3,2},{4,5},{5,4},{6,7},{7,6},{8,9},{9,8},{10,11... | collective-permute-start | bytes 1966088 | tf_op jit(solution)/shard_map/ppermute | solution.py:113
  42.1 17.6 %collective-permute-start.14 = (bf16[256,10,128]{2,0,1:T(8,128)(2,1)}, bf16[256,10,128]{2,0,1:T(8,128)(2,1)}, u32[]{:S(2)}, u32[]{:S(2)}) collective-permute-start(bf16[256,10,128]{2,0,1:T(8,128)(2,1)} %copy.32), channel_id=1, source_target_pairs={{0,1},{1,0},{2,3},{3,2},{4,5},{5,4},{6,7},{7,6},{8,9},{9,8},{10,11... | collective-permute-start | bytes 1966088 | tf_op jit(solution)/shard_map/ppermute | solution.py:113
  53.6 48.4 %collective-permute-start.11 = (bf16[4,2,80,1280]{3,2,1,0:T(8,128)(2,1)S(1)}, bf16[4,2,80,1280]{3,2,1,0:T(8,128)(2,1)}, u32[]{:S(2)}, u32[]{:S(2)}) collective-permute-start(bf16[4,2,80,1280]{3,2,1,0:T(8,128)(2,1)S(1)} %pad_maximum_fusion.8), channel_id=1, source_target_pairs={{0,4},{4,8},{8,12},{12,0},{1,5},{5,9},{9,13},{13,1},{2,6},{6,10},{... | collective-permute-start | bytes 4915208 | tf_op jit(solution)/shard_map/ppermute | solution.py:29
  55.4 46.7 %collective-permute-start.12 = (bf16[4,2,80,1280]{3,2,1,0:T(8,128)(2,1)S(1)}, bf16[4,2,80,1280]{3,2,1,0:T(8,128)(2,1)}, u32[]{:S(2)}, u32[]{:S(2)}) collective-permute-start(bf16[4,2,80,1280]{3,2,1,0:T(8,128)(2,1)S(1)} %pad_maximum_fusion.8), channel_id=1, source_target_pairs={{0,12},{4,0},{8,4},{12,8},{1,13},{5,1},{9,5},{13,9},{2,14},{6,2},{... | collective-permute-start | bytes 4915208 | tf_op jit(solution)/shard_map/ppermute | solution.py:29
  57.1 44.9 %collective-permute-start.10 = (bf16[4,2,80,1280]{3,2,1,0:T(8,128)(2,1)S(1)}, bf16[4,2,80,1280]{3,2,1,0:T(8,128)(2,1)}, u32[]{:S(2)}, u32[]{:S(2)}) collective-permute-start(bf16[4,2,80,1280]{3,2,1,0:T(8,128)(2,1)S(1)} %pad_maximum_fusion.7), channel_id=1, source_target_pairs={{0,96},{32,0},{64,32},{96,64},{1,97},{33,1},{65,33},{97,65},{2,98}... | collective-permute-start | bytes 4915208 | tf_op jit(solution)/shard_map/ppermute | solution.py:29
  58.3 43.7 %collective-permute-start.9 = (bf16[4,2,80,1280]{3,2,1,0:T(8,128)(2,1)S(1)}, bf16[4,2,80,1280]{3,2,1,0:T(8,128)(2,1)}, u32[]{:S(2)}, u32[]{:S(2)}) collective-permute-start(bf16[4,2,80,1280]{3,2,1,0:T(8,128)(2,1)S(1)} %pad_maximum_fusion.7), channel_id=1, source_target_pairs={{0,32},{32,64},{64,96},{96,0},{1,33},{33,65},{65,97},{97,1},{2,34}... | collective-permute-start | bytes 4915208 | tf_op jit(solution)/shard_map/ppermute | solution.py:29
  59.8 24.2 %collective-permute-start.19 = (bf16[256,10,128]{0,2,1:T(8,128)(2,1)}, bf16[256,10,128]{0,2,1:T(8,128)(2,1)}, u32[]{:S(2)}, u32[]{:S(2)}) collective-permute-start(bf16[256,10,128]{0,2,1:T(8,128)(2,1)} %get-tuple-element.105), channel_id=1, source_target_pairs={{0,1},{1,0},{2,3},{3,2},{4,5},{5,4},{6,7},{7,6},{8,9},{9,8},{10,11... | collective-permute-start | bytes 1966088 | tf_op jit(solution)/shard_map/ppermute | solution.py:113
  103.2 21.2 %collective-permute-start.17 = (bf16[2,2,80,1280]{3,2,1,0:T(8,128)(2,1)S(1)}, bf16[2,2,80,1280]{3,2,1,0:T(8,128)(2,1)S(1)}, u32[]{:S(2)}, u32[]{:S(2)}) collective-permute-start(bf16[2,2,80,1280]{3,2,1,0:T(8,128)(2,1)S(1)} %slice.29), channel_id=1, source_target_pairs={{0,4},{4,8},{8,12},{12,0},{1,5},{5,9},{9,13},{13,1},{2,6},{6,10},{... | collective-permute-start | bytes 2457608 | tf_op jit(solution)/shard_map/ppermute | solution.py:41
  104.5 20.1 %collective-permute-start.18 = (bf16[2,2,80,1280]{3,2,1,0:T(8,128)(2,1)S(1)}, bf16[2,2,80,1280]{3,2,1,0:T(8,128)(2,1)S(1)}, u32[]{:S(2)}, u32[]{:S(2)}) collective-permute-start(bf16[2,2,80,1280]{3,2,1,0:T(8,128)(2,1)S(1)} %slice.30), channel_id=1, source_target_pairs={{0,12},{4,0},{8,4},{12,8},{1,13},{5,1},{9,5},{13,9},{2,14},{6,2},{... | collective-permute-start | bytes 2457608 | tf_op jit(solution)/shard_map/ppermute | solution.py:42
  107.3 30.6 %collective-permute-start.20 = (f32[10,256,128]{2,1,0:T(8,128)S(1)}, f32[10,256,128]{2,1,0:T(8,128)S(1)}, u32[]{:S(2)}, u32[]{:S(2)}) collective-permute-start(f32[10,256,128]{2,1,0:T(8,128)S(1)} %get-tuple-element.81), channel_id=1, source_target_pairs={{0,2},{1,3},{4,6},{5,7},{8,10},{9,11},{12,14},{13,15},{16,18},{17,... | collective-permute-start | bytes 3932168 | tf_op jit(solution)/shard_map/ppermute | solution.py:165
  112.5 20.3 %collective-permute-start.15 = (bf16[2,2,80,1280]{3,2,1,0:T(8,128)(2,1)}, bf16[2,2,80,1280]{3,2,1,0:T(8,128)(2,1)S(1)}, u32[]{:S(2)}, u32[]{:S(2)}) collective-permute-start(bf16[2,2,80,1280]{3,2,1,0:T(8,128)(2,1)} %slice.27), channel_id=1, source_target_pairs={{0,32},{32,64},{64,96},{96,0},{1,33},{33,65},{65,97},{97,1},{2,34}... | collective-permute-start | bytes 2457608 | tf_op jit(solution)/shard_map/ppermute | solution.py:41
  115.3 18.9 %collective-permute-start.16 = (bf16[2,2,80,1280]{3,2,1,0:T(8,128)(2,1)}, bf16[2,2,80,1280]{3,2,1,0:T(8,128)(2,1)}, u32[]{:S(2)}, u32[]{:S(2)}) collective-permute-start(bf16[2,2,80,1280]{3,2,1,0:T(8,128)(2,1)} %slice.28), channel_id=1, source_target_pairs={{0,96},{32,0},{64,32},{96,64},{1,97},{33,1},{65,33},{97,65},{2,98}... | collective-permute-start | bytes 2457608 | tf_op jit(solution)/shard_map/ppermute | solution.py:42
  151.3 6.8 %collective-permute-start.21 = (bf16[256,10,128]{2,0,1:T(8,128)(2,1)}, bf16[256,10,128]{2,0,1:T(8,128)(2,1)}, u32[]{:S(2)}, u32[]{:S(2)}) collective-permute-start(bf16[256,10,128]{2,0,1:T(8,128)(2,1)} %get-tuple-element.101), channel_id=1, source_target_pairs={{0,1},{1,0},{2,3},{3,2},{4,5},{5,4},{6,7},{7,6},{8,9},{9,8},{10,11... | collective-permute-start | bytes 1966088 | tf_op jit(solution)/shard_map/ppermute | solution.py:113
  162.2 11.2 %collective-permute-start.22 = (bf16[256,2560]{0,1:T(8,128)(2,1)}, bf16[256,2560]{0,1:T(8,128)(2,1)S(1)}, u32[]{:S(2)}, u32[]{:S(2)}) collective-permute-start(bf16[256,2560]{0,1:T(8,128)(2,1)} %bitcast.27), channel_id=1, source_target_pairs={{0,1},{1,0},{2,3},{3,2},{4,5},{5,4},{6,7},{7,6},{8,9},{9,8},{10,11... | collective-permute-start | bytes 3932168 | tf_op jit(solution)/shard_map/ppermute | solution.py:113
  186.7 11.4 %collective-permute-start.24 = (bf16[256,1280]{1,0:T(8,128)(2,1)}, bf16[256,1280]{1,0:T(8,128)(2,1)}, u32[]{:S(2)}, u32[]{:S(2)}) collective-permute-start(bf16[256,1280]{1,0:T(8,128)(2,1)} %get-tuple-element.97), channel_id=1, source_target_pairs={{0,1},{1,0},{2,3},{3,2},{4,5},{5,4},{6,7},{7,6},{8,9},{9,8},{10,11... | collective-permute-start | bytes 1966088 | tf_op jit(solution)/shard_map/ppermute | solution.py:113
  (10 other events, 191.2 us)

commit v16 on v13

--- a/solution.py
+++ b/solution.py
@@ -181,12 +181,12 @@
         "cihf,chfe->cihe", query_blocks, before, preferred_element_type=jnp.float32
     )
     attended = (inside_block + from_before).reshape(span, heads_here, HEAD)
+    sent, attended = lax.optimization_barrier((sent, attended))
     gain_rows = lax.dynamic_slice_in_dim(head_gain, core * heads_here, heads_here, 0)
     normed_group = normalize(attended, gain_rows)
     normed_own = pair_exchange(normed_group, core, 0, 1)
     normed_own = normed_own.reshape(tokens_here, H * HEAD)
     tokens = jnp.concatenate([normed_own, swap(normed_own, "c")], axis=0)
-    sent, tokens = lax.optimization_barrier((sent, tokens))
     by_block = tokens.reshape(tokens.shape[0], 32, -1)
     wide = []
     for rows, source in gather_finish(parts, sent):

time: 216 us -> 201 us (0.931)
  waiting for transfers between devices: 69.7 us -> 43.9 us
  other arithmetic: 42.4 us -> 48.5 us
  local copies, waits for them, and re-layouts: 38.4 us -> 43.8 us
    ppermute x1, waiting for transfers between devices: 15.2 us -> 0.01 us  [on_device(): earlier = lax.ppermute(chip_total, 'xh', [(0, 1)])]
    ppermute x2, waiting for transfers between devices: 12.4 us -> 0.01 us  [ring_far(): lax.ppermute(from_left[:half], axis, forward)]
    dot_general x2, matrix products: 7.24 us -> 13 us  [on_device(): jnp.dot(features, rows, preferred_element_type=jnp.float32)]
    another operation x4, other arithmetic: 11.4 us -> 16.2 us  [ring_finish(): return jnp.stack((x,) + tuple(received))]
    unnamed x39 -> x41, local copies, waits for them, and re-layouts: 5.85 us -> 9.89 us
    select_n x2, other arithmetic: 0.59 us -> 3.44 us  [pair_exchange(): jnp.where(core == 0, jnp.concatenate([mine, received], axis=join_axis), j...]
    dot_general x1, matrix products: 4.46 us -> 1.98 us  [on_device(): jnp.einsum('cjhf,cjhe->chfe', key_blocks, value_blocks, preferred_element...]
    ppermute x4, waiting for transfers between devices: 8.89 us -> 11.3 us  [ring_send(): return (lax.ppermute(x, axis, forward), lax.ppermute(x, axis, backward))]
  transfers between devices with their start and end apart: 25 -> 25, of which waited for: 14 -> 11; matrix products, arithmetic and copies ran while one was open for 35% -> 40% of each run, Pallas kernels for 0% -> 0%
where the time goes in v16:
time: 201 us; the launch traced here: 199 us
  other arithmetic  48.5 us (24%)
  waiting for transfers between devices  43.9 us (22%)
  local copies, waits for them, and re-layouts  43.8 us (22%)
  starting transfers between devices  38.7 us (19%)
  matrix products  23.3 us (12%)
    ppermute x6, waiting for transfers between devices, ring_direct(): lax.ppermute(x, axis, [(k, (k + shift) % size) for k in range(size)])  19.7 us
    another operation x4, other arithmetic, ring_finish(): return jnp.stack((x,) + tuple(received))  16.2 us
    dot_general x2, matrix products, on_device(): jnp.dot(features, rows, preferred_element_type=jnp.float32)  13 us
    max x4, local copies, waits for them, and re-layouts, featurize(): rectified = jnp.maximum(block.astype(jnp.float32), 0.0)  11.9 us
    ppermute x9, starting transfers between devices, swap(): return lax.ppermute(x, axis, [(0, 1), (1, 0)])  11.5 us
    ppermute x4, waiting for transfers between devices, ring_send(): return (lax.ppermute(x, axis, forward), lax.ppermute(x, axis, backward))  11.3 us
    ppermute x6, starting transfers between devices, ring_direct(): lax.ppermute(x, axis, [(k, (k + shift) % size) for k in range(size)])  10.9 us
    unnamed x41, local copies, waits for them, and re-layouts  9.89 us
  transfers between devices with their start and end apart: 25, of which 11 were waited for; matrix products, arithmetic and copies ran while one was open for 40% of the time, Pallas kernels for 0%

profile of v16, /device:TPU:1, one launch (start us, length us, event | category | flops | bytes accessed | tf_op | source)
XLA Modules:
  0.0 199.2 jit_solution(4538426684130621948)
XLA Ops:
  3.4 3.6 %collective-permute-start.1 = (bf16[80,1280]{1,0:T(8,128)(2,1)S(1)}, bf16[80,1280]{1,0:T(8,128)(2,1)S(1)}, u32[]{:S(2)}, u32[]{:S(2)}) collective-permute-start(bf16[80,1280]{1,0:T(8,128)(2,1)S(1)} %get-tuple-element.93), channel_id=1, source_target_pairs={{0,2},{2,0},{1,3},{3,1},{4,6},{6,4},{5,7},{7,5},{8,10},{10,8},{9,1... | collective-permute-start | bytes 614408 | tf_op jit(solution)/shard_map/ppermute | solution.py:116
  11.2 5.6 %collective-permute-done.2 = bf16[80,1280]{1,0:T(8,128)(2,1)S(1)} collective-permute-done((bf16[80,1280]{1,0:T(8,128)(2,1)S(1)}, bf16[80,1280]{1,0:T(8,128)(2,1)S(1)}, u32[]{:S(2)}, u32[]{:S(2)}) %collective-permute-start.2) | collective-permute-done | bytes 204832 | tf_op jit(solution)/shard_map/ppermute | solution.py:71
  20.3 3.3 %collective-permute-start.9 = (bf16[2,80,1280]{2,1,0:T(8,128)(2,1)}, bf16[2,80,1280]{2,1,0:T(8,128)(2,1)}, u32[]{:S(2)}, u32[]{:S(2)}) collective-permute-start(bf16[2,80,1280]{2,1,0:T(8,128)(2,1)} %pad_maximum_fusion.18), channel_id=1, source_target_pairs={{0,64},{32,96},{64,0},{96,32},{1,65},{33,97},{65,1},{97,33},{2,66}... | collective-permute-start | bytes 1228808 | tf_op jit(solution)/shard_map/ppermute | solution.py:62
  33.4 8.3 %collective-permute-done.9 = bf16[2,80,1280]{2,1,0:T(8,128)(2,1)} collective-permute-done((bf16[2,80,1280]{2,1,0:T(8,128)(2,1)}, bf16[2,80,1280]{2,1,0:T(8,128)(2,1)}, u32[]{:S(2)}, u32[]{:S(2)}) %collective-permute-start.9) | collective-permute-done | bytes 409632 | tf_op jit(solution)/shard_map/ppermute | solution.py:62
  41.8 2.9 %collective-permute-start.4 = (bf16[2,80,1280]{2,1,0:T(8,128)(2,1)}, bf16[2,80,1280]{2,1,0:T(8,128)(2,1)S(1)}, u32[]{:S(2)}, u32[]{:S(2)}) collective-permute-start(bf16[2,80,1280]{2,1,0:T(8,128)(2,1)} %pad_maximum_fusion.17), channel_id=1, source_target_pairs={{0,8},{4,12},{8,0},{12,4},{1,9},{5,13},{9,1},{13,5},{2,10},{6,14},... | collective-permute-start | bytes 1228808 | tf_op jit(solution)/shard_map/ppermute | solution.py:62
  46.4 3.4 %fusion.31 = (bf16[1,4,2,80,1280]{4,3,2,1,0:T(8,128)(2,1)}, bf16[4,2,80,1280]{3,2,1,0:T(8,128)(2,1)}) fusion(bf16[1,2,80,1280]{3,2,1,0:T(8,128)(2,1)} %bitcast.16, bf16[1,2,80,1280]{3,2,1,0:T(8,128)(2,1)} %bitcast.15, bf16[1,2,80,1280]{3,2,1,0:T(8,128)(2,1)} %bitcast.14, bf16[1,2,80,1280]{3,2,1,0:T(8,128)(2,1)} %bitcast.13), kind=kLoop, calls=%fused_computation.112 | loop fusion | flops 2457600 | bytes 4915200 | tf_op jit(solution)/shard_map/stack | solution.py:50
  54.4 8.6 %collective-permute-done.5 = bf16[2,80,1280]{2,1,0:T(8,128)(2,1)S(1)} collective-permute-done((bf16[2,80,1280]{2,1,0:T(8,128)(2,1)}, bf16[2,80,1280]{2,1,0:T(8,128)(2,1)S(1)}, u32[]{:S(2)}, u32[]{:S(2)}) %collective-permute-start.5) | collective-permute-done | bytes 409632 | tf_op jit(solution)/shard_map/ppermute | solution.py:62
  63.1 3.3 %collective-permute-start.12 = (bf16[4,2,80,1280]{3,2,1,0:T(8,128)(2,1)}, bf16[4,2,80,1280]{3,2,1,0:T(8,128)(2,1)}, u32[]{:S(2)}, u32[]{:S(2)}) collective-permute-start(bf16[4,2,80,1280]{3,2,1,0:T(8,128)(2,1)} %get-tuple-element.102), channel_id=1, source_target_pairs={{0,12},{4,0},{8,4},{12,8},{1,13},{5,1},{9,5},{13,9},{2,14},{6,2},{... | collective-permute-start | bytes 4915208 | tf_op jit(solution)/shard_map/ppermute | solution.py:29
  73.0 3.9 %convert_maximum_fusion = (f32[512,10,128]{0,2,1:T(8,128)S(1)}, f32[512,10,128]{0,2,1:T(8,128)}) fusion(bf16[256,10,128]{0,2,1:T(8,128)(2,1)} %collective-permute-done.19, bf16[256,10,128]{0,2,1:T(8,128)(2,1)} %get-tuple-element.111, pred[]{:T(512)S(6)} %eq.17, bf16[256,10,128]{0,2,1:T(8,128)(2,1)S(1)} %copy-done.14, ...), kind=kLoop, calls=%fused_computation.22 | loop fusion | flops 14417920 | bytes 7864321 | tf_op jit(solution)/shard_map/max | solution.py:100
  76.8 3.2 %copy.15 = f32[512,10,128]{2,0,1:T(8,128)} copy(f32[512,10,128]{0,2,1:T(8,128)} %get-tuple-element.124) | data formatting | bytes 5242880 | tf_op jit(solution)/shard_map/max | solution.py:100
  80.0 3.2 %copy.16 = f32[4,128,10,128]{1,3,2,0:T(8,128)} copy(f32[4,128,10,128]{3,1,0,2:T(8,128)} %bitcast.57) | data formatting | bytes 5242880 | tf_op jit(solution)/shard_map/max | solution.py:100
  85.4 3.4 %copy.22 = f32[4,128,10,128]{1,3,2,0:T(8,128)} copy(f32[4,128,10,128]{3,1,0,2:T(8,128)} %bitcast.58) | data formatting | bytes 5242880 | tf_op jit(solution)/shard_map/max | solution.py:100
  88.7 4.4 %multiply_convert_fusion.4 = (bf16[4,128,10,128]{1,3,2,0:T(8,128)(2,1)S(1)}, bf16[4,128,10,128]{1,3,2,0:T(8,128)(2,1)S(1)}, bf16[4,128,10,128]{1,3,2,0:T(8,128)(2,1)}, bf16[4,128,10,128]{1,3,2,0:T(8,128)(2,1)}) fusion(f32[4,128,10,128]{1,3,2,0:T(8,128)S(1)} %copy-done.3, f32[4,128]{1,0:T(4,128)S(1)} %get-tuple-element.126, ...), kind=kLoop, calls=%fused_computation.24 | loop fusion | flops 5242880 | bytes 10489856 | tf_op jit(solution)/shard_map/convert.2
  95.1 6.2 %collective-permute-done.12 = bf16[4,2,80,1280]{3,2,1,0:T(8,128)(2,1)} collective-permute-done((bf16[4,2,80,1280]{3,2,1,0:T(8,128)(2,1)}, bf16[4,2,80,1280]{3,2,1,0:T(8,128)(2,1)}, u32[]{:S(2)}, u32[]{:S(2)}) %collective-permute-start.12) | collective-permute-done | bytes 1638432 | tf_op jit(solution)/shard_map/ppermute | solution.py:29
  101.4 5.0 %collective-permute-done.6 = bf16[4,2,80,1280]{3,2,1,0:T(8,128)(2,1)} collective-permute-done((bf16[4,2,80,1280]{3,2,1,0:T(8,128)(2,1)}, bf16[4,2,80,1280]{3,2,1,0:T(8,128)(2,1)}, u32[]{:S(2)}, u32[]{:S(2)}) %collective-permute-start.6) | collective-permute-done | bytes 1638432 | tf_op jit(solution)/shard_map/ppermute | solution.py:29
  106.4 3.0 %collective-permute-start.20 = (f32[10,256,128]{2,1,0:T(8,128)}, f32[10,256,128]{2,1,0:T(8,128)}, u32[]{:S(2)}, u32[]{:S(2)}) collective-permute-start(f32[10,256,128]{2,1,0:T(8,128)} %get-tuple-element.81), channel_id=1, source_target_pairs={{0,2},{1,3},{4,6},{5,7},{8,10},{9,11},{12,14},{13,15},{16,18},{17,... | collective-permute-start | bytes 3932168 | tf_op jit(solution)/shard_map/ppermute | solution.py:168
  129.1 4.9 %fusion.3 = f32[4,10,128,128]{2,3,1,0:T(8,128)} fusion(bf16[4,128,10,128]{1,3,2,0:T(8,128)(2,1)S(1)} %copy-done.7, bf16[4,128,10,128]{1,3,2,0:T(8,128)(2,1)S(1)} %copy-done.8, bf16[4,128,10,128]{1,3,2,0:T(8,128)(2,1)} %copy-done.11, bf16[4,128,10,128]{1,3,2,0:T(8,128)(2,1)} %copy-done.10, pred[128,128]{1,0:T(8,128)(4,1)S(1)} %iota_compare_fusion, ...), kind=kOutput, calls=%fused_computation.33 | convolution fusion | flops 515112960 | bytes 9191424 | tf_op jit(solution)/shard_map/chij,cjhe->cihe/dot_general | solution.py:174
  141.0 3.5 %add_bitcast_fusion = f32[4,128,10,128]{3,1,2,0:T(8,128)S(1)} fusion(f32[4,10,128,128]{2,3,1,0:T(8,128)} %fusion.3, f32[3,10,256,128]{3,2,1,0:T(8,128)S(1)} %slice-done, f32[10,256,128]{2,1,0:T(8,128)} %collective-permute-done.20, bf16[4,128,10,128]{1,3,2,0:T(8,128)(2,1)S(1)} %copy-done.7, bf16[4,128,10,128]{1,3,2,0:T(8,128)(2,1)S(1)} %copy-done.9), kind=kOutput, calls=%fused_computation.17 | convolution fusion | flops 344064000 | bytes 13107200 | tf_op jit(solution)/shard_map/cihf,chfe->cihe/dot_general | solution.py:180
  147.4 3.7 %collective-permute-start.21 = (bf16[256,10,128]{2,0,1:T(8,128)(2,1)S(1)}, bf16[256,10,128]{2,0,1:T(8,128)(2,1)S(1)}, u32[]{:S(2)}, u32[]{:S(2)}) collective-permute-start(bf16[256,10,128]{2,0,1:T(8,128)(2,1)S(1)} %get-tuple-element.110), channel_id=1, source_target_pairs={{0,1},{1,0},{2,3},{3,2},{4,5},{5,4},{6,7},{7,6},{8,9},{9,8},{10,11... | collective-permute-start | bytes 1966088 | tf_op jit(solution)/shard_map/ppermute | solution.py:116
  153.7 3.1 %maximum_select_fusion.3 = bf16[256,20,128]{2,0,1:T(8,128)(2,1)} fusion(bf16[256,10,128]{2,0,1:T(8,128)(2,1)} %copy-done.18, bf16[256,10,128]{2,0,1:T(8,128)(2,1)} %get-tuple-element.109, pred[]{:T(512)S(6)} %eq.17), kind=kLoop, calls=%fused_computation.37 | loop fusion | flops 1966080 | bytes 2621441 | tf_op jit(solution)/shard_map/jit(_where)/select_n | solution.py:124
  159.6 5.4 %pad_maximum_fusion.1 = bf16[4,4,2,80,1280]{4,3,2,1,0:T(8,128)(2,1)} fusion(bf16[1,4,2,80,1280]{4,3,2,1,0:T(8,128)(2,1)} %bitcast.39, bf16[1,4,2,80,1280]{4,3,2,1,0:T(8,128)(2,1)S(1)} %bitcast.59, bf16[1,4,2,80,1280]{4,3,2,1,0:T(8,128)(2,1)} %bitcast.37, bf16[1,4,2,80,1280]{4,3,2,1,0:T(8,128)(2,1)S(1)} %copy-done.4), kind=kLoop, calls=%fused_computation.7 | loop fusion | flops 9830400 | bytes 13107200 | tf_op jit(solution)/shard_map/stack | solution.py:50
  165.0 5.4 %pad_maximum_fusion = bf16[4,4,2,80,1280]{4,3,2,1,0:T(8,128)(2,1)} fusion(bf16[1,4,2,80,1280]{4,3,2,1,0:T(8,128)(2,1)} %bitcast.32, bf16[1,4,2,80,1280]{4,3,2,1,0:T(8,128)(2,1)S(1)} %bitcast.60, bf16[1,4,2,80,1280]{4,3,2,1,0:T(8,128)(2,1)} %bitcast.30, bf16[1,4,2,80,1280]{4,3,2,1,0:T(8,128)(2,1)S(1)} %copy-done.5), kind=kLoop, calls=%fused_computation.6 | loop fusion | flops 9830400 | bytes 13107200 | tf_op jit(solution)/shard_map/stack | solution.py:50
  175.0 6.5 %convolution_convert_fusion = bf16[512,1280]{1,0:T(8,128)(2,1)S(1)} fusion(bf16[512,2560]{0,1:T(8,128)(2,1)S(1)} %bitcast.70, bf16[2560,1280]{1,0:T(8,128)(2,1)} %bitcast.62), kind=kOutput, calls=%fused_computation.9 | convolution fusion | flops 3356098560 | bytes 10485760 | tf_op jit(solution)/shard_map/dot_general | solution.py:195
  186.8 6.5 %convolution_convert_fusion.1 = bf16[512,1280]{1,0:T(8,128)(2,1)S(1)} fusion(bf16[512,2560]{0,1:T(8,128)(2,1)S(1)} %bitcast.71, bf16[2560,1280]{1,0:T(8,128)(2,1)} %bitcast.61), kind=kOutput, calls=%fused_computation.10 | convolution fusion | flops 3356098560 | bytes 10485760 | tf_op jit(solution)/shard_map/dot_general | solution.py:195
  (121 shorter events, 90.8 us)
Async XLA Ops:
  3.4 7.9 %collective-permute-start.1 = (bf16[80,1280]{1,0:T(8,128)(2,1)S(1)}, bf16[80,1280]{1,0:T(8,128)(2,1)S(1)}, u32[]{:S(2)}, u32[]{:S(2)}) collective-permute-start(bf16[80,1280]{1,0:T(8,128)(2,1)S(1)} %get-tuple-element.93), channel_id=1, source_target_pairs={{0,2},{2,0},{1,3},{3,1},{4,6},{6,4},{5,7},{7,5},{8,10},{10,8},{9,1... | collective-permute-start | bytes 614408 | tf_op jit(solution)/shard_map/ppermute | solution.py:116
  6.9 9.9 %collective-permute-start.2 = (bf16[80,1280]{1,0:T(8,128)(2,1)S(1)}, bf16[80,1280]{1,0:T(8,128)(2,1)S(1)}, u32[]{:S(2)}, u32[]{:S(2)}) collective-permute-start(bf16[80,1280]{1,0:T(8,128)(2,1)S(1)} %get-tuple-element.93), channel_id=1, source_target_pairs={{0,18},{2,16},{16,2},{18,0},{1,19},{3,17},{17,3},{19,1},{4,22},{6,... | collective-permute-start | bytes 614408 | tf_op jit(solution)/shard_map/ppermute | solution.py:71
  7.8 9.9 %collective-permute-start = (bf16[80,1280]{1,0:T(8,128)(2,1)S(1)}, bf16[80,1280]{1,0:T(8,128)(2,1)S(1)}, u32[]{:S(2)}, u32[]{:S(2)}) collective-permute-start(bf16[80,1280]{1,0:T(8,128)(2,1)S(1)} %get-tuple-element.93), channel_id=1, source_target_pairs={{0,16},{16,0},{1,17},{17,1},{2,18},{18,2},{3,19},{19,3},{4,20},{20... | collective-permute-start | bytes 614408 | tf_op jit(solution)/shard_map/ppermute | solution.py:116
  18.5 13.7 %collective-permute-start.8 = (bf16[2,80,1280]{2,1,0:T(8,128)(2,1)}, bf16[2,80,1280]{2,1,0:T(8,128)(2,1)}, u32[]{:S(2)}, u32[]{:S(2)}) collective-permute-start(bf16[2,80,1280]{2,1,0:T(8,128)(2,1)} %pad_maximum_fusion.18), channel_id=1, source_target_pairs={{0,32},{32,64},{64,96},{96,0},{1,33},{33,65},{65,97},{97,1},{2,34}... | collective-permute-start | bytes 1228808 | tf_op jit(solution)/shard_map/ppermute | solution.py:62
  20.3 21.5 %collective-permute-start.9 = (bf16[2,80,1280]{2,1,0:T(8,128)(2,1)}, bf16[2,80,1280]{2,1,0:T(8,128)(2,1)}, u32[]{:S(2)}, u32[]{:S(2)}) collective-permute-start(bf16[2,80,1280]{2,1,0:T(8,128)(2,1)} %pad_maximum_fusion.18), channel_id=1, source_target_pairs={{0,64},{32,96},{64,0},{96,32},{1,65},{33,97},{65,1},{97,33},{2,66}... | collective-permute-start | bytes 1228808 | tf_op jit(solution)/shard_map/ppermute | solution.py:62
  23.6 21.1 %collective-permute-start.10 = (bf16[2,80,1280]{2,1,0:T(8,128)(2,1)}, bf16[2,80,1280]{2,1,0:T(8,128)(2,1)}, u32[]{:S(2)}, u32[]{:S(2)}) collective-permute-start(bf16[2,80,1280]{2,1,0:T(8,128)(2,1)} %pad_maximum_fusion.18), channel_id=1, source_target_pairs={{0,96},{32,0},{64,32},{96,64},{1,97},{33,1},{65,33},{97,65},{2,98}... | collective-permute-start | bytes 1228808 | tf_op jit(solution)/shard_map/ppermute | solution.py:62
  27.1 41.2 %collective-permute-start.13 = (bf16[256,10,128]{0,2,1:T(8,128)(2,1)}, bf16[256,10,128]{0,2,1:T(8,128)(2,1)}, u32[]{:S(2)}, u32[]{:S(2)}) collective-permute-start(bf16[256,10,128]{0,2,1:T(8,128)(2,1)} %get-tuple-element.116), channel_id=1, source_target_pairs={{0,1},{1,0},{2,3},{3,2},{4,5},{5,4},{6,7},{7,6},{8,9},{9,8},{10,11... | collective-permute-start | bytes 1966088 | tf_op jit(solution)/shard_map/ppermute | solution.py:116
  31.0 37.4 %collective-permute-start.14 = (bf16[256,10,128]{0,2,1:T(8,128)(2,1)}, bf16[256,10,128]{0,2,1:T(8,128)(2,1)S(1)}, u32[]{:S(2)}, u32[]{:S(2)}) collective-permute-start(bf16[256,10,128]{0,2,1:T(8,128)(2,1)} %get-tuple-element.114), channel_id=1, source_target_pairs={{0,1},{1,0},{2,3},{3,2},{4,5},{5,4},{6,7},{7,6},{8,9},{9,8},{10,11... | collective-permute-start | bytes 1966088 | tf_op jit(solution)/shard_map/ppermute | solution.py:116
  32.1 17.7 %collective-permute-start.3 = (bf16[2,80,1280]{2,1,0:T(8,128)(2,1)}, bf16[2,80,1280]{2,1,0:T(8,128)(2,1)S(1)}, u32[]{:S(2)}, u32[]{:S(2)}) collective-permute-start(bf16[2,80,1280]{2,1,0:T(8,128)(2,1)} %pad_maximum_fusion.17), channel_id=1, source_target_pairs={{0,4},{4,8},{8,12},{12,0},{1,5},{5,9},{9,13},{13,1},{2,6},{6,10},{... | collective-permute-start | bytes 1228808 | tf_op jit(solution)/shard_map/ppermute | solution.py:62
  41.8 11.5 %collective-permute-start.4 = (bf16[2,80,1280]{2,1,0:T(8,128)(2,1)}, bf16[2,80,1280]{2,1,0:T(8,128)(2,1)S(1)}, u32[]{:S(2)}, u32[]{:S(2)}) collective-permute-start(bf16[2,80,1280]{2,1,0:T(8,128)(2,1)} %pad_maximum_fusion.17), channel_id=1, source_target_pairs={{0,8},{4,12},{8,0},{12,4},{1,9},{5,13},{9,1},{13,5},{2,10},{6,14},... | collective-permute-start | bytes 1228808 | tf_op jit(solution)/shard_map/ppermute | solution.py:62
  44.7 18.4 %collective-permute-start.5 = (bf16[2,80,1280]{2,1,0:T(8,128)(2,1)}, bf16[2,80,1280]{2,1,0:T(8,128)(2,1)S(1)}, u32[]{:S(2)}, u32[]{:S(2)}) collective-permute-start(bf16[2,80,1280]{2,1,0:T(8,128)(2,1)} %pad_maximum_fusion.17), channel_id=1, source_target_pairs={{0,12},{4,0},{8,4},{12,8},{1,13},{5,1},{9,5},{13,9},{2,14},{6,2},{... | collective-permute-start | bytes 1228808 | tf_op jit(solution)/shard_map/ppermute | solution.py:62
  49.8 23.2 %collective-permute-start.19 = (bf16[256,10,128]{0,2,1:T(8,128)(2,1)S(1)}, bf16[256,10,128]{0,2,1:T(8,128)(2,1)}, u32[]{:S(2)}, u32[]{:S(2)}) collective-permute-start(bf16[256,10,128]{0,2,1:T(8,128)(2,1)S(1)} %get-tuple-element.112), channel_id=1, source_target_pairs={{0,1},{1,0},{2,3},{3,2},{4,5},{5,4},{6,7},{7,6},{8,9},{9,8},{10,11... | collective-permute-start | bytes 1966088 | tf_op jit(solution)/shard_map/ppermute | solution.py:116
  53.3 41.9 %collective-permute-start.11 = (bf16[4,2,80,1280]{3,2,1,0:T(8,128)(2,1)}, bf16[4,2,80,1280]{3,2,1,0:T(8,128)(2,1)}, u32[]{:S(2)}, u32[]{:S(2)}) collective-permute-start(bf16[4,2,80,1280]{3,2,1,0:T(8,128)(2,1)} %get-tuple-element.102), channel_id=1, source_target_pairs={{0,4},{4,8},{8,12},{12,0},{1,5},{5,9},{9,13},{13,1},{2,6},{6,10},{... | collective-permute-start | bytes 4915208 | tf_op jit(solution)/shard_map/ppermute | solution.py:29
  63.1 38.3 %collective-permute-start.12 = (bf16[4,2,80,1280]{3,2,1,0:T(8,128)(2,1)}, bf16[4,2,80,1280]{3,2,1,0:T(8,128)(2,1)}, u32[]{:S(2)}, u32[]{:S(2)}) collective-permute-start(bf16[4,2,80,1280]{3,2,1,0:T(8,128)(2,1)} %get-tuple-element.102), channel_id=1, source_target_pairs={{0,12},{4,0},{8,4},{12,8},{1,13},{5,1},{9,5},{13,9},{2,14},{6,2},{... | collective-permute-start | bytes 4915208 | tf_op jit(solution)/shard_map/ppermute | solution.py:29
  68.3 38.1 %collective-permute-start.6 = (bf16[4,2,80,1280]{3,2,1,0:T(8,128)(2,1)}, bf16[4,2,80,1280]{3,2,1,0:T(8,128)(2,1)}, u32[]{:S(2)}, u32[]{:S(2)}) collective-permute-start(bf16[4,2,80,1280]{3,2,1,0:T(8,128)(2,1)} %get-tuple-element.104), channel_id=1, source_target_pairs={{0,32},{32,64},{64,96},{96,0},{1,33},{33,65},{65,97},{97,1},{2,34}... | collective-permute-start | bytes 4915208 | tf_op jit(solution)/shard_map/ppermute | solution.py:29
  68.4 38.1 %collective-permute-start.7 = (bf16[4,2,80,1280]{3,2,1,0:T(8,128)(2,1)}, bf16[4,2,80,1280]{3,2,1,0:T(8,128)(2,1)}, u32[]{:S(2)}, u32[]{:S(2)}) collective-permute-start(bf16[4,2,80,1280]{3,2,1,0:T(8,128)(2,1)} %get-tuple-element.104), channel_id=1, source_target_pairs={{0,96},{32,0},{64,32},{96,64},{1,97},{33,1},{65,33},{97,65},{2,98}... | collective-permute-start | bytes 4915208 | tf_op jit(solution)/shard_map/ppermute | solution.py:29
  106.4 34.6 %collective-permute-start.20 = (f32[10,256,128]{2,1,0:T(8,128)}, f32[10,256,128]{2,1,0:T(8,128)}, u32[]{:S(2)}, u32[]{:S(2)}) collective-permute-start(f32[10,256,128]{2,1,0:T(8,128)} %get-tuple-element.81), channel_id=1, source_target_pairs={{0,2},{1,3},{4,6},{5,7},{8,10},{9,11},{12,14},{13,15},{16,18},{17,... | collective-permute-start | bytes 3932168 | tf_op jit(solution)/shard_map/ppermute | solution.py:168
  111.5 22.5 %collective-permute-start.17 = (bf16[2,2,80,1280]{3,2,1,0:T(8,128)(2,1)}, bf16[2,2,80,1280]{3,2,1,0:T(8,128)(2,1)S(1)}, u32[]{:S(2)}, u32[]{:S(2)}) collective-permute-start(bf16[2,2,80,1280]{3,2,1,0:T(8,128)(2,1)} %slice.29), channel_id=1, source_target_pairs={{0,4},{4,8},{8,12},{12,0},{1,5},{5,9},{9,13},{13,1},{2,6},{6,10},{... | collective-permute-start | bytes 2457608 | tf_op jit(solution)/shard_map/ppermute | solution.py:41
  113.6 21.3 %collective-permute-start.18 = (bf16[2,2,80,1280]{3,2,1,0:T(8,128)(2,1)}, bf16[2,2,80,1280]{3,2,1,0:T(8,128)(2,1)}, u32[]{:S(2)}, u32[]{:S(2)}) collective-permute-start(bf16[2,2,80,1280]{3,2,1,0:T(8,128)(2,1)} %slice.30), channel_id=1, source_target_pairs={{0,12},{4,0},{8,4},{12,8},{1,13},{5,1},{9,5},{13,9},{2,14},{6,2},{... | collective-permute-start | bytes 2457608 | tf_op jit(solution)/shard_map/ppermute | solution.py:42
  118.4 18.8 %collective-permute-start.15 = (bf16[2,2,80,1280]{3,2,1,0:T(8,128)(2,1)}, bf16[2,2,80,1280]{3,2,1,0:T(8,128)(2,1)}, u32[]{:S(2)}, u32[]{:S(2)}) collective-permute-start(bf16[2,2,80,1280]{3,2,1,0:T(8,128)(2,1)} %slice.27), channel_id=1, source_target_pairs={{0,32},{32,64},{64,96},{96,0},{1,33},{33,65},{65,97},{97,1},{2,34}... | collective-permute-start | bytes 2457608 | tf_op jit(solution)/shard_map/ppermute | solution.py:41
  120.6 17.7 %collective-permute-start.16 = (bf16[2,2,80,1280]{3,2,1,0:T(8,128)(2,1)}, bf16[2,2,80,1280]{3,2,1,0:T(8,128)(2,1)}, u32[]{:S(2)}, u32[]{:S(2)}) collective-permute-start(bf16[2,2,80,1280]{3,2,1,0:T(8,128)(2,1)} %slice.28), channel_id=1, source_target_pairs={{0,96},{32,0},{64,32},{96,64},{1,97},{33,1},{65,33},{97,65},{2,98}... | collective-permute-start | bytes 2457608 | tf_op jit(solution)/shard_map/ppermute | solution.py:42
  147.4 5.4 %collective-permute-start.21 = (bf16[256,10,128]{2,0,1:T(8,128)(2,1)S(1)}, bf16[256,10,128]{2,0,1:T(8,128)(2,1)S(1)}, u32[]{:S(2)}, u32[]{:S(2)}) collective-permute-start(bf16[256,10,128]{2,0,1:T(8,128)(2,1)S(1)} %get-tuple-element.110), channel_id=1, source_target_pairs={{0,1},{1,0},{2,3},{3,2},{4,5},{5,4},{6,7},{7,6},{8,9},{9,8},{10,11... | collective-permute-start | bytes 1966088 | tf_op jit(solution)/shard_map/ppermute | solution.py:116
  159.2 11.3 %collective-permute-start.22 = (bf16[256,2560]{0,1:T(8,128)(2,1)}, bf16[256,2560]{0,1:T(8,128)(2,1)S(1)}, u32[]{:S(2)}, u32[]{:S(2)}) collective-permute-start(bf16[256,2560]{0,1:T(8,128)(2,1)} %bitcast.65), channel_id=1, source_target_pairs={{0,1},{1,0},{2,3},{3,2},{4,5},{5,4},{6,7},{7,6},{8,9},{9,8},{10,11... | collective-permute-start | bytes 3932168 | tf_op jit(solution)/shard_map/ppermute | solution.py:116
  182.5 11.4 %collective-permute-start.24 = (bf16[256,1280]{1,0:T(8,128)(2,1)}, bf16[256,1280]{1,0:T(8,128)(2,1)}, u32[]{:S(2)}, u32[]{:S(2)}) collective-permute-start(bf16[256,1280]{1,0:T(8,128)(2,1)} %get-tuple-element.105), channel_id=1, source_target_pairs={{0,1},{1,0},{2,3},{3,2},{4,5},{5,4},{6,7},{7,6},{8,9},{9,8},{10,11... | collective-permute-start | bytes 1966088 | tf_op jit(solution)/shard_map/ppermute | solution.py:116
  (21 other events, 160.7 us)

commit v17 on v10

--- a/solution.py
+++ b/solution.py
@@ -186,7 +186,7 @@
     by_block = tokens.reshape(tokens.shape[0], 32, -1)
     wide = []
     for rows, source in gather_finish(parts, sent):
-        features = jnp.take(by_block, source, axis=1).reshape(tokens.shape)
+        features = jnp.take(by_block, source, axis=1, mode="clip").reshape(tokens.shape)
         wide.append(
             jnp.dot(features, rows, preferred_element_type=jnp.float32).astype(jnp.bfloat16)
         )

time: 188 us -> 187 us (level)
  other arithmetic: 45.4 us -> 41.2 us
    select_n x2 -> x0, other arithmetic: 4.07 us -> none  [on_device(): features = jnp.take(by_block, source, axis=1).reshape(tokens.shape)]
    unnamed x41 -> x43, local copies, waits for them, and re-layouts: 8.06 us -> 8.06 us
where the time goes in v17:
time: 187 us; the launch traced here: 186 us
  local copies, waits for them, and re-layouts  43.4 us (23%)
  other arithmetic  41.2 us (22%)
  starting transfers between devices  38.2 us (20%)
  waiting for transfers between devices  37.2 us (20%)
  matrix products  24.9 us (13%)
    dot_general x2, matrix products, on_device(): jnp.dot(features, rows, preferred_element_type=jnp.float32)  14.5 us
    ppermute x4, waiting for transfers between devices, ring_send(): return (lax.ppermute(x, axis, forward), lax.ppermute(x, axis, backward))  12.5 us
    ppermute x6, starting transfers between devices, ring_direct(): lax.ppermute(x, axis, [(k, (k + shift) % size) for k in range(size)])  12.2 us
    max x4, local copies, waits for them, and re-layouts, featurize(): rectified = jnp.maximum(block.astype(jnp.float32), 0.0)  12 us
    ppermute x9, starting transfers between devices, swap(): return lax.ppermute(x, axis, [(0, 1), (1, 0)])  11.7 us
    another operation x2, other arithmetic, ring_finish(): return jnp.stack((x,) + tuple(received))  11.6 us
    ppermute x6, waiting for transfers between devices, ring_direct(): lax.ppermute(x, axis, [(k, (k + shift) % size) for k in range(size)])  9.95 us
    unnamed x43, local copies, waits for them, and re-layouts  8.06 us
  transfers between devices with their start and end apart: 25, of which 11 were waited for; matrix products, arithmetic and copies ran while one was open for 41% of the time, Pallas kernels for 0%

profile of v17, /device:TPU:1, one launch (start us, length us, event | category | flops | bytes accessed | tf_op | source)
XLA Modules:
  0.0 185.8 jit_solution(852095477197914884)
XLA Ops:
  0.7 2.7 %fusion.35 = (bf16[80,1280]{1,0:T(8,128)(2,1)S(1)}, f32[80,1280]{1,0:T(8,128)}, f32[80,1280]{1,0:T(8,128)}, f32[80,1280]{1,0:T(8,128)}) fusion(f32[80,1280]{1,0:T(8,128)} %param.16, f32[80,1280]{1,0:T(8,128)} %param.17, f32[80,1280]{1,0:T(8,128)} %param.18, f32[80,1280]{1,0:T(8,128)} %param.19), kind=kLoop, calls=%fused_computation.110 | loop fusion | flops 1638400 | bytes 3072000 | tf_op jit(solution)/shard_map/convert_element_type | solution.py:139
  3.4 3.6 %collective-permute-start.4 = (bf16[80,1280]{1,0:T(8,128)(2,1)S(1)}, bf16[80,1280]{1,0:T(8,128)(2,1)S(1)}, u32[]{:S(2)}, u32[]{:S(2)}) collective-permute-start(bf16[80,1280]{1,0:T(8,128)(2,1)S(1)} %get-tuple-element.88), channel_id=1, source_target_pairs={{0,2},{2,0},{1,3},{3,1},{4,6},{6,4},{5,7},{7,5},{8,10},{10,8},{9,1... | collective-permute-start | bytes 614408 | tf_op jit(solution)/shard_map/ppermute | solution.py:113
  7.8 3.5 %collective-permute-done.4 = bf16[80,1280]{1,0:T(8,128)(2,1)S(1)} collective-permute-done((bf16[80,1280]{1,0:T(8,128)(2,1)S(1)}, bf16[80,1280]{1,0:T(8,128)(2,1)S(1)}, u32[]{:S(2)}, u32[]{:S(2)}) %collective-permute-start.4) | collective-permute-done | bytes 204832 | tf_op jit(solution)/shard_map/ppermute | solution.py:113
  11.2 5.6 %collective-permute-done.5 = bf16[80,1280]{1,0:T(8,128)(2,1)S(1)} collective-permute-done((bf16[80,1280]{1,0:T(8,128)(2,1)S(1)}, bf16[80,1280]{1,0:T(8,128)(2,1)S(1)}, u32[]{:S(2)}, u32[]{:S(2)}) %collective-permute-start.5) | collective-permute-done | bytes 204832 | tf_op jit(solution)/shard_map/ppermute | solution.py:71
  20.3 3.4 %collective-permute-start.7 = (bf16[2,80,1280]{2,1,0:T(8,128)(2,1)}, bf16[2,80,1280]{2,1,0:T(8,128)(2,1)}, u32[]{:S(2)}, u32[]{:S(2)}) collective-permute-start(bf16[2,80,1280]{2,1,0:T(8,128)(2,1)} %get-tuple-element.109), channel_id=1, source_target_pairs={{0,64},{32,96},{64,0},{96,32},{1,65},{33,97},{65,1},{97,33},{2,66}... | collective-permute-start | bytes 1228808 | tf_op jit(solution)/shard_map/ppermute | solution.py:62
  35.1 6.0 %collective-permute-done.7 = bf16[2,80,1280]{2,1,0:T(8,128)(2,1)} collective-permute-done((bf16[2,80,1280]{2,1,0:T(8,128)(2,1)}, bf16[2,80,1280]{2,1,0:T(8,128)(2,1)}, u32[]{:S(2)}, u32[]{:S(2)}) %collective-permute-start.7) | collective-permute-done | bytes 409632 | tf_op jit(solution)/shard_map/ppermute | solution.py:62
  45.1 3.7 %collective-permute-done.2 = bf16[2,80,1280]{2,1,0:T(8,128)(2,1)S(1)} collective-permute-done((bf16[2,80,1280]{2,1,0:T(8,128)(2,1)S(1)}, bf16[2,80,1280]{2,1,0:T(8,128)(2,1)S(1)}, u32[]{:S(2)}, u32[]{:S(2)}) %collective-permute-start.2) | collective-permute-done | bytes 409632 | tf_op jit(solution)/shard_map/ppermute | solution.py:62
  59.8 4.0 %convert_maximum_fusion = (f32[512,10,128]{0,2,1:T(8,128)S(1)}, f32[512,10,128]{0,2,1:T(8,128)}) fusion(bf16[256,10,128]{0,2,1:T(8,128)(2,1)} %collective-permute-done.19, bf16[256,10,128]{0,2,1:T(8,128)(2,1)} %get-tuple-element.102, pred[]{:T(512)S(6)} %eq.17, bf16[256,10,128]{0,2,1:T(8,128)(2,1)S(1)} %copy-done.12, bf16[256,10,128]{0,2,1:T(8,128)(2,1)} %copy-done.17), kind=kLoop, calls=%fused_computation.22 | loop fusion | flops 14417920 | bytes 7864321 | tf_op jit(solution)/shard_map/max | solution.py:97
  63.8 3.3 %copy.15 = f32[512,10,128]{2,0,1:T(8,128)} copy(f32[512,10,128]{0,2,1:T(8,128)} %get-tuple-element.119) | data formatting | bytes 5242880 | tf_op jit(solution)/shard_map/max | solution.py:97
  67.0 3.2 %copy.16 = f32[4,128,10,128]{1,3,2,0:T(8,128)} copy(f32[4,128,10,128]{3,1,0,2:T(8,128)} %bitcast.61) | data formatting | bytes 5242880 | tf_op jit(solution)/shard_map/max | solution.py:97
  72.4 3.4 %copy.22 = f32[4,128,10,128]{1,3,2,0:T(8,128)} copy(f32[4,128,10,128]{3,1,0,2:T(8,128)} %bitcast.62) | data formatting | bytes 5242880 | tf_op jit(solution)/shard_map/max | solution.py:97
  75.8 4.3 %multiply_convert_fusion.4 = (bf16[4,128,10,128]{1,3,2,0:T(8,128)(2,1)S(1)}, bf16[4,128,10,128]{1,3,2,0:T(8,128)(2,1)S(1)}, bf16[4,128,10,128]{1,3,2,0:T(8,128)(2,1)}, bf16[4,128,10,128]{1,3,2,0:T(8,128)(2,1)}) fusion(f32[4,128,10,128]{1,3,2,0:T(8,128)S(1)} %copy-done.3, f32[4,128]{1,0:T(4,128)S(1)} %get-tuple-element.121, ...), kind=kLoop, calls=%fused_computation.24 | loop fusion | flops 5242880 | bytes 10489856 | tf_op jit(solution)/shard_map/convert.2
  82.0 11.4 %collective-permute-done.10 = bf16[4,2,80,1280]{3,2,1,0:T(8,128)(2,1)} collective-permute-done((bf16[4,2,80,1280]{3,2,1,0:T(8,128)(2,1)}, bf16[4,2,80,1280]{3,2,1,0:T(8,128)(2,1)}, u32[]{:S(2)}, u32[]{:S(2)}) %collective-permute-start.10) | collective-permute-done | bytes 1638432 | tf_op jit(solution)/shard_map/ppermute | solution.py:29
  94.5 4.0 %collective-permute-start.20 = (f32[10,256,128]{2,1,0:T(8,128)}, f32[10,256,128]{2,1,0:T(8,128)}, u32[]{:S(2)}, u32[]{:S(2)}) collective-permute-start(f32[10,256,128]{2,1,0:T(8,128)} %get-tuple-element.80), channel_id=1, source_target_pairs={{0,2},{1,3},{4,6},{5,7},{8,10},{9,11},{12,14},{13,15},{16,18},{17,... | collective-permute-start | bytes 3932168 | tf_op jit(solution)/shard_map/ppermute | solution.py:164
  118.2 4.8 %fusion.3 = f32[4,10,128,128]{2,3,1,0:T(8,128)} fusion(bf16[4,128,10,128]{1,3,2,0:T(8,128)(2,1)S(1)} %copy-done.4, bf16[4,128,10,128]{1,3,2,0:T(8,128)(2,1)S(1)} %copy-done.6, bf16[4,128,10,128]{1,3,2,0:T(8,128)(2,1)} %copy-done.9, bf16[4,128,10,128]{1,3,2,0:T(8,128)(2,1)} %copy-done.8, pred[128,128]{1,0:T(8,128)(4,1)S(1)} %iota_compare_fusion, ...), kind=kOutput, calls=%fused_computation.31 | convolution fusion | flops 515112960 | bytes 9191424 | tf_op jit(solution)/shard_map/chij,cjhe->cihe/dot_general | solution.py:170
  129.0 3.5 %add_bitcast_fusion = f32[4,128,10,128]{3,1,2,0:T(8,128)S(1)} fusion(f32[4,10,128,128]{2,3,1,0:T(8,128)} %fusion.3, f32[3,10,256,128]{3,2,1,0:T(8,128)S(1)} %slice-done, f32[10,256,128]{2,1,0:T(8,128)} %collective-permute-done.20, bf16[4,128,10,128]{1,3,2,0:T(8,128)(2,1)S(1)} %copy-done.5, bf16[4,128,10,128]{1,3,2,0:T(8,128)(2,1)S(1)} %copy-done.7), kind=kOutput, calls=%fused_computation.17 | convolution fusion | flops 344064000 | bytes 13107200 | tf_op jit(solution)/shard_map/cihf,chfe->cihe/dot_general | solution.py:176
  135.5 3.7 %collective-permute-start.21 = (bf16[256,10,128]{2,0,1:T(8,128)(2,1)}, bf16[256,10,128]{2,0,1:T(8,128)(2,1)}, u32[]{:S(2)}, u32[]{:S(2)}) collective-permute-start(bf16[256,10,128]{2,0,1:T(8,128)(2,1)} %get-tuple-element.101), channel_id=1, source_target_pairs={{0,1},{1,0},{2,3},{3,2},{4,5},{5,4},{6,7},{7,6},{8,9},{9,8},{10,11... | collective-permute-start | bytes 1966088 | tf_op jit(solution)/shard_map/ppermute | solution.py:113
  141.3 2.9 %maximum_select_fusion.3 = bf16[256,20,128]{2,0,1:T(8,128)(2,1)} fusion(bf16[256,10,128]{2,0,1:T(8,128)(2,1)} %collective-permute-done.21, bf16[256,10,128]{2,0,1:T(8,128)(2,1)} %get-tuple-element.100, pred[]{:T(512)S(6)} %eq.17), kind=kLoop, calls=%fused_computation.35 | loop fusion | flops 1966080 | bytes 2621441 | tf_op jit(solution)/shard_map/jit(_where)/select_n | solution.py:121
  147.0 5.7 %pad_maximum_fusion.1 = bf16[4,4,2,80,1280]{4,3,2,1,0:T(8,128)(2,1)} fusion(bf16[1,4,2,80,1280]{4,3,2,1,0:T(8,128)(2,1)} %bitcast.41, bf16[1,4,2,80,1280]{4,3,2,1,0:T(8,128)(2,1)S(1)} %bitcast.65, bf16[1,4,2,80,1280]{4,3,2,1,0:T(8,128)(2,1)} %bitcast.39, bf16[1,4,2,80,1280]{4,3,2,1,0:T(8,128)(2,1)} %bitcast.38), kind=kLoop, calls=%fused_computation.7 | loop fusion | flops 9830400 | bytes 13107200 | tf_op jit(solution)/shard_map/stack | solution.py:50
  152.8 5.8 %pad_maximum_fusion = bf16[4,4,2,80,1280]{4,3,2,1,0:T(8,128)(2,1)} fusion(bf16[1,4,2,80,1280]{4,3,2,1,0:T(8,128)(2,1)} %bitcast.33, bf16[1,4,2,80,1280]{4,3,2,1,0:T(8,128)(2,1)S(1)} %bitcast.66, bf16[1,4,2,80,1280]{4,3,2,1,0:T(8,128)(2,1)} %bitcast.31, bf16[1,4,2,80,1280]{4,3,2,1,0:T(8,128)(2,1)} %bitcast.30), kind=kLoop, calls=%fused_computation.6 | loop fusion | flops 9830400 | bytes 13107200 | tf_op jit(solution)/shard_map/stack | solution.py:50
  161.2 7.3 %convolution_convert_fusion = bf16[512,1280]{1,0:T(8,128)(2,1)S(1)} fusion(bf16[512,2560]{0,1:T(8,128)(2,1)} %bitcast.64, bf16[2560,1280]{1,0:T(8,128)(2,1)} %bitcast.68), kind=kOutput, calls=%fused_computation.9 | convolution fusion | flops 3356098560 | bytes 10485760 | tf_op jit(solution)/shard_map/dot_general | solution.py:191
  171.7 7.3 %convolution_convert_fusion.1 = bf16[512,1280]{1,0:T(8,128)(2,1)S(1)} fusion(bf16[512,2560]{0,1:T(8,128)(2,1)} %bitcast.63, bf16[2560,1280]{1,0:T(8,128)(2,1)} %bitcast.67), kind=kOutput, calls=%fused_computation.10 | convolution fusion | flops 3356098560 | bytes 10485760 | tf_op jit(solution)/shard_map/dot_general | solution.py:191
  182.2 2.9 %conditional.1 = (bf16[1,256,5120]{2,1,0:T(8,128)(2,1)}) conditional(s32[]{:T(128)} %clamp.3, (bf16[256,1280]{1,0:T(8,128)(2,1)S(1)}, bf16[256,1280]{1,0:T(8,128)(2,1)S(1)}, bf16[256,1280]{1,0:T(8,128)(2,1)S(1)}, bf16[256,1280]{1,0:T(8,128)(2,1)}) %tuple.30, (bf16[256,1280]{1,0:T(8,128)(2,1)S(1)}, ...), branch_computations={%region_3.4_spmd, %region_4.5_spmd, %region_5.6_spmd, %region_6.7_... | conditional | flops 10485760 | bytes 5242888 | solution.py:205
  182.2 2.9 %maximum_bitcast_fusion.1 = bf16[1,256,5120]{2,1,0:T(8,128)(2,1)} fusion(bf16[256,1280]{1,0:T(8,128)(2,1)S(1)} %get-tuple-element.45, bf16[256,1280]{1,0:T(8,128)(2,1)} %get-tuple-element.44, bf16[256,1280]{1,0:T(8,128)(2,1)S(1)} %get-tuple-element.43, bf16[256,1280]{1,0:T(8,128)(2,1)S(1)} %get-tuple-element.42), kind=kLoop, calls=%fused_computation.3 | loop fusion | flops 10485760 | bytes 5242880 | tf_op jit(solution)/shard_map/broadcast_in_dim | solution.py:206
  (121 shorter events, 78.9 us)
Async XLA Ops:
  3.4 7.9 %collective-permute-start.4 = (bf16[80,1280]{1,0:T(8,128)(2,1)S(1)}, bf16[80,1280]{1,0:T(8,128)(2,1)S(1)}, u32[]{:S(2)}, u32[]{:S(2)}) collective-permute-start(bf16[80,1280]{1,0:T(8,128)(2,1)S(1)} %get-tuple-element.88), channel_id=1, source_target_pairs={{0,2},{2,0},{1,3},{3,1},{4,6},{6,4},{5,7},{7,5},{8,10},{10,8},{9,1... | collective-permute-start | bytes 614408 | tf_op jit(solution)/shard_map/ppermute | solution.py:113
  6.9 9.9 %collective-permute-start.5 = (bf16[80,1280]{1,0:T(8,128)(2,1)S(1)}, bf16[80,1280]{1,0:T(8,128)(2,1)S(1)}, u32[]{:S(2)}, u32[]{:S(2)}) collective-permute-start(bf16[80,1280]{1,0:T(8,128)(2,1)S(1)} %get-tuple-element.88), channel_id=1, source_target_pairs={{0,18},{2,16},{16,2},{18,0},{1,19},{3,17},{17,3},{19,1},{4,22},{6,... | collective-permute-start | bytes 614408 | tf_op jit(solution)/shard_map/ppermute | solution.py:71
  7.8 20.0 %collective-permute-start = (bf16[80,1280]{1,0:T(8,128)(2,1)S(1)}, bf16[80,1280]{1,0:T(8,128)(2,1)S(1)}, u32[]{:S(2)}, u32[]{:S(2)}) collective-permute-start(bf16[80,1280]{1,0:T(8,128)(2,1)S(1)} %get-tuple-element.88), channel_id=1, source_target_pairs={{0,16},{16,0},{1,17},{17,1},{2,18},{18,2},{3,19},{19,3},{4,20},{20... | collective-permute-start | bytes 614408 | tf_op jit(solution)/shard_map/ppermute | solution.py:113
  17.8 14.1 %collective-permute-start.6 = (bf16[2,80,1280]{2,1,0:T(8,128)(2,1)}, bf16[2,80,1280]{2,1,0:T(8,128)(2,1)S(1)}, u32[]{:S(2)}, u32[]{:S(2)}) collective-permute-start(bf16[2,80,1280]{2,1,0:T(8,128)(2,1)} %get-tuple-element.109), channel_id=1, source_target_pairs={{0,32},{32,64},{64,96},{96,0},{1,33},{33,65},{65,97},{97,1},{2,34}... | collective-permute-start | bytes 1228808 | tf_op jit(solution)/shard_map/ppermute | solution.py:62
  20.3 20.8 %collective-permute-start.7 = (bf16[2,80,1280]{2,1,0:T(8,128)(2,1)}, bf16[2,80,1280]{2,1,0:T(8,128)(2,1)}, u32[]{:S(2)}, u32[]{:S(2)}) collective-permute-start(bf16[2,80,1280]{2,1,0:T(8,128)(2,1)} %get-tuple-element.109), channel_id=1, source_target_pairs={{0,64},{32,96},{64,0},{96,32},{1,65},{33,97},{65,1},{97,33},{2,66}... | collective-permute-start | bytes 1228808 | tf_op jit(solution)/shard_map/ppermute | solution.py:62
  23.7 18.8 %collective-permute-start.8 = (bf16[2,80,1280]{2,1,0:T(8,128)(2,1)}, bf16[2,80,1280]{2,1,0:T(8,128)(2,1)}, u32[]{:S(2)}, u32[]{:S(2)}) collective-permute-start(bf16[2,80,1280]{2,1,0:T(8,128)(2,1)} %get-tuple-element.109), channel_id=1, source_target_pairs={{0,96},{32,0},{64,32},{96,64},{1,97},{33,1},{65,33},{97,65},{2,98}... | collective-permute-start | bytes 1228808 | tf_op jit(solution)/shard_map/ppermute | solution.py:62
  27.9 17.2 %collective-permute-start.1 = (bf16[2,80,1280]{2,1,0:T(8,128)(2,1)S(1)}, bf16[2,80,1280]{2,1,0:T(8,128)(2,1)S(1)}, u32[]{:S(2)}, u32[]{:S(2)}) collective-permute-start(bf16[2,80,1280]{2,1,0:T(8,128)(2,1)S(1)} %get-tuple-element.111), channel_id=1, source_target_pairs={{0,4},{4,8},{8,12},{12,0},{1,5},{5,9},{9,13},{13,1},{2,6},{6,10},{... | collective-permute-start | bytes 1228808 | tf_op jit(solution)/shard_map/ppermute | solution.py:62
  29.2 19.6 %collective-permute-start.2 = (bf16[2,80,1280]{2,1,0:T(8,128)(2,1)S(1)}, bf16[2,80,1280]{2,1,0:T(8,128)(2,1)S(1)}, u32[]{:S(2)}, u32[]{:S(2)}) collective-permute-start(bf16[2,80,1280]{2,1,0:T(8,128)(2,1)S(1)} %get-tuple-element.111), channel_id=1, source_target_pairs={{0,8},{4,12},{8,0},{12,4},{1,9},{5,13},{9,1},{13,5},{2,10},{6,14},... | collective-permute-start | bytes 1228808 | tf_op jit(solution)/shard_map/ppermute | solution.py:62
  31.9 17.2 %collective-permute-start.3 = (bf16[2,80,1280]{2,1,0:T(8,128)(2,1)S(1)}, bf16[2,80,1280]{2,1,0:T(8,128)(2,1)S(1)}, u32[]{:S(2)}, u32[]{:S(2)}) collective-permute-start(bf16[2,80,1280]{2,1,0:T(8,128)(2,1)S(1)} %get-tuple-element.111), channel_id=1, source_target_pairs={{0,12},{4,0},{8,4},{12,8},{1,13},{5,1},{9,5},{13,9},{2,14},{6,2},{... | collective-permute-start | bytes 1228808 | tf_op jit(solution)/shard_map/ppermute | solution.py:62
  41.1 15.2 %collective-permute-start.13 = (bf16[256,10,128]{0,2,1:T(8,128)(2,1)}, bf16[256,10,128]{0,2,1:T(8,128)(2,1)S(1)}, u32[]{:S(2)}, u32[]{:S(2)}) collective-permute-start(bf16[256,10,128]{0,2,1:T(8,128)(2,1)} %get-tuple-element.107), channel_id=1, source_target_pairs={{0,1},{1,0},{2,3},{3,2},{4,5},{5,4},{6,7},{7,6},{8,9},{9,8},{10,11... | collective-permute-start | bytes 1966088 | tf_op jit(solution)/shard_map/ppermute | solution.py:113
  42.5 13.9 %collective-permute-start.14 = (bf16[256,10,128]{0,2,1:T(8,128)(2,1)}, bf16[256,10,128]{0,2,1:T(8,128)(2,1)S(1)}, u32[]{:S(2)}, u32[]{:S(2)}) collective-permute-start(bf16[256,10,128]{0,2,1:T(8,128)(2,1)} %get-tuple-element.105), channel_id=1, source_target_pairs={{0,1},{1,0},{2,3},{3,2},{4,5},{5,4},{6,7},{7,6},{8,9},{9,8},{10,11... | collective-permute-start | bytes 1966088 | tf_op jit(solution)/shard_map/ppermute | solution.py:113
  51.6 8.1 %collective-permute-start.19 = (bf16[256,10,128]{0,2,1:T(8,128)(2,1)}, bf16[256,10,128]{0,2,1:T(8,128)(2,1)}, u32[]{:S(2)}, u32[]{:S(2)}) collective-permute-start(bf16[256,10,128]{0,2,1:T(8,128)(2,1)} %get-tuple-element.103), channel_id=1, source_target_pairs={{0,1},{1,0},{2,3},{3,2},{4,5},{5,4},{6,7},{7,6},{8,9},{9,8},{10,11... | collective-permute-start | bytes 1966088 | tf_op jit(solution)/shard_map/ppermute | solution.py:113
  53.7 39.8 %collective-permute-start.11 = (bf16[4,2,80,1280]{3,2,1,0:T(8,128)(2,1)}, bf16[4,2,80,1280]{3,2,1,0:T(8,128)(2,1)}, u32[]{:S(2)}, u32[]{:S(2)}) collective-permute-start(bf16[4,2,80,1280]{3,2,1,0:T(8,128)(2,1)} %pad_maximum_fusion.10), channel_id=1, source_target_pairs={{0,4},{4,8},{8,12},{12,0},{1,5},{5,9},{9,13},{13,1},{2,6},{6,10},{... | collective-permute-start | bytes 4915208 | tf_op jit(solution)/shard_map/ppermute | solution.py:29
  55.3 38.2 %collective-permute-start.12 = (bf16[4,2,80,1280]{3,2,1,0:T(8,128)(2,1)}, bf16[4,2,80,1280]{3,2,1,0:T(8,128)(2,1)}, u32[]{:S(2)}, u32[]{:S(2)}) collective-permute-start(bf16[4,2,80,1280]{3,2,1,0:T(8,128)(2,1)} %pad_maximum_fusion.10), channel_id=1, source_target_pairs={{0,12},{4,0},{8,4},{12,8},{1,13},{5,1},{9,5},{13,9},{2,14},{6,2},{... | collective-permute-start | bytes 4915208 | tf_op jit(solution)/shard_map/ppermute | solution.py:29
  56.3 37.1 %collective-permute-start.10 = (bf16[4,2,80,1280]{3,2,1,0:T(8,128)(2,1)}, bf16[4,2,80,1280]{3,2,1,0:T(8,128)(2,1)}, u32[]{:S(2)}, u32[]{:S(2)}) collective-permute-start(bf16[4,2,80,1280]{3,2,1,0:T(8,128)(2,1)} %pad_maximum_fusion.9), channel_id=1, source_target_pairs={{0,96},{32,0},{64,32},{96,64},{1,97},{33,1},{65,33},{97,65},{2,98}... | collective-permute-start | bytes 4915208 | tf_op jit(solution)/shard_map/ppermute | solution.py:29
  56.4 38.2 %collective-permute-start.9 = (bf16[4,2,80,1280]{3,2,1,0:T(8,128)(2,1)}, bf16[4,2,80,1280]{3,2,1,0:T(8,128)(2,1)}, u32[]{:S(2)}, u32[]{:S(2)}) collective-permute-start(bf16[4,2,80,1280]{3,2,1,0:T(8,128)(2,1)} %pad_maximum_fusion.9), channel_id=1, source_target_pairs={{0,32},{32,64},{64,96},{96,0},{1,33},{33,65},{65,97},{97,1},{2,34}... | collective-permute-start | bytes 4915208 | tf_op jit(solution)/shard_map/ppermute | solution.py:29
  94.5 34.4 %collective-permute-start.20 = (f32[10,256,128]{2,1,0:T(8,128)}, f32[10,256,128]{2,1,0:T(8,128)}, u32[]{:S(2)}, u32[]{:S(2)}) collective-permute-start(f32[10,256,128]{2,1,0:T(8,128)} %get-tuple-element.80), channel_id=1, source_target_pairs={{0,2},{1,3},{4,6},{5,7},{8,10},{9,11},{12,14},{13,15},{16,18},{17,... | collective-permute-start | bytes 3932168 | tf_op jit(solution)/shard_map/ppermute | solution.py:164
  100.6 22.4 %collective-permute-start.17 = (bf16[2,2,80,1280]{3,2,1,0:T(8,128)(2,1)}, bf16[2,2,80,1280]{3,2,1,0:T(8,128)(2,1)}, u32[]{:S(2)}, u32[]{:S(2)}) collective-permute-start(bf16[2,2,80,1280]{3,2,1,0:T(8,128)(2,1)} %slice.29), channel_id=1, source_target_pairs={{0,4},{4,8},{8,12},{12,0},{1,5},{5,9},{9,13},{13,1},{2,6},{6,10},{... | collective-permute-start | bytes 2457608 | tf_op jit(solution)/shard_map/ppermute | solution.py:41
  102.9 20.1 %collective-permute-start.18 = (bf16[2,2,80,1280]{3,2,1,0:T(8,128)(2,1)}, bf16[2,2,80,1280]{3,2,1,0:T(8,128)(2,1)}, u32[]{:S(2)}, u32[]{:S(2)}) collective-permute-start(bf16[2,2,80,1280]{3,2,1,0:T(8,128)(2,1)} %slice.30), channel_id=1, source_target_pairs={{0,12},{4,0},{8,4},{12,8},{1,13},{5,1},{9,5},{13,9},{2,14},{6,2},{... | collective-permute-start | bytes 2457608 | tf_op jit(solution)/shard_map/ppermute | solution.py:42
  107.5 18.7 %collective-permute-start.15 = (bf16[2,2,80,1280]{3,2,1,0:T(8,128)(2,1)}, bf16[2,2,80,1280]{3,2,1,0:T(8,128)(2,1)S(1)}, u32[]{:S(2)}, u32[]{:S(2)}) collective-permute-start(bf16[2,2,80,1280]{3,2,1,0:T(8,128)(2,1)} %slice.27), channel_id=1, source_target_pairs={{0,32},{32,64},{64,96},{96,0},{1,33},{33,65},{65,97},{97,1},{2,34}... | collective-permute-start | bytes 2457608 | tf_op jit(solution)/shard_map/ppermute | solution.py:41
  109.7 17.7 %collective-permute-start.16 = (bf16[2,2,80,1280]{3,2,1,0:T(8,128)(2,1)}, bf16[2,2,80,1280]{3,2,1,0:T(8,128)(2,1)}, u32[]{:S(2)}, u32[]{:S(2)}) collective-permute-start(bf16[2,2,80,1280]{3,2,1,0:T(8,128)(2,1)} %slice.28), channel_id=1, source_target_pairs={{0,96},{32,0},{64,32},{96,64},{1,97},{33,1},{65,33},{97,65},{2,98}... | collective-permute-start | bytes 2457608 | tf_op jit(solution)/shard_map/ppermute | solution.py:42
  135.5 5.8 %collective-permute-start.21 = (bf16[256,10,128]{2,0,1:T(8,128)(2,1)}, bf16[256,10,128]{2,0,1:T(8,128)(2,1)}, u32[]{:S(2)}, u32[]{:S(2)}) collective-permute-start(bf16[256,10,128]{2,0,1:T(8,128)(2,1)} %get-tuple-element.101), channel_id=1, source_target_pairs={{0,1},{1,0},{2,3},{3,2},{4,5},{5,4},{6,7},{7,6},{8,9},{9,8},{10,11... | collective-permute-start | bytes 1966088 | tf_op jit(solution)/shard_map/ppermute | solution.py:113
  146.7 11.9 %collective-permute-start.22 = (bf16[256,2560]{0,1:T(8,128)(2,1)}, bf16[256,2560]{0,1:T(8,128)(2,1)S(1)}, u32[]{:S(2)}, u32[]{:S(2)}) collective-permute-start(bf16[256,2560]{0,1:T(8,128)(2,1)} %bitcast.71), channel_id=1, source_target_pairs={{0,1},{1,0},{2,3},{3,2},{4,5},{5,4},{6,7},{7,6},{8,9},{9,8},{10,11... | collective-permute-start | bytes 3932168 | tf_op jit(solution)/shard_map/ppermute | solution.py:113
  169.4 10.9 %collective-permute-start.24 = (bf16[256,1280]{1,0:T(8,128)(2,1)}, bf16[256,1280]{1,0:T(8,128)(2,1)}, u32[]{:S(2)}, u32[]{:S(2)}) collective-permute-start(bf16[256,1280]{1,0:T(8,128)(2,1)} %get-tuple-element.96), channel_id=1, source_target_pairs={{0,1},{1,0},{2,3},{3,2},{4,5},{5,4},{6,7},{7,6},{8,9},{9,8},{10,11... | collective-permute-start | bytes 1966088 | tf_op jit(solution)/shard_map/ppermute | solution.py:113
  (22 other events, 158.2 us)

commit v18 on v17

--- a/solution.py
+++ b/solution.py
@@ -191,7 +191,8 @@
             jnp.dot(features, rows, preferred_element_type=jnp.float32).astype(jnp.bfloat16)
         )
     own = [piece[:tokens_here] for piece in wide]
-    returned = [swap(piece[tokens_here:], "c") for piece in wide]
+    returned = swap(jnp.stack([piece[tokens_here:] for piece in wide]), "c")
+    returned = [returned[0], returned[1]]
     candidates = own + returned
 
     def place(chip, side):

time: 187 us -> 189 us (1.011)
    ppermute x9 -> x8, waiting for transfers between devices: 7.41 us -> 8.72 us  [swap(): return lax.ppermute(x, axis, [(0, 1), (1, 0)])]
    another operation x1 -> x2, other arithmetic: 4.29 us -> 5.47 us
    unnamed x43 -> x45, local copies, waits for them, and re-layouts: 8.06 us -> 9.03 us
    ppermute x9 -> x8, starting transfers between devices: 11.7 us -> 11.3 us  [swap(): return lax.ppermute(x, axis, [(0, 1), (1, 0)])]
  transfers between devices with their start and end apart: 25 -> 24, of which waited for: 11 -> 11; matrix products, arithmetic and copies ran while one was open for 41% -> 35% of each run, Pallas kernels for 0% -> 0%
where the time goes in v18:
time: 189 us; the launch traced here: 188 us
  local copies, waits for them, and re-layouts  45 us (24%)
  other arithmetic  41.1 us (22%)
  waiting for transfers between devices  38.5 us (20%)
  starting transfers between devices  37.8 us (20%)
  matrix products  24.9 us (13%)
    dot_general x2, matrix products, on_device(): jnp.dot(features, rows, preferred_element_type=jnp.float32)  14.5 us
    ppermute x4, waiting for transfers between devices, ring_send(): return (lax.ppermute(x, axis, forward), lax.ppermute(x, axis, backward))  12.4 us
    ppermute x6, starting transfers between devices, ring_direct(): lax.ppermute(x, axis, [(k, (k + shift) % size) for k in range(size)])  12.2 us
    max x4, local copies, waits for them, and re-layouts, featurize(): rectified = jnp.maximum(block.astype(jnp.float32), 0.0)  12 us
    another operation x2, other arithmetic, ring_finish(): return jnp.stack((x,) + tuple(received))  11.5 us
    ppermute x8, starting transfers between devices, swap(): return lax.ppermute(x, axis, [(0, 1), (1, 0)])  11.3 us
    ppermute x6, waiting for transfers between devices, ring_direct(): lax.ppermute(x, axis, [(k, (k + shift) % size) for k in range(size)])  9.96 us
    unnamed x45, local copies, waits for them, and re-layouts  9.03 us
  transfers between devices with their start and end apart: 24, of which 11 were waited for; matrix products, arithmetic and copies ran while one was open for 35% of the time, Pallas kernels for 0%

profile of v18, /device:TPU:1, one launch (start us, length us, event | category | flops | bytes accessed | tf_op | source)
XLA Modules:
  0.0 188.3 jit_solution(6854802956422082586)
XLA Ops:
  0.7 2.7 %fusion.35 = (bf16[80,1280]{1,0:T(8,128)(2,1)S(1)}, f32[80,1280]{1,0:T(8,128)}, f32[80,1280]{1,0:T(8,128)}, f32[80,1280]{1,0:T(8,128)}) fusion(f32[80,1280]{1,0:T(8,128)} %param.16, f32[80,1280]{1,0:T(8,128)} %param.17, f32[80,1280]{1,0:T(8,128)} %param.18, f32[80,1280]{1,0:T(8,128)} %param.19), kind=kLoop, calls=%fused_computation.115 | loop fusion | flops 1638400 | bytes 3072000 | tf_op jit(solution)/shard_map/convert_element_type | solution.py:139
  3.4 3.6 %collective-permute-start.4 = (bf16[80,1280]{1,0:T(8,128)(2,1)S(1)}, bf16[80,1280]{1,0:T(8,128)(2,1)S(1)}, u32[]{:S(2)}, u32[]{:S(2)}) collective-permute-start(bf16[80,1280]{1,0:T(8,128)(2,1)S(1)} %get-tuple-element.88), channel_id=1, source_target_pairs={{0,2},{2,0},{1,3},{3,1},{4,6},{6,4},{5,7},{7,5},{8,10},{10,8},{9,1... | collective-permute-start | bytes 614408 | tf_op jit(solution)/shard_map/ppermute | solution.py:113
  7.8 3.5 %collective-permute-done.4 = bf16[80,1280]{1,0:T(8,128)(2,1)S(1)} collective-permute-done((bf16[80,1280]{1,0:T(8,128)(2,1)S(1)}, bf16[80,1280]{1,0:T(8,128)(2,1)S(1)}, u32[]{:S(2)}, u32[]{:S(2)}) %collective-permute-start.4) | collective-permute-done | bytes 204832 | tf_op jit(solution)/shard_map/ppermute | solution.py:113
  11.2 5.6 %collective-permute-done.5 = bf16[80,1280]{1,0:T(8,128)(2,1)S(1)} collective-permute-done((bf16[80,1280]{1,0:T(8,128)(2,1)S(1)}, bf16[80,1280]{1,0:T(8,128)(2,1)S(1)}, u32[]{:S(2)}, u32[]{:S(2)}) %collective-permute-start.5) | collective-permute-done | bytes 204832 | tf_op jit(solution)/shard_map/ppermute | solution.py:71
  20.3 3.4 %collective-permute-start.7 = (bf16[2,80,1280]{2,1,0:T(8,128)(2,1)}, bf16[2,80,1280]{2,1,0:T(8,128)(2,1)}, u32[]{:S(2)}, u32[]{:S(2)}) collective-permute-start(bf16[2,80,1280]{2,1,0:T(8,128)(2,1)} %get-tuple-element.111), channel_id=1, source_target_pairs={{0,64},{32,96},{64,0},{96,32},{1,65},{33,97},{65,1},{97,33},{2,66}... | collective-permute-start | bytes 1228808 | tf_op jit(solution)/shard_map/ppermute | solution.py:62
  35.1 6.0 %collective-permute-done.7 = bf16[2,80,1280]{2,1,0:T(8,128)(2,1)} collective-permute-done((bf16[2,80,1280]{2,1,0:T(8,128)(2,1)}, bf16[2,80,1280]{2,1,0:T(8,128)(2,1)}, u32[]{:S(2)}, u32[]{:S(2)}) %collective-permute-start.7) | collective-permute-done | bytes 409632 | tf_op jit(solution)/shard_map/ppermute | solution.py:62
  45.1 3.7 %collective-permute-done.2 = bf16[2,80,1280]{2,1,0:T(8,128)(2,1)S(1)} collective-permute-done((bf16[2,80,1280]{2,1,0:T(8,128)(2,1)S(1)}, bf16[2,80,1280]{2,1,0:T(8,128)(2,1)S(1)}, u32[]{:S(2)}, u32[]{:S(2)}) %collective-permute-start.2) | collective-permute-done | bytes 409632 | tf_op jit(solution)/shard_map/ppermute | solution.py:62
  59.8 4.0 %convert_maximum_fusion = (f32[512,10,128]{0,2,1:T(8,128)S(1)}, f32[512,10,128]{0,2,1:T(8,128)}) fusion(bf16[256,10,128]{0,2,1:T(8,128)(2,1)} %collective-permute-done.19, bf16[256,10,128]{0,2,1:T(8,128)(2,1)} %get-tuple-element.104, pred[]{:T(512)S(6)} %eq.17, bf16[256,10,128]{0,2,1:T(8,128)(2,1)S(1)} %copy-done.13, bf16[256,10,128]{0,2,1:T(8,128)(2,1)} %copy-done.18), kind=kLoop, calls=%fused_computation.22 | loop fusion | flops 14417920 | bytes 7864321 | tf_op jit(solution)/shard_map/max | solution.py:97
  63.8 3.3 %copy.15 = f32[512,10,128]{2,0,1:T(8,128)} copy(f32[512,10,128]{0,2,1:T(8,128)} %get-tuple-element.121) | data formatting | bytes 5242880 | tf_op jit(solution)/shard_map/max | solution.py:97
  67.1 3.2 %copy.16 = f32[4,128,10,128]{1,3,2,0:T(8,128)} copy(f32[4,128,10,128]{3,1,0,2:T(8,128)} %bitcast.69) | data formatting | bytes 5242880 | tf_op jit(solution)/shard_map/max | solution.py:97
  72.5 3.3 %copy.22 = f32[4,128,10,128]{1,3,2,0:T(8,128)} copy(f32[4,128,10,128]{3,1,0,2:T(8,128)} %bitcast.70) | data formatting | bytes 5242880 | tf_op jit(solution)/shard_map/max | solution.py:97
  75.9 4.3 %multiply_convert_fusion.4 = (bf16[4,128,10,128]{1,3,2,0:T(8,128)(2,1)S(1)}, bf16[4,128,10,128]{1,3,2,0:T(8,128)(2,1)S(1)}, bf16[4,128,10,128]{1,3,2,0:T(8,128)(2,1)}, bf16[4,128,10,128]{1,3,2,0:T(8,128)(2,1)}) fusion(f32[4,128,10,128]{1,3,2,0:T(8,128)S(1)} %copy-done.3, f32[4,128]{1,0:T(4,128)S(1)} %get-tuple-element.123, ...), kind=kLoop, calls=%fused_computation.24 | loop fusion | flops 5242880 | bytes 10489856 | tf_op jit(solution)/shard_map/convert.2
  82.1 11.3 %collective-permute-done.10 = bf16[4,2,80,1280]{3,2,1,0:T(8,128)(2,1)} collective-permute-done((bf16[4,2,80,1280]{3,2,1,0:T(8,128)(2,1)}, bf16[4,2,80,1280]{3,2,1,0:T(8,128)(2,1)}, u32[]{:S(2)}, u32[]{:S(2)}) %collective-permute-start.10) | collective-permute-done | bytes 1638432 | tf_op jit(solution)/shard_map/ppermute | solution.py:29
  94.5 4.0 %collective-permute-start.20 = (f32[10,256,128]{2,1,0:T(8,128)}, f32[10,256,128]{2,1,0:T(8,128)}, u32[]{:S(2)}, u32[]{:S(2)}) collective-permute-start(f32[10,256,128]{2,1,0:T(8,128)} %get-tuple-element.80), channel_id=1, source_target_pairs={{0,2},{1,3},{4,6},{5,7},{8,10},{9,11},{12,14},{13,15},{16,18},{17,... | collective-permute-start | bytes 3932168 | tf_op jit(solution)/shard_map/ppermute | solution.py:164
  114.6 2.6 %copy-done.2 = f32[4,10,256,128]{3,2,1,0:T(8,128)} copy-done((f32[4,10,256,128]{3,2,1,0:T(8,128)}, f32[4,10,256,128]{3,2,1,0:T(8,128)S(1)}, u32[]{:S(2)}) %copy-start.2) | copy-done | bytes 5242904
  118.2 4.8 %fusion.3 = f32[4,10,128,128]{2,3,1,0:T(8,128)} fusion(bf16[4,128,10,128]{1,3,2,0:T(8,128)(2,1)S(1)} %copy-done.4, bf16[4,128,10,128]{1,3,2,0:T(8,128)(2,1)S(1)} %copy-done.6, bf16[4,128,10,128]{1,3,2,0:T(8,128)(2,1)} %copy-done.9, bf16[4,128,10,128]{1,3,2,0:T(8,128)(2,1)} %copy-done.8, pred[128,128]{1,0:T(8,128)(4,1)S(1)} %iota_compare_fusion, ...), kind=kOutput, calls=%fused_computation.31 | convolution fusion | flops 515112960 | bytes 9191424 | tf_op jit(solution)/shard_map/chij,cjhe->cihe/dot_general | solution.py:170
  129.0 3.5 %add_bitcast_fusion = f32[4,128,10,128]{3,1,2,0:T(8,128)S(1)} fusion(f32[4,10,128,128]{2,3,1,0:T(8,128)} %fusion.3, f32[3,10,256,128]{3,2,1,0:T(8,128)S(1)} %slice-done, f32[10,256,128]{2,1,0:T(8,128)} %collective-permute-done.20, bf16[4,128,10,128]{1,3,2,0:T(8,128)(2,1)S(1)} %copy-done.5, bf16[4,128,10,128]{1,3,2,0:T(8,128)(2,1)S(1)} %copy-done.7), kind=kOutput, calls=%fused_computation.17 | convolution fusion | flops 344064000 | bytes 13107200 | tf_op jit(solution)/shard_map/cihf,chfe->cihe/dot_general | solution.py:176
  135.6 3.7 %collective-permute-start.21 = (bf16[256,10,128]{2,0,1:T(8,128)(2,1)}, bf16[256,10,128]{2,0,1:T(8,128)(2,1)}, u32[]{:S(2)}, u32[]{:S(2)}) collective-permute-start(bf16[256,10,128]{2,0,1:T(8,128)(2,1)} %get-tuple-element.103), channel_id=1, source_target_pairs={{0,1},{1,0},{2,3},{3,2},{4,5},{5,4},{6,7},{7,6},{8,9},{9,8},{10,11... | collective-permute-start | bytes 1966088 | tf_op jit(solution)/shard_map/ppermute | solution.py:113
  141.3 2.9 %maximum_select_fusion.3 = bf16[256,20,128]{2,0,1:T(8,128)(2,1)} fusion(bf16[256,10,128]{2,0,1:T(8,128)(2,1)} %collective-permute-done.21, bf16[256,10,128]{2,0,1:T(8,128)(2,1)} %get-tuple-element.102, pred[]{:T(512)S(6)} %eq.17), kind=kLoop, calls=%fused_computation.35 | loop fusion | flops 1966080 | bytes 2621441 | tf_op jit(solution)/shard_map/jit(_where)/select_n | solution.py:121
  147.1 5.7 %pad_maximum_fusion.1 = bf16[4,4,2,80,1280]{4,3,2,1,0:T(8,128)(2,1)} fusion(bf16[1,4,2,80,1280]{4,3,2,1,0:T(8,128)(2,1)} %bitcast.42, bf16[1,4,2,80,1280]{4,3,2,1,0:T(8,128)(2,1)S(1)} %bitcast.73, bf16[1,4,2,80,1280]{4,3,2,1,0:T(8,128)(2,1)} %bitcast.40, bf16[1,4,2,80,1280]{4,3,2,1,0:T(8,128)(2,1)} %bitcast.39), kind=kLoop, calls=%fused_computation.7 | loop fusion | flops 9830400 | bytes 13107200 | tf_op jit(solution)/shard_map/stack | solution.py:50
  152.8 5.8 %pad_maximum_fusion = bf16[4,4,2,80,1280]{4,3,2,1,0:T(8,128)(2,1)} fusion(bf16[1,4,2,80,1280]{4,3,2,1,0:T(8,128)(2,1)} %bitcast.33, bf16[1,4,2,80,1280]{4,3,2,1,0:T(8,128)(2,1)S(1)} %bitcast.74, bf16[1,4,2,80,1280]{4,3,2,1,0:T(8,128)(2,1)} %bitcast.31, bf16[1,4,2,80,1280]{4,3,2,1,0:T(8,128)(2,1)} %bitcast.30), kind=kLoop, calls=%fused_computation.6 | loop fusion | flops 9830400 | bytes 13107200 | tf_op jit(solution)/shard_map/stack | solution.py:50
  161.2 7.3 %convolution_convert_fusion = bf16[512,1280]{1,0:T(8,128)(2,1)S(1)} fusion(bf16[512,2560]{0,1:T(8,128)(2,1)} %bitcast.72, bf16[2560,1280]{1,0:T(8,128)(2,1)} %bitcast.76), kind=kOutput, calls=%fused_computation.9 | convolution fusion | flops 3356098560 | bytes 10485760 | tf_op jit(solution)/shard_map/dot_general | solution.py:191
  171.6 7.3 %convolution_convert_fusion.1 = bf16[512,1280]{1,0:T(8,128)(2,1)S(1)} fusion(bf16[512,2560]{0,1:T(8,128)(2,1)} %bitcast.71, bf16[2560,1280]{1,0:T(8,128)(2,1)} %bitcast.75), kind=kOutput, calls=%fused_computation.10 | convolution fusion | flops 3356098560 | bytes 10485760 | tf_op jit(solution)/shard_map/dot_general | solution.py:191
  181.3 3.2 %collective-permute-done.23 = bf16[2,256,1280]{2,1,0:T(8,128)(2,1)} collective-permute-done((bf16[2,256,1280]{2,1,0:T(8,128)(2,1)}, bf16[2,256,1280]{2,1,0:T(8,128)(2,1)}, u32[]{:S(2)}, u32[]{:S(2)}) %collective-permute-start.23) | collective-permute-done | bytes 1310752 | tf_op jit(solution)/shard_map/ppermute | solution.py:113
  (123 shorter events, 80.1 us)
Async XLA Ops:
  3.4 7.9 %collective-permute-start.4 = (bf16[80,1280]{1,0:T(8,128)(2,1)S(1)}, bf16[80,1280]{1,0:T(8,128)(2,1)S(1)}, u32[]{:S(2)}, u32[]{:S(2)}) collective-permute-start(bf16[80,1280]{1,0:T(8,128)(2,1)S(1)} %get-tuple-element.88), channel_id=1, source_target_pairs={{0,2},{2,0},{1,3},{3,1},{4,6},{6,4},{5,7},{7,5},{8,10},{10,8},{9,1... | collective-permute-start | bytes 614408 | tf_op jit(solution)/shard_map/ppermute | solution.py:113
  6.9 9.9 %collective-permute-start.5 = (bf16[80,1280]{1,0:T(8,128)(2,1)S(1)}, bf16[80,1280]{1,0:T(8,128)(2,1)S(1)}, u32[]{:S(2)}, u32[]{:S(2)}) collective-permute-start(bf16[80,1280]{1,0:T(8,128)(2,1)S(1)} %get-tuple-element.88), channel_id=1, source_target_pairs={{0,18},{2,16},{16,2},{18,0},{1,19},{3,17},{17,3},{19,1},{4,22},{6,... | collective-permute-start | bytes 614408 | tf_op jit(solution)/shard_map/ppermute | solution.py:71
  7.8 20.0 %collective-permute-start = (bf16[80,1280]{1,0:T(8,128)(2,1)S(1)}, bf16[80,1280]{1,0:T(8,128)(2,1)S(1)}, u32[]{:S(2)}, u32[]{:S(2)}) collective-permute-start(bf16[80,1280]{1,0:T(8,128)(2,1)S(1)} %get-tuple-element.88), channel_id=1, source_target_pairs={{0,16},{16,0},{1,17},{17,1},{2,18},{18,2},{3,19},{19,3},{4,20},{20... | collective-permute-start | bytes 614408 | tf_op jit(solution)/shard_map/ppermute | solution.py:113
  17.8 14.1 %collective-permute-start.6 = (bf16[2,80,1280]{2,1,0:T(8,128)(2,1)}, bf16[2,80,1280]{2,1,0:T(8,128)(2,1)S(1)}, u32[]{:S(2)}, u32[]{:S(2)}) collective-permute-start(bf16[2,80,1280]{2,1,0:T(8,128)(2,1)} %get-tuple-element.111), channel_id=1, source_target_pairs={{0,32},{32,64},{64,96},{96,0},{1,33},{33,65},{65,97},{97,1},{2,34}... | collective-permute-start | bytes 1228808 | tf_op jit(solution)/shard_map/ppermute | solution.py:62
  20.3 20.8 %collective-permute-start.7 = (bf16[2,80,1280]{2,1,0:T(8,128)(2,1)}, bf16[2,80,1280]{2,1,0:T(8,128)(2,1)}, u32[]{:S(2)}, u32[]{:S(2)}) collective-permute-start(bf16[2,80,1280]{2,1,0:T(8,128)(2,1)} %get-tuple-element.111), channel_id=1, source_target_pairs={{0,64},{32,96},{64,0},{96,32},{1,65},{33,97},{65,1},{97,33},{2,66}... | collective-permute-start | bytes 1228808 | tf_op jit(solution)/shard_map/ppermute | solution.py:62
  23.7 18.8 %collective-permute-start.8 = (bf16[2,80,1280]{2,1,0:T(8,128)(2,1)}, bf16[2,80,1280]{2,1,0:T(8,128)(2,1)}, u32[]{:S(2)}, u32[]{:S(2)}) collective-permute-start(bf16[2,80,1280]{2,1,0:T(8,128)(2,1)} %get-tuple-element.111), channel_id=1, source_target_pairs={{0,96},{32,0},{64,32},{96,64},{1,97},{33,1},{65,33},{97,65},{2,98}... | collective-permute-start | bytes 1228808 | tf_op jit(solution)/shard_map/ppermute | solution.py:62
  27.9 17.2 %collective-permute-start.1 = (bf16[2,80,1280]{2,1,0:T(8,128)(2,1)S(1)}, bf16[2,80,1280]{2,1,0:T(8,128)(2,1)S(1)}, u32[]{:S(2)}, u32[]{:S(2)}) collective-permute-start(bf16[2,80,1280]{2,1,0:T(8,128)(2,1)S(1)} %get-tuple-element.113), channel_id=1, source_target_pairs={{0,4},{4,8},{8,12},{12,0},{1,5},{5,9},{9,13},{13,1},{2,6},{6,10},{... | collective-permute-start | bytes 1228808 | tf_op jit(solution)/shard_map/ppermute | solution.py:62
  29.3 19.6 %collective-permute-start.2 = (bf16[2,80,1280]{2,1,0:T(8,128)(2,1)S(1)}, bf16[2,80,1280]{2,1,0:T(8,128)(2,1)S(1)}, u32[]{:S(2)}, u32[]{:S(2)}) collective-permute-start(bf16[2,80,1280]{2,1,0:T(8,128)(2,1)S(1)} %get-tuple-element.113), channel_id=1, source_target_pairs={{0,8},{4,12},{8,0},{12,4},{1,9},{5,13},{9,1},{13,5},{2,10},{6,14},... | collective-permute-start | bytes 1228808 | tf_op jit(solution)/shard_map/ppermute | solution.py:62
  31.9 17.2 %collective-permute-start.3 = (bf16[2,80,1280]{2,1,0:T(8,128)(2,1)S(1)}, bf16[2,80,1280]{2,1,0:T(8,128)(2,1)S(1)}, u32[]{:S(2)}, u32[]{:S(2)}) collective-permute-start(bf16[2,80,1280]{2,1,0:T(8,128)(2,1)S(1)} %get-tuple-element.113), channel_id=1, source_target_pairs={{0,12},{4,0},{8,4},{12,8},{1,13},{5,1},{9,5},{13,9},{2,14},{6,2},{... | collective-permute-start | bytes 1228808 | tf_op jit(solution)/shard_map/ppermute | solution.py:62
  41.1 15.3 %collective-permute-start.13 = (bf16[256,10,128]{0,2,1:T(8,128)(2,1)}, bf16[256,10,128]{0,2,1:T(8,128)(2,1)S(1)}, u32[]{:S(2)}, u32[]{:S(2)}) collective-permute-start(bf16[256,10,128]{0,2,1:T(8,128)(2,1)} %get-tuple-element.109), channel_id=1, source_target_pairs={{0,1},{1,0},{2,3},{3,2},{4,5},{5,4},{6,7},{7,6},{8,9},{9,8},{10,11... | collective-permute-start | bytes 1966088 | tf_op jit(solution)/shard_map/ppermute | solution.py:113
  42.5 13.9 %collective-permute-start.14 = (bf16[256,10,128]{0,2,1:T(8,128)(2,1)}, bf16[256,10,128]{0,2,1:T(8,128)(2,1)S(1)}, u32[]{:S(2)}, u32[]{:S(2)}) collective-permute-start(bf16[256,10,128]{0,2,1:T(8,128)(2,1)} %get-tuple-element.107), channel_id=1, source_target_pairs={{0,1},{1,0},{2,3},{3,2},{4,5},{5,4},{6,7},{7,6},{8,9},{9,8},{10,11... | collective-permute-start | bytes 1966088 | tf_op jit(solution)/shard_map/ppermute | solution.py:113
  51.7 8.2 %collective-permute-start.19 = (bf16[256,10,128]{0,2,1:T(8,128)(2,1)}, bf16[256,10,128]{0,2,1:T(8,128)(2,1)}, u32[]{:S(2)}, u32[]{:S(2)}) collective-permute-start(bf16[256,10,128]{0,2,1:T(8,128)(2,1)} %get-tuple-element.105), channel_id=1, source_target_pairs={{0,1},{1,0},{2,3},{3,2},{4,5},{5,4},{6,7},{7,6},{8,9},{9,8},{10,11... | collective-permute-start | bytes 1966088 | tf_op jit(solution)/shard_map/ppermute | solution.py:113
  53.7 39.8 %collective-permute-start.11 = (bf16[4,2,80,1280]{3,2,1,0:T(8,128)(2,1)}, bf16[4,2,80,1280]{3,2,1,0:T(8,128)(2,1)}, u32[]{:S(2)}, u32[]{:S(2)}) collective-permute-start(bf16[4,2,80,1280]{3,2,1,0:T(8,128)(2,1)} %pad_maximum_fusion.10), channel_id=1, source_target_pairs={{0,4},{4,8},{8,12},{12,0},{1,5},{5,9},{9,13},{13,1},{2,6},{6,10},{... | collective-permute-start | bytes 4915208 | tf_op jit(solution)/shard_map/ppermute | solution.py:29
  55.3 38.2 %collective-permute-start.12 = (bf16[4,2,80,1280]{3,2,1,0:T(8,128)(2,1)}, bf16[4,2,80,1280]{3,2,1,0:T(8,128)(2,1)}, u32[]{:S(2)}, u32[]{:S(2)}) collective-permute-start(bf16[4,2,80,1280]{3,2,1,0:T(8,128)(2,1)} %pad_maximum_fusion.10), channel_id=1, source_target_pairs={{0,12},{4,0},{8,4},{12,8},{1,13},{5,1},{9,5},{13,9},{2,14},{6,2},{... | collective-permute-start | bytes 4915208 | tf_op jit(solution)/shard_map/ppermute | solution.py:29
  56.4 37.1 %collective-permute-start.10 = (bf16[4,2,80,1280]{3,2,1,0:T(8,128)(2,1)}, bf16[4,2,80,1280]{3,2,1,0:T(8,128)(2,1)}, u32[]{:S(2)}, u32[]{:S(2)}) collective-permute-start(bf16[4,2,80,1280]{3,2,1,0:T(8,128)(2,1)} %pad_maximum_fusion.9), channel_id=1, source_target_pairs={{0,96},{32,0},{64,32},{96,64},{1,97},{33,1},{65,33},{97,65},{2,98}... | collective-permute-start | bytes 4915208 | tf_op jit(solution)/shard_map/ppermute | solution.py:29
  56.4 38.2 %collective-permute-start.9 = (bf16[4,2,80,1280]{3,2,1,0:T(8,128)(2,1)}, bf16[4,2,80,1280]{3,2,1,0:T(8,128)(2,1)}, u32[]{:S(2)}, u32[]{:S(2)}) collective-permute-start(bf16[4,2,80,1280]{3,2,1,0:T(8,128)(2,1)} %pad_maximum_fusion.9), channel_id=1, source_target_pairs={{0,32},{32,64},{64,96},{96,0},{1,33},{33,65},{65,97},{97,1},{2,34}... | collective-permute-start | bytes 4915208 | tf_op jit(solution)/shard_map/ppermute | solution.py:29
  94.5 34.4 %collective-permute-start.20 = (f32[10,256,128]{2,1,0:T(8,128)}, f32[10,256,128]{2,1,0:T(8,128)}, u32[]{:S(2)}, u32[]{:S(2)}) collective-permute-start(f32[10,256,128]{2,1,0:T(8,128)} %get-tuple-element.80), channel_id=1, source_target_pairs={{0,2},{1,3},{4,6},{5,7},{8,10},{9,11},{12,14},{13,15},{16,18},{17,... | collective-permute-start | bytes 3932168 | tf_op jit(solution)/shard_map/ppermute | solution.py:164
  100.6 22.4 %collective-permute-start.17 = (bf16[2,2,80,1280]{3,2,1,0:T(8,128)(2,1)}, bf16[2,2,80,1280]{3,2,1,0:T(8,128)(2,1)}, u32[]{:S(2)}, u32[]{:S(2)}) collective-permute-start(bf16[2,2,80,1280]{3,2,1,0:T(8,128)(2,1)} %slice.35), channel_id=1, source_target_pairs={{0,4},{4,8},{8,12},{12,0},{1,5},{5,9},{9,13},{13,1},{2,6},{6,10},{... | collective-permute-start | bytes 2457608 | tf_op jit(solution)/shard_map/ppermute | solution.py:41
  103.0 20.1 %collective-permute-start.18 = (bf16[2,2,80,1280]{3,2,1,0:T(8,128)(2,1)}, bf16[2,2,80,1280]{3,2,1,0:T(8,128)(2,1)}, u32[]{:S(2)}, u32[]{:S(2)}) collective-permute-start(bf16[2,2,80,1280]{3,2,1,0:T(8,128)(2,1)} %slice.36), channel_id=1, source_target_pairs={{0,12},{4,0},{8,4},{12,8},{1,13},{5,1},{9,5},{13,9},{2,14},{6,2},{... | collective-permute-start | bytes 2457608 | tf_op jit(solution)/shard_map/ppermute | solution.py:42
  107.5 18.7 %collective-permute-start.15 = (bf16[2,2,80,1280]{3,2,1,0:T(8,128)(2,1)}, bf16[2,2,80,1280]{3,2,1,0:T(8,128)(2,1)S(1)}, u32[]{:S(2)}, u32[]{:S(2)}) collective-permute-start(bf16[2,2,80,1280]{3,2,1,0:T(8,128)(2,1)} %slice.33), channel_id=1, source_target_pairs={{0,32},{32,64},{64,96},{96,0},{1,33},{33,65},{65,97},{97,1},{2,34}... | collective-permute-start | bytes 2457608 | tf_op jit(solution)/shard_map/ppermute | solution.py:41
  109.7 17.7 %collective-permute-start.16 = (bf16[2,2,80,1280]{3,2,1,0:T(8,128)(2,1)}, bf16[2,2,80,1280]{3,2,1,0:T(8,128)(2,1)}, u32[]{:S(2)}, u32[]{:S(2)}) collective-permute-start(bf16[2,2,80,1280]{3,2,1,0:T(8,128)(2,1)} %slice.34), channel_id=1, source_target_pairs={{0,96},{32,0},{64,32},{96,64},{1,97},{33,1},{65,33},{97,65},{2,98}... | collective-permute-start | bytes 2457608 | tf_op jit(solution)/shard_map/ppermute | solution.py:42
  135.6 5.8 %collective-permute-start.21 = (bf16[256,10,128]{2,0,1:T(8,128)(2,1)}, bf16[256,10,128]{2,0,1:T(8,128)(2,1)}, u32[]{:S(2)}, u32[]{:S(2)}) collective-permute-start(bf16[256,10,128]{2,0,1:T(8,128)(2,1)} %get-tuple-element.103), channel_id=1, source_target_pairs={{0,1},{1,0},{2,3},{3,2},{4,5},{5,4},{6,7},{7,6},{8,9},{9,8},{10,11... | collective-permute-start | bytes 1966088 | tf_op jit(solution)/shard_map/ppermute | solution.py:113
  146.7 11.9 %collective-permute-start.22 = (bf16[256,2560]{0,1:T(8,128)(2,1)}, bf16[256,2560]{0,1:T(8,128)(2,1)S(1)}, u32[]{:S(2)}, u32[]{:S(2)}) collective-permute-start(bf16[256,2560]{0,1:T(8,128)(2,1)} %bitcast.79), channel_id=1, source_target_pairs={{0,1},{1,0},{2,3},{3,2},{4,5},{5,4},{6,7},{7,6},{8,9},{9,8},{10,11... | collective-permute-start | bytes 3932168 | tf_op jit(solution)/shard_map/ppermute | solution.py:113
  181.1 3.4 %collective-permute-start.23 = (bf16[2,256,1280]{2,1,0:T(8,128)(2,1)}, bf16[2,256,1280]{2,1,0:T(8,128)(2,1)}, u32[]{:S(2)}, u32[]{:S(2)}) collective-permute-start(bf16[2,256,1280]{2,1,0:T(8,128)(2,1)} %pad_maximum_fusion.17), channel_id=1, source_target_pairs={{0,1},{1,0},{2,3},{3,2},{4,5},{5,4},{6,7},{7,6},{8,9},{9,8},{10,11... | collective-permute-start | bytes 3932168 | tf_op jit(solution)/shard_map/ppermute | solution.py:113
  (22 other events, 156.9 us)

commit v19 on v17

--- a/solution.py
+++ b/solution.py
@@ -180,9 +180,12 @@
     sent, attended = lax.optimization_barrier((sent, attended))
     gain_rows = lax.dynamic_slice_in_dim(head_gain, core * heads_here, heads_here, 0)
     normed_group = normalize(attended, gain_rows)
-    normed_own = pair_exchange(normed_group, core, 0, 1)
-    normed_own = normed_own.reshape(tokens_here, H * HEAD)
-    tokens = jnp.concatenate([normed_own, swap(normed_own, "c")], axis=0)
+    other_heads = swap(normed_group, "c")
+    tokens = jnp.where(
+        core == 0,
+        jnp.concatenate([normed_group, other_heads], axis=1),
+        jnp.concatenate([other_heads, normed_group], axis=1),
+    ).reshape(span, H * HEAD)
     by_block = tokens.reshape(tokens.shape[0], 32, -1)
     wide = []
     for rows, source in gather_finish(parts, sent):
@@ -190,8 +193,11 @@
         wide.append(
             jnp.dot(features, rows, preferred_element_type=jnp.float32).astype(jnp.bfloat16)
         )
-    own = [piece[:tokens_here] for piece in wide]
-    returned = [swap(piece[tokens_here:], "c") for piece in wide]
+    own = [lax.dynamic_slice_in_dim(piece, core * tokens_here, tokens_here, 0) for piece in wide]
+    returned = [
+        swap(lax.dynamic_slice_in_dim(piece, (1 - core) * tokens_here, tokens_here, 0), "c")
+        for piece in wide
+    ]
     candidates = own + returned
 
     def place(chip, side):

time: 187 us -> 183 us (0.979)
  waiting for transfers between devices: 37.2 us -> 34.1 us
    another operation x4, other arithmetic: 4.89 us -> 8.22 us  [ring_direct(): return jnp.stack([x] + shifted)]
    select_n x0 -> x1, local copies, waits for them, and re-layouts: none -> 2.97 us  [on_device(): jnp.where(core == 0, jnp.concatenate([normed_group, other_heads], axis=1)...]
    select_n x2 -> x1, other arithmetic: 3.33 us -> 0.39 us  [pair_exchange(): jnp.where(core == 0, jnp.concatenate([mine, received], axis=join_axis), j...]
    select_n x2 -> x1, local copies, waits for them, and re-layouts: 3.9 us -> 1.43 us  [pair_exchange(): jnp.where(core == 0, jnp.concatenate([mine, received], axis=join_axis), j...]
    ppermute x6, waiting for transfers between devices: 9.95 us -> 7.88 us  [ring_direct(): lax.ppermute(x, axis, [(k, (k + shift) % size) for k in range(size)])]
    ppermute x9 -> x8, waiting for transfers between devices: 7.41 us -> 5.4 us  [swap(): return lax.ppermute(x, axis, [(0, 1), (1, 0)])]
    dynamic_slice x0 -> x2, local copies, waits for them, and re-layouts: none -> 1.87 us  [on_device(): lax.dynamic_slice_in_dim(piece, (1 - core) * tokens_here, tokens_here, 0)]
    dynamic_slice x4 -> x3, local copies, waits for them, and re-layouts: 4.56 us -> 2.9 us  [pair_exchange(): mine = lax.dynamic_slice_in_dim(x, core * size, size, keep_axis)]
  transfers between devices with their start and end apart: 25 -> 24, of which waited for: 11 -> 11; matrix products, arithmetic and copies ran while one was open for 41% -> 44% of each run, Pallas kernels for 0% -> 0%
where the time goes in v19:
time: 183 us; the launch traced here: 182 us
  other arithmetic  42.6 us (23%)
  local copies, waits for them, and re-layouts  42.4 us (23%)
  starting transfers between devices  38.5 us (21%)
  waiting for transfers between devices  34.1 us (19%)
  matrix products  23.9 us (13%)
    dot_general x2, matrix products, on_device(): jnp.dot(features, rows, preferred_element_type=jnp.float32)  14.5 us
    ppermute x8, starting transfers between devices, swap(): return lax.ppermute(x, axis, [(0, 1), (1, 0)])  12.7 us
    ppermute x4, waiting for transfers between devices, ring_send(): return (lax.ppermute(x, axis, forward), lax.ppermute(x, axis, backward))  12.6 us
    max x4, local copies, waits for them, and re-layouts, featurize(): rectified = jnp.maximum(block.astype(jnp.float32), 0.0)  12 us
    another operation x2, other arithmetic, ring_finish(): return jnp.stack((x,) + tuple(received))  11.4 us
    ppermute x6, starting transfers between devices, ring_direct(): lax.ppermute(x, axis, [(k, (k + shift) % size) for k in range(size)])  11.3 us
    another operation x4, other arithmetic, ring_direct(): return jnp.stack([x] + shifted)  8.22 us
    unnamed x29, local copies, waits for them, and re-layouts  8.12 us
  transfers between devices with their start and end apart: 24, of which 11 were waited for; matrix products, arithmetic and copies ran while one was open for 44% of the time, Pallas kernels for 0%

profile of v19, /device:TPU:1, one launch (start us, length us, event | category | flops | bytes accessed | tf_op | source)
XLA Modules:
  0.0 182.4 jit_solution(17640084660232954069)
XLA Ops:
  0.7 2.7 %fusion.35 = (bf16[80,1280]{1,0:T(8,128)(2,1)S(1)}, f32[80,1280]{1,0:T(8,128)}, f32[80,1280]{1,0:T(8,128)}, f32[80,1280]{1,0:T(8,128)}) fusion(f32[80,1280]{1,0:T(8,128)} %param.16, f32[80,1280]{1,0:T(8,128)} %param.17, f32[80,1280]{1,0:T(8,128)} %param.18, f32[80,1280]{1,0:T(8,128)} %param.19), kind=kLoop, calls=%fused_computation.111 | loop fusion | flops 1638400 | bytes 3072000 | tf_op jit(solution)/shard_map/convert_element_type | solution.py:139
  3.4 3.6 %collective-permute-start.4 = (bf16[80,1280]{1,0:T(8,128)(2,1)S(1)}, bf16[80,1280]{1,0:T(8,128)(2,1)S(1)}, u32[]{:S(2)}, u32[]{:S(2)}) collective-permute-start(bf16[80,1280]{1,0:T(8,128)(2,1)S(1)} %get-tuple-element.88), channel_id=1, source_target_pairs={{0,2},{2,0},{1,3},{3,1},{4,6},{6,4},{5,7},{7,5},{8,10},{10,8},{9,1... | collective-permute-start | bytes 614408 | tf_op jit(solution)/shard_map/ppermute | solution.py:113
  7.8 3.5 %collective-permute-done.4 = bf16[80,1280]{1,0:T(8,128)(2,1)S(1)} collective-permute-done((bf16[80,1280]{1,0:T(8,128)(2,1)S(1)}, bf16[80,1280]{1,0:T(8,128)(2,1)S(1)}, u32[]{:S(2)}, u32[]{:S(2)}) %collective-permute-start.4) | collective-permute-done | bytes 204832 | tf_op jit(solution)/shard_map/ppermute | solution.py:113
  11.2 5.6 %collective-permute-done.5 = bf16[80,1280]{1,0:T(8,128)(2,1)S(1)} collective-permute-done((bf16[80,1280]{1,0:T(8,128)(2,1)S(1)}, bf16[80,1280]{1,0:T(8,128)(2,1)S(1)}, u32[]{:S(2)}, u32[]{:S(2)}) %collective-permute-start.5) | collective-permute-done | bytes 204832 | tf_op jit(solution)/shard_map/ppermute | solution.py:71
  22.8 3.3 %collective-permute-start.7 = (bf16[2,80,1280]{2,1,0:T(8,128)(2,1)}, bf16[2,80,1280]{2,1,0:T(8,128)(2,1)}, u32[]{:S(2)}, u32[]{:S(2)}) collective-permute-start(bf16[2,80,1280]{2,1,0:T(8,128)(2,1)} %get-tuple-element.107), channel_id=1, source_target_pairs={{0,64},{32,96},{64,0},{96,32},{1,65},{33,97},{65,1},{97,33},{2,66}... | collective-permute-start | bytes 1228808 | tf_op jit(solution)/shard_map/ppermute | solution.py:62
  36.8 4.3 %collective-permute-done.7 = bf16[2,80,1280]{2,1,0:T(8,128)(2,1)} collective-permute-done((bf16[2,80,1280]{2,1,0:T(8,128)(2,1)}, bf16[2,80,1280]{2,1,0:T(8,128)(2,1)}, u32[]{:S(2)}, u32[]{:S(2)}) %collective-permute-start.7) | collective-permute-done | bytes 409632 | tf_op jit(solution)/shard_map/ppermute | solution.py:62
  45.1 2.6 %pad_maximum_fusion.9 = bf16[4,2,80,1280]{3,2,1,0:T(8,128)(2,1)} fusion(bf16[1,2,80,1280]{3,2,1,0:T(8,128)(2,1)} %bitcast.15, bf16[1,2,80,1280]{3,2,1,0:T(8,128)(2,1)} %bitcast.14, bf16[1,2,80,1280]{3,2,1,0:T(8,128)(2,1)} %bitcast.13, bf16[1,2,80,1280]{3,2,1,0:T(8,128)(2,1)S(1)} %copy-done.10), kind=kLoop, calls=%fused_computation.28 | loop fusion | flops 2457600 | bytes 3276800 | tf_op jit(solution)/shard_map/stack | solution.py:65
  50.1 2.7 %pad_maximum_fusion.8 = bf16[4,2,80,1280]{3,2,1,0:T(8,128)(2,1)} fusion(bf16[1,2,80,1280]{3,2,1,0:T(8,128)(2,1)} %bitcast.9, bf16[1,2,80,1280]{3,2,1,0:T(8,128)(2,1)} %bitcast.8, bf16[1,2,80,1280]{3,2,1,0:T(8,128)(2,1)} %bitcast.7, bf16[1,2,80,1280]{3,2,1,0:T(8,128)(2,1)} %get-tuple-element.108), kind=kLoop, calls=%fused_computation.27 | loop fusion | flops 2457600 | bytes 3276800 | tf_op jit(solution)/shard_map/stack | solution.py:65
  62.1 4.1 %convert_maximum_fusion = (f32[512,10,128]{0,2,1:T(8,128)S(1)}, f32[512,10,128]{0,2,1:T(8,128)}) fusion(bf16[256,10,128]{0,2,1:T(8,128)(2,1)} %collective-permute-done.19, bf16[256,10,128]{0,2,1:T(8,128)(2,1)} %get-tuple-element.100, pred[]{:T(512)S(6)} %eq.17, bf16[256,10,128]{0,2,1:T(8,128)(2,1)S(1)} %get-tuple-element.104, bf16[256,10,128]{0,2,1:T(8,128)(2,1)} %copy-done.12), kind=kLoop, calls=%fused_computation.22 | loop fusion | flops 14417920 | bytes 7864321 | tf_op jit(solution)/shard_map/max | solution.py:97
  66.1 3.3 %copy.15 = f32[512,10,128]{2,0,1:T(8,128)} copy(f32[512,10,128]{0,2,1:T(8,128)} %get-tuple-element.117) | data formatting | bytes 5242880 | tf_op jit(solution)/shard_map/max | solution.py:97
  69.4 3.2 %copy.16 = f32[4,128,10,128]{1,3,2,0:T(8,128)} copy(f32[4,128,10,128]{3,1,0,2:T(8,128)} %bitcast.61) | data formatting | bytes 5242880 | tf_op jit(solution)/shard_map/max | solution.py:97
  74.7 3.4 %copy.22 = f32[4,128,10,128]{1,3,2,0:T(8,128)} copy(f32[4,128,10,128]{3,1,0,2:T(8,128)} %bitcast.62) | data formatting | bytes 5242880 | tf_op jit(solution)/shard_map/max | solution.py:97
  78.1 4.2 %multiply_convert_fusion.4 = (bf16[4,128,10,128]{1,3,2,0:T(8,128)(2,1)S(1)}, bf16[4,128,10,128]{1,3,2,0:T(8,128)(2,1)S(1)}, bf16[4,128,10,128]{1,3,2,0:T(8,128)(2,1)}, bf16[4,128,10,128]{1,3,2,0:T(8,128)(2,1)}) fusion(f32[4,128,10,128]{1,3,2,0:T(8,128)S(1)} %copy-done.3, f32[4,128]{1,0:T(4,128)S(1)} %get-tuple-element.119, ...), kind=kLoop, calls=%fused_computation.24 | loop fusion | flops 5242880 | bytes 10489856 | tf_op jit(solution)/shard_map/convert.2
  84.3 11.5 %collective-permute-done.10 = bf16[4,2,80,1280]{3,2,1,0:T(8,128)(2,1)} collective-permute-done((bf16[4,2,80,1280]{3,2,1,0:T(8,128)(2,1)}, bf16[4,2,80,1280]{3,2,1,0:T(8,128)(2,1)}, u32[]{:S(2)}, u32[]{:S(2)}) %collective-permute-start.10) | collective-permute-done | bytes 1638432 | tf_op jit(solution)/shard_map/ppermute | solution.py:29
  96.9 4.1 %collective-permute-start.20 = (f32[10,256,128]{2,1,0:T(8,128)}, f32[10,256,128]{2,1,0:T(8,128)}, u32[]{:S(2)}, u32[]{:S(2)}) collective-permute-start(f32[10,256,128]{2,1,0:T(8,128)} %get-tuple-element.80), channel_id=1, source_target_pairs={{0,2},{1,3},{4,6},{5,7},{8,10},{9,11},{12,14},{13,15},{16,18},{17,... | collective-permute-start | bytes 3932168 | tf_op jit(solution)/shard_map/ppermute | solution.py:164
  120.7 4.8 %fusion.3 = f32[4,10,128,128]{2,3,1,0:T(8,128)} fusion(bf16[4,128,10,128]{1,3,2,0:T(8,128)(2,1)S(1)} %copy-done.4, bf16[4,128,10,128]{1,3,2,0:T(8,128)(2,1)S(1)} %copy-done.5, bf16[4,128,10,128]{1,3,2,0:T(8,128)(2,1)} %copy-done.7, bf16[4,128,10,128]{1,3,2,0:T(8,128)(2,1)} %copy-done.6, pred[128,128]{1,0:T(8,128)(4,1)S(1)} %iota_compare_fusion, ...), kind=kOutput, calls=%fused_computation.31 | convolution fusion | flops 515112960 | bytes 9191424 | tf_op jit(solution)/shard_map/chij,cjhe->cihe/dot_general | solution.py:170
  135.6 3.8 %collective-permute-start.21 = (bf16[512,10,128]{2,0,1:T(8,128)(2,1)S(1)}, bf16[512,10,128]{2,0,1:T(8,128)(2,1)S(1)}, u32[]{:S(2)}, u32[]{:S(2)}) collective-permute-start(bf16[512,10,128]{2,0,1:T(8,128)(2,1)S(1)} %multiply_convert_fusion), channel_id=1, source_target_pairs={{0,1},{1,0},{2,3},{3,2},{4,5},{5,4},{6,7},{7,6},{8,9},{9,8},{10,11... | collective-permute-start | bytes 3932168 | tf_op jit(solution)/shard_map/ppermute | solution.py:113
  139.4 5.7 %pad_maximum_fusion.1 = bf16[4,4,2,80,1280]{4,3,2,1,0:T(8,128)(2,1)} fusion(bf16[1,4,2,80,1280]{4,3,2,1,0:T(8,128)(2,1)} %bitcast.39, bf16[1,4,2,80,1280]{4,3,2,1,0:T(8,128)(2,1)S(1)} %bitcast.65, bf16[1,4,2,80,1280]{4,3,2,1,0:T(8,128)(2,1)} %bitcast.37, bf16[1,4,2,80,1280]{4,3,2,1,0:T(8,128)(2,1)} %bitcast.36), kind=kLoop, calls=%fused_computation.7 | loop fusion | flops 9830400 | bytes 13107200 | tf_op jit(solution)/shard_map/stack | solution.py:50
  145.1 5.7 %pad_maximum_fusion = bf16[4,4,2,80,1280]{4,3,2,1,0:T(8,128)(2,1)} fusion(bf16[1,4,2,80,1280]{4,3,2,1,0:T(8,128)(2,1)} %bitcast.31, bf16[1,4,2,80,1280]{4,3,2,1,0:T(8,128)(2,1)S(1)} %bitcast.66, bf16[1,4,2,80,1280]{4,3,2,1,0:T(8,128)(2,1)} %bitcast.29, bf16[1,4,2,80,1280]{4,3,2,1,0:T(8,128)(2,1)} %bitcast.28), kind=kLoop, calls=%fused_computation.6 | loop fusion | flops 9830400 | bytes 13107200 | tf_op jit(solution)/shard_map/stack | solution.py:50
  152.5 3.0 %copy.27 = bf16[512,20,128]{0,2,1:T(8,128)(2,1)S(1)} copy(bf16[512,20,128]{2,0,1:T(8,128)(2,1)} %maximum_select_fusion) | data formatting | bytes 5242880 | tf_op jit(solution)/shard_map/jit(_where)/select_n | solution.py:184
  157.7 7.3 %convolution_convert_fusion = bf16[512,1280]{1,0:T(8,128)(2,1)S(1)} fusion(bf16[512,2560]{0,1:T(8,128)(2,1)} %bitcast.64, bf16[2560,1280]{1,0:T(8,128)(2,1)} %bitcast.68), kind=kOutput, calls=%fused_computation.9 | convolution fusion | flops 3356098560 | bytes 10485760 | tf_op jit(solution)/shard_map/dot_general | solution.py:194
  168.2 7.3 %convolution_convert_fusion.1 = bf16[512,1280]{1,0:T(8,128)(2,1)S(1)} fusion(bf16[512,2560]{0,1:T(8,128)(2,1)} %bitcast.63, bf16[2560,1280]{1,0:T(8,128)(2,1)} %bitcast.67), kind=kOutput, calls=%fused_computation.10 | convolution fusion | flops 3356098560 | bytes 10485760 | tf_op jit(solution)/shard_map/dot_general | solution.py:194
  178.8 2.9 %conditional.1 = (bf16[1,256,5120]{2,1,0:T(8,128)(2,1)}) conditional(s32[]{:T(128)} %clamp.3, (bf16[256,1280]{1,0:T(8,128)(2,1)S(1)}, bf16[256,1280]{1,0:T(8,128)(2,1)S(1)}, bf16[256,1280]{1,0:T(8,128)(2,1)S(1)}, bf16[256,1280]{1,0:T(8,128)(2,1)}) %tuple.30, (bf16[256,1280]{1,0:T(8,128)(2,1)S(1)}, ...), branch_computations={%region_3.4_spmd, %region_4.5_spmd, %region_5.6_spmd, %region_6.7_... | conditional | flops 10485760 | bytes 5242888 | solution.py:211
  178.8 2.9 %maximum_bitcast_fusion.1 = bf16[1,256,5120]{2,1,0:T(8,128)(2,1)} fusion(bf16[256,1280]{1,0:T(8,128)(2,1)S(1)} %get-tuple-element.45, bf16[256,1280]{1,0:T(8,128)(2,1)} %get-tuple-element.44, bf16[256,1280]{1,0:T(8,128)(2,1)S(1)} %get-tuple-element.43, bf16[256,1280]{1,0:T(8,128)(2,1)S(1)} %get-tuple-element.42), kind=kLoop, calls=%fused_computation.3 | loop fusion | flops 10485760 | bytes 5242880 | tf_op jit(solution)/shard_map/broadcast_in_dim | solution.py:212
  (103 shorter events, 79.0 us)
Async XLA Ops:
  3.4 7.9 %collective-permute-start.4 = (bf16[80,1280]{1,0:T(8,128)(2,1)S(1)}, bf16[80,1280]{1,0:T(8,128)(2,1)S(1)}, u32[]{:S(2)}, u32[]{:S(2)}) collective-permute-start(bf16[80,1280]{1,0:T(8,128)(2,1)S(1)} %get-tuple-element.88), channel_id=1, source_target_pairs={{0,2},{2,0},{1,3},{3,1},{4,6},{6,4},{5,7},{7,5},{8,10},{10,8},{9,1... | collective-permute-start | bytes 614408 | tf_op jit(solution)/shard_map/ppermute | solution.py:113
  6.9 9.9 %collective-permute-start.5 = (bf16[80,1280]{1,0:T(8,128)(2,1)S(1)}, bf16[80,1280]{1,0:T(8,128)(2,1)S(1)}, u32[]{:S(2)}, u32[]{:S(2)}) collective-permute-start(bf16[80,1280]{1,0:T(8,128)(2,1)S(1)} %get-tuple-element.88), channel_id=1, source_target_pairs={{0,18},{2,16},{16,2},{18,0},{1,19},{3,17},{17,3},{19,1},{4,22},{6,... | collective-permute-start | bytes 614408 | tf_op jit(solution)/shard_map/ppermute | solution.py:71
  7.8 19.1 %collective-permute-start = (bf16[80,1280]{1,0:T(8,128)(2,1)S(1)}, bf16[80,1280]{1,0:T(8,128)(2,1)}, u32[]{:S(2)}, u32[]{:S(2)}) collective-permute-start(bf16[80,1280]{1,0:T(8,128)(2,1)S(1)} %get-tuple-element.88), channel_id=1, source_target_pairs={{0,16},{16,0},{1,17},{17,1},{2,18},{18,2},{3,19},{19,3},{4,20},{20... | collective-permute-start | bytes 614408 | tf_op jit(solution)/shard_map/ppermute | solution.py:113
  17.8 14.9 %collective-permute-start.6 = (bf16[2,80,1280]{2,1,0:T(8,128)(2,1)}, bf16[2,80,1280]{2,1,0:T(8,128)(2,1)}, u32[]{:S(2)}, u32[]{:S(2)}) collective-permute-start(bf16[2,80,1280]{2,1,0:T(8,128)(2,1)} %get-tuple-element.107), channel_id=1, source_target_pairs={{0,32},{32,64},{64,96},{96,0},{1,33},{33,65},{65,97},{97,1},{2,34}... | collective-permute-start | bytes 1228808 | tf_op jit(solution)/shard_map/ppermute | solution.py:62
  22.8 18.3 %collective-permute-start.7 = (bf16[2,80,1280]{2,1,0:T(8,128)(2,1)}, bf16[2,80,1280]{2,1,0:T(8,128)(2,1)}, u32[]{:S(2)}, u32[]{:S(2)}) collective-permute-start(bf16[2,80,1280]{2,1,0:T(8,128)(2,1)} %get-tuple-element.107), channel_id=1, source_target_pairs={{0,64},{32,96},{64,0},{96,32},{1,65},{33,97},{65,1},{97,33},{2,66}... | collective-permute-start | bytes 1228808 | tf_op jit(solution)/shard_map/ppermute | solution.py:62
  26.1 17.6 %collective-permute-start.8 = (bf16[2,80,1280]{2,1,0:T(8,128)(2,1)}, bf16[2,80,1280]{2,1,0:T(8,128)(2,1)}, u32[]{:S(2)}, u32[]{:S(2)}) collective-permute-start(bf16[2,80,1280]{2,1,0:T(8,128)(2,1)} %get-tuple-element.107), channel_id=1, source_target_pairs={{0,96},{32,0},{64,32},{96,64},{1,97},{33,1},{65,33},{97,65},{2,98}... | collective-permute-start | bytes 1228808 | tf_op jit(solution)/shard_map/ppermute | solution.py:62
  28.8 19.0 %collective-permute-start.1 = (bf16[2,80,1280]{2,1,0:T(8,128)(2,1)}, bf16[2,80,1280]{2,1,0:T(8,128)(2,1)}, u32[]{:S(2)}, u32[]{:S(2)}) collective-permute-start(bf16[2,80,1280]{2,1,0:T(8,128)(2,1)} %get-tuple-element.109), channel_id=1, source_target_pairs={{0,4},{4,8},{8,12},{12,0},{1,5},{5,9},{9,13},{13,1},{2,6},{6,10},{... | collective-permute-start | bytes 1228808 | tf_op jit(solution)/shard_map/ppermute | solution.py:62
  30.1 19.9 %collective-permute-start.2 = (bf16[2,80,1280]{2,1,0:T(8,128)(2,1)}, bf16[2,80,1280]{2,1,0:T(8,128)(2,1)}, u32[]{:S(2)}, u32[]{:S(2)}) collective-permute-start(bf16[2,80,1280]{2,1,0:T(8,128)(2,1)} %get-tuple-element.109), channel_id=1, source_target_pairs={{0,8},{4,12},{8,0},{12,4},{1,9},{5,13},{9,1},{13,5},{2,10},{6,14},... | collective-permute-start | bytes 1228808 | tf_op jit(solution)/shard_map/ppermute | solution.py:62
  32.7 17.4 %collective-permute-start.3 = (bf16[2,80,1280]{2,1,0:T(8,128)(2,1)}, bf16[2,80,1280]{2,1,0:T(8,128)(2,1)}, u32[]{:S(2)}, u32[]{:S(2)}) collective-permute-start(bf16[2,80,1280]{2,1,0:T(8,128)(2,1)} %get-tuple-element.109), channel_id=1, source_target_pairs={{0,12},{4,0},{8,4},{12,8},{1,13},{5,1},{9,5},{13,9},{2,14},{6,2},{... | collective-permute-start | bytes 1228808 | tf_op jit(solution)/shard_map/ppermute | solution.py:62
  41.1 17.6 %collective-permute-start.13 = (bf16[256,10,128]{0,2,1:T(8,128)(2,1)}, bf16[256,10,128]{0,2,1:T(8,128)(2,1)S(1)}, u32[]{:S(2)}, u32[]{:S(2)}) collective-permute-start(bf16[256,10,128]{0,2,1:T(8,128)(2,1)} %get-tuple-element.105), channel_id=1, source_target_pairs={{0,1},{1,0},{2,3},{3,2},{4,5},{5,4},{6,7},{7,6},{8,9},{9,8},{10,11... | collective-permute-start | bytes 1966088 | tf_op jit(solution)/shard_map/ppermute | solution.py:113
  43.7 15.0 %collective-permute-start.14 = (bf16[256,10,128]{0,2,1:T(8,128)(2,1)}, bf16[256,10,128]{0,2,1:T(8,128)(2,1)S(1)}, u32[]{:S(2)}, u32[]{:S(2)}) collective-permute-start(bf16[256,10,128]{0,2,1:T(8,128)(2,1)} %get-tuple-element.103), channel_id=1, source_target_pairs={{0,1},{1,0},{2,3},{3,2},{4,5},{5,4},{6,7},{7,6},{8,9},{9,8},{10,11... | collective-permute-start | bytes 1966088 | tf_op jit(solution)/shard_map/ppermute | solution.py:113
  53.8 8.3 %collective-permute-start.19 = (bf16[256,10,128]{0,2,1:T(8,128)(2,1)S(1)}, bf16[256,10,128]{0,2,1:T(8,128)(2,1)}, u32[]{:S(2)}, u32[]{:S(2)}) collective-permute-start(bf16[256,10,128]{0,2,1:T(8,128)(2,1)S(1)} %get-tuple-element.101), channel_id=1, source_target_pairs={{0,1},{1,0},{2,3},{3,2},{4,5},{5,4},{6,7},{7,6},{8,9},{9,8},{10,11... | collective-permute-start | bytes 1966088 | tf_op jit(solution)/shard_map/ppermute | solution.py:113
  55.9 39.9 %collective-permute-start.11 = (bf16[4,2,80,1280]{3,2,1,0:T(8,128)(2,1)}, bf16[4,2,80,1280]{3,2,1,0:T(8,128)(2,1)}, u32[]{:S(2)}, u32[]{:S(2)}) collective-permute-start(bf16[4,2,80,1280]{3,2,1,0:T(8,128)(2,1)} %pad_maximum_fusion.9), channel_id=1, source_target_pairs={{0,4},{4,8},{8,12},{12,0},{1,5},{5,9},{9,13},{13,1},{2,6},{6,10},{... | collective-permute-start | bytes 4915208 | tf_op jit(solution)/shard_map/ppermute | solution.py:29
  57.6 38.2 %collective-permute-start.12 = (bf16[4,2,80,1280]{3,2,1,0:T(8,128)(2,1)}, bf16[4,2,80,1280]{3,2,1,0:T(8,128)(2,1)}, u32[]{:S(2)}, u32[]{:S(2)}) collective-permute-start(bf16[4,2,80,1280]{3,2,1,0:T(8,128)(2,1)} %pad_maximum_fusion.9), channel_id=1, source_target_pairs={{0,12},{4,0},{8,4},{12,8},{1,13},{5,1},{9,5},{13,9},{2,14},{6,2},{... | collective-permute-start | bytes 4915208 | tf_op jit(solution)/shard_map/ppermute | solution.py:29
  58.7 37.1 %collective-permute-start.10 = (bf16[4,2,80,1280]{3,2,1,0:T(8,128)(2,1)}, bf16[4,2,80,1280]{3,2,1,0:T(8,128)(2,1)}, u32[]{:S(2)}, u32[]{:S(2)}) collective-permute-start(bf16[4,2,80,1280]{3,2,1,0:T(8,128)(2,1)} %pad_maximum_fusion.8), channel_id=1, source_target_pairs={{0,96},{32,0},{64,32},{96,64},{1,97},{33,1},{65,33},{97,65},{2,98}... | collective-permute-start | bytes 4915208 | tf_op jit(solution)/shard_map/ppermute | solution.py:29
  58.7 38.2 %collective-permute-start.9 = (bf16[4,2,80,1280]{3,2,1,0:T(8,128)(2,1)}, bf16[4,2,80,1280]{3,2,1,0:T(8,128)(2,1)}, u32[]{:S(2)}, u32[]{:S(2)}) collective-permute-start(bf16[4,2,80,1280]{3,2,1,0:T(8,128)(2,1)} %pad_maximum_fusion.8), channel_id=1, source_target_pairs={{0,32},{32,64},{64,96},{96,0},{1,33},{33,65},{65,97},{97,1},{2,34}... | collective-permute-start | bytes 4915208 | tf_op jit(solution)/shard_map/ppermute | solution.py:29
  96.9 34.3 %collective-permute-start.20 = (f32[10,256,128]{2,1,0:T(8,128)}, f32[10,256,128]{2,1,0:T(8,128)}, u32[]{:S(2)}, u32[]{:S(2)}) collective-permute-start(f32[10,256,128]{2,1,0:T(8,128)} %get-tuple-element.80), channel_id=1, source_target_pairs={{0,2},{1,3},{4,6},{5,7},{8,10},{9,11},{12,14},{13,15},{16,18},{17,... | collective-permute-start | bytes 3932168 | tf_op jit(solution)/shard_map/ppermute | solution.py:164
  103.1 22.5 %collective-permute-start.17 = (bf16[2,2,80,1280]{3,2,1,0:T(8,128)(2,1)}, bf16[2,2,80,1280]{3,2,1,0:T(8,128)(2,1)}, u32[]{:S(2)}, u32[]{:S(2)}) collective-permute-start(bf16[2,2,80,1280]{3,2,1,0:T(8,128)(2,1)} %slice.17), channel_id=1, source_target_pairs={{0,4},{4,8},{8,12},{12,0},{1,5},{5,9},{9,13},{13,1},{2,6},{6,10},{... | collective-permute-start | bytes 2457608 | tf_op jit(solution)/shard_map/ppermute | solution.py:41
  105.5 20.1 %collective-permute-start.18 = (bf16[2,2,80,1280]{3,2,1,0:T(8,128)(2,1)}, bf16[2,2,80,1280]{3,2,1,0:T(8,128)(2,1)}, u32[]{:S(2)}, u32[]{:S(2)}) collective-permute-start(bf16[2,2,80,1280]{3,2,1,0:T(8,128)(2,1)} %slice.18), channel_id=1, source_target_pairs={{0,12},{4,0},{8,4},{12,8},{1,13},{5,1},{9,5},{13,9},{2,14},{6,2},{... | collective-permute-start | bytes 2457608 | tf_op jit(solution)/shard_map/ppermute | solution.py:42
  110.0 18.7 %collective-permute-start.15 = (bf16[2,2,80,1280]{3,2,1,0:T(8,128)(2,1)}, bf16[2,2,80,1280]{3,2,1,0:T(8,128)(2,1)S(1)}, u32[]{:S(2)}, u32[]{:S(2)}) collective-permute-start(bf16[2,2,80,1280]{3,2,1,0:T(8,128)(2,1)} %slice.15), channel_id=1, source_target_pairs={{0,32},{32,64},{64,96},{96,0},{1,33},{33,65},{65,97},{97,1},{2,34}... | collective-permute-start | bytes 2457608 | tf_op jit(solution)/shard_map/ppermute | solution.py:41
  112.2 17.7 %collective-permute-start.16 = (bf16[2,2,80,1280]{3,2,1,0:T(8,128)(2,1)}, bf16[2,2,80,1280]{3,2,1,0:T(8,128)(2,1)}, u32[]{:S(2)}, u32[]{:S(2)}) collective-permute-start(bf16[2,2,80,1280]{3,2,1,0:T(8,128)(2,1)} %slice.16), channel_id=1, source_target_pairs={{0,96},{32,0},{64,32},{96,64},{1,97},{33,1},{65,33},{97,65},{2,98}... | collective-permute-start | bytes 2457608 | tf_op jit(solution)/shard_map/ppermute | solution.py:42
  135.6 15.2 %collective-permute-start.21 = (bf16[512,10,128]{2,0,1:T(8,128)(2,1)S(1)}, bf16[512,10,128]{2,0,1:T(8,128)(2,1)S(1)}, u32[]{:S(2)}, u32[]{:S(2)}) collective-permute-start(bf16[512,10,128]{2,0,1:T(8,128)(2,1)S(1)} %multiply_convert_fusion), channel_id=1, source_target_pairs={{0,1},{1,0},{2,3},{3,2},{4,5},{5,4},{6,7},{7,6},{8,9},{9,8},{10,11... | collective-permute-start | bytes 3932168 | tf_op jit(solution)/shard_map/ppermute | solution.py:113
  165.9 10.9 %collective-permute-start.23 = (bf16[256,1280]{1,0:T(8,128)(2,1)}, bf16[256,1280]{1,0:T(8,128)(2,1)}, u32[]{:S(2)}, u32[]{:S(2)}) collective-permute-start(bf16[256,1280]{1,0:T(8,128)(2,1)} %get-tuple-element.96), channel_id=1, source_target_pairs={{0,1},{1,0},{2,3},{3,2},{4,5},{5,4},{6,7},{7,6},{8,9},{9,8},{10,11... | collective-permute-start | bytes 1966088 | tf_op jit(solution)/shard_map/ppermute | solution.py:113
  176.4 2.4 %collective-permute-start.22 = (bf16[256,1280]{1,0:T(8,128)(2,1)}, bf16[256,1280]{1,0:T(8,128)(2,1)S(1)}, u32[]{:S(2)}, u32[]{:S(2)}) collective-permute-start(bf16[256,1280]{1,0:T(8,128)(2,1)} %get-tuple-element.98), channel_id=1, source_target_pairs={{0,1},{1,0},{2,3},{3,2},{4,5},{5,4},{6,7},{7,6},{8,9},{9,8},{10,11... | collective-permute-start | bytes 1966088 | tf_op jit(solution)/shard_map/ppermute | solution.py:113
  (14 other events, 123.5 us)
